TPU v7x, 32 devices: a whole 2x2x4 slice. The times are simulated.
32 devices in a mesh: blk: 4 (over z), rows: 8 (over y, x, core).
Axes of the slice: x: 2, y: 2, z: 4, core: 2. Of those that a mesh axis runs over, the one named last changes fastest.
Arguments:
- features: bfloat16 [4, 4096, 2048], P(None, ('blk', 'rows')), may hold values from -6 to 6
- owner_ids: int32 [4096, 1], P(('blk', 'rows')), may hold values from 0 to 7; in each aligned block of 128 rows (0 to 127, 128 to 255, ...) at most 32 rows name the same one
- test_blocks: bfloat16 [4, 192, 2048], P(None, 'blk'), may hold values from -0.0625 to 0.0625
Outputs:
- scores: bfloat16 [8192, 192], P(('blk', 'rows'))
Inputs may be any that keep to these rules, and one draw needn't show every extreme that they name: `owner_ids`: within each aligned block of 128 rows (the rows of one device) no owner is named more than 32 times.
All inputs are finite; a program needn't handle non-finite values.
Results may differ from a plain program's by a relative error of at most 0.001.
Values may be sent and summed in bfloat16 or wider, within the bound.
No kernel may reach another device: no remote copies, remote signals or barrier semaphores. Data moves between devices by JAX's collectives and lax.ppermute only.
A program may use at most 128 MiB of HBM per device.

v0:
```python
import jax
import jax.numpy as jnp
from jax import lax
from jax.sharding import PartitionSpec as P


def passed_along(value, axis, steps):
    count = lax.axis_size(axis)
    pairs = [(source, (source + steps) % count) for source in range(count)]
    return lax.ppermute(value, axis, pairs)


def score_block(train_rows, piece):
    return jnp.einsum("rlk,rnk->ln", train_rows, piece, preferred_element_type=jnp.float32)


def all_scores(train_rows, test_blocks):
    count = lax.axis_size("blk")
    here = lax.axis_index("blk")
    width = test_blocks.shape[1]
    empty = jnp.zeros((train_rows.shape[1], count * width), jnp.float32)

    def place(total, block, step):
        anchor = (here - step) % count
        return lax.dynamic_update_slice(
            total, score_block(train_rows, block), (jnp.int32(0), anchor * width)
        )

    def advance(step, carry):
        total, block = carry
        total = place(total, block, step)
        block = passed_along(block, "blk", 1)
        return (total, block)

    total, block = lax.fori_loop(0, count - 1, advance, (empty, test_blocks))
    return place(total, block, count - 1)


def on_device(features, owner_ids, test_blocks):
    owners_n = lax.axis_size("rows")
    local_rows = features.shape[1]
    capacity = 2 * local_rows // owners_n
    owner = owner_ids[:, 0]
    onehot = (owner[:, None] == jnp.arange(owners_n, dtype=jnp.int32)[None, :]).astype(jnp.int32)
    before = jnp.cumsum(onehot, axis=0) - onehot
    rank = jnp.sum(before * onehot, axis=1)
    slot = owner * capacity + rank
    outbox = jnp.zeros((features.shape[0], owners_n * capacity, features.shape[2]), jnp.bfloat16)
    outbox = outbox.at[:, slot].set(features)
    arrived = lax.all_to_all(outbox, "rows", split_axis=1, concat_axis=1, tiled=True)
    return all_scores(arrived, test_blocks).astype(jnp.bfloat16)


def solution(mesh):
    return jax.shard_map(
        on_device,
        mesh=mesh,
        in_specs=(P(None, ("blk", "rows"), None), P(("blk", "rows"), None), P(None, "blk", None)),
        out_specs=P(("blk", "rows"), None),
        check_vma=False,
    )
```

profile of v0, /device:TPU:2, one launch (start us, length us, event | category | flops | bytes accessed | tf_op | source)
XLA Modules:
  0.0 155.0 jit_solution(18293060421333860618)
XLA Ops:
  0.0 0.7 fusion.2
  0.7 0.2 reduce_window_sum.11
  0.9 0.8 select_reduce_fusion
  1.7 0.7 fusion.3
  2.4 3.2 %copy.6 = bf16[128,4,2048]{2,1,0:T(4,128)(2,1)S(1)} copy(bf16[128,4,2048]{2,0,1:T(8,128)(2,1)} %bitcast.25) | data formatting | bytes 4194304 | tf_op args[0]
  5.6 4.1 %broadcast_in_dim.9 = bf16[4,256,2048]{2,0,1:T(4,128)(2,1)} broadcast(bf16[]{:T(256)} %constant.92.clone.1), dimensions={} | broadcast | bytes 4194306 | tf_op jit(solution)/shard_map/broadcast_in_dim | solution.py:48
  9.7 15.8 %scatter_fusion = bf16[4,256,2048]{2,0,1:T(4,128)(2,1)} fusion(bf16[4,256,2048]{2,0,1:T(4,128)(2,1)} %broadcast_in_dim.9, s32[128]{0:T(128)S(1)} %fusion.3, bf16[128,4,2048]{2,1,0:T(4,128)(2,1)S(1)} %copy.6), kind=kCustom, calls=%fused_computation | custom fusion | bytes 6291968 | tf_op jit(solution)/shard_map/scatter | solution.py:49
  25.5 4.7 %all-to-all-start = ((bf16[4,256,2048]{2,0,1:T(4,128)(2,1)}), bf16[4,256,2048]{2,0,1:T(4,128)(2,1)}, u32[]{:S(2)}, u32[]{:S(2)}) async-start(bf16[4,256,2048]{2,0,1:T(4,128)(2,1)} %scatter_fusion), calls=%async_computation | async-start | bytes 8388608 | tf_op jit(solution)/shard_map/all_to_all | solution.py:50
  30.2 0.0 copy-start
  30.2 47.3 %all-to-all-done = bf16[4,256,2048]{2,0,1:T(4,128)(2,1)} async-done(((bf16[4,256,2048]{2,0,1:T(4,128)(2,1)}), bf16[4,256,2048]{2,0,1:T(4,128)(2,1)}, u32[]{:S(2)}, u32[]{:S(2)}) %all-to-all-start) | async-done | bytes 4194336 | tf_op jit(solution)/shard_map/all_to_all | solution.py:50
  77.5 6.5 %copy.7 = bf16[4,256,2048]{2,1,0:T(8,128)(2,1)} copy(bf16[4,256,2048]{2,0,1:T(4,128)(2,1)} %all-to-all-done) | data formatting | bytes 8388608 | tf_op jit(solution)/shard_map/while | solution.py:35
  84.0 0.0 copy-done
  84.0 63.0 %while.17 = (s32[]{:T(128)}, bf16[256,192]{0,1:T(8,128)(2,1)S(1)}, bf16[4,48,2048]{2,1,0:T(8,128)(2,1)S(1)}, bf16[4,256,2048]{2,1,0:T(8,128)(2,1)}, s32[]{:T(128...) while((s32[]{:T(128)}, bf16[256,192]{0,1:T(8,128)(2,1)S(1)}, ...), condition=%wide.region_4.5_spmd, body=%wide.region_3.4_spmd.sunk | while | flops 201326608 | bytes 9748800 | solution.py:35
  84.0 0.1 copy.18
  84.1 2.2 %collective-permute-start = (bf16[4,48,2048]{2,1,0:T(8,128)(2,1)S(1)}, bf16[4,48,2048]{2,1,0:T(8,128)(2,1)S(1)}, u32[]{:S(2)}, u32[]{:S(2)}) collective-permute-start(bf16[4,48,2048]{2,1,0:T(8,128)(2,1)S(1)} %copy.18), channel_id=1, source_target_pairs={{0,8},{8,16},{16,24},{24,0},{1,9},{9,17},{17,25},{25,1},{2,10},{10... | collective-permute-start | bytes 2359304 | tf_op jit(solution)/shard_map/while/body/eval_jaxpr/ppermute | solution.py:10
  86.3 3.6 %fusion.13 = bf16[256,192]{0,1:T(8,128)(2,1)S(1)} fusion(bf16[256,192]{0,1:T(8,128)(2,1)S(1)} %get-tuple-element.199, s32[]{:T(128)S(6)} %select_n.50, bf16[4,256,2048]{2,1,0:T(8,128)(2,1)} %get-tuple-element.212, bf16[4,48,2048]{2,1,0:T(8,128)(2,1)S(1)} %copy.18), kind=kOutput, calls=%fused_computation.2.clone.1 | convolution fusion | flops 201326592 | bytes 5029892 | tf_op jit(solution)/shard_map/while/body/eval_jaxpr/rlk,rnk->ln/dot_general | solution.py:14
  89.9 16.2 %collective-permute-done = bf16[4,48,2048]{2,1,0:T(8,128)(2,1)S(1)} collective-permute-done((bf16[4,48,2048]{2,1,0:T(8,128)(2,1)S(1)}, bf16[4,48,2048]{2,1,0:T(8,128)(2,1)S(1)}, u32[]{:S(2)}, u32[]{:S(2)}) %collective-permute-start) | collective-permute-done | bytes 786464 | tf_op jit(solution)/shard_map/while/body/eval_jaxpr/ppermute | solution.py:10
  106.1 0.1 copy.18
  106.2 0.1 collective-permute-start
  106.3 3.6 %fusion.13 = bf16[256,192]{0,1:T(8,128)(2,1)S(1)} fusion(bf16[256,192]{0,1:T(8,128)(2,1)S(1)} %get-tuple-element.199, s32[]{:T(128)S(6)} %select_n.50, bf16[4,256,2048]{2,1,0:T(8,128)(2,1)} %get-tuple-element.212, bf16[4,48,2048]{2,1,0:T(8,128)(2,1)S(1)} %copy.18), kind=kOutput, calls=%fused_computation.2.clone.1 | convolution fusion | flops 201326592 | bytes 5029892 | tf_op jit(solution)/shard_map/while/body/eval_jaxpr/rlk,rnk->ln/dot_general | solution.py:14
  109.9 17.2 %collective-permute-done = bf16[4,48,2048]{2,1,0:T(8,128)(2,1)S(1)} collective-permute-done((bf16[4,48,2048]{2,1,0:T(8,128)(2,1)S(1)}, bf16[4,48,2048]{2,1,0:T(8,128)(2,1)S(1)}, u32[]{:S(2)}, u32[]{:S(2)}) %collective-permute-start) | collective-permute-done | bytes 786464 | tf_op jit(solution)/shard_map/while/body/eval_jaxpr/ppermute | solution.py:10
  127.0 0.1 copy.18
  127.1 0.1 collective-permute-start
  127.2 3.6 %fusion.13 = bf16[256,192]{0,1:T(8,128)(2,1)S(1)} fusion(bf16[256,192]{0,1:T(8,128)(2,1)S(1)} %get-tuple-element.199, s32[]{:T(128)S(6)} %select_n.50, bf16[4,256,2048]{2,1,0:T(8,128)(2,1)} %get-tuple-element.212, bf16[4,48,2048]{2,1,0:T(8,128)(2,1)S(1)} %copy.18), kind=kOutput, calls=%fused_computation.2.clone.1 | convolution fusion | flops 201326592 | bytes 5029892 | tf_op jit(solution)/shard_map/while/body/eval_jaxpr/rlk,rnk->ln/dot_general | solution.py:14
  130.8 16.3 %collective-permute-done = bf16[4,48,2048]{2,1,0:T(8,128)(2,1)S(1)} collective-permute-done((bf16[4,48,2048]{2,1,0:T(8,128)(2,1)S(1)}, bf16[4,48,2048]{2,1,0:T(8,128)(2,1)S(1)}, u32[]{:S(2)}, u32[]{:S(2)}) %collective-permute-start) | collective-permute-done | bytes 786464 | tf_op jit(solution)/shard_map/while/body/eval_jaxpr/ppermute | solution.py:10
  147.0 0.0 copy-start.1
  147.0 0.6 copy-done.1
  147.7 7.3 %fusion.1 = bf16[256,192]{0,1:T(8,128)(2,1)} fusion(bf16[256,192]{0,1:T(8,128)(2,1)} %copy-done.1, s32[]{:T(128)S(6)} %select_n.43, bf16[4,48,2048]{2,1,0:T(8,128)(2,1)S(1)} %get-tuple-element.140, bf16[4,256,2048]{2,0,1:T(4,128)(2,1)} %all-to-all-done), kind=kOutput, calls=%fused_computation.4 | convolution fusion | flops 201326592 | bytes 5029892 | tf_op jit(solution)/shard_map/rlk,rnk->ln/dot_general | solution.py:14
  (1 shorter events, 0.0 us)
Async XLA Ops:
  25.5 52.0 %all-to-all-start = ((bf16[4,256,2048]{2,0,1:T(4,128)(2,1)}), bf16[4,256,2048]{2,0,1:T(4,128)(2,1)}, u32[]{:S(2)}, u32[]{:S(2)}) async-start(bf16[4,256,2048]{2,0,1:T(4,128)(2,1)} %scatter_fusion), calls=%async_computation | async-start | bytes 8388608 | tf_op jit(solution)/shard_map/all_to_all | solution.py:50
  30.2 53.8 %copy-start = (bf16[4,48,2048]{2,1,0:T(8,128)(2,1)S(1)}, bf16[4,48,2048]{2,1,0:T(8,128)(2,1)}, u32[]{:S(2)}) copy-start(bf16[4,48,2048]{2,1,0:T(8,128)(2,1)} %param.7) | copy-start | bytes 2359300
  84.1 22.0 %collective-permute-start = (bf16[4,48,2048]{2,1,0:T(8,128)(2,1)S(1)}, bf16[4,48,2048]{2,1,0:T(8,128)(2,1)S(1)}, u32[]{:S(2)}, u32[]{:S(2)}) collective-permute-start(bf16[4,48,2048]{2,1,0:T(8,128)(2,1)S(1)} %copy.18), channel_id=1, source_target_pairs={{0,8},{8,16},{16,24},{24,0},{1,9},{9,17},{17,25},{25,1},{2,10},{10... | collective-permute-start | bytes 2359304 | tf_op jit(solution)/shard_map/while/body/eval_jaxpr/ppermute | solution.py:10
  106.2 20.8 %collective-permute-start = (bf16[4,48,2048]{2,1,0:T(8,128)(2,1)S(1)}, bf16[4,48,2048]{2,1,0:T(8,128)(2,1)S(1)}, u32[]{:S(2)}, u32[]{:S(2)}) collective-permute-start(bf16[4,48,2048]{2,1,0:T(8,128)(2,1)S(1)} %copy.18), channel_id=1, source_target_pairs={{0,8},{8,16},{16,24},{24,0},{1,9},{9,17},{17,25},{25,1},{2,10},{10... | collective-permute-start | bytes 2359304 | tf_op jit(solution)/shard_map/while/body/eval_jaxpr/ppermute | solution.py:10
  127.1 19.9 %collective-permute-start = (bf16[4,48,2048]{2,1,0:T(8,128)(2,1)S(1)}, bf16[4,48,2048]{2,1,0:T(8,128)(2,1)S(1)}, u32[]{:S(2)}, u32[]{:S(2)}) collective-permute-start(bf16[4,48,2048]{2,1,0:T(8,128)(2,1)S(1)} %copy.18), channel_id=1, source_target_pairs={{0,8},{8,16},{16,24},{24,0},{1,9},{9,17},{17,25},{25,1},{2,10},{10... | collective-permute-start | bytes 2359304 | tf_op jit(solution)/shard_map/while/body/eval_jaxpr/ppermute | solution.py:10
  147.0 0.6 copy-start.1
where the time goes:
time: 156 us; the launch traced here: 155 us
  waiting for transfers between devices  97 us (62%)
  local copies, waits for them, and re-layouts  30.4 us (19%)
  matrix products  18 us (12%)
  starting transfers between devices  7.04 us (5%)
  other arithmetic  2.4 us (2%)
    ppermute x3, waiting for transfers between devices, passed_along(): return lax.ppermute(value, axis, pairs)  49.7 us
    all_to_all x1, waiting for transfers between devices, on_device(): lax.all_to_all(outbox, 'rows', split_axis=1, concat_axis=1, tiled=True)  47.3 us
    dot_general x4, matrix products, score_block(): jnp.einsum('rlk,rnk->ln', train_rows, piece, preferred_element_type=jnp.f...  18 us
    scatter x1, local copies, waits for them, and re-layouts, on_device(): outbox = outbox.at[:, slot].set(features)  15.8 us
    while x1, local copies, waits for them, and re-layouts, all_scores(): total, block = lax.fori_loop(0, count - 1, advance, (empty, test_blocks))  6.45 us
    all_to_all x1, starting transfers between devices, on_device(): lax.all_to_all(outbox, 'rows', split_axis=1, concat_axis=1, tiled=True)  4.7 us
    broadcast_in_dim x1, local copies, waits for them, and re-layouts, on_device(): jnp.zeros((features.shape[0], owners_n * capacity, features.shape[2]), jn...  4.09 us
    unnamed x5, local copies, waits for them, and re-layouts  3.86 us
  transfers between devices with their start and end apart: 4, of which 4 were waited for; matrix products, arithmetic and copies ran while one was open for 7% of the time, Pallas kernels for 0%

commit v1 on v0

v1 whole, which is shorter than its diff:
```python
import jax
import jax.numpy as jnp
from jax import lax
from jax.sharding import PartitionSpec as P


def slot_matrix(owner_ids, owners_n, capacity):
    owner = owner_ids[:, 0]
    onehot = (owner[:, None] == jnp.arange(owners_n, dtype=jnp.int32)[None, :]).astype(jnp.int32)
    before = jnp.cumsum(onehot, axis=0) - onehot
    rank = jnp.sum(before * onehot, axis=1)
    slot = owner * capacity + rank
    slots = jnp.arange(owners_n * capacity, dtype=jnp.int32)
    return (slots[:, None] == slot[None, :]).astype(jnp.bfloat16)


def on_device(features, owner_ids, test_blocks):
    owners_n = lax.axis_size("rows")
    local_rows = features.shape[1]
    capacity = 2 * local_rows // owners_n
    tests = lax.all_gather(test_blocks, "blk", axis=1, tiled=True)
    total = jnp.einsum("rsk,rtk->st", features, tests, preferred_element_type=jnp.float32)
    row_scores = total.astype(jnp.bfloat16)
    placed = jnp.dot(
        slot_matrix(owner_ids, owners_n, capacity), row_scores, preferred_element_type=jnp.float32
    ).astype(jnp.bfloat16)
    return lax.all_to_all(placed, "rows", split_axis=0, concat_axis=0, tiled=True)


def solution(mesh):
    return jax.shard_map(
        on_device,
        mesh=mesh,
        in_specs=(P(None, ("blk", "rows"), None), P(("blk", "rows"), None), P(None, "blk", None)),
        out_specs=P(("blk", "rows"), None),
        check_vma=False,
    )
```

time: 156 us -> 95.3 us (0.61)
  the two profiles are of different devices: /device:TPU:2 before, /device:TPU:0 now
where the time goes in v1:
time: 95.3 us; the launch traced here: 95.1 us
  waiting for transfers between devices  66.2 us (69%)
  between operations  13.4 us (14%)
  blocking collectives  8.93 us (9%)
  matrix products  3.37 us (4%)
  other arithmetic  2.4 us (3%)
    all_gather x1, waiting for transfers between devices, on_device(): tests = lax.all_gather(test_blocks, 'blk', axis=1, tiled=True)  65.4 us
    all_to_all x1, blocking collectives, on_device(): lax.all_to_all(placed, 'rows', split_axis=0, concat_axis=0, tiled=True)  8.93 us
    dot_general x1, matrix products, on_device(): jnp.dot(slot_matrix(owner_ids, owners_n, capacity), row_scores, preferred...  3.37 us
  transfers between devices with their start and end apart: 1, of which 1 were waited for; matrix products, arithmetic and copies ran while one was open for 3% of the time, Pallas kernels for 0%

profile of v1, /device:TPU:0, one launch (start us, length us, event | category | flops | bytes accessed | tf_op | source)
XLA Modules:
  0.0 95.1 jit_solution(11568899653987399284)
XLA Ops:
  6.5 0.0 copy-start
  6.5 0.0 all-gather.2.cloned.1.call-start
  6.5 0.7 all-gather.2.cloned.1.call-update
  7.3 0.7 fusion.2
  8.0 0.2 reduce_window_sum.11
  8.2 0.8 select_reduce_fusion
  9.0 0.7 multiply_add_fusion
  9.7 65.4 %all-gather.2.cloned.1.call-done = bf16[4,192,2048]{2,1,0:T(8,128)(2,1)} async-done(((bf16[4,48,2048]{2,1,0:T(8,128)(2,1)}), bf16[4,192,2048]{2,1,0:T(8,128)(2,1)}) %all-gather.2.cloned.1.call-update) | async-done | bytes 3145744 | tf_op jit(solution)/shard_map/all_gather | solution.py:21
  75.1 0.0 copy-done
  75.1 3.4 %convolution_convert_fusion = bf16[256,192]{0,1:T(8,128)(2,1)S(1)} fusion(bf16[4,128,2048]{2,1,0:T(8,128)(2,1)S(1)} %copy-done, bf16[4,192,2048]{2,1,0:T(8,128)(2,1)} %all-gather.2.cloned.1.call-done, s32[128]{0:T(128)S(1)} %multiply_add_fusion), kind=kOutput, calls=%fused_computation | convolution fusion | flops 415342592 | bytes 5341696 | tf_op jit(solution)/shard_map/dot_general | solution.py:24
  78.5 0.1 copy.4
  78.6 8.9 %all_to_all.12 = bf16[8,32,192]{2,1,0:T(8,128)(2,1)S(1)} all-to-all(bf16[8,32,192]{2,1,0:T(8,128)(2,1)S(1)} %bitcast.12), channel_id=1, replica_groups=mesh['blk'=4,'rows'=8] {'rows'}, dimensions={0} | all-to-all | bytes 196608 | tf_op jit(solution)/shard_map/all_to_all | solution.py:27
  87.5 0.7 copy.5
Async XLA Ops:
  6.5 68.6 %copy-start = (bf16[4,128,2048]{2,1,0:T(8,128)(2,1)S(1)}, bf16[4,128,2048]{2,1,0:T(8,128)(2,1)}, u32[]{:S(2)}) copy-start(bf16[4,128,2048]{2,1,0:T(8,128)(2,1)} %param.3) | copy-start | bytes 6291460
  6.5 68.6 %all-gather.2.cloned.1.call-start = ((), (), s32[]{:S(2)}) async-start(), calls=%async_computation.1 | async-start | bytes 3932160 | tf_op jit(solution)/shard_map/all_gather | solution.py:21
Sparse Core Ops, SparseCore 0:
  8.9 66.1 all-gather.1

commit v2 on v1

--- a/solution.py
+++ b/solution.py
@@ -14,12 +14,49 @@
     return (slots[:, None] == slot[None, :]).astype(jnp.bfloat16)
 
 
+def plane_bits(owners_n):
+    bits = [i for i in range(1, owners_n.bit_length() - 1)]
+    return bits + [0] if owners_n > 1 else []
+
+
+def gathered_pieces(test_blocks, chunk):
+    blocks_n = lax.axis_size("blk")
+    owners_n = lax.axis_size("rows")
+    here = lax.axis_index("rows")
+    piece = lax.dynamic_slice_in_dim(test_blocks, here * chunk, chunk, axis=2)
+    arrived = []
+    for step in range(1, blocks_n):
+        pairs = [(b, (b - step) % blocks_n) for b in range(blocks_n)]
+        arrived.append(lax.ppermute(piece, "blk", pairs))
+    stack = jnp.concatenate(arrived, axis=1)[None]
+    masks = [0]
+    for bit in plane_bits(owners_n):
+        pairs = [(s, s ^ (1 << bit)) for s in range(owners_n)]
+        stack = jnp.concatenate([stack, lax.ppermute(stack, "rows", pairs)], axis=0)
+        masks = masks + [m ^ (1 << bit) for m in masks]
+    return stack, masks
+
+
 def on_device(features, owner_ids, test_blocks):
     owners_n = lax.axis_size("rows")
+    blocks_n = lax.axis_size("blk")
     local_rows = features.shape[1]
+    width = test_blocks.shape[1]
     capacity = 2 * local_rows // owners_n
-    tests = lax.all_gather(test_blocks, "blk", axis=1, tiled=True)
-    total = jnp.einsum("rsk,rtk->st", features, tests, preferred_element_type=jnp.float32)
+    chunk = features.shape[2] // owners_n
+    here = lax.axis_index("rows")
+    block = lax.axis_index("blk")
+    stack, masks = gathered_pieces(test_blocks, chunk)
+    own = jnp.einsum("rsk,rtk->st", features, test_blocks, preferred_element_type=jnp.float32)
+    remote = None
+    for j, mask in enumerate(masks):
+        part = lax.dynamic_slice_in_dim(features, (here ^ mask) * chunk, chunk, axis=2)
+        term = jnp.einsum("rsk,rtk->st", part, stack[j], preferred_element_type=jnp.float32)
+        remote = term if remote is None else remote + term
+    relative = jnp.concatenate([own, remote], axis=1)
+    doubled = jnp.concatenate([relative, relative], axis=1)
+    start = ((blocks_n - block) % blocks_n) * width
+    total = lax.dynamic_slice_in_dim(doubled, start, blocks_n * width, axis=1)
     row_scores = total.astype(jnp.bfloat16)
     placed = jnp.dot(
         slot_matrix(owner_ids, owners_n, capacity), row_scores, preferred_element_type=jnp.float32

time: 95.3 us -> 57.6 us (0.60)
  waiting for transfers between devices: 66.2 us -> 26.4 us
  between operations: 13.4 us -> 0.17 us
  starting transfers between devices: 0.01 us -> 9.19 us
  matrix products: 3.37 us -> 8.01 us
  local copies, waits for them, and re-layouts: 0.85 us -> 1.92 us
    all_gather x1 -> x0, waiting for transfers between devices: 65.4 us -> none  [on_device(): tests = lax.all_gather(test_blocks, 'blk', axis=1, tiled=True)]
    ppermute x0 -> x6, waiting for transfers between devices: none -> 26.4 us  [the longest x3 18.1 us: gathered_pieces(): stack = jnp.concatenate([stack, lax.ppermute(stack, 'rows', pairs)], axis=0)]
    ppermute x0 -> x6, starting transfers between devices: none -> 9.19 us  [the longest x3 6.11 us: gathered_pieces(): arrived.append(lax.ppermute(piece, 'blk', pairs))]
    dot_general x0 -> x9, matrix products: none -> 7.65 us  [the longest x8 5.83 us: on_device(): jnp.einsum('rsk,rtk->st', part, stack[j], preferred_element_type=jnp.floa...]
    dot_general x1, matrix products: 3.37 us -> 0.36 us  [on_device(): jnp.dot(slot_matrix(owner_ids, owners_n, capacity), row_scores, preferred...]
    concatenate x0 -> x2, other arithmetic: none -> 2 us  [gathered_pieces(): stack = jnp.concatenate([stack, lax.ppermute(stack, 'rows', pairs)], axis=0)]
    dynamic_slice x0 -> x1, local copies, waits for them, and re-layouts: none -> 1.05 us  [gathered_pieces(): piece = lax.dynamic_slice_in_dim(test_blocks, here * chunk, chunk, axis=2)]
  transfers between devices with their start and end apart: 1 -> 6, of which waited for: 1 -> 5; matrix products, arithmetic and copies ran while one was open for 3% -> 5% of each run, Pallas kernels for 0% -> 0%
where the time goes in v2:
time: 57.6 us; the launch traced here: 57.2 us
  waiting for transfers between devices  26.4 us (46%)
  starting transfers between devices  9.19 us (16%)
  blocking collectives  9.07 us (16%)
  matrix products  8.01 us (14%)
  other arithmetic  2.43 us (4%)
  local copies, waits for them, and re-layouts  1.92 us (3%)
    ppermute x3, waiting for transfers between devices, gathered_pieces(): stack = jnp.concatenate([stack, lax.ppermute(stack, 'rows', pairs)], axis=0)  18.1 us
    all_to_all x1, blocking collectives, on_device(): lax.all_to_all(placed, 'rows', split_axis=0, concat_axis=0, tiled=True)  9.07 us
    ppermute x3, waiting for transfers between devices, gathered_pieces(): arrived.append(lax.ppermute(piece, 'blk', pairs))  8.35 us
    ppermute x3, starting transfers between devices, gathered_pieces(): arrived.append(lax.ppermute(piece, 'blk', pairs))  6.11 us
    dot_general x8, matrix products, on_device(): jnp.einsum('rsk,rtk->st', part, stack[j], preferred_element_type=jnp.floa...  5.83 us
    ppermute x3, starting transfers between devices, gathered_pieces(): stack = jnp.concatenate([stack, lax.ppermute(stack, 'rows', pairs)], axis=0)  3.08 us
    concatenate x2, other arithmetic, gathered_pieces(): stack = jnp.concatenate([stack, lax.ppermute(stack, 'rows', pairs)], axis=0)  2 us
    dot_general x1, matrix products, on_device(): jnp.einsum('rsk,rtk->st', features, test_blocks, preferred_element_type=j...  1.82 us
  transfers between devices with their start and end apart: 6, of which 5 were waited for; matrix products, arithmetic and copies ran while one was open for 5% of the time, Pallas kernels for 0%

profile of v2, /device:TPU:0, one launch (start us, length us, event | category | flops | bytes accessed | tf_op | source)
XLA Modules:
  0.0 57.2 jit_solution(17868090622798705992)
XLA Ops:
  0.0 0.0 copy-start
  0.0 1.0 %constant_dynamic-slice_fusion = bf16[4,48,256]{2,1,0:T(8,128)(2,1)S(1)} fusion(bf16[4,48,2048]{2,1,0:T(8,128)(2,1)} %param.5, s32[]{:T(128)S(6)} %select_n.35), kind=kLoop, calls=%fused_computation.57 | loop fusion | bytes 196612 | tf_op jit(solution)/shard_map/dynamic_slice | solution.py:26
  1.1 0.0 copy-start.1
  1.1 5.1 %collective-permute-start = (bf16[4,48,256]{2,1,0:T(8,128)(2,1)S(1)}, bf16[4,48,256]{2,1,0:T(8,128)(2,1)S(1)}, u32[]{:S(2)}, u32[]{:S(2)}) collective-permute-start(bf16[4,48,256]{2,1,0:T(8,128)(2,1)S(1)} %constant_dynamic-slice_fusion), channel_id=1, source_target_pairs={{0,24},{8,0},{16,8},{24,16},{1,25},{9,1},{17,9},{25,17},{2,26},{10... | collective-permute-start | bytes 294920 | tf_op jit(solution)/shard_map/ppermute | solution.py:30
  6.2 0.0 collective-permute-start.2
  6.2 1.0 %collective-permute-start.1 = (bf16[4,48,256]{2,1,0:T(8,128)(2,1)S(1)}, bf16[4,48,256]{2,1,0:T(8,128)(2,1)S(1)}, u32[]{:S(2)}, u32[]{:S(2)}) collective-permute-start(bf16[4,48,256]{2,1,0:T(8,128)(2,1)S(1)} %constant_dynamic-slice_fusion), channel_id=1, source_target_pairs={{0,16},{8,24},{16,0},{24,8},{1,17},{9,25},{17,1},{25,9},{2,18},{10... | collective-permute-start | bytes 294920 | tf_op jit(solution)/shard_map/ppermute | solution.py:30
  7.2 2.2 %collective-permute-done = bf16[4,48,256]{2,1,0:T(8,128)(2,1)S(1)} collective-permute-done((bf16[4,48,256]{2,1,0:T(8,128)(2,1)S(1)}, bf16[4,48,256]{2,1,0:T(8,128)(2,1)S(1)}, u32[]{:S(2)}, u32[]{:S(2)}) %collective-permute-start) | collective-permute-done | bytes 98336 | tf_op jit(solution)/shard_map/ppermute | solution.py:30
  9.4 6.2 %collective-permute-done.1 = bf16[4,48,256]{2,1,0:T(8,128)(2,1)S(1)} collective-permute-done((bf16[4,48,256]{2,1,0:T(8,128)(2,1)S(1)}, bf16[4,48,256]{2,1,0:T(8,128)(2,1)S(1)}, u32[]{:S(2)}, u32[]{:S(2)}) %collective-permute-start.1) | collective-permute-done | bytes 98336 | tf_op jit(solution)/shard_map/ppermute | solution.py:30
  15.5 0.0 collective-permute-done.2
  15.6 1.6 %collective-permute-start.3 = (bf16[1,4,144,256]{3,2,1,0:T(8,128)(2,1)S(1)}, bf16[1,4,144,256]{3,2,1,0:T(8,128)(2,1)S(1)}, u32[]{:S(2)}, u32[]{:S(2)}) collective-permute-start(bf16[1,4,144,256]{3,2,1,0:T(8,128)(2,1)S(1)} %bitcast.61), channel_id=1, source_target_pairs={{0,2},{1,3},{2,0},{3,1},{4,6},{5,7},{6,4},{7,5},{8,10},{9,11},{10,... | collective-permute-start | bytes 884744 | tf_op jit(solution)/shard_map/ppermute | solution.py:35
  17.1 6.2 %collective-permute-done.3 = bf16[1,4,144,256]{3,2,1,0:T(8,128)(2,1)S(1)} collective-permute-done((bf16[1,4,144,256]{3,2,1,0:T(8,128)(2,1)S(1)}, bf16[1,4,144,256]{3,2,1,0:T(8,128)(2,1)S(1)}, u32[]{:S(2)}, u32[]{:S(2)}) %collective-permute-start.3) | collective-permute-done | bytes 294944 | tf_op jit(solution)/shard_map/ppermute | solution.py:35
  23.3 0.9 %pad_maximum_fusion.1 = bf16[2,4,144,256]{3,2,1,0:T(8,128)(2,1)} fusion(bf16[1,4,144,256]{3,2,1,0:T(8,128)(2,1)S(1)} %collective-permute-done.3, bf16[1,4,144,256]{3,2,1,0:T(8,128)(2,1)S(1)} %bitcast.62), kind=kLoop, calls=%fused_computation.18 | loop fusion | flops 294912 | bytes 1179648 | tf_op jit(solution)/shard_map/concatenate | solution.py:35
  24.2 1.5 %collective-permute-start.4 = (bf16[2,4,144,256]{3,2,1,0:T(8,128)(2,1)}, bf16[2,4,144,256]{3,2,1,0:T(8,128)(2,1)S(1)}, u32[]{:S(2)}, u32[]{:S(2)}) collective-permute-start(bf16[2,4,144,256]{3,2,1,0:T(8,128)(2,1)} %pad_maximum_fusion.1), channel_id=1, source_target_pairs={{0,4},{1,5},{2,6},{3,7},{4,0},{5,1},{6,2},{7,3},{8,12},{9,13},{10,... | collective-permute-start | bytes 1769480 | tf_op jit(solution)/shard_map/ppermute | solution.py:35
  25.7 11.8 %collective-permute-done.4 = bf16[2,4,144,256]{3,2,1,0:T(8,128)(2,1)S(1)} collective-permute-done((bf16[2,4,144,256]{3,2,1,0:T(8,128)(2,1)}, bf16[2,4,144,256]{3,2,1,0:T(8,128)(2,1)S(1)}, u32[]{:S(2)}, u32[]{:S(2)}) %collective-permute-start.4) | collective-permute-done | bytes 589856 | tf_op jit(solution)/shard_map/ppermute | solution.py:35
  37.5 1.1 %pad_maximum_fusion = bf16[4,4,144,256]{3,2,1,0:T(8,128)(2,1)} fusion(bf16[2,4,144,256]{3,2,1,0:T(8,128)(2,1)S(1)} %collective-permute-done.4, bf16[1,4,144,256]{3,2,1,0:T(8,128)(2,1)S(1)} %collective-permute-done.3, bf16[1,4,144,256]{3,2,1,0:T(8,128)(2,1)S(1)} %bitcast.63), kind=kLoop, calls=%fused_computation | loop fusion | flops 1179648 | bytes 2359296 | tf_op jit(solution)/shard_map/concatenate | solution.py:35
  38.6 0.0 collective-permute-start.5
  38.6 0.0 copy-done.1
  38.6 0.1 fusion.21
  38.7 0.2 reduce_window_sum.11
  38.9 0.2 select_reduce_fusion
  39.1 0.0 copy-done
  39.1 1.8 %convolution_bitcast_fusion.8 = bf16[128,48]{1,0:T(8,128)(2,1)S(1)} fusion(bf16[4,128,2048]{2,1,0:T(8,128)(2,1)S(1)} %copy-done, bf16[4,48,2048]{2,1,0:T(8,128)(2,1)} %param.5), kind=kOutput, calls=%fused_computation.17 | convolution fusion | flops 100663296 | bytes 2895872 | tf_op jit(solution)/shard_map/rsk,rtk->st/dot_general | solution.py:50
  40.9 0.2 convolution_bitcast_fusion.6
  41.2 0.2 convolution_bitcast_fusion.4
  41.4 0.2 convolution_bitcast_fusion.5
  41.7 0.1 collective-permute-done.5
  41.8 1.2 %convolution_bitcast_fusion = f32[128,144]{1,0:T(8,128)S(1)} fusion(bf16[4,4,144,256]{3,2,1,0:T(8,128)(2,1)} %collective-permute-done.5, bf16[4,128,2048]{2,1,0:T(8,128)(2,1)S(1)} %copy-done, s32[]{:T(128)S(6)} %select_n.42), kind=kOutput, calls=%fused_computation.2 | convolution fusion | flops 37748736 | bytes 630788 | tf_op jit(solution)/shard_map/rsk,rtk->st/dot_general | solution.py:54
  43.0 1.2 %convolution_bitcast_fusion.1 = f32[128,144]{1,0:T(8,128)S(1)} fusion(bf16[4,4,144,256]{3,2,1,0:T(8,128)(2,1)} %collective-permute-done.5, bf16[4,128,2048]{2,1,0:T(8,128)(2,1)S(1)} %copy-done, s32[]{:T(128)S(6)} %select_n.41), kind=kOutput, calls=%fused_computation.3 | convolution fusion | flops 37748736 | bytes 630788 | tf_op jit(solution)/shard_map/rsk,rtk->st/dot_general | solution.py:54
  44.2 1.2 %convolution_bitcast_fusion.2 = f32[128,144]{1,0:T(8,128)S(1)} fusion(bf16[4,4,144,256]{3,2,1,0:T(8,128)(2,1)} %collective-permute-done.5, bf16[4,128,2048]{2,1,0:T(8,128)(2,1)S(1)} %copy-done, s32[]{:T(128)S(6)} %select_n.40), kind=kOutput, calls=%fused_computation.4 | convolution fusion | flops 37748736 | bytes 630788 | tf_op jit(solution)/shard_map/rsk,rtk->st/dot_general | solution.py:54
  45.4 1.2 %convolution_bitcast_fusion.3 = f32[128,144]{1,0:T(8,128)S(1)} fusion(bf16[4,4,144,256]{3,2,1,0:T(8,128)(2,1)} %collective-permute-done.5, bf16[4,128,2048]{2,1,0:T(8,128)(2,1)S(1)} %copy-done, s32[]{:T(128)S(6)} %select_n.39), kind=kOutput, calls=%fused_computation.5 | convolution fusion | flops 37748736 | bytes 630788 | tf_op jit(solution)/shard_map/rsk,rtk->st/dot_general | solution.py:54
  46.7 0.3 fusion.6
  46.9 0.4 convolution_convert_fusion
  47.3 0.1 copy.4
  47.4 9.1 %all_to_all.12 = bf16[8,32,192]{2,1,0:T(8,128)(2,1)S(1)} all-to-all(bf16[8,32,192]{2,1,0:T(8,128)(2,1)S(1)} %bitcast.64), channel_id=1, replica_groups=mesh['blk'=4,'rows'=8] {'rows'}, dimensions={0} | all-to-all | bytes 196608 | tf_op jit(solution)/shard_map/all_to_all | solution.py:64
  56.5 0.7 %copy.5 = bf16[256,192]{0,1:T(8,128)(2,1)} copy(bf16[256,192]{1,0:T(8,128)(2,1)S(1)} %bitcast.65) | data formatting | bytes 196608 | tf_op jit(solution)/shard_map/all_to_all | solution.py:64
  (4 shorter events, 0.0 us)
Async XLA Ops:
  0.0 39.1 %copy-start = (bf16[4,128,2048]{2,1,0:T(8,128)(2,1)S(1)}, bf16[4,128,2048]{2,1,0:T(8,128)(2,1)}, u32[]{:S(2)}) copy-start(bf16[4,128,2048]{2,1,0:T(8,128)(2,1)} %param.3) | copy-start | bytes 6291460
  1.1 37.6 %copy-start.1 = (s32[128,1]{0,1:T(1,128)S(1)}, s32[128,1]{0,1:T(1,128)}, u32[]{:S(2)}) copy-start(s32[128,1]{0,1:T(1,128)} %param.4) | copy-start | bytes 1540
  1.1 8.3 %collective-permute-start = (bf16[4,48,256]{2,1,0:T(8,128)(2,1)S(1)}, bf16[4,48,256]{2,1,0:T(8,128)(2,1)S(1)}, u32[]{:S(2)}, u32[]{:S(2)}) collective-permute-start(bf16[4,48,256]{2,1,0:T(8,128)(2,1)S(1)} %constant_dynamic-slice_fusion), channel_id=1, source_target_pairs={{0,24},{8,0},{16,8},{24,16},{1,25},{9,1},{17,9},{25,17},{2,26},{10... | collective-permute-start | bytes 294920 | tf_op jit(solution)/shard_map/ppermute | solution.py:30
  6.2 9.4 %collective-permute-start.2 = (bf16[4,48,256]{2,1,0:T(8,128)(2,1)S(1)}, bf16[4,48,256]{2,1,0:T(8,128)(2,1)S(1)}, u32[]{:S(2)}, u32[]{:S(2)}) collective-permute-start(bf16[4,48,256]{2,1,0:T(8,128)(2,1)S(1)} %constant_dynamic-slice_fusion), channel_id=1, source_target_pairs={{0,8},{8,16},{16,24},{24,0},{1,9},{9,17},{17,25},{25,1},{2,10},{10... | collective-permute-start | bytes 294920 | tf_op jit(solution)/shard_map/ppermute | solution.py:30
  6.2 9.4 %collective-permute-start.1 = (bf16[4,48,256]{2,1,0:T(8,128)(2,1)S(1)}, bf16[4,48,256]{2,1,0:T(8,128)(2,1)S(1)}, u32[]{:S(2)}, u32[]{:S(2)}) collective-permute-start(bf16[4,48,256]{2,1,0:T(8,128)(2,1)S(1)} %constant_dynamic-slice_fusion), channel_id=1, source_target_pairs={{0,16},{8,24},{16,0},{24,8},{1,17},{9,25},{17,1},{25,9},{2,18},{10... | collective-permute-start | bytes 294920 | tf_op jit(solution)/shard_map/ppermute | solution.py:30
  15.6 7.7 %collective-permute-start.3 = (bf16[1,4,144,256]{3,2,1,0:T(8,128)(2,1)S(1)}, bf16[1,4,144,256]{3,2,1,0:T(8,128)(2,1)S(1)}, u32[]{:S(2)}, u32[]{:S(2)}) collective-permute-start(bf16[1,4,144,256]{3,2,1,0:T(8,128)(2,1)S(1)} %bitcast.61), channel_id=1, source_target_pairs={{0,2},{1,3},{2,0},{3,1},{4,6},{5,7},{6,4},{7,5},{8,10},{9,11},{10,... | collective-permute-start | bytes 884744 | tf_op jit(solution)/shard_map/ppermute | solution.py:35
  24.2 13.3 %collective-permute-start.4 = (bf16[2,4,144,256]{3,2,1,0:T(8,128)(2,1)}, bf16[2,4,144,256]{3,2,1,0:T(8,128)(2,1)S(1)}, u32[]{:S(2)}, u32[]{:S(2)}) collective-permute-start(bf16[2,4,144,256]{3,2,1,0:T(8,128)(2,1)} %pad_maximum_fusion.1), channel_id=1, source_target_pairs={{0,4},{1,5},{2,6},{3,7},{4,0},{5,1},{6,2},{7,3},{8,12},{9,13},{10,... | collective-permute-start | bytes 1769480 | tf_op jit(solution)/shard_map/ppermute | solution.py:35
  38.6 3.2 %collective-permute-start.5 = (bf16[4,4,144,256]{3,2,1,0:T(8,128)(2,1)}, bf16[4,4,144,256]{3,2,1,0:T(8,128)(2,1)}, u32[]{:S(2)}, u32[]{:S(2)}) collective-permute-start(bf16[4,4,144,256]{3,2,1,0:T(8,128)(2,1)} %pad_maximum_fusion), channel_id=1, source_target_pairs={{0,1},{1,0},{2,3},{3,2},{4,5},{5,4},{6,7},{7,6},{8,9},{9,8},{10,11... | collective-permute-start | bytes 3538952 | tf_op jit(solution)/shard_map/ppermute | solution.py:35

commit v3 on v1

--- a/solution.py
+++ b/solution.py
@@ -14,12 +14,64 @@
     return (slots[:, None] == slot[None, :]).astype(jnp.bfloat16)
 
 
+def xor_pairs(count, mask):
+    return [(s, s ^ mask) for s in range(count)]
+
+
 def on_device(features, owner_ids, test_blocks):
     owners_n = lax.axis_size("rows")
+    blocks_n = lax.axis_size("blk")
     local_rows = features.shape[1]
+    width = test_blocks.shape[1]
     capacity = 2 * local_rows // owners_n
-    tests = lax.all_gather(test_blocks, "blk", axis=1, tiled=True)
-    total = jnp.einsum("rsk,rtk->st", features, tests, preferred_element_type=jnp.float32)
+    chunk = features.shape[2] // owners_n
+    here = lax.axis_index("rows")
+    block = lax.axis_index("blk")
+
+    def term(offset, size, tests):
+        part = lax.dynamic_slice_in_dim(features, offset, size, axis=2)
+        return jnp.einsum("rsk,rtk->st", part, tests, preferred_element_type=jnp.float32)
+
+    piece = lax.dynamic_slice_in_dim(test_blocks, here * chunk, chunk, axis=2)
+    arrived = []
+    for step in range(1, blocks_n):
+        pairs = [(b, (b - step) % blocks_n) for b in range(blocks_n)]
+        arrived.append(lax.ppermute(piece, "blk", pairs))
+    mine = jnp.concatenate(arrived, axis=1)
+    own = jnp.einsum("rsk,rtk->st", features, test_blocks, preferred_element_type=jnp.float32)
+    remote = term(here * chunk, chunk, mine)
+    chip_bits = [1 << i for i in range(1, owners_n.bit_length() - 1)]
+    if len(chip_bits) == 2:
+        bx, by = chip_bits
+        along_x = lax.ppermute(mine, "rows", xor_pairs(owners_n, bx))
+        along_y = lax.ppermute(mine, "rows", xor_pairs(owners_n, by))
+        remote = remote + term((here ^ bx) * chunk, chunk, along_x)
+        remote = remote + term((here ^ by) * chunk, chunk, along_y)
+        half = chunk // 2
+        first = lax.ppermute(along_y[:, :, :half], "rows", xor_pairs(owners_n, bx))
+        second = lax.ppermute(along_x[:, :, half:], "rows", xor_pairs(owners_n, by))
+        corner = (here ^ bx ^ by) * chunk
+        remote = remote + term(corner, half, first) + term(corner + half, half, second)
+        diagonal = jnp.concatenate([first, second], axis=2)
+        held = jnp.stack([mine, along_x, along_y, diagonal])
+        masks = [0, bx, by, bx ^ by]
+    else:
+        held = mine[None]
+        masks = [0]
+        for mask in chip_bits:
+            got = lax.ppermute(held, "rows", xor_pairs(owners_n, mask))
+            for j, m in enumerate(masks):
+                remote = remote + term((here ^ mask ^ m) * chunk, chunk, got[j])
+            held = jnp.concatenate([held, got], axis=0)
+            masks = masks + [m ^ mask for m in masks]
+    if owners_n > 1:
+        got = lax.ppermute(held, "rows", xor_pairs(owners_n, 1))
+        for j, m in enumerate(masks):
+            remote = remote + term((here ^ 1 ^ m) * chunk, chunk, got[j])
+    relative = jnp.concatenate([own, remote], axis=1)
+    doubled = jnp.concatenate([relative, relative], axis=1)
+    start = ((blocks_n - block) % blocks_n) * width
+    total = lax.dynamic_slice_in_dim(doubled, start, blocks_n * width, axis=1)
     row_scores = total.astype(jnp.bfloat16)
     placed = jnp.dot(
         slot_matrix(owner_ids, owners_n, capacity), row_scores, preferred_element_type=jnp.float32

time: 95.3 us -> 49.9 us (0.52)
  waiting for transfers between devices: 66.2 us -> 17.2 us
  between operations: 13.4 us -> 0.26 us
  starting transfers between devices: 0.01 us -> 12 us
  matrix products: 3.37 us -> 8.17 us
  local copies, waits for them, and re-layouts: 0.85 us -> 1.98 us
    all_gather x1 -> x0, waiting for transfers between devices: 65.4 us -> none  [on_device(): tests = lax.all_gather(test_blocks, 'blk', axis=1, tiled=True)]
    ppermute x0 -> x8, waiting for transfers between devices: none -> 17.2 us  [the longest x3 8.35 us: on_device(): arrived.append(lax.ppermute(piece, 'blk', pairs))]
    ppermute x0 -> x8, starting transfers between devices: none -> 12 us  [the longest x3 6.11 us: on_device(): arrived.append(lax.ppermute(piece, 'blk', pairs))]
    dot_general x0 -> x10, matrix products: none -> 7.8 us  [the longest x9 5.98 us: term(): jnp.einsum('rsk,rtk->st', part, tests, preferred_element_type=jnp.float32)]
    dot_general x1, matrix products: 3.37 us -> 0.36 us  [on_device(): jnp.dot(slot_matrix(owner_ids, owners_n, capacity), row_scores, preferred...]
    another operation x0 -> x2, other arithmetic: none -> 1.2 us  [on_device(): held = jnp.stack([mine, along_x, along_y, diagonal])]
    dynamic_slice x0 -> x1, local copies, waits for them, and re-layouts: none -> 1.05 us  [on_device(): piece = lax.dynamic_slice_in_dim(test_blocks, here * chunk, chunk, axis=2)]
  transfers between devices with their start and end apart: 1 -> 8, of which waited for: 1 -> 6; matrix products, arithmetic and copies ran while one was open for 3% -> 6% of each run, Pallas kernels for 0% -> 0%
where the time goes in v3:
time: 49.9 us; the launch traced here: 49.5 us
  waiting for transfers between devices  17.2 us (34%)
  starting transfers between devices  12 us (24%)
  blocking collectives  8.23 us (16%)
  matrix products  8.17 us (16%)
  local copies, waits for them, and re-layouts  1.98 us (4%)
  other arithmetic  1.63 us (3%)
    ppermute x3, waiting for transfers between devices, on_device(): arrived.append(lax.ppermute(piece, 'blk', pairs))  8.35 us
    all_to_all x1, blocking collectives, on_device(): lax.all_to_all(placed, 'rows', split_axis=0, concat_axis=0, tiled=True)  8.23 us
    ppermute x3, starting transfers between devices, on_device(): arrived.append(lax.ppermute(piece, 'blk', pairs))  6.11 us
    dot_general x9, matrix products, term(): jnp.einsum('rsk,rtk->st', part, tests, preferred_element_type=jnp.float32)  5.98 us
    ppermute x1, waiting for transfers between devices, on_device(): along_y = lax.ppermute(mine, 'rows', xor_pairs(owners_n, by))  4.67 us
    ppermute x1, waiting for transfers between devices, on_device(): first = lax.ppermute(along_y[:, :, :half], 'rows', xor_pairs(owners_n, bx))  2.03 us
    ppermute x1, waiting for transfers between devices, on_device(): second = lax.ppermute(along_x[:, :, half:], 'rows', xor_pairs(owners_n, by))  1.88 us
    dot_general x1, matrix products, on_device(): jnp.einsum('rsk,rtk->st', features, test_blocks, preferred_element_type=j...  1.82 us
  transfers between devices with their start and end apart: 8, of which 6 were waited for; matrix products, arithmetic and copies ran while one was open for 6% of the time, Pallas kernels for 0%

profile of v3, /device:TPU:0, one launch (start us, length us, event | category | flops | bytes accessed | tf_op | source)
XLA Modules:
  0.0 49.5 jit_solution(1927388954837348372)
XLA Ops:
  0.0 0.0 copy-start
  0.0 1.0 %constant_dynamic-slice_fusion = bf16[4,48,256]{2,1,0:T(8,128)(2,1)S(1)} fusion(bf16[4,48,2048]{2,1,0:T(8,128)(2,1)} %param.5, s32[]{:T(128)S(6)} %select_n.38), kind=kLoop, calls=%fused_computation.58 | loop fusion | bytes 196612 | tf_op jit(solution)/shard_map/dynamic_slice | solution.py:35
  1.1 0.0 copy-start.1
  1.1 5.1 %collective-permute-start = (bf16[4,48,256]{2,1,0:T(8,128)(2,1)S(1)}, bf16[4,48,256]{2,1,0:T(8,128)(2,1)S(1)}, u32[]{:S(2)}, u32[]{:S(2)}) collective-permute-start(bf16[4,48,256]{2,1,0:T(8,128)(2,1)S(1)} %constant_dynamic-slice_fusion), channel_id=1, source_target_pairs={{0,24},{8,0},{16,8},{24,16},{1,25},{9,1},{17,9},{25,17},{2,26},{10... | collective-permute-start | bytes 294920 | tf_op jit(solution)/shard_map/ppermute | solution.py:39
  6.2 0.0 collective-permute-start.2
  6.2 1.0 %collective-permute-start.1 = (bf16[4,48,256]{2,1,0:T(8,128)(2,1)S(1)}, bf16[4,48,256]{2,1,0:T(8,128)(2,1)S(1)}, u32[]{:S(2)}, u32[]{:S(2)}) collective-permute-start(bf16[4,48,256]{2,1,0:T(8,128)(2,1)S(1)} %constant_dynamic-slice_fusion), channel_id=1, source_target_pairs={{0,16},{8,24},{16,0},{24,8},{1,17},{9,25},{17,1},{25,9},{2,18},{10... | collective-permute-start | bytes 294920 | tf_op jit(solution)/shard_map/ppermute | solution.py:39
  7.2 2.2 %collective-permute-done = bf16[4,48,256]{2,1,0:T(8,128)(2,1)S(1)} collective-permute-done((bf16[4,48,256]{2,1,0:T(8,128)(2,1)S(1)}, bf16[4,48,256]{2,1,0:T(8,128)(2,1)S(1)}, u32[]{:S(2)}, u32[]{:S(2)}) %collective-permute-start) | collective-permute-done | bytes 98336 | tf_op jit(solution)/shard_map/ppermute | solution.py:39
  9.4 6.2 %collective-permute-done.1 = bf16[4,48,256]{2,1,0:T(8,128)(2,1)S(1)} collective-permute-done((bf16[4,48,256]{2,1,0:T(8,128)(2,1)S(1)}, bf16[4,48,256]{2,1,0:T(8,128)(2,1)S(1)}, u32[]{:S(2)}, u32[]{:S(2)}) %collective-permute-start.1) | collective-permute-done | bytes 98336 | tf_op jit(solution)/shard_map/ppermute | solution.py:39
  15.5 0.0 collective-permute-done.2
  15.6 1.6 %collective-permute-start.4 = (bf16[4,144,256]{2,1,0:T(8,128)(2,1)S(1)}, bf16[4,144,256]{2,1,0:T(8,128)(2,1)S(1)}, u32[]{:S(2)}, u32[]{:S(2)}) collective-permute-start(bf16[4,144,256]{2,1,0:T(8,128)(2,1)S(1)} %constant_dynamic-update-slice_fusion), channel_id=1, source_target_pairs={{0,4},{1,5},{2,6},{3,7},{4,0},{5,1},{6,2},{7,3},{8,12},{9,13},{10,... | collective-permute-start | bytes 884744 | tf_op jit(solution)/shard_map/ppermute | solution.py:47
  17.2 1.5 %collective-permute-start.3 = (bf16[4,144,256]{2,1,0:T(8,128)(2,1)S(1)}, bf16[4,144,256]{2,1,0:T(8,128)(2,1)S(1)}, u32[]{:S(2)}, u32[]{:S(2)}) collective-permute-start(bf16[4,144,256]{2,1,0:T(8,128)(2,1)S(1)} %constant_dynamic-update-slice_fusion), channel_id=1, source_target_pairs={{0,2},{1,3},{2,0},{3,1},{4,6},{5,7},{6,4},{7,5},{8,10},{9,11},{10,... | collective-permute-start | bytes 884744 | tf_op jit(solution)/shard_map/ppermute | solution.py:46
  18.6 4.7 %collective-permute-done.4 = bf16[4,144,256]{2,1,0:T(8,128)(2,1)S(1)} collective-permute-done((bf16[4,144,256]{2,1,0:T(8,128)(2,1)S(1)}, bf16[4,144,256]{2,1,0:T(8,128)(2,1)S(1)}, u32[]{:S(2)}, u32[]{:S(2)}) %collective-permute-start.4) | collective-permute-done | bytes 294944 | tf_op jit(solution)/shard_map/ppermute | solution.py:47
  23.3 1.6 %collective-permute-start.5 = (bf16[4,144,128]{2,1,0:T(8,128)(2,1)S(1)}, bf16[4,144,128]{2,1,0:T(8,128)(2,1)S(1)}, u32[]{:S(2)}, u32[]{:S(2)}) collective-permute-start(bf16[4,144,128]{2,1,0:T(8,128)(2,1)S(1)} %slice.24), channel_id=1, source_target_pairs={{0,2},{1,3},{2,0},{3,1},{4,6},{5,7},{6,4},{7,5},{8,10},{9,11},{10,... | collective-permute-start | bytes 442376 | tf_op jit(solution)/shard_map/ppermute | solution.py:51
  24.9 0.3 collective-permute-done.3
  25.2 1.3 %collective-permute-start.6 = (bf16[4,144,128]{2,1,0:T(8,128)(2,1)S(1)}, bf16[4,144,128]{2,1,0:T(8,128)(2,1)S(1)}, u32[]{:S(2)}, u32[]{:S(2)}) collective-permute-start(bf16[4,144,128]{2,1,0:T(8,128)(2,1)S(1)} %slice.25), channel_id=1, source_target_pairs={{0,4},{1,5},{2,6},{3,7},{4,0},{5,1},{6,2},{7,3},{8,12},{9,13},{10,... | collective-permute-start | bytes 442376 | tf_op jit(solution)/shard_map/ppermute | solution.py:52
  26.5 2.0 %collective-permute-done.5 = bf16[4,144,128]{2,1,0:T(8,128)(2,1)S(1)} collective-permute-done((bf16[4,144,128]{2,1,0:T(8,128)(2,1)S(1)}, bf16[4,144,128]{2,1,0:T(8,128)(2,1)S(1)}, u32[]{:S(2)}, u32[]{:S(2)}) %collective-permute-start.5) | collective-permute-done | bytes 147488 | tf_op jit(solution)/shard_map/ppermute | solution.py:51
  28.6 1.9 %collective-permute-done.6 = bf16[4,144,128]{2,1,0:T(8,128)(2,1)S(1)} collective-permute-done((bf16[4,144,128]{2,1,0:T(8,128)(2,1)S(1)}, bf16[4,144,128]{2,1,0:T(8,128)(2,1)S(1)}, u32[]{:S(2)}, u32[]{:S(2)}) %collective-permute-start.6) | collective-permute-done | bytes 147488 | tf_op jit(solution)/shard_map/ppermute | solution.py:52
  30.5 1.2 %pad_maximum_fusion = bf16[4,4,144,256]{3,2,1,0:T(8,128)(2,1)} fusion(bf16[1,4,144,256]{3,2,1,0:T(8,128)(2,1)S(1)} %maximum_bitcast_fusion, bf16[1,4,144,256]{3,2,1,0:T(8,128)(2,1)S(1)} %bitcast.64, bf16[1,4,144,256]{3,2,1,0:T(8,128)(2,1)S(1)} %bitcast.65, bf16[1,4,144,256]{3,2,1,0:T(8,128)(2,1)S(1)} %bitcast.66), kind=kLoop, calls=%fused_computation | loop fusion | flops 1769472 | bytes 2359296 | tf_op jit(solution)/shard_map/stack | solution.py:56
  31.6 0.0 collective-permute-start.7
  31.6 0.0 copy-done.1
  31.6 0.1 fusion.22
  31.8 0.2 reduce_window_sum.11
  32.0 0.2 select_reduce_fusion
  32.2 0.0 copy-done
  32.2 1.8 %convolution_bitcast_fusion.9 = bf16[128,48]{1,0:T(8,128)(2,1)S(1)} fusion(bf16[4,128,2048]{2,1,0:T(8,128)(2,1)S(1)} %copy-done, bf16[4,48,2048]{2,1,0:T(8,128)(2,1)} %param.5), kind=kOutput, calls=%fused_computation.19 | convolution fusion | flops 100663296 | bytes 2895872 | tf_op jit(solution)/shard_map/rsk,rtk->st/dot_general | solution.py:41
  34.0 0.2 convolution_bitcast_fusion.4
  34.3 0.2 convolution_bitcast_fusion.5
  34.5 0.2 convolution_bitcast_fusion.8
  34.7 0.2 convolution_bitcast_fusion.7
  34.9 0.0 collective-permute-done.7
  34.9 1.2 %convolution_bitcast_fusion = f32[128,144]{1,0:T(8,128)S(1)} fusion(bf16[4,4,144,256]{3,2,1,0:T(8,128)(2,1)} %collective-permute-done.7, bf16[4,128,2048]{2,1,0:T(8,128)(2,1)S(1)} %copy-done, s32[]{:T(128)S(6)} %select_n.46), kind=kOutput, calls=%fused_computation.2 | convolution fusion | flops 37748736 | bytes 630788 | tf_op jit(solution)/shard_map/rsk,rtk->st/dot_general | solution.py:33
  36.2 1.2 %convolution_bitcast_fusion.1 = f32[128,144]{1,0:T(8,128)S(1)} fusion(bf16[4,4,144,256]{3,2,1,0:T(8,128)(2,1)} %collective-permute-done.7, bf16[4,128,2048]{2,1,0:T(8,128)(2,1)S(1)} %copy-done, s32[]{:T(128)S(6)} %select_n.45), kind=kOutput, calls=%fused_computation.3 | convolution fusion | flops 37748736 | bytes 630788 | tf_op jit(solution)/shard_map/rsk,rtk->st/dot_general | solution.py:33
  37.4 1.2 %convolution_bitcast_fusion.2 = f32[128,144]{1,0:T(8,128)S(1)} fusion(bf16[4,4,144,256]{3,2,1,0:T(8,128)(2,1)} %collective-permute-done.7, bf16[4,128,2048]{2,1,0:T(8,128)(2,1)S(1)} %copy-done, s32[]{:T(128)S(6)} %select_n.44), kind=kOutput, calls=%fused_computation.4 | convolution fusion | flops 37748736 | bytes 630788 | tf_op jit(solution)/shard_map/rsk,rtk->st/dot_general | solution.py:33
  38.6 1.2 %convolution_bitcast_fusion.3 = f32[128,144]{1,0:T(8,128)S(1)} fusion(bf16[4,4,144,256]{3,2,1,0:T(8,128)(2,1)} %collective-permute-done.7, bf16[4,128,2048]{2,1,0:T(8,128)(2,1)S(1)} %copy-done, s32[]{:T(128)S(6)} %select_n.43), kind=kOutput, calls=%fused_computation.5 | convolution fusion | flops 37748736 | bytes 630788 | tf_op jit(solution)/shard_map/rsk,rtk->st/dot_general | solution.py:33
  39.8 0.3 fusion.7
  40.1 0.4 convolution_convert_fusion
  40.4 0.1 copy.4
  40.6 8.2 %all_to_all.12 = bf16[8,32,192]{2,1,0:T(8,128)(2,1)S(1)} all-to-all(bf16[8,32,192]{2,1,0:T(8,128)(2,1)S(1)} %bitcast.67), channel_id=1, replica_groups=mesh['blk'=4,'rows'=8] {'rows'}, dimensions={0} | all-to-all | bytes 196608 | tf_op jit(solution)/shard_map/all_to_all | solution.py:79
  48.8 0.7 %copy.5 = bf16[256,192]{0,1:T(8,128)(2,1)} copy(bf16[256,192]{1,0:T(8,128)(2,1)S(1)} %bitcast.68) | data formatting | bytes 196608 | tf_op jit(solution)/shard_map/all_to_all | solution.py:79
  (7 shorter events, 0.1 us)
Async XLA Ops:
  0.0 32.2 %copy-start = (bf16[4,128,2048]{2,1,0:T(8,128)(2,1)S(1)}, bf16[4,128,2048]{2,1,0:T(8,128)(2,1)}, u32[]{:S(2)}) copy-start(bf16[4,128,2048]{2,1,0:T(8,128)(2,1)} %param.3) | copy-start | bytes 6291460
  1.1 30.6 %copy-start.1 = (s32[128,1]{0,1:T(1,128)S(1)}, s32[128,1]{0,1:T(1,128)}, u32[]{:S(2)}) copy-start(s32[128,1]{0,1:T(1,128)} %param.4) | copy-start | bytes 1540
  1.1 8.3 %collective-permute-start = (bf16[4,48,256]{2,1,0:T(8,128)(2,1)S(1)}, bf16[4,48,256]{2,1,0:T(8,128)(2,1)S(1)}, u32[]{:S(2)}, u32[]{:S(2)}) collective-permute-start(bf16[4,48,256]{2,1,0:T(8,128)(2,1)S(1)} %constant_dynamic-slice_fusion), channel_id=1, source_target_pairs={{0,24},{8,0},{16,8},{24,16},{1,25},{9,1},{17,9},{25,17},{2,26},{10... | collective-permute-start | bytes 294920 | tf_op jit(solution)/shard_map/ppermute | solution.py:39
  6.2 9.4 %collective-permute-start.2 = (bf16[4,48,256]{2,1,0:T(8,128)(2,1)S(1)}, bf16[4,48,256]{2,1,0:T(8,128)(2,1)S(1)}, u32[]{:S(2)}, u32[]{:S(2)}) collective-permute-start(bf16[4,48,256]{2,1,0:T(8,128)(2,1)S(1)} %constant_dynamic-slice_fusion), channel_id=1, source_target_pairs={{0,8},{8,16},{16,24},{24,0},{1,9},{9,17},{17,25},{25,1},{2,10},{10... | collective-permute-start | bytes 294920 | tf_op jit(solution)/shard_map/ppermute | solution.py:39
  6.2 9.4 %collective-permute-start.1 = (bf16[4,48,256]{2,1,0:T(8,128)(2,1)S(1)}, bf16[4,48,256]{2,1,0:T(8,128)(2,1)S(1)}, u32[]{:S(2)}, u32[]{:S(2)}) collective-permute-start(bf16[4,48,256]{2,1,0:T(8,128)(2,1)S(1)} %constant_dynamic-slice_fusion), channel_id=1, source_target_pairs={{0,16},{8,24},{16,0},{24,8},{1,17},{9,25},{17,1},{25,9},{2,18},{10... | collective-permute-start | bytes 294920 | tf_op jit(solution)/shard_map/ppermute | solution.py:39
  15.6 7.7 %collective-permute-start.4 = (bf16[4,144,256]{2,1,0:T(8,128)(2,1)S(1)}, bf16[4,144,256]{2,1,0:T(8,128)(2,1)S(1)}, u32[]{:S(2)}, u32[]{:S(2)}) collective-permute-start(bf16[4,144,256]{2,1,0:T(8,128)(2,1)S(1)} %constant_dynamic-update-slice_fusion), channel_id=1, source_target_pairs={{0,4},{1,5},{2,6},{3,7},{4,0},{5,1},{6,2},{7,3},{8,12},{9,13},{10,... | collective-permute-start | bytes 884744 | tf_op jit(solution)/shard_map/ppermute | solution.py:47
  17.2 8.0 %collective-permute-start.3 = (bf16[4,144,256]{2,1,0:T(8,128)(2,1)S(1)}, bf16[4,144,256]{2,1,0:T(8,128)(2,1)S(1)}, u32[]{:S(2)}, u32[]{:S(2)}) collective-permute-start(bf16[4,144,256]{2,1,0:T(8,128)(2,1)S(1)} %constant_dynamic-update-slice_fusion), channel_id=1, source_target_pairs={{0,2},{1,3},{2,0},{3,1},{4,6},{5,7},{6,4},{7,5},{8,10},{9,11},{10,... | collective-permute-start | bytes 884744 | tf_op jit(solution)/shard_map/ppermute | solution.py:46
  23.3 5.2 %collective-permute-start.5 = (bf16[4,144,128]{2,1,0:T(8,128)(2,1)S(1)}, bf16[4,144,128]{2,1,0:T(8,128)(2,1)S(1)}, u32[]{:S(2)}, u32[]{:S(2)}) collective-permute-start(bf16[4,144,128]{2,1,0:T(8,128)(2,1)S(1)} %slice.24), channel_id=1, source_target_pairs={{0,2},{1,3},{2,0},{3,1},{4,6},{5,7},{6,4},{7,5},{8,10},{9,11},{10,... | collective-permute-start | bytes 442376 | tf_op jit(solution)/shard_map/ppermute | solution.py:51
  25.2 5.2 %collective-permute-start.6 = (bf16[4,144,128]{2,1,0:T(8,128)(2,1)S(1)}, bf16[4,144,128]{2,1,0:T(8,128)(2,1)S(1)}, u32[]{:S(2)}, u32[]{:S(2)}) collective-permute-start(bf16[4,144,128]{2,1,0:T(8,128)(2,1)S(1)} %slice.25), channel_id=1, source_target_pairs={{0,4},{1,5},{2,6},{3,7},{4,0},{5,1},{6,2},{7,3},{8,12},{9,13},{10,... | collective-permute-start | bytes 442376 | tf_op jit(solution)/shard_map/ppermute | solution.py:52
  31.6 3.3 %collective-permute-start.7 = (bf16[4,4,144,256]{3,2,1,0:T(8,128)(2,1)}, bf16[4,4,144,256]{3,2,1,0:T(8,128)(2,1)}, u32[]{:S(2)}, u32[]{:S(2)}) collective-permute-start(bf16[4,4,144,256]{3,2,1,0:T(8,128)(2,1)} %pad_maximum_fusion), channel_id=1, source_target_pairs={{0,1},{1,0},{2,3},{3,2},{4,5},{5,4},{6,7},{7,6},{8,9},{9,8},{10,11... | collective-permute-start | bytes 3538952 | tf_op jit(solution)/shard_map/ppermute | solution.py:68

commit v4 on v3

--- a/solution.py
+++ b/solution.py
@@ -39,35 +39,37 @@
         arrived.append(lax.ppermute(piece, "blk", pairs))
     mine = jnp.concatenate(arrived, axis=1)
     own = jnp.einsum("rsk,rtk->st", features, test_blocks, preferred_element_type=jnp.float32)
+    mine, own = lax.optimization_barrier((mine, own))
     remote = term(here * chunk, chunk, mine)
     chip_bits = [1 << i for i in range(1, owners_n.bit_length() - 1)]
     if len(chip_bits) == 2:
         bx, by = chip_bits
         along_x = lax.ppermute(mine, "rows", xor_pairs(owners_n, bx))
         along_y = lax.ppermute(mine, "rows", xor_pairs(owners_n, by))
-        remote = remote + term((here ^ bx) * chunk, chunk, along_x)
-        remote = remote + term((here ^ by) * chunk, chunk, along_y)
+        sibling = lax.ppermute(jnp.stack([mine, along_x, along_y]), "rows", xor_pairs(owners_n, 1))
         half = chunk // 2
         first = lax.ppermute(along_y[:, :, :half], "rows", xor_pairs(owners_n, bx))
         second = lax.ppermute(along_x[:, :, half:], "rows", xor_pairs(owners_n, by))
+        remote = remote + term((here ^ bx) * chunk, chunk, along_x)
+        remote = remote + term((here ^ by) * chunk, chunk, along_y)
         corner = (here ^ bx ^ by) * chunk
         remote = remote + term(corner, half, first) + term(corner + half, half, second)
         diagonal = jnp.concatenate([first, second], axis=2)
-        held = jnp.stack([mine, along_x, along_y, diagonal])
-        masks = [0, bx, by, bx ^ by]
+        late = lax.ppermute(diagonal, "rows", xor_pairs(owners_n, 1))
+        parts = jnp.stack(
+            [lax.dynamic_slice_in_dim(features, (here ^ 1 ^ m) * chunk, chunk, axis=2) for m in (0, bx, by)]
+        )
+        remote = remote + jnp.einsum("jrsk,jrtk->st", parts, sibling, preferred_element_type=jnp.float32)
+        remote = remote + term((here ^ 1 ^ bx ^ by) * chunk, chunk, late)
     else:
         held = mine[None]
         masks = [0]
-        for mask in chip_bits:
+        for mask in chip_bits + [1]:
             got = lax.ppermute(held, "rows", xor_pairs(owners_n, mask))
             for j, m in enumerate(masks):
                 remote = remote + term((here ^ mask ^ m) * chunk, chunk, got[j])
             held = jnp.concatenate([held, got], axis=0)
             masks = masks + [m ^ mask for m in masks]
-    if owners_n > 1:
-        got = lax.ppermute(held, "rows", xor_pairs(owners_n, 1))
-        for j, m in enumerate(masks):
-            remote = remote + term((here ^ 1 ^ m) * chunk, chunk, got[j])
     relative = jnp.concatenate([own, remote], axis=1)
     doubled = jnp.concatenate([relative, relative], axis=1)
     start = ((blocks_n - block) % blocks_n) * width

time: 49.9 us -> 52.3 us (1.048)
  local copies, waits for them, and re-layouts: 1.98 us -> 4.41 us
  waiting for transfers between devices: 17.2 us -> 14.9 us
  other arithmetic: 1.63 us -> 3.41 us
  blocking collectives: 8.23 us -> 9.14 us
  starting transfers between devices: 12 us -> 11.3 us
    ppermute x1, waiting for transfers between devices: 0.29 us -> 5.24 us  [on_device(): along_x = lax.ppermute(mine, 'rows', xor_pairs(owners_n, bx))]
    ppermute x1, waiting for transfers between devices: 4.67 us -> 1.21 us  [on_device(): along_y = lax.ppermute(mine, 'rows', xor_pairs(owners_n, by))]
    ppermute x3, waiting for transfers between devices: 8.35 us -> 4.99 us  [on_device(): arrived.append(lax.ppermute(piece, 'blk', pairs))]
    concatenate x0 -> x2, other arithmetic: none -> 1.93 us  [the longest x1 1.01 us: on_device(): diagonal = jnp.concatenate([first, second], axis=2)]
    dot_general x9 -> x6, matrix products: 5.98 us -> 4.17 us  [term(): jnp.einsum('rsk,rtk->st', part, tests, preferred_element_type=jnp.float32)]
    dot_general x0 -> x1, matrix products: none -> 1.57 us  [on_device(): jnp.einsum('jrsk,jrtk->st', parts, sibling, preferred_element_type=jnp.fl...]
    unnamed x6 -> x14, local copies, waits for them, and re-layouts: 0.02 us -> 1.16 us
    dynamic_slice x1, local copies, waits for them, and re-layouts: 1.05 us -> 0.01 us  [on_device(): piece = lax.dynamic_slice_in_dim(test_blocks, here * chunk, chunk, axis=2)]
  transfers between devices with their start and end apart: 8 -> 9, of which waited for: 6 -> 5; matrix products, arithmetic and copies ran while one was open for 6% -> 20% of each run, Pallas kernels for 0% -> 0%
where the time goes in v4:
time: 52.3 us; the launch traced here: 51.9 us
  waiting for transfers between devices  14.9 us (28%)
  starting transfers between devices  11.3 us (22%)
  blocking collectives  9.14 us (17%)
  matrix products  8.52 us (16%)
  local copies, waits for them, and re-layouts  4.41 us (8%)
  other arithmetic  3.41 us (7%)
    all_to_all x1, blocking collectives, on_device(): lax.all_to_all(placed, 'rows', split_axis=0, concat_axis=0, tiled=True)  9.14 us
    ppermute x3, starting transfers between devices, on_device(): arrived.append(lax.ppermute(piece, 'blk', pairs))  6.11 us
    ppermute x1, waiting for transfers between devices, on_device(): along_x = lax.ppermute(mine, 'rows', xor_pairs(owners_n, bx))  5.24 us
    ppermute x3, waiting for transfers between devices, on_device(): arrived.append(lax.ppermute(piece, 'blk', pairs))  4.99 us
    dot_general x6, matrix products, term(): jnp.einsum('rsk,rtk->st', part, tests, preferred_element_type=jnp.float32)  4.17 us
    ppermute x1, waiting for transfers between devices, on_device(): first = lax.ppermute(along_y[:, :, :half], 'rows', xor_pairs(owners_n, bx))  2.52 us
    dot_general x1, matrix products, on_device(): jnp.einsum('rsk,rtk->st', features, test_blocks, preferred_element_type=j...  2.42 us
    dot_general x1, matrix products, on_device(): jnp.einsum('jrsk,jrtk->st', parts, sibling, preferred_element_type=jnp.fl...  1.57 us
  transfers between devices with their start and end apart: 9, of which 5 were waited for; matrix products, arithmetic and copies ran while one was open for 20% of the time, Pallas kernels for 0%

profile of v4, /device:TPU:0, one launch (start us, length us, event | category | flops | bytes accessed | tf_op | source)
XLA Modules:
  0.0 51.9 jit_solution(967385872128937929)
XLA Ops:
  0.0 0.0 copy-start
  0.0 0.0 copy-start.6
  0.0 1.1 %copy-done = bf16[4,48,2048]{2,1,0:T(8,128)(2,1)S(1)} copy-done((bf16[4,48,2048]{2,1,0:T(8,128)(2,1)S(1)}, bf16[4,48,2048]{2,1,0:T(8,128)(2,1)}, u32[]{:S(2)}) %copy-start) | copy-done | bytes 786456
  1.2 5.1 %collective-permute-start = (bf16[4,48,256]{2,1,0:T(8,128)(2,1)S(1)}, bf16[4,48,256]{2,1,0:T(8,128)(2,1)S(1)}, u32[]{:S(2)}, u32[]{:S(2)}) collective-permute-start(bf16[4,48,256]{2,1,0:T(8,128)(2,1)S(1)} %constant_dynamic-slice_fusion), channel_id=1, source_target_pairs={{0,24},{8,0},{16,8},{24,16},{1,25},{9,1},{17,9},{25,17},{2,26},{10... | collective-permute-start | bytes 294920 | tf_op jit(solution)/shard_map/ppermute | solution.py:39
  6.3 0.0 collective-permute-start.1
  6.3 1.0 %collective-permute-start.2 = (bf16[4,48,256]{2,1,0:T(8,128)(2,1)S(1)}, bf16[4,48,256]{2,1,0:T(8,128)(2,1)}, u32[]{:S(2)}, u32[]{:S(2)}) collective-permute-start(bf16[4,48,256]{2,1,0:T(8,128)(2,1)S(1)} %constant_dynamic-slice_fusion), channel_id=1, source_target_pairs={{0,8},{8,16},{16,24},{24,0},{1,9},{9,17},{17,25},{25,1},{2,10},{10... | collective-permute-start | bytes 294920 | tf_op jit(solution)/shard_map/ppermute | solution.py:39
  7.3 2.4 %convolution_bitcast_fusion.7 = bf16[128,48]{0,1:T(8,128)(2,1)S(1)} fusion(bf16[4,128,2048]{2,1,0:T(8,128)(2,1)} %param.3, bf16[4,48,2048]{2,1,0:T(8,128)(2,1)S(1)} %copy-done), kind=kOutput, calls=%fused_computation.14 | convolution fusion | flops 100663296 | bytes 2895872 | tf_op jit(solution)/shard_map/rsk,rtk->st/dot_general | solution.py:41
  9.7 0.0 copy-start.1
  9.7 0.0 copy-done.6
  9.7 0.1 fusion.22
  9.8 0.2 reduce_window_sum.11
  10.0 0.0 collective-permute-done
  10.0 5.0 %collective-permute-done.1 = bf16[4,48,256]{2,1,0:T(8,128)(2,1)S(1)} collective-permute-done((bf16[4,48,256]{2,1,0:T(8,128)(2,1)S(1)}, bf16[4,48,256]{2,1,0:T(8,128)(2,1)S(1)}, u32[]{:S(2)}, u32[]{:S(2)}) %collective-permute-start.1) | collective-permute-done | bytes 98336 | tf_op jit(solution)/shard_map/ppermute | solution.py:39
  15.0 0.0 collective-permute-done.2
  15.0 0.9 %pad_maximum_fusion.1 = bf16[4,144,256]{2,1,0:T(8,128)(2,1)S(1)} fusion(bf16[4,48,256]{2,1,0:T(8,128)(2,1)} %collective-permute-done.2, bf16[4,48,256]{2,1,0:T(8,128)(2,1)S(1)} %collective-permute-done.1, bf16[4,48,256]{2,1,0:T(8,128)(2,1)S(1)} %collective-permute-done), kind=kLoop, calls=%fused_computation.21 | loop fusion | flops 884736 | bytes 589824 | tf_op jit(solution)/shard_map/concatenate | solution.py:40
  15.9 1.6 %collective-permute-start.3 = (bf16[4,144,256]{2,1,0:T(8,128)(2,1)S(1)}, bf16[4,144,256]{2,1,0:T(8,128)(2,1)S(1)}, u32[]{:S(2)}, u32[]{:S(2)}) collective-permute-start(bf16[4,144,256]{2,1,0:T(8,128)(2,1)S(1)} %pad_maximum_fusion.1), channel_id=1, source_target_pairs={{0,2},{1,3},{2,0},{3,1},{4,6},{5,7},{6,4},{7,5},{8,10},{9,11},{10,... | collective-permute-start | bytes 884744 | tf_op jit(solution)/shard_map/ppermute | solution.py:47
  17.5 1.5 %collective-permute-start.4 = (bf16[4,144,256]{2,1,0:T(8,128)(2,1)S(1)}, bf16[4,144,256]{2,1,0:T(8,128)(2,1)S(1)}, u32[]{:S(2)}, u32[]{:S(2)}) collective-permute-start(bf16[4,144,256]{2,1,0:T(8,128)(2,1)S(1)} %pad_maximum_fusion.1), channel_id=1, source_target_pairs={{0,4},{1,5},{2,6},{3,7},{4,0},{5,1},{6,2},{7,3},{8,12},{9,13},{10,... | collective-permute-start | bytes 884744 | tf_op jit(solution)/shard_map/ppermute | solution.py:48
  19.0 0.2 select_reduce_fusion
  19.2 5.2 %collective-permute-done.3 = bf16[4,144,256]{2,1,0:T(8,128)(2,1)S(1)} collective-permute-done((bf16[4,144,256]{2,1,0:T(8,128)(2,1)S(1)}, bf16[4,144,256]{2,1,0:T(8,128)(2,1)S(1)}, u32[]{:S(2)}, u32[]{:S(2)}) %collective-permute-start.3) | collective-permute-done | bytes 294944 | tf_op jit(solution)/shard_map/ppermute | solution.py:47
  24.4 1.2 %collective-permute-done.4 = bf16[4,144,256]{2,1,0:T(8,128)(2,1)S(1)} collective-permute-done((bf16[4,144,256]{2,1,0:T(8,128)(2,1)S(1)}, bf16[4,144,256]{2,1,0:T(8,128)(2,1)S(1)}, u32[]{:S(2)}, u32[]{:S(2)}) %collective-permute-start.4) | collective-permute-done | bytes 294944 | tf_op jit(solution)/shard_map/ppermute | solution.py:48
  25.6 0.0 copy-start.2
  25.6 1.0 %pad_maximum_fusion = bf16[3,4,144,256]{3,2,1,0:T(8,128)(2,1)} fusion(bf16[1,4,144,256]{3,2,1,0:T(8,128)(2,1)S(1)} %bitcast.54, bf16[1,4,144,256]{3,2,1,0:T(8,128)(2,1)S(1)} %bitcast.53, bf16[1,4,144,256]{3,2,1,0:T(8,128)(2,1)S(1)} %bitcast.52), kind=kLoop, calls=%fused_computation.15 | loop fusion | flops 884736 | bytes 1769472 | tf_op jit(solution)/shard_map/stack | solution.py:49
  26.7 0.0 collective-permute-start.7
  26.7 0.0 copy-done.2
  26.7 0.7 %slice.8 = bf16[4,144,128]{2,1,0:T(8,128)(2,1)} slice(bf16[4,144,256]{2,1,0:T(8,128)(2,1)S(1)} %collective-permute-done.4), slice={[0:4], [0:144], [0:128]} | slice | bytes 294912 | tf_op jit(solution)/shard_map/slice | solution.py:51
  27.4 0.5 %collective-permute-start.5 = (bf16[4,144,128]{2,1,0:T(8,128)(2,1)}, bf16[4,144,128]{2,1,0:T(8,128)(2,1)}, u32[]{:S(2)}, u32[]{:S(2)}) collective-permute-start(bf16[4,144,128]{2,1,0:T(8,128)(2,1)} %slice.8), channel_id=1, source_target_pairs={{0,2},{1,3},{2,0},{3,1},{4,6},{5,7},{6,4},{7,5},{8,10},{9,11},{10,... | collective-permute-start | bytes 442376 | tf_op jit(solution)/shard_map/ppermute | solution.py:51
  27.9 0.7 %slice.9 = bf16[4,144,128]{2,1,0:T(8,128)(2,1)} slice(bf16[4,144,256]{2,1,0:T(8,128)(2,1)S(1)} %collective-permute-done.3), slice={[0:4], [0:144], [128:256]} | slice | bytes 294912 | tf_op jit(solution)/shard_map/slice | solution.py:52
  28.6 1.5 %collective-permute-start.6 = (bf16[4,144,128]{2,1,0:T(8,128)(2,1)}, bf16[4,144,128]{2,1,0:T(8,128)(2,1)}, u32[]{:S(2)}, u32[]{:S(2)}) collective-permute-start(bf16[4,144,128]{2,1,0:T(8,128)(2,1)} %slice.9), channel_id=1, source_target_pairs={{0,4},{1,5},{2,6},{3,7},{4,0},{5,1},{6,2},{7,3},{8,12},{9,13},{10,... | collective-permute-start | bytes 442376 | tf_op jit(solution)/shard_map/ppermute | solution.py:52
  30.1 0.0 copy-done.1
  30.1 0.9 %dynamic-slice_bitcast_fusion.2 = (bf16[1,4,128,256]{3,2,1,0:T(8,128)(2,1)}, bf16[1,4,128,256]{3,2,1,0:T(8,128)(2,1)}, bf16[1,4,128,256]{3,2,1,0:T(8,128)(2,1)}) fusion(bf16[4,128,2048]{2,1,0:T(8,128)(2,1)S(1)} %copy-done.1, s32[]{:T(128)S(6)} %select_n.43, s32[]{:T(128)S(6)} %select_n.44, s32[]{:T(128)S(6)} %select_n.45), kind=kLoop, calls=%fused_computation.26 | loop fusion | bytes 1572876 | tf_op jit(solution)/shard_map/stack | solution.py:59
  31.0 0.1 copy.6
  31.2 0.0 copy-start.3
  31.2 0.0 copy-start.4
  31.2 0.0 copy-start.5
  31.2 0.2 convolution_bitcast_fusion.3
  31.4 2.5 %collective-permute-done.5 = bf16[4,144,128]{2,1,0:T(8,128)(2,1)} collective-permute-done((bf16[4,144,128]{2,1,0:T(8,128)(2,1)}, bf16[4,144,128]{2,1,0:T(8,128)(2,1)}, u32[]{:S(2)}, u32[]{:S(2)}) %collective-permute-start.5) | collective-permute-done | bytes 147488 | tf_op jit(solution)/shard_map/ppermute | solution.py:51
  34.0 0.9 %collective-permute-done.6 = bf16[4,144,128]{2,1,0:T(8,128)(2,1)} collective-permute-done((bf16[4,144,128]{2,1,0:T(8,128)(2,1)}, bf16[4,144,128]{2,1,0:T(8,128)(2,1)}, u32[]{:S(2)}, u32[]{:S(2)}) %collective-permute-start.6) | collective-permute-done | bytes 147488 | tf_op jit(solution)/shard_map/ppermute | solution.py:52
  34.9 1.0 %pad_maximum_fusion.2 = bf16[4,144,256]{2,1,0:T(8,128)(2,1)S(1)} fusion(bf16[4,144,128]{2,1,0:T(8,128)(2,1)} %collective-permute-done.6, bf16[4,144,128]{2,1,0:T(8,128)(2,1)} %collective-permute-done.5), kind=kLoop, calls=%fused_computation.22 | loop fusion | flops 589824 | bytes 589824 | tf_op jit(solution)/shard_map/concatenate | solution.py:57
  35.9 0.1 collective-permute-start.8
  36.0 1.2 %convolution_bitcast_fusion.1 = f32[128,144]{1,0:T(8,128)S(1)} fusion(bf16[4,144,256]{2,1,0:T(8,128)(2,1)} %copy-done.2, bf16[4,128,2048]{2,1,0:T(8,128)(2,1)S(1)} %copy-done.1, s32[]{:T(128)S(6)} %select_n.40), kind=kOutput, calls=%fused_computation.2 | convolution fusion | flops 37748736 | bytes 630788 | tf_op jit(solution)/shard_map/rsk,rtk->st/dot_general | solution.py:33
  37.2 1.1 %convolution_bitcast_fusion.4 = f32[128,144]{1,0:T(8,128)S(1)} fusion(bf16[4,144,128]{2,1,0:T(8,128)(2,1)} %collective-permute-done.6, bf16[4,128,2048]{2,1,0:T(8,128)(2,1)S(1)} %copy-done.1, s32[]{:T(128)S(6)} %select_n.42), kind=kOutput, calls=%fused_computation.5 | convolution fusion | flops 18874368 | bytes 352260 | tf_op jit(solution)/shard_map/rsk,rtk->st/dot_general | solution.py:33
  38.3 1.1 %convolution_bitcast_fusion.5 = f32[128,144]{1,0:T(8,128)S(1)} fusion(bf16[4,144,128]{2,1,0:T(8,128)(2,1)} %collective-permute-done.5, bf16[4,128,2048]{2,1,0:T(8,128)(2,1)S(1)} %copy-done.1, s32[]{:T(128)S(6)} %select_n.41), kind=kOutput, calls=%fused_computation.6 | convolution fusion | flops 18874368 | bytes 352260 | tf_op jit(solution)/shard_map/rsk,rtk->st/dot_general | solution.py:33
  39.4 0.0 collective-permute-done.8
  39.4 0.2 convolution_bitcast_fusion
  39.7 0.0 collective-permute-done.7
  39.7 0.0 copy-done.3
  39.7 0.0 copy-done.4
  39.7 0.0 copy-done.5
  39.7 1.6 %convolution_bitcast_fusion.6 = f32[128,144]{1,0:T(8,128)S(1)} fusion(bf16[3,4,144,256]{3,2,1,0:T(8,128)(2,1)} %collective-permute-done.7, bf16[1,4,128,256]{3,2,1,0:T(8,128)(2,1)S(1)} %copy-done.5, bf16[1,4,128,256]{3,2,1,0:T(8,128)(2,1)S(1)} %copy-done.4, bf16[1,4,128,256]{3,2,1,0:T(8,128)(2,1)S(1)} %copy-done.3), kind=kOutput, calls=%fused_computation.7 | convolution fusion | flops 114032640 | bytes 1744896 | tf_op jit(solution)/shard_map/jrsk,jrtk->st/dot_general | solution.py:62
  41.3 0.2 fusion.5
  41.6 0.4 convolution_convert_fusion
  41.9 0.1 copy.8
  42.0 9.1 %all_to_all.12 = bf16[8,32,192]{2,1,0:T(8,128)(2,1)S(1)} all-to-all(bf16[8,32,192]{2,1,0:T(8,128)(2,1)S(1)} %bitcast.55), channel_id=1, replica_groups=mesh['blk'=4,'rows'=8] {'rows'}, dimensions={0} | all-to-all | bytes 196608 | tf_op jit(solution)/shard_map/all_to_all | solution.py:81
  51.2 0.7 %copy.9 = bf16[256,192]{0,1:T(8,128)(2,1)} copy(bf16[256,192]{1,0:T(8,128)(2,1)S(1)} %bitcast.56) | data formatting | bytes 196608 | tf_op jit(solution)/shard_map/all_to_all | solution.py:81
  (2 shorter events, 0.0 us)
Async XLA Ops:
  0.0 1.1 %copy-start = (bf16[4,48,2048]{2,1,0:T(8,128)(2,1)S(1)}, bf16[4,48,2048]{2,1,0:T(8,128)(2,1)}, u32[]{:S(2)}) copy-start(bf16[4,48,2048]{2,1,0:T(8,128)(2,1)} %param.5) | copy-start | bytes 2359300
  0.0 9.7 %copy-start.6 = (s32[128,1]{0,1:T(1,128)S(1)}, s32[128,1]{0,1:T(1,128)}, u32[]{:S(2)}) copy-start(s32[128,1]{0,1:T(1,128)} %param.4) | copy-start | bytes 1540
  1.2 8.9 %collective-permute-start = (bf16[4,48,256]{2,1,0:T(8,128)(2,1)S(1)}, bf16[4,48,256]{2,1,0:T(8,128)(2,1)S(1)}, u32[]{:S(2)}, u32[]{:S(2)}) collective-permute-start(bf16[4,48,256]{2,1,0:T(8,128)(2,1)S(1)} %constant_dynamic-slice_fusion), channel_id=1, source_target_pairs={{0,24},{8,0},{16,8},{24,16},{1,25},{9,1},{17,9},{25,17},{2,26},{10... | collective-permute-start | bytes 294920 | tf_op jit(solution)/shard_map/ppermute | solution.py:39
  6.3 8.7 %collective-permute-start.1 = (bf16[4,48,256]{2,1,0:T(8,128)(2,1)S(1)}, bf16[4,48,256]{2,1,0:T(8,128)(2,1)S(1)}, u32[]{:S(2)}, u32[]{:S(2)}) collective-permute-start(bf16[4,48,256]{2,1,0:T(8,128)(2,1)S(1)} %constant_dynamic-slice_fusion), channel_id=1, source_target_pairs={{0,16},{8,24},{16,0},{24,8},{1,17},{9,25},{17,1},{25,9},{2,18},{10... | collective-permute-start | bytes 294920 | tf_op jit(solution)/shard_map/ppermute | solution.py:39
  6.3 8.7 %collective-permute-start.2 = (bf16[4,48,256]{2,1,0:T(8,128)(2,1)S(1)}, bf16[4,48,256]{2,1,0:T(8,128)(2,1)}, u32[]{:S(2)}, u32[]{:S(2)}) collective-permute-start(bf16[4,48,256]{2,1,0:T(8,128)(2,1)S(1)} %constant_dynamic-slice_fusion), channel_id=1, source_target_pairs={{0,8},{8,16},{16,24},{24,0},{1,9},{9,17},{17,25},{25,1},{2,10},{10... | collective-permute-start | bytes 294920 | tf_op jit(solution)/shard_map/ppermute | solution.py:39
  9.7 20.4 %copy-start.1 = (bf16[4,128,2048]{2,1,0:T(8,128)(2,1)S(1)}, bf16[4,128,2048]{2,1,0:T(8,128)(2,1)}, u32[]{:S(2)}) copy-start(bf16[4,128,2048]{2,1,0:T(8,128)(2,1)} %param.3) | copy-start | bytes 6291460
  15.9 8.5 %collective-permute-start.3 = (bf16[4,144,256]{2,1,0:T(8,128)(2,1)S(1)}, bf16[4,144,256]{2,1,0:T(8,128)(2,1)S(1)}, u32[]{:S(2)}, u32[]{:S(2)}) collective-permute-start(bf16[4,144,256]{2,1,0:T(8,128)(2,1)S(1)} %pad_maximum_fusion.1), channel_id=1, source_target_pairs={{0,2},{1,3},{2,0},{3,1},{4,6},{5,7},{6,4},{7,5},{8,10},{9,11},{10,... | collective-permute-start | bytes 884744 | tf_op jit(solution)/shard_map/ppermute | solution.py:47
  17.5 8.2 %collective-permute-start.4 = (bf16[4,144,256]{2,1,0:T(8,128)(2,1)S(1)}, bf16[4,144,256]{2,1,0:T(8,128)(2,1)S(1)}, u32[]{:S(2)}, u32[]{:S(2)}) collective-permute-start(bf16[4,144,256]{2,1,0:T(8,128)(2,1)S(1)} %pad_maximum_fusion.1), channel_id=1, source_target_pairs={{0,4},{1,5},{2,6},{3,7},{4,0},{5,1},{6,2},{7,3},{8,12},{9,13},{10,... | collective-permute-start | bytes 884744 | tf_op jit(solution)/shard_map/ppermute | solution.py:48
  25.6 1.1 %copy-start.2 = (bf16[4,144,256]{2,1,0:T(8,128)(2,1)}, bf16[4,144,256]{2,1,0:T(8,128)(2,1)S(1)}, u32[]{:S(2)}) copy-start(bf16[4,144,256]{2,1,0:T(8,128)(2,1)S(1)} %collective-permute-done.4) | copy-start | bytes 884740
  26.7 13.0 %collective-permute-start.7 = (bf16[3,4,144,256]{3,2,1,0:T(8,128)(2,1)}, bf16[3,4,144,256]{3,2,1,0:T(8,128)(2,1)}, u32[]{:S(2)}, u32[]{:S(2)}) collective-permute-start(bf16[3,4,144,256]{3,2,1,0:T(8,128)(2,1)} %pad_maximum_fusion), channel_id=1, source_target_pairs={{0,1},{1,0},{2,3},{3,2},{4,5},{5,4},{6,7},{7,6},{8,9},{9,8},{10,11... | collective-permute-start | bytes 2654216 | tf_op jit(solution)/shard_map/ppermute | solution.py:49
  27.4 6.6 %collective-permute-start.5 = (bf16[4,144,128]{2,1,0:T(8,128)(2,1)}, bf16[4,144,128]{2,1,0:T(8,128)(2,1)}, u32[]{:S(2)}, u32[]{:S(2)}) collective-permute-start(bf16[4,144,128]{2,1,0:T(8,128)(2,1)} %slice.8), channel_id=1, source_target_pairs={{0,2},{1,3},{2,0},{3,1},{4,6},{5,7},{6,4},{7,5},{8,10},{9,11},{10,... | collective-permute-start | bytes 442376 | tf_op jit(solution)/shard_map/ppermute | solution.py:51
  28.6 6.3 %collective-permute-start.6 = (bf16[4,144,128]{2,1,0:T(8,128)(2,1)}, bf16[4,144,128]{2,1,0:T(8,128)(2,1)}, u32[]{:S(2)}, u32[]{:S(2)}) collective-permute-start(bf16[4,144,128]{2,1,0:T(8,128)(2,1)} %slice.9), channel_id=1, source_target_pairs={{0,4},{1,5},{2,6},{3,7},{4,0},{5,1},{6,2},{7,3},{8,12},{9,13},{10,... | collective-permute-start | bytes 442376 | tf_op jit(solution)/shard_map/ppermute | solution.py:52
  31.2 8.6 %copy-start.3 = (bf16[1,4,128,256]{3,2,1,0:T(8,128)(2,1)S(1)}, bf16[1,4,128,256]{3,2,1,0:T(8,128)(2,1)}, u32[]{:S(2)}) copy-start(bf16[1,4,128,256]{3,2,1,0:T(8,128)(2,1)} %get-tuple-element.9) | copy-start | bytes 786436
  31.2 8.6 %copy-start.4 = (bf16[1,4,128,256]{3,2,1,0:T(8,128)(2,1)S(1)}, bf16[1,4,128,256]{3,2,1,0:T(8,128)(2,1)}, u32[]{:S(2)}) copy-start(bf16[1,4,128,256]{3,2,1,0:T(8,128)(2,1)} %get-tuple-element.10) | copy-start | bytes 786436
  31.2 8.6 %copy-start.5 = (bf16[1,4,128,256]{3,2,1,0:T(8,128)(2,1)S(1)}, bf16[1,4,128,256]{3,2,1,0:T(8,128)(2,1)}, u32[]{:S(2)}) copy-start(bf16[1,4,128,256]{3,2,1,0:T(8,128)(2,1)} %get-tuple-element.11) | copy-start | bytes 786436
  35.9 3.5 %collective-permute-start.8 = (bf16[4,144,256]{2,1,0:T(8,128)(2,1)S(1)}, bf16[4,144,256]{2,1,0:T(8,128)(2,1)S(1)}, u32[]{:S(2)}, u32[]{:S(2)}) collective-permute-start(bf16[4,144,256]{2,1,0:T(8,128)(2,1)S(1)} %pad_maximum_fusion.2), channel_id=1, source_target_pairs={{0,1},{1,0},{2,3},{3,2},{4,5},{5,4},{6,7},{7,6},{8,9},{9,8},{10,11... | collective-permute-start | bytes 884744 | tf_op jit(solution)/shard_map/ppermute | solution.py:58

commit v5 on v4

--- a/solution.py
+++ b/solution.py
@@ -40,28 +40,36 @@
     mine = jnp.concatenate(arrived, axis=1)
     own = jnp.einsum("rsk,rtk->st", features, test_blocks, preferred_element_type=jnp.float32)
     mine, own = lax.optimization_barrier((mine, own))
-    remote = term(here * chunk, chunk, mine)
     chip_bits = [1 << i for i in range(1, owners_n.bit_length() - 1)]
     if len(chip_bits) == 2:
         bx, by = chip_bits
+        masks = [0, bx, by, bx ^ by]
+        lent = jnp.stack(
+            [lax.dynamic_slice_in_dim(features, (here ^ 1 ^ m) * chunk, chunk, axis=2) for m in masks]
+        )
+        lent = lax.ppermute(lent, "rows", xor_pairs(owners_n, 1))
+        both = [
+            jnp.concatenate(
+                [lax.dynamic_slice_in_dim(features, (here ^ m) * chunk, chunk, axis=2), lent[j]], axis=1
+            )
+            for j, m in enumerate(masks)
+        ]
+
+        def pair_term(j, tests, lo=0, size=chunk):
+            rows = both[j][:, :, lo:lo + size]
+            return jnp.einsum("rsk,rtk->st", rows, tests, preferred_element_type=jnp.float32)
+
         along_x = lax.ppermute(mine, "rows", xor_pairs(owners_n, bx))
         along_y = lax.ppermute(mine, "rows", xor_pairs(owners_n, by))
-        sibling = lax.ppermute(jnp.stack([mine, along_x, along_y]), "rows", xor_pairs(owners_n, 1))
         half = chunk // 2
         first = lax.ppermute(along_y[:, :, :half], "rows", xor_pairs(owners_n, bx))
         second = lax.ppermute(along_x[:, :, half:], "rows", xor_pairs(owners_n, by))
-        remote = remote + term((here ^ bx) * chunk, chunk, along_x)
-        remote = remote + term((here ^ by) * chunk, chunk, along_y)
-        corner = (here ^ bx ^ by) * chunk
-        remote = remote + term(corner, half, first) + term(corner + half, half, second)
-        diagonal = jnp.concatenate([first, second], axis=2)
-        late = lax.ppermute(diagonal, "rows", xor_pairs(owners_n, 1))
-        parts = jnp.stack(
-            [lax.dynamic_slice_in_dim(features, (here ^ 1 ^ m) * chunk, chunk, axis=2) for m in (0, bx, by)]
-        )
-        remote = remote + jnp.einsum("jrsk,jrtk->st", parts, sibling, preferred_element_type=jnp.float32)
-        remote = remote + term((here ^ 1 ^ bx ^ by) * chunk, chunk, late)
+        paired = pair_term(0, mine) + pair_term(1, along_x) + pair_term(2, along_y)
+        paired = paired + pair_term(3, first, 0, half) + pair_term(3, second, half, half)
+        returned = lax.ppermute(paired[local_rows:], "rows", xor_pairs(owners_n, 1))
+        remote = paired[:local_rows] + returned
     else:
+        remote = term(here * chunk, chunk, mine)
         held = mine[None]
         masks = [0]
         for mask in chip_bits + [1]:

time: 52.3 us -> 50.7 us (0.969)
  matrix products: 8.52 us -> 4.6 us
  waiting for transfers between devices: 14.9 us -> 17.6 us
  other arithmetic: 3.41 us -> 2.06 us
  local copies, waits for them, and re-layouts: 4.41 us -> 5.37 us
    ppermute x1, waiting for transfers between devices: 5.24 us -> 0.01 us  [on_device(): along_x = lax.ppermute(mine, 'rows', xor_pairs(owners_n, bx))]
    ppermute x1, waiting for transfers between devices: 1.21 us -> 5.16 us  [on_device(): along_y = lax.ppermute(mine, 'rows', xor_pairs(owners_n, by))]
    ppermute x3, waiting for transfers between devices: 4.99 us -> 7.9 us  [on_device(): arrived.append(lax.ppermute(piece, 'blk', pairs))]
    dynamic_slice x0 -> x1, local copies, waits for them, and re-layouts: none -> 2.56 us  [on_device(): lax.dynamic_slice_in_dim(features, (here ^ m) * chunk, chunk, axis=2)]
    dot_general x7 -> x5, matrix products: 5.73 us -> 3.33 us  [pair_term(): jnp.einsum('rsk,rtk->st', rows, tests, preferred_element_type=jnp.float32)]
    dot_general x1, matrix products: 2.42 us -> 0.83 us  [on_device(): jnp.einsum('rsk,rtk->st', features, test_blocks, preferred_element_type=j...]
    ppermute x2, waiting for transfers between devices: 0.01 us -> 1.22 us  [the longest x1 1.22 us: on_device(): returned = lax.ppermute(paired[local_rows:], 'rows', xor_pairs(owners_n, 1))]
    unnamed x14 -> x12, local copies, waits for them, and re-layouts: 1.16 us -> 0.03 us
  transfers between devices with their start and end apart: 9 -> 9, of which waited for: 5 -> 6; matrix products, arithmetic and copies ran while one was open for 20% -> 10% of each run, Pallas kernels for 0% -> 0%
where the time goes in v5:
time: 50.7 us; the launch traced here: 50.4 us
  waiting for transfers between devices  17.6 us (35%)
  starting transfers between devices  11.5 us (23%)
  blocking collectives  9.05 us (18%)
  local copies, waits for them, and re-layouts  5.37 us (11%)
  matrix products  4.6 us (9%)
  other arithmetic  2.06 us (4%)
    all_to_all x1, blocking collectives, on_device(): lax.all_to_all(placed, 'rows', split_axis=0, concat_axis=0, tiled=True)  9.05 us
    ppermute x3, waiting for transfers between devices, on_device(): arrived.append(lax.ppermute(piece, 'blk', pairs))  7.9 us
    ppermute x3, starting transfers between devices, on_device(): arrived.append(lax.ppermute(piece, 'blk', pairs))  5.7 us
    ppermute x1, waiting for transfers between devices, on_device(): along_y = lax.ppermute(mine, 'rows', xor_pairs(owners_n, by))  5.16 us
    dot_general x5, matrix products, pair_term(): jnp.einsum('rsk,rtk->st', rows, tests, preferred_element_type=jnp.float32)  3.33 us
    dynamic_slice x1, local copies, waits for them, and re-layouts, on_device(): lax.dynamic_slice_in_dim(features, (here ^ m) * chunk, chunk, axis=2)  2.56 us
    ppermute x1, waiting for transfers between devices, on_device(): first = lax.ppermute(along_y[:, :, :half], 'rows', xor_pairs(owners_n, bx))  2.01 us
    ppermute x1, starting transfers between devices, on_device(): second = lax.ppermute(along_x[:, :, half:], 'rows', xor_pairs(owners_n, by))  1.58 us
  transfers between devices with their start and end apart: 9, of which 6 were waited for; matrix products, arithmetic and copies ran while one was open for 10% of the time, Pallas kernels for 0%

profile of v5, /device:TPU:0, one launch (start us, length us, event | category | flops | bytes accessed | tf_op | source)
XLA Modules:
  0.0 50.4 jit_solution(14357904950182746887)
XLA Ops:
  0.0 0.0 copy-start
  0.0 2.6 %constant_dynamic-slice_fusion.3 = (bf16[4,128,256]{2,1,0:T(8,128)(2,1)}, bf16[4,128,256]{2,1,0:T(8,128)(2,1)}, bf16[1,4,128,256]{3,2,1,0:T(8,128)(2,1)S(1)}, bf...) fusion(bf16[4,128,2048]{2,1,0:T(8,128)(2,1)} %param.3, ...), kind=kLoop, calls=%fused_computation.52 | loop fusion | bytes 4194336 | tf_op jit(solution)/shard_map/dynamic_slice | solution.py:53
  2.6 0.0 copy-start.1
  2.6 0.1 pad_maximum_fusion
  2.7 0.0 copy-start.5
  2.7 0.5 %collective-permute-start.3 = (bf16[4,4,128,256]{3,2,1,0:T(8,128)(2,1)S(1)}, bf16[4,4,128,256]{3,2,1,0:T(8,128)(2,1)S(1)}, u32[]{:S(2)}, u32[]{:S(2)}) collective-permute-start(bf16[4,4,128,256]{3,2,1,0:T(8,128)(2,1)S(1)} %pad_maximum_fusion), channel_id=1, source_target_pairs={{0,1},{1,0},{2,3},{3,2},{4,5},{5,4},{6,7},{7,6},{8,9},{9,8},{10,11... | collective-permute-start | bytes 3145736 | tf_op jit(solution)/shard_map/ppermute | solution.py:50
  3.2 0.0 copy-done
  3.3 4.7 %collective-permute-start = (bf16[4,48,256]{2,1,0:T(8,128)(2,1)S(1)}, bf16[4,48,256]{2,1,0:T(8,128)(2,1)S(1)}, u32[]{:S(2)}, u32[]{:S(2)}) collective-permute-start(bf16[4,48,256]{2,1,0:T(8,128)(2,1)S(1)} %constant_dynamic-slice_fusion.4), channel_id=1, source_target_pairs={{0,24},{8,0},{16,8},{24,16},{1,25},{9,1},{17,9},{25,17},{2,26},{10... | collective-permute-start | bytes 294920 | tf_op jit(solution)/shard_map/ppermute | solution.py:39
  7.9 0.0 collective-permute-start.1
  7.9 1.0 %collective-permute-start.2 = (bf16[4,48,256]{2,1,0:T(8,128)(2,1)S(1)}, bf16[4,48,256]{2,1,0:T(8,128)(2,1)S(1)}, u32[]{:S(2)}, u32[]{:S(2)}) collective-permute-start(bf16[4,48,256]{2,1,0:T(8,128)(2,1)S(1)} %constant_dynamic-slice_fusion.4), channel_id=1, source_target_pairs={{0,8},{8,16},{16,24},{24,0},{1,9},{9,17},{17,25},{25,1},{2,10},{10... | collective-permute-start | bytes 294920 | tf_op jit(solution)/shard_map/ppermute | solution.py:39
  9.0 0.0 copy-done.1
  9.0 0.8 %convolution_bitcast_fusion.5 = bf16[128,48]{0,1:T(8,128)(2,1)S(1)} fusion(bf16[4,128,2048]{2,1,0:T(8,128)(2,1)S(1)} %copy-done.1, bf16[4,48,2048]{2,1,0:T(8,128)(2,1)S(1)} %copy-done), kind=kOutput, calls=%fused_computation.10 | convolution fusion | flops 100663296 | bytes 2895872 | tf_op jit(solution)/shard_map/rsk,rtk->st/dot_general | solution.py:41
  9.8 1.3 %collective-permute-done = bf16[4,48,256]{2,1,0:T(8,128)(2,1)S(1)} collective-permute-done((bf16[4,48,256]{2,1,0:T(8,128)(2,1)S(1)}, bf16[4,48,256]{2,1,0:T(8,128)(2,1)S(1)}, u32[]{:S(2)}, u32[]{:S(2)}) %collective-permute-start) | collective-permute-done | bytes 98336 | tf_op jit(solution)/shard_map/ppermute | solution.py:39
  11.1 6.6 %collective-permute-done.1 = bf16[4,48,256]{2,1,0:T(8,128)(2,1)S(1)} collective-permute-done((bf16[4,48,256]{2,1,0:T(8,128)(2,1)S(1)}, bf16[4,48,256]{2,1,0:T(8,128)(2,1)S(1)}, u32[]{:S(2)}, u32[]{:S(2)}) %collective-permute-start.1) | collective-permute-done | bytes 98336 | tf_op jit(solution)/shard_map/ppermute | solution.py:39
  17.7 0.0 collective-permute-done.2
  17.7 1.6 %collective-permute-start.4 = (bf16[4,144,256]{2,1,0:T(8,128)(2,1)S(1)}, bf16[4,144,256]{2,1,0:T(8,128)(2,1)}, u32[]{:S(2)}, u32[]{:S(2)}) collective-permute-start(bf16[4,144,256]{2,1,0:T(8,128)(2,1)S(1)} %pad_maximum_fusion.1), channel_id=1, source_target_pairs={{0,2},{1,3},{2,0},{3,1},{4,6},{5,7},{6,4},{7,5},{8,10},{9,11},{10,... | collective-permute-start | bytes 884744 | tf_op jit(solution)/shard_map/ppermute | solution.py:62
  19.3 1.5 %collective-permute-start.5 = (bf16[4,144,256]{2,1,0:T(8,128)(2,1)S(1)}, bf16[4,144,256]{2,1,0:T(8,128)(2,1)}, u32[]{:S(2)}, u32[]{:S(2)}) collective-permute-start(bf16[4,144,256]{2,1,0:T(8,128)(2,1)S(1)} %pad_maximum_fusion.1), channel_id=1, source_target_pairs={{0,4},{1,5},{2,6},{3,7},{4,0},{5,1},{6,2},{7,3},{8,12},{9,13},{10,... | collective-permute-start | bytes 884744 | tf_op jit(solution)/shard_map/ppermute | solution.py:63
  20.8 0.0 copy-done.5
  20.8 0.7 %fusion.21 = s32[128,8]{1,0:T(8,128)} fusion(s32[128]{0:T(128)S(1)} %bitcast.49), kind=kLoop, calls=%fused_computation.48 | loop fusion | flops 2048 | bytes 4608 | tf_op jit(solution)/shard_map/convert_element_type | solution.py:9
  21.5 1.0 %reduce_window_sum.11 = s32[128,8]{1,0:T(8,128)S(1)} reduce-window(s32[128,8]{1,0:T(8,128)} %fusion.21, s32[]{:T(128)} %constant.14.clone.1), window={size=128x1 pad=127_0x0_0}, to_apply=%region_0.1 | reduce-window | flops 130048 | bytes 8196 | tf_op jit(solution)/shard_map/jit(cumsum)/reduce_window_sum | solution.py:10
  22.5 0.2 select_reduce_fusion
  22.7 5.2 %collective-permute-done.5 = bf16[4,144,256]{2,1,0:T(8,128)(2,1)} collective-permute-done((bf16[4,144,256]{2,1,0:T(8,128)(2,1)S(1)}, bf16[4,144,256]{2,1,0:T(8,128)(2,1)}, u32[]{:S(2)}, u32[]{:S(2)}) %collective-permute-start.5) | collective-permute-done | bytes 294944 | tf_op jit(solution)/shard_map/ppermute | solution.py:63
  27.9 0.9 %slice.46 = bf16[4,144,128]{2,1,0:T(8,128)(2,1)S(1)} slice(bf16[4,144,256]{2,1,0:T(8,128)(2,1)} %collective-permute-done.5), slice={[0:4], [0:144], [0:128]} | slice | bytes 294912 | tf_op jit(solution)/shard_map/slice | solution.py:65
  28.8 0.0 copy-start.4
  28.8 0.6 %collective-permute-start.6 = (bf16[4,144,128]{2,1,0:T(8,128)(2,1)S(1)}, bf16[4,144,128]{2,1,0:T(8,128)(2,1)S(1)}, u32[]{:S(2)}, u32[]{:S(2)}) collective-permute-start(bf16[4,144,128]{2,1,0:T(8,128)(2,1)S(1)} %slice.46), channel_id=1, source_target_pairs={{0,2},{1,3},{2,0},{3,1},{4,6},{5,7},{6,4},{7,5},{8,10},{9,11},{10,... | collective-permute-start | bytes 442376 | tf_op jit(solution)/shard_map/ppermute | solution.py:65
  29.4 0.0 collective-permute-done.4
  29.4 0.9 %slice.47 = bf16[4,144,128]{2,1,0:T(8,128)(2,1)S(1)} slice(bf16[4,144,256]{2,1,0:T(8,128)(2,1)} %collective-permute-done.4), slice={[0:4], [0:144], [128:256]} | slice | bytes 294912 | tf_op jit(solution)/shard_map/slice | solution.py:66
  30.3 0.0 copy-start.3
  30.3 1.6 %collective-permute-start.7 = (bf16[4,144,128]{2,1,0:T(8,128)(2,1)S(1)}, bf16[4,144,128]{2,1,0:T(8,128)(2,1)S(1)}, u32[]{:S(2)}, u32[]{:S(2)}) collective-permute-start(bf16[4,144,128]{2,1,0:T(8,128)(2,1)S(1)} %slice.47), channel_id=1, source_target_pairs={{0,4},{1,5},{2,6},{3,7},{4,0},{5,1},{6,2},{7,3},{8,12},{9,13},{10,... | collective-permute-start | bytes 442376 | tf_op jit(solution)/shard_map/ppermute | solution.py:66
  31.9 0.0 collective-permute-done.3
  31.9 0.1 slice_bitcast_fusion.3
  32.0 2.0 %collective-permute-done.6 = bf16[4,144,128]{2,1,0:T(8,128)(2,1)S(1)} collective-permute-done((bf16[4,144,128]{2,1,0:T(8,128)(2,1)S(1)}, bf16[4,144,128]{2,1,0:T(8,128)(2,1)S(1)}, u32[]{:S(2)}, u32[]{:S(2)}) %collective-permute-start.6) | collective-permute-done | bytes 147488 | tf_op jit(solution)/shard_map/ppermute | solution.py:65
  34.0 0.0 copy-start.2
  34.0 0.2 convolution_bitcast_fusion.1
  34.2 1.3 %collective-permute-done.7 = bf16[4,144,128]{2,1,0:T(8,128)(2,1)S(1)} collective-permute-done((bf16[4,144,128]{2,1,0:T(8,128)(2,1)S(1)}, bf16[4,144,128]{2,1,0:T(8,128)(2,1)S(1)}, u32[]{:S(2)}, u32[]{:S(2)}) %collective-permute-start.7) | collective-permute-done | bytes 147488 | tf_op jit(solution)/shard_map/ppermute | solution.py:66
  35.5 0.2 convolution_bitcast_fusion
  35.8 0.0 copy-done.4
  35.8 1.3 %convolution_bitcast_fusion.3 = f32[256,144]{0,1:T(8,128)S(1)} fusion(bf16[4,144,256]{2,1,0:T(8,128)(2,1)} %collective-permute-done.4, bf16[4,128,256]{2,1,0:T(8,128)(2,1)S(1)} %get-tuple-element.20, bf16[4,128,256]{2,1,0:T(8,128)(2,1)S(1)} %copy-done.4), kind=kOutput, calls=%fused_computation.3 | convolution fusion | flops 76546048 | bytes 966656 | tf_op jit(solution)/shard_map/rsk,rtk->st/dot_general | solution.py:60
  37.1 0.0 copy-done.3
  37.1 1.3 %convolution_bitcast_fusion.2 = f32[256,144]{0,1:T(8,128)S(1)} fusion(bf16[4,144,256]{2,1,0:T(8,128)(2,1)} %collective-permute-done.5, bf16[4,128,256]{2,1,0:T(8,128)(2,1)S(1)} %get-tuple-element.19, bf16[4,128,256]{2,1,0:T(8,128)(2,1)S(1)} %copy-done.3), kind=kOutput, calls=%fused_computation.2 | convolution fusion | flops 76546048 | bytes 966656 | tf_op jit(solution)/shard_map/rsk,rtk->st/dot_general | solution.py:60
  38.4 0.0 copy-done.2
  38.4 0.3 fusion.3
  38.7 0.1 collective-permute-start.8
  38.8 1.2 %collective-permute-done.8 = f32[128,144]{0,1:T(8,128)S(1)} collective-permute-done((f32[128,144]{0,1:T(8,128)S(1)}, f32[128,144]{0,1:T(8,128)S(1)}, u32[]{:S(2)}, u32[]{:S(2)}) %collective-permute-start.8) | collective-permute-done | bytes 73760 | tf_op jit(solution)/shard_map/ppermute | solution.py:69
  40.1 0.4 convolution_convert_fusion
  40.5 0.1 copy.4
  40.6 9.1 %all_to_all.12 = bf16[8,32,192]{2,1,0:T(8,128)(2,1)S(1)} all-to-all(bf16[8,32,192]{2,1,0:T(8,128)(2,1)S(1)} %bitcast.47), channel_id=1, replica_groups=mesh['blk'=4,'rows'=8] {'rows'}, dimensions={0} | all-to-all | bytes 196608 | tf_op jit(solution)/shard_map/all_to_all | solution.py:89
  49.7 0.7 %copy.5 = bf16[256,192]{0,1:T(8,128)(2,1)} copy(bf16[256,192]{1,0:T(8,128)(2,1)S(1)} %bitcast.48) | data formatting | bytes 196608 | tf_op jit(solution)/shard_map/all_to_all | solution.py:89
  (5 shorter events, 0.1 us)
Async XLA Ops:
  0.0 3.2 %copy-start = (bf16[4,48,2048]{2,1,0:T(8,128)(2,1)S(1)}, bf16[4,48,2048]{2,1,0:T(8,128)(2,1)}, u32[]{:S(2)}) copy-start(bf16[4,48,2048]{2,1,0:T(8,128)(2,1)} %param.5) | copy-start | bytes 2359300
  2.6 6.4 %copy-start.1 = (bf16[4,128,2048]{2,1,0:T(8,128)(2,1)S(1)}, bf16[4,128,2048]{2,1,0:T(8,128)(2,1)}, u32[]{:S(2)}) copy-start(bf16[4,128,2048]{2,1,0:T(8,128)(2,1)} %param.3) | copy-start | bytes 6291460
  2.7 18.1 %copy-start.5 = (s32[128,1]{0,1:T(1,128)S(1)}, s32[128,1]{0,1:T(1,128)}, u32[]{:S(2)}) copy-start(s32[128,1]{0,1:T(1,128)} %param.4) | copy-start | bytes 1540
  2.7 29.2 %collective-permute-start.3 = (bf16[4,4,128,256]{3,2,1,0:T(8,128)(2,1)S(1)}, bf16[4,4,128,256]{3,2,1,0:T(8,128)(2,1)S(1)}, u32[]{:S(2)}, u32[]{:S(2)}) collective-permute-start(bf16[4,4,128,256]{3,2,1,0:T(8,128)(2,1)S(1)} %pad_maximum_fusion), channel_id=1, source_target_pairs={{0,1},{1,0},{2,3},{3,2},{4,5},{5,4},{6,7},{7,6},{8,9},{9,8},{10,11... | collective-permute-start | bytes 3145736 | tf_op jit(solution)/shard_map/ppermute | solution.py:50
  3.3 7.8 %collective-permute-start = (bf16[4,48,256]{2,1,0:T(8,128)(2,1)S(1)}, bf16[4,48,256]{2,1,0:T(8,128)(2,1)S(1)}, u32[]{:S(2)}, u32[]{:S(2)}) collective-permute-start(bf16[4,48,256]{2,1,0:T(8,128)(2,1)S(1)} %constant_dynamic-slice_fusion.4), channel_id=1, source_target_pairs={{0,24},{8,0},{16,8},{24,16},{1,25},{9,1},{17,9},{25,17},{2,26},{10... | collective-permute-start | bytes 294920 | tf_op jit(solution)/shard_map/ppermute | solution.py:39
  7.9 9.7 %collective-permute-start.1 = (bf16[4,48,256]{2,1,0:T(8,128)(2,1)S(1)}, bf16[4,48,256]{2,1,0:T(8,128)(2,1)S(1)}, u32[]{:S(2)}, u32[]{:S(2)}) collective-permute-start(bf16[4,48,256]{2,1,0:T(8,128)(2,1)S(1)} %constant_dynamic-slice_fusion.4), channel_id=1, source_target_pairs={{0,16},{8,24},{16,0},{24,8},{1,17},{9,25},{17,1},{25,9},{2,18},{10... | collective-permute-start | bytes 294920 | tf_op jit(solution)/shard_map/ppermute | solution.py:39
  7.9 9.7 %collective-permute-start.2 = (bf16[4,48,256]{2,1,0:T(8,128)(2,1)S(1)}, bf16[4,48,256]{2,1,0:T(8,128)(2,1)S(1)}, u32[]{:S(2)}, u32[]{:S(2)}) collective-permute-start(bf16[4,48,256]{2,1,0:T(8,128)(2,1)S(1)} %constant_dynamic-slice_fusion.4), channel_id=1, source_target_pairs={{0,8},{8,16},{16,24},{24,0},{1,9},{9,17},{17,25},{25,1},{2,10},{10... | collective-permute-start | bytes 294920 | tf_op jit(solution)/shard_map/ppermute | solution.py:39
  17.7 11.7 %collective-permute-start.4 = (bf16[4,144,256]{2,1,0:T(8,128)(2,1)S(1)}, bf16[4,144,256]{2,1,0:T(8,128)(2,1)}, u32[]{:S(2)}, u32[]{:S(2)}) collective-permute-start(bf16[4,144,256]{2,1,0:T(8,128)(2,1)S(1)} %pad_maximum_fusion.1), channel_id=1, source_target_pairs={{0,2},{1,3},{2,0},{3,1},{4,6},{5,7},{6,4},{7,5},{8,10},{9,11},{10,... | collective-permute-start | bytes 884744 | tf_op jit(solution)/shard_map/ppermute | solution.py:62
  19.3 8.6 %collective-permute-start.5 = (bf16[4,144,256]{2,1,0:T(8,128)(2,1)S(1)}, bf16[4,144,256]{2,1,0:T(8,128)(2,1)}, u32[]{:S(2)}, u32[]{:S(2)}) collective-permute-start(bf16[4,144,256]{2,1,0:T(8,128)(2,1)S(1)} %pad_maximum_fusion.1), channel_id=1, source_target_pairs={{0,4},{1,5},{2,6},{3,7},{4,0},{5,1},{6,2},{7,3},{8,12},{9,13},{10,... | collective-permute-start | bytes 884744 | tf_op jit(solution)/shard_map/ppermute | solution.py:63
  28.8 7.0 %copy-start.4 = (bf16[4,128,256]{2,1,0:T(8,128)(2,1)S(1)}, bf16[4,128,256]{2,1,0:T(8,128)(2,1)}, u32[]{:S(2)}) copy-start(bf16[4,128,256]{2,1,0:T(8,128)(2,1)} %get-tuple-element.10) | copy-start | bytes 786436
  28.8 5.2 %collective-permute-start.6 = (bf16[4,144,128]{2,1,0:T(8,128)(2,1)S(1)}, bf16[4,144,128]{2,1,0:T(8,128)(2,1)S(1)}, u32[]{:S(2)}, u32[]{:S(2)}) collective-permute-start(bf16[4,144,128]{2,1,0:T(8,128)(2,1)S(1)} %slice.46), channel_id=1, source_target_pairs={{0,2},{1,3},{2,0},{3,1},{4,6},{5,7},{6,4},{7,5},{8,10},{9,11},{10,... | collective-permute-start | bytes 442376 | tf_op jit(solution)/shard_map/ppermute | solution.py:65
  30.3 6.7 %copy-start.3 = (bf16[4,128,256]{2,1,0:T(8,128)(2,1)S(1)}, bf16[4,128,256]{2,1,0:T(8,128)(2,1)}, u32[]{:S(2)}) copy-start(bf16[4,128,256]{2,1,0:T(8,128)(2,1)} %get-tuple-element.16) | copy-start | bytes 786436
  30.3 5.2 %collective-permute-start.7 = (bf16[4,144,128]{2,1,0:T(8,128)(2,1)S(1)}, bf16[4,144,128]{2,1,0:T(8,128)(2,1)S(1)}, u32[]{:S(2)}, u32[]{:S(2)}) collective-permute-start(bf16[4,144,128]{2,1,0:T(8,128)(2,1)S(1)} %slice.47), channel_id=1, source_target_pairs={{0,4},{1,5},{2,6},{3,7},{4,0},{5,1},{6,2},{7,3},{8,12},{9,13},{10,... | collective-permute-start | bytes 442376 | tf_op jit(solution)/shard_map/ppermute | solution.py:66
  34.0 4.3 %copy-start.2 = (bf16[4,128,256]{2,1,0:T(8,128)(2,1)S(1)}, bf16[4,128,256]{2,1,0:T(8,128)(2,1)}, u32[]{:S(2)}) copy-start(bf16[4,128,256]{2,1,0:T(8,128)(2,1)} %get-tuple-element.9) | copy-start | bytes 786436
  38.7 1.3 %collective-permute-start.8 = (f32[128,144]{0,1:T(8,128)S(1)}, f32[128,144]{0,1:T(8,128)S(1)}, u32[]{:S(2)}, u32[]{:S(2)}) collective-permute-start(f32[128,144]{0,1:T(8,128)S(1)} %slice.49), channel_id=1, source_target_pairs={{0,1},{1,0},{2,3},{3,2},{4,5},{5,4},{6,7},{7,6},{8,9},{9,8},{10,11... | collective-permute-start | bytes 221192 | tf_op jit(solution)/shard_map/ppermute | solution.py:69

commit v6 on v5

--- a/solution.py
+++ b/solution.py
@@ -39,7 +39,6 @@
         arrived.append(lax.ppermute(piece, "blk", pairs))
     mine = jnp.concatenate(arrived, axis=1)
     own = jnp.einsum("rsk,rtk->st", features, test_blocks, preferred_element_type=jnp.float32)
-    mine, own = lax.optimization_barrier((mine, own))
     chip_bits = [1 << i for i in range(1, owners_n.bit_length() - 1)]
     if len(chip_bits) == 2:
         bx, by = chip_bits
@@ -47,6 +46,7 @@
         lent = jnp.stack(
             [lax.dynamic_slice_in_dim(features, (here ^ 1 ^ m) * chunk, chunk, axis=2) for m in masks]
         )
+        mine, own, lent = lax.optimization_barrier((mine, own, lent))
         lent = lax.ppermute(lent, "rows", xor_pairs(owners_n, 1))
         both = [
             jnp.concatenate(
@@ -55,20 +55,21 @@
             for j, m in enumerate(masks)
         ]
 
-        def pair_term(j, tests, lo=0, size=chunk):
-            rows = both[j][:, :, lo:lo + size]
+        def pair_term(j, tests, lo=0, size=None):
+            rows = both[j][lo:lo + (size or both[j].shape[0])]
             return jnp.einsum("rsk,rtk->st", rows, tests, preferred_element_type=jnp.float32)
 
         along_x = lax.ppermute(mine, "rows", xor_pairs(owners_n, bx))
         along_y = lax.ppermute(mine, "rows", xor_pairs(owners_n, by))
-        half = chunk // 2
-        first = lax.ppermute(along_y[:, :, :half], "rows", xor_pairs(owners_n, bx))
-        second = lax.ppermute(along_x[:, :, half:], "rows", xor_pairs(owners_n, by))
+        half = features.shape[0] // 2
+        first = lax.ppermute(along_y[:half], "rows", xor_pairs(owners_n, bx))
+        second = lax.ppermute(along_x[half:], "rows", xor_pairs(owners_n, by))
         paired = pair_term(0, mine) + pair_term(1, along_x) + pair_term(2, along_y)
-        paired = paired + pair_term(3, first, 0, half) + pair_term(3, second, half, half)
+        paired = paired + pair_term(3, first, 0, half) + pair_term(3, second, half, features.shape[0] - half)
         returned = lax.ppermute(paired[local_rows:], "rows", xor_pairs(owners_n, 1))
         remote = paired[:local_rows] + returned
     else:
+        mine, own = lax.optimization_barrier((mine, own))
         remote = term(here * chunk, chunk, mine)
         held = mine[None]
         masks = [0]

time: 50.7 us -> 50.6 us (level)
  waiting for transfers between devices: 17.6 us -> 14.6 us
  matrix products: 4.6 us -> 6.18 us
  other arithmetic: 2.06 us -> 3 us
    ppermute x3, waiting for transfers between devices: 7.9 us -> 4.33 us  [on_device(): arrived.append(lax.ppermute(piece, 'blk', pairs))]
    dot_general x1, matrix products: 0.83 us -> 2.42 us  [on_device(): jnp.einsum('rsk,rtk->st', features, test_blocks, preferred_element_type=j...]
    dynamic_slice x1, local copies, waits for them, and re-layouts: 2.56 us -> 1.1 us  [on_device(): lax.dynamic_slice_in_dim(features, (here ^ m) * chunk, chunk, axis=2)]
    unnamed x12, local copies, waits for them, and re-layouts: 0.03 us -> 1.15 us
    concatenate x1, other arithmetic: 0.02 us -> 0.96 us  [on_device(): mine = jnp.concatenate(arrived, axis=1)]
    dynamic_slice x1, local copies, waits for them, and re-layouts: 0.01 us -> 0.65 us  [on_device(): piece = lax.dynamic_slice_in_dim(test_blocks, here * chunk, chunk, axis=2)]
    ppermute x1, waiting for transfers between devices: 5.16 us -> 5.76 us  [on_device(): along_y = lax.ppermute(mine, 'rows', xor_pairs(owners_n, by))]
  transfers between devices with their start and end apart: 9 -> 9, of which waited for: 6 -> 5; matrix products, arithmetic and copies ran while one was open for 10% -> 15% of each run, Pallas kernels for 0% -> 0%
where the time goes in v6:
time: 50.6 us; the launch traced here: 50.2 us
  waiting for transfers between devices  14.6 us (29%)
  starting transfers between devices  11.5 us (23%)
  blocking collectives  9.05 us (18%)
  matrix products  6.18 us (12%)
  local copies, waits for them, and re-layouts  5.69 us (11%)
  other arithmetic  3 us (6%)
    all_to_all x1, blocking collectives, on_device(): lax.all_to_all(placed, 'rows', split_axis=0, concat_axis=0, tiled=True)  9.05 us
    ppermute x3, starting transfers between devices, on_device(): arrived.append(lax.ppermute(piece, 'blk', pairs))  6.06 us
    ppermute x1, waiting for transfers between devices, on_device(): along_y = lax.ppermute(mine, 'rows', xor_pairs(owners_n, by))  5.76 us
    ppermute x3, waiting for transfers between devices, on_device(): arrived.append(lax.ppermute(piece, 'blk', pairs))  4.33 us
    dot_general x5, matrix products, pair_term(): jnp.einsum('rsk,rtk->st', rows, tests, preferred_element_type=jnp.float32)  3.32 us
    dot_general x1, matrix products, on_device(): jnp.einsum('rsk,rtk->st', features, test_blocks, preferred_element_type=j...  2.42 us
    ppermute x1, waiting for transfers between devices, on_device(): first = lax.ppermute(along_y[:half], 'rows', xor_pairs(owners_n, bx))  1.98 us
    ppermute x1, starting transfers between devices, on_device(): second = lax.ppermute(along_x[half:], 'rows', xor_pairs(owners_n, by))  1.58 us
  transfers between devices with their start and end apart: 9, of which 5 were waited for; matrix products, arithmetic and copies ran while one was open for 15% of the time, Pallas kernels for 0%

profile of v6, /device:TPU:0, one launch (start us, length us, event | category | flops | bytes accessed | tf_op | source)
XLA Modules:
  0.0 50.2 jit_solution(6240494976316307037)
XLA Ops:
  0.0 0.0 copy-start
  0.0 0.0 copy-start.1
  0.0 1.1 %copy-done = bf16[4,48,2048]{2,1,0:T(8,128)(2,1)S(1)} copy-done((bf16[4,48,2048]{2,1,0:T(8,128)(2,1)S(1)}, bf16[4,48,2048]{2,1,0:T(8,128)(2,1)}, u32[]{:S(2)}) %copy-start) | copy-done | bytes 786456
  1.1 0.7 %constant_dynamic-slice_fusion.4 = bf16[4,48,256]{2,1,0:T(8,128)(2,1)} fusion(bf16[4,48,2048]{2,1,0:T(8,128)(2,1)S(1)} %copy-done, s32[]{:T(128)S(6)} %select_n.35), kind=kLoop, calls=%fused_computation.49 | loop fusion | bytes 196612 | tf_op jit(solution)/shard_map/dynamic_slice | solution.py:35
  1.8 5.0 %collective-permute-start = (bf16[4,48,256]{2,1,0:T(8,128)(2,1)}, bf16[4,48,256]{2,1,0:T(8,128)(2,1)S(1)}, u32[]{:S(2)}, u32[]{:S(2)}) collective-permute-start(bf16[4,48,256]{2,1,0:T(8,128)(2,1)} %constant_dynamic-slice_fusion.4), channel_id=1, source_target_pairs={{0,24},{8,0},{16,8},{24,16},{1,25},{9,1},{17,9},{25,17},{2,26},{10... | collective-permute-start | bytes 294920 | tf_op jit(solution)/shard_map/ppermute | solution.py:39
  6.8 0.0 collective-permute-start.1
  6.8 1.0 %collective-permute-start.2 = (bf16[4,48,256]{2,1,0:T(8,128)(2,1)}, bf16[4,48,256]{2,1,0:T(8,128)(2,1)}, u32[]{:S(2)}, u32[]{:S(2)}) collective-permute-start(bf16[4,48,256]{2,1,0:T(8,128)(2,1)} %constant_dynamic-slice_fusion.4), channel_id=1, source_target_pairs={{0,8},{8,16},{16,24},{24,0},{1,9},{9,17},{17,25},{25,1},{2,10},{10... | collective-permute-start | bytes 294920 | tf_op jit(solution)/shard_map/ppermute | solution.py:39
  7.9 2.4 %convolution_bitcast_fusion.5 = bf16[128,48]{0,1:T(8,128)(2,1)S(1)} fusion(bf16[4,128,2048]{2,1,0:T(8,128)(2,1)} %param.3, bf16[4,48,2048]{2,1,0:T(8,128)(2,1)S(1)} %copy-done), kind=kOutput, calls=%fused_computation.10 | convolution fusion | flops 100663296 | bytes 2895872 | tf_op jit(solution)/shard_map/rsk,rtk->st/dot_general | solution.py:41
  10.3 0.0 copy-done.1
  10.3 1.1 %constant_dynamic-slice_fusion.3 = (bf16[4,128,256]{2,1,0:T(8,128)(2,1)S(1)}, bf16[4,128,256]{2,1,0:T(8,128)(2,1)}, bf16[1,4,128,256]{3,2,1,0:T(8,128)(2,1)S(1)}...) fusion(bf16[4,128,2048]{2,1,0:T(8,128)(2,1)S(1)} %copy-done.1, ...), kind=kLoop, calls=%fused_computation.48 | loop fusion | bytes 4194336 | tf_op jit(solution)/shard_map/dynamic_slice | solution.py:53
  11.4 0.0 copy-start.5
  11.4 0.1 pad_maximum_fusion
  11.6 0.0 collective-permute-done
  11.6 4.3 %collective-permute-done.1 = bf16[4,48,256]{2,1,0:T(8,128)(2,1)} collective-permute-done((bf16[4,48,256]{2,1,0:T(8,128)(2,1)}, bf16[4,48,256]{2,1,0:T(8,128)(2,1)}, u32[]{:S(2)}, u32[]{:S(2)}) %collective-permute-start.1) | collective-permute-done | bytes 98336 | tf_op jit(solution)/shard_map/ppermute | solution.py:39
  15.9 0.0 collective-permute-done.2
  15.9 1.0 %pad_maximum_fusion.4 = bf16[4,144,256]{2,1,0:T(8,128)(2,1)S(1)} fusion(bf16[4,48,256]{2,1,0:T(8,128)(2,1)} %collective-permute-done.2, bf16[4,48,256]{2,1,0:T(8,128)(2,1)} %collective-permute-done.1, bf16[4,48,256]{2,1,0:T(8,128)(2,1)S(1)} %collective-permute-done), kind=kLoop, calls=%fused_computation.22 | loop fusion | flops 884736 | bytes 589824 | tf_op jit(solution)/shard_map/concatenate | solution.py:40
  16.9 0.1 collective-permute-start.3
  16.9 1.6 %collective-permute-start.4 = (bf16[4,144,256]{2,1,0:T(8,128)(2,1)S(1)}, bf16[4,144,256]{2,1,0:T(8,128)(2,1)}, u32[]{:S(2)}, u32[]{:S(2)}) collective-permute-start(bf16[4,144,256]{2,1,0:T(8,128)(2,1)S(1)} %pad_maximum_fusion.4), channel_id=1, source_target_pairs={{0,2},{1,3},{2,0},{3,1},{4,6},{5,7},{6,4},{7,5},{8,10},{9,11},{10,... | collective-permute-start | bytes 884744 | tf_op jit(solution)/shard_map/ppermute | solution.py:62
  18.5 1.5 %collective-permute-start.5 = (bf16[4,144,256]{2,1,0:T(8,128)(2,1)S(1)}, bf16[4,144,256]{2,1,0:T(8,128)(2,1)}, u32[]{:S(2)}, u32[]{:S(2)}) collective-permute-start(bf16[4,144,256]{2,1,0:T(8,128)(2,1)S(1)} %pad_maximum_fusion.4), channel_id=1, source_target_pairs={{0,4},{1,5},{2,6},{3,7},{4,0},{5,1},{6,2},{7,3},{8,12},{9,13},{10,... | collective-permute-start | bytes 884744 | tf_op jit(solution)/shard_map/ppermute | solution.py:63
  20.0 0.0 copy-done.5
  20.0 0.7 %fusion.18 = s32[128,8]{1,0:T(8,128)} fusion(s32[128]{0:T(128)S(1)} %bitcast.49), kind=kLoop, calls=%fused_computation.44 | loop fusion | flops 2048 | bytes 4608 | tf_op jit(solution)/shard_map/convert_element_type | solution.py:9
  20.7 1.0 %reduce_window_sum.11 = s32[128,8]{1,0:T(8,128)S(1)} reduce-window(s32[128,8]{1,0:T(8,128)} %fusion.18, s32[]{:T(128)} %constant.14.clone.1), window={size=128x1 pad=127_0x0_0}, to_apply=%region_0.1 | reduce-window | flops 130048 | bytes 8196 | tf_op jit(solution)/shard_map/jit(cumsum)/reduce_window_sum | solution.py:10
  21.8 0.0 copy-start.4
  21.8 0.2 select_reduce_fusion
  21.9 5.8 %collective-permute-done.5 = bf16[4,144,256]{2,1,0:T(8,128)(2,1)} collective-permute-done((bf16[4,144,256]{2,1,0:T(8,128)(2,1)S(1)}, bf16[4,144,256]{2,1,0:T(8,128)(2,1)}, u32[]{:S(2)}, u32[]{:S(2)}) %collective-permute-start.5) | collective-permute-done | bytes 294944 | tf_op jit(solution)/shard_map/ppermute | solution.py:63
  27.7 0.9 %slice.44 = bf16[2,144,256]{2,1,0:T(8,128)(2,1)S(1)} slice(bf16[4,144,256]{2,1,0:T(8,128)(2,1)} %collective-permute-done.5), slice={[0:2], [0:144], [0:256]} | slice | bytes 294912 | tf_op jit(solution)/shard_map/slice | solution.py:65
  28.6 0.6 %collective-permute-start.6 = (bf16[2,144,256]{2,1,0:T(8,128)(2,1)S(1)}, bf16[2,144,256]{2,1,0:T(8,128)(2,1)S(1)}, u32[]{:S(2)}, u32[]{:S(2)}) collective-permute-start(bf16[2,144,256]{2,1,0:T(8,128)(2,1)S(1)} %slice.44), channel_id=1, source_target_pairs={{0,2},{1,3},{2,0},{3,1},{4,6},{5,7},{6,4},{7,5},{8,10},{9,11},{10,... | collective-permute-start | bytes 442376 | tf_op jit(solution)/shard_map/ppermute | solution.py:65
  29.2 0.0 collective-permute-done.4
  29.2 0.9 %slice.45 = bf16[2,144,256]{2,1,0:T(8,128)(2,1)S(1)} slice(bf16[4,144,256]{2,1,0:T(8,128)(2,1)} %collective-permute-done.4), slice={[2:4], [0:144], [0:256]} | slice | bytes 294912 | tf_op jit(solution)/shard_map/slice | solution.py:66
  30.1 0.0 copy-start.3
  30.1 1.6 %collective-permute-start.7 = (bf16[2,144,256]{2,1,0:T(8,128)(2,1)S(1)}, bf16[2,144,256]{2,1,0:T(8,128)(2,1)S(1)}, u32[]{:S(2)}, u32[]{:S(2)}) collective-permute-start(bf16[2,144,256]{2,1,0:T(8,128)(2,1)S(1)} %slice.45), channel_id=1, source_target_pairs={{0,4},{1,5},{2,6},{3,7},{4,0},{5,1},{6,2},{7,3},{8,12},{9,13},{10,... | collective-permute-start | bytes 442376 | tf_op jit(solution)/shard_map/ppermute | solution.py:66
  31.7 0.0 collective-permute-done.3
  31.7 0.1 slice_bitcast_fusion.3
  31.8 0.0 copy-start.2
  31.8 2.0 %collective-permute-done.6 = bf16[2,144,256]{2,1,0:T(8,128)(2,1)S(1)} collective-permute-done((bf16[2,144,256]{2,1,0:T(8,128)(2,1)S(1)}, bf16[2,144,256]{2,1,0:T(8,128)(2,1)S(1)}, u32[]{:S(2)}, u32[]{:S(2)}) %collective-permute-start.6) | collective-permute-done | bytes 147488 | tf_op jit(solution)/shard_map/ppermute | solution.py:65
  33.8 0.0 copy-done.4
  33.8 0.2 convolution_bitcast_fusion.1
  34.1 1.3 %collective-permute-done.7 = bf16[2,144,256]{2,1,0:T(8,128)(2,1)S(1)} collective-permute-done((bf16[2,144,256]{2,1,0:T(8,128)(2,1)S(1)}, bf16[2,144,256]{2,1,0:T(8,128)(2,1)S(1)}, u32[]{:S(2)}, u32[]{:S(2)}) %collective-permute-start.7) | collective-permute-done | bytes 147488 | tf_op jit(solution)/shard_map/ppermute | solution.py:66
  35.4 0.2 convolution_bitcast_fusion
  35.6 0.0 copy-done.3
  35.6 1.3 %convolution_bitcast_fusion.3 = f32[256,144]{0,1:T(8,128)S(1)} fusion(bf16[4,144,256]{2,1,0:T(8,128)(2,1)} %collective-permute-done.4, bf16[4,128,256]{2,1,0:T(8,128)(2,1)S(1)} %get-tuple-element.22, bf16[4,128,256]{2,1,0:T(8,128)(2,1)S(1)} %copy-done.3), kind=kOutput, calls=%fused_computation.3 | convolution fusion | flops 76546048 | bytes 966656 | tf_op jit(solution)/shard_map/rsk,rtk->st/dot_general | solution.py:60
  36.9 0.0 copy-done.2
  36.9 1.3 %convolution_bitcast_fusion.2 = f32[256,144]{0,1:T(8,128)S(1)} fusion(bf16[4,144,256]{2,1,0:T(8,128)(2,1)} %collective-permute-done.5, bf16[4,128,256]{2,1,0:T(8,128)(2,1)S(1)} %get-tuple-element.21, bf16[4,128,256]{2,1,0:T(8,128)(2,1)S(1)} %copy-done.2), kind=kOutput, calls=%fused_computation.2 | convolution fusion | flops 76546048 | bytes 966656 | tf_op jit(solution)/shard_map/rsk,rtk->st/dot_general | solution.py:60
  38.2 0.3 fusion.3
  38.5 0.1 collective-permute-start.8
  38.6 1.2 %collective-permute-done.8 = f32[128,144]{0,1:T(8,128)S(1)} collective-permute-done((f32[128,144]{0,1:T(8,128)S(1)}, f32[128,144]{0,1:T(8,128)S(1)}, u32[]{:S(2)}, u32[]{:S(2)}) %collective-permute-start.8) | collective-permute-done | bytes 73760 | tf_op jit(solution)/shard_map/ppermute | solution.py:69
  39.9 0.4 convolution_convert_fusion
  40.3 0.1 copy.4
  40.4 9.1 %all_to_all.12 = bf16[8,32,192]{2,1,0:T(8,128)(2,1)S(1)} all-to-all(bf16[8,32,192]{2,1,0:T(8,128)(2,1)S(1)} %bitcast.47), channel_id=1, replica_groups=mesh['blk'=4,'rows'=8] {'rows'}, dimensions={0} | all-to-all | bytes 196608 | tf_op jit(solution)/shard_map/all_to_all | solution.py:90
  49.5 0.7 %copy.5 = bf16[256,192]{0,1:T(8,128)(2,1)} copy(bf16[256,192]{1,0:T(8,128)(2,1)S(1)} %bitcast.48) | data formatting | bytes 196608 | tf_op jit(solution)/shard_map/all_to_all | solution.py:90
  (3 shorter events, 0.0 us)
Async XLA Ops:
  0.0 1.1 %copy-start = (bf16[4,48,2048]{2,1,0:T(8,128)(2,1)S(1)}, bf16[4,48,2048]{2,1,0:T(8,128)(2,1)}, u32[]{:S(2)}) copy-start(bf16[4,48,2048]{2,1,0:T(8,128)(2,1)} %param.5) | copy-start | bytes 2359300
  0.0 10.3 %copy-start.1 = (bf16[4,128,2048]{2,1,0:T(8,128)(2,1)S(1)}, bf16[4,128,2048]{2,1,0:T(8,128)(2,1)}, u32[]{:S(2)}) copy-start(bf16[4,128,2048]{2,1,0:T(8,128)(2,1)} %param.3) | copy-start | bytes 6291460
  1.8 9.8 %collective-permute-start = (bf16[4,48,256]{2,1,0:T(8,128)(2,1)}, bf16[4,48,256]{2,1,0:T(8,128)(2,1)S(1)}, u32[]{:S(2)}, u32[]{:S(2)}) collective-permute-start(bf16[4,48,256]{2,1,0:T(8,128)(2,1)} %constant_dynamic-slice_fusion.4), channel_id=1, source_target_pairs={{0,24},{8,0},{16,8},{24,16},{1,25},{9,1},{17,9},{25,17},{2,26},{10... | collective-permute-start | bytes 294920 | tf_op jit(solution)/shard_map/ppermute | solution.py:39
  6.8 9.1 %collective-permute-start.1 = (bf16[4,48,256]{2,1,0:T(8,128)(2,1)}, bf16[4,48,256]{2,1,0:T(8,128)(2,1)}, u32[]{:S(2)}, u32[]{:S(2)}) collective-permute-start(bf16[4,48,256]{2,1,0:T(8,128)(2,1)} %constant_dynamic-slice_fusion.4), channel_id=1, source_target_pairs={{0,16},{8,24},{16,0},{24,8},{1,17},{9,25},{17,1},{25,9},{2,18},{10... | collective-permute-start | bytes 294920 | tf_op jit(solution)/shard_map/ppermute | solution.py:39
  6.8 9.1 %collective-permute-start.2 = (bf16[4,48,256]{2,1,0:T(8,128)(2,1)}, bf16[4,48,256]{2,1,0:T(8,128)(2,1)}, u32[]{:S(2)}, u32[]{:S(2)}) collective-permute-start(bf16[4,48,256]{2,1,0:T(8,128)(2,1)} %constant_dynamic-slice_fusion.4), channel_id=1, source_target_pairs={{0,8},{8,16},{16,24},{24,0},{1,9},{9,17},{17,25},{25,1},{2,10},{10... | collective-permute-start | bytes 294920 | tf_op jit(solution)/shard_map/ppermute | solution.py:39
  11.4 8.6 %copy-start.5 = (s32[128,1]{0,1:T(1,128)S(1)}, s32[128,1]{0,1:T(1,128)}, u32[]{:S(2)}) copy-start(s32[128,1]{0,1:T(1,128)} %param.4) | copy-start | bytes 1540
  16.9 14.9 %collective-permute-start.3 = (bf16[4,4,128,256]{3,2,1,0:T(8,128)(2,1)S(1)}, bf16[4,4,128,256]{3,2,1,0:T(8,128)(2,1)S(1)}, u32[]{:S(2)}, u32[]{:S(2)}) collective-permute-start(bf16[4,4,128,256]{3,2,1,0:T(8,128)(2,1)S(1)} %pad_maximum_fusion), channel_id=1, source_target_pairs={{0,1},{1,0},{2,3},{3,2},{4,5},{5,4},{6,7},{7,6},{8,9},{9,8},{10,11... | collective-permute-start | bytes 3145736 | tf_op jit(solution)/shard_map/ppermute | solution.py:50
  16.9 12.3 %collective-permute-start.4 = (bf16[4,144,256]{2,1,0:T(8,128)(2,1)S(1)}, bf16[4,144,256]{2,1,0:T(8,128)(2,1)}, u32[]{:S(2)}, u32[]{:S(2)}) collective-permute-start(bf16[4,144,256]{2,1,0:T(8,128)(2,1)S(1)} %pad_maximum_fusion.4), channel_id=1, source_target_pairs={{0,2},{1,3},{2,0},{3,1},{4,6},{5,7},{6,4},{7,5},{8,10},{9,11},{10,... | collective-permute-start | bytes 884744 | tf_op jit(solution)/shard_map/ppermute | solution.py:62
  18.5 9.2 %collective-permute-start.5 = (bf16[4,144,256]{2,1,0:T(8,128)(2,1)S(1)}, bf16[4,144,256]{2,1,0:T(8,128)(2,1)}, u32[]{:S(2)}, u32[]{:S(2)}) collective-permute-start(bf16[4,144,256]{2,1,0:T(8,128)(2,1)S(1)} %pad_maximum_fusion.4), channel_id=1, source_target_pairs={{0,4},{1,5},{2,6},{3,7},{4,0},{5,1},{6,2},{7,3},{8,12},{9,13},{10,... | collective-permute-start | bytes 884744 | tf_op jit(solution)/shard_map/ppermute | solution.py:63
  21.8 12.1 %copy-start.4 = (bf16[4,128,256]{2,1,0:T(8,128)(2,1)S(1)}, bf16[4,128,256]{2,1,0:T(8,128)(2,1)}, u32[]{:S(2)}) copy-start(bf16[4,128,256]{2,1,0:T(8,128)(2,1)} %get-tuple-element.17) | copy-start | bytes 786436
  28.6 5.2 %collective-permute-start.6 = (bf16[2,144,256]{2,1,0:T(8,128)(2,1)S(1)}, bf16[2,144,256]{2,1,0:T(8,128)(2,1)S(1)}, u32[]{:S(2)}, u32[]{:S(2)}) collective-permute-start(bf16[2,144,256]{2,1,0:T(8,128)(2,1)S(1)} %slice.44), channel_id=1, source_target_pairs={{0,2},{1,3},{2,0},{3,1},{4,6},{5,7},{6,4},{7,5},{8,10},{9,11},{10,... | collective-permute-start | bytes 442376 | tf_op jit(solution)/shard_map/ppermute | solution.py:65
  30.1 5.5 %copy-start.3 = (bf16[4,128,256]{2,1,0:T(8,128)(2,1)S(1)}, bf16[4,128,256]{2,1,0:T(8,128)(2,1)}, u32[]{:S(2)}) copy-start(bf16[4,128,256]{2,1,0:T(8,128)(2,1)} %get-tuple-element.12) | copy-start | bytes 786436
  30.1 5.2 %collective-permute-start.7 = (bf16[2,144,256]{2,1,0:T(8,128)(2,1)S(1)}, bf16[2,144,256]{2,1,0:T(8,128)(2,1)S(1)}, u32[]{:S(2)}, u32[]{:S(2)}) collective-permute-start(bf16[2,144,256]{2,1,0:T(8,128)(2,1)S(1)} %slice.45), channel_id=1, source_target_pairs={{0,4},{1,5},{2,6},{3,7},{4,0},{5,1},{6,2},{7,3},{8,12},{9,13},{10,... | collective-permute-start | bytes 442376 | tf_op jit(solution)/shard_map/ppermute | solution.py:66
  31.8 5.1 %copy-start.2 = (bf16[4,128,256]{2,1,0:T(8,128)(2,1)S(1)}, bf16[4,128,256]{2,1,0:T(8,128)(2,1)}, u32[]{:S(2)}) copy-start(bf16[4,128,256]{2,1,0:T(8,128)(2,1)} %get-tuple-element.18) | copy-start | bytes 786436
  38.5 1.3 %collective-permute-start.8 = (f32[128,144]{0,1:T(8,128)S(1)}, f32[128,144]{0,1:T(8,128)S(1)}, u32[]{:S(2)}, u32[]{:S(2)}) collective-permute-start(f32[128,144]{0,1:T(8,128)S(1)} %slice.47), channel_id=1, source_target_pairs={{0,1},{1,0},{2,3},{3,2},{4,5},{5,4},{6,7},{7,6},{8,9},{9,8},{10,11... | collective-permute-start | bytes 221192 | tf_op jit(solution)/shard_map/ppermute | solution.py:69

commit v7 on v3

--- a/solution.py
+++ b/solution.py
@@ -39,6 +39,8 @@
         arrived.append(lax.ppermute(piece, "blk", pairs))
     mine = jnp.concatenate(arrived, axis=1)
     own = jnp.einsum("rsk,rtk->st", features, test_blocks, preferred_element_type=jnp.float32)
+    slotting = slot_matrix(owner_ids, owners_n, capacity)
+    mine, own, slotting = lax.optimization_barrier((mine, own, slotting))
     remote = term(here * chunk, chunk, mine)
     chip_bits = [1 << i for i in range(1, owners_n.bit_length() - 1)]
     if len(chip_bits) == 2:
@@ -74,7 +76,7 @@
     total = lax.dynamic_slice_in_dim(doubled, start, blocks_n * width, axis=1)
     row_scores = total.astype(jnp.bfloat16)
     placed = jnp.dot(
-        slot_matrix(owner_ids, owners_n, capacity), row_scores, preferred_element_type=jnp.float32
+        slotting, row_scores, preferred_element_type=jnp.float32
     ).astype(jnp.bfloat16)
     return lax.all_to_all(placed, "rows", split_axis=0, concat_axis=0, tiled=True)
 

time: 49.9 us -> 48.2 us (0.966)
  waiting for transfers between devices: 17.2 us -> 14.4 us
  starting transfers between devices: 12 us -> 13.2 us
    ppermute x3, waiting for transfers between devices: 8.35 us -> 2.8 us  [on_device(): arrived.append(lax.ppermute(piece, 'blk', pairs))]
    ppermute x1, waiting for transfers between devices: 0.01 us -> 2.15 us  [on_device(): got = lax.ppermute(held, 'rows', xor_pairs(owners_n, 1))]
    ppermute x1, waiting for transfers between devices: 4.67 us -> 5.78 us  [on_device(): along_y = lax.ppermute(mine, 'rows', xor_pairs(owners_n, by))]
    ppermute x3, starting transfers between devices: 6.11 us -> 6.96 us  [on_device(): arrived.append(lax.ppermute(piece, 'blk', pairs))]
  transfers between devices with their start and end apart: 8 -> 8, of which waited for: 6 -> 5; matrix products, arithmetic and copies ran while one was open for 6% -> 7% of each run, Pallas kernels for 0% -> 0%
where the time goes in v7:
time: 48.2 us; the launch traced here: 47.9 us
  waiting for transfers between devices  14.4 us (30%)
  starting transfers between devices  13.2 us (27%)
  matrix products  8.33 us (17%)
  blocking collectives  8.11 us (17%)
  local copies, waits for them, and re-layouts  2.07 us (4%)
  other arithmetic  1.68 us (3%)
    all_to_all x1, blocking collectives, on_device(): lax.all_to_all(placed, 'rows', split_axis=0, concat_axis=0, tiled=True)  8.11 us
    ppermute x3, starting transfers between devices, on_device(): arrived.append(lax.ppermute(piece, 'blk', pairs))  6.96 us
    dot_general x9, matrix products, term(): jnp.einsum('rsk,rtk->st', part, tests, preferred_element_type=jnp.float32)  6 us
    ppermute x1, waiting for transfers between devices, on_device(): along_y = lax.ppermute(mine, 'rows', xor_pairs(owners_n, by))  5.78 us
    ppermute x3, waiting for transfers between devices, on_device(): arrived.append(lax.ppermute(piece, 'blk', pairs))  2.8 us
    ppermute x1, waiting for transfers between devices, on_device(): got = lax.ppermute(held, 'rows', xor_pairs(owners_n, 1))  2.15 us
    ppermute x1, waiting for transfers between devices, on_device(): first = lax.ppermute(along_y[:, :, :half], 'rows', xor_pairs(owners_n, bx))  2.03 us
    dot_general x1, matrix products, on_device(): jnp.einsum('rsk,rtk->st', features, test_blocks, preferred_element_type=j...  1.96 us
  transfers between devices with their start and end apart: 8, of which 5 were waited for; matrix products, arithmetic and copies ran while one was open for 7% of the time, Pallas kernels for 0%

profile of v7, /device:TPU:0, one launch (start us, length us, event | category | flops | bytes accessed | tf_op | source)
XLA Modules:
  0.0 47.9 jit_solution(16876982717991004683)
XLA Ops:
  0.0 0.0 copy-start
  0.0 0.0 copy-start.1
  0.0 1.0 %constant_dynamic-slice_fusion = bf16[4,48,256]{2,1,0:T(8,128)(2,1)S(1)} fusion(bf16[4,48,2048]{2,1,0:T(8,128)(2,1)} %param.5, s32[]{:T(128)S(6)} %select_n.38), kind=kLoop, calls=%fused_computation.58 | loop fusion | bytes 196612 | tf_op jit(solution)/shard_map/dynamic_slice | solution.py:35
  1.1 3.0 %collective-permute-start.2 = (bf16[4,48,256]{2,1,0:T(8,128)(2,1)S(1)}, bf16[4,48,256]{2,1,0:T(8,128)(2,1)S(1)}, u32[]{:S(2)}, u32[]{:S(2)}) collective-permute-start(bf16[4,48,256]{2,1,0:T(8,128)(2,1)S(1)} %constant_dynamic-slice_fusion), channel_id=1, source_target_pairs={{0,8},{8,16},{16,24},{24,0},{1,9},{9,17},{17,25},{25,1},{2,10},{10... | collective-permute-start | bytes 294920 | tf_op jit(solution)/shard_map/ppermute | solution.py:39
  4.1 2.6 %collective-permute-start.1 = (bf16[4,48,256]{2,1,0:T(8,128)(2,1)S(1)}, bf16[4,48,256]{2,1,0:T(8,128)(2,1)S(1)}, u32[]{:S(2)}, u32[]{:S(2)}) collective-permute-start(bf16[4,48,256]{2,1,0:T(8,128)(2,1)S(1)} %constant_dynamic-slice_fusion), channel_id=1, source_target_pairs={{0,16},{8,24},{16,0},{24,8},{1,17},{9,25},{17,1},{25,9},{2,18},{10... | collective-permute-start | bytes 294920 | tf_op jit(solution)/shard_map/ppermute | solution.py:39
  6.7 1.3 %collective-permute-start = (bf16[4,48,256]{2,1,0:T(8,128)(2,1)S(1)}, bf16[4,48,256]{2,1,0:T(8,128)(2,1)S(1)}, u32[]{:S(2)}, u32[]{:S(2)}) collective-permute-start(bf16[4,48,256]{2,1,0:T(8,128)(2,1)S(1)} %constant_dynamic-slice_fusion), channel_id=1, source_target_pairs={{0,24},{8,0},{16,8},{24,16},{1,25},{9,1},{17,9},{25,17},{2,26},{10... | collective-permute-start | bytes 294920 | tf_op jit(solution)/shard_map/ppermute | solution.py:39
  8.0 0.0 copy-done
  8.0 2.0 %convolution_bitcast_fusion.9 = bf16[128,48]{0,1:T(8,128)(2,1)S(1)} fusion(bf16[4,128,2048]{2,1,0:T(8,128)(2,1)S(1)} %copy-done, bf16[4,48,2048]{2,1,0:T(8,128)(2,1)} %param.5), kind=kOutput, calls=%fused_computation.19 | convolution fusion | flops 100663296 | bytes 2895872 | tf_op jit(solution)/shard_map/rsk,rtk->st/dot_general | solution.py:41
  10.0 0.0 copy-done.1
  10.0 0.1 fusion.23
  10.1 0.2 reduce_window_sum.11
  10.3 0.2 select_reduce_fusion
  10.5 0.0 collective-permute-done.2
  10.5 2.8 %collective-permute-done.1 = bf16[4,48,256]{2,1,0:T(8,128)(2,1)S(1)} collective-permute-done((bf16[4,48,256]{2,1,0:T(8,128)(2,1)S(1)}, bf16[4,48,256]{2,1,0:T(8,128)(2,1)S(1)}, u32[]{:S(2)}, u32[]{:S(2)}) %collective-permute-start.1) | collective-permute-done | bytes 98336 | tf_op jit(solution)/shard_map/ppermute | solution.py:39
  13.2 0.0 collective-permute-done
  13.3 1.6 %collective-permute-start.4 = (bf16[4,144,256]{2,1,0:T(8,128)(2,1)S(1)}, bf16[4,144,256]{2,1,0:T(8,128)(2,1)S(1)}, u32[]{:S(2)}, u32[]{:S(2)}) collective-permute-start(bf16[4,144,256]{2,1,0:T(8,128)(2,1)S(1)} %pad_maximum_fusion.1), channel_id=1, source_target_pairs={{0,4},{1,5},{2,6},{3,7},{4,0},{5,1},{6,2},{7,3},{8,12},{9,13},{10,... | collective-permute-start | bytes 884744 | tf_op jit(solution)/shard_map/ppermute | solution.py:49
  14.9 1.5 %collective-permute-start.3 = (bf16[4,144,256]{2,1,0:T(8,128)(2,1)S(1)}, bf16[4,144,256]{2,1,0:T(8,128)(2,1)S(1)}, u32[]{:S(2)}, u32[]{:S(2)}) collective-permute-start(bf16[4,144,256]{2,1,0:T(8,128)(2,1)S(1)} %pad_maximum_fusion.1), channel_id=1, source_target_pairs={{0,2},{1,3},{2,0},{3,1},{4,6},{5,7},{6,4},{7,5},{8,10},{9,11},{10,... | collective-permute-start | bytes 884744 | tf_op jit(solution)/shard_map/ppermute | solution.py:48
  16.4 5.8 %collective-permute-done.4 = bf16[4,144,256]{2,1,0:T(8,128)(2,1)S(1)} collective-permute-done((bf16[4,144,256]{2,1,0:T(8,128)(2,1)S(1)}, bf16[4,144,256]{2,1,0:T(8,128)(2,1)S(1)}, u32[]{:S(2)}, u32[]{:S(2)}) %collective-permute-start.4) | collective-permute-done | bytes 294944 | tf_op jit(solution)/shard_map/ppermute | solution.py:49
  22.2 1.6 %collective-permute-start.5 = (bf16[4,144,128]{2,1,0:T(8,128)(2,1)S(1)}, bf16[4,144,128]{2,1,0:T(8,128)(2,1)S(1)}, u32[]{:S(2)}, u32[]{:S(2)}) collective-permute-start(bf16[4,144,128]{2,1,0:T(8,128)(2,1)S(1)} %slice.24), channel_id=1, source_target_pairs={{0,2},{1,3},{2,0},{3,1},{4,6},{5,7},{6,4},{7,5},{8,10},{9,11},{10,... | collective-permute-start | bytes 442376 | tf_op jit(solution)/shard_map/ppermute | solution.py:53
  23.8 0.0 collective-permute-done.3
  23.8 1.6 %collective-permute-start.6 = (bf16[4,144,128]{2,1,0:T(8,128)(2,1)S(1)}, bf16[4,144,128]{2,1,0:T(8,128)(2,1)S(1)}, u32[]{:S(2)}, u32[]{:S(2)}) collective-permute-start(bf16[4,144,128]{2,1,0:T(8,128)(2,1)S(1)} %slice.25), channel_id=1, source_target_pairs={{0,4},{1,5},{2,6},{3,7},{4,0},{5,1},{6,2},{7,3},{8,12},{9,13},{10,... | collective-permute-start | bytes 442376 | tf_op jit(solution)/shard_map/ppermute | solution.py:54
  25.4 2.0 %collective-permute-done.5 = bf16[4,144,128]{2,1,0:T(8,128)(2,1)S(1)} collective-permute-done((bf16[4,144,128]{2,1,0:T(8,128)(2,1)S(1)}, bf16[4,144,128]{2,1,0:T(8,128)(2,1)S(1)}, u32[]{:S(2)}, u32[]{:S(2)}) %collective-permute-start.5) | collective-permute-done | bytes 147488 | tf_op jit(solution)/shard_map/ppermute | solution.py:53
  27.4 1.6 %collective-permute-done.6 = bf16[4,144,128]{2,1,0:T(8,128)(2,1)S(1)} collective-permute-done((bf16[4,144,128]{2,1,0:T(8,128)(2,1)S(1)}, bf16[4,144,128]{2,1,0:T(8,128)(2,1)S(1)}, u32[]{:S(2)}, u32[]{:S(2)}) %collective-permute-start.6) | collective-permute-done | bytes 147488 | tf_op jit(solution)/shard_map/ppermute | solution.py:54
  29.0 1.2 %pad_maximum_fusion = bf16[4,4,144,256]{3,2,1,0:T(8,128)(2,1)} fusion(bf16[1,4,144,256]{3,2,1,0:T(8,128)(2,1)S(1)} %maximum_bitcast_fusion, bf16[1,4,144,256]{3,2,1,0:T(8,128)(2,1)S(1)} %bitcast.66, bf16[1,4,144,256]{3,2,1,0:T(8,128)(2,1)S(1)} %bitcast.67, bf16[1,4,144,256]{3,2,1,0:T(8,128)(2,1)S(1)} %bitcast.65), kind=kLoop, calls=%fused_computation | loop fusion | flops 1769472 | bytes 2359296 | tf_op jit(solution)/shard_map/stack | solution.py:58
  30.2 0.0 collective-permute-start.7
  30.2 0.1 copy.6
  30.3 0.3 convolution_bitcast_fusion.6
  30.6 0.2 convolution_bitcast_fusion.4
  30.8 0.2 convolution_bitcast_fusion.8
  31.1 0.2 convolution_bitcast_fusion.7
  31.3 2.2 %collective-permute-done.7 = bf16[4,4,144,256]{3,2,1,0:T(8,128)(2,1)} collective-permute-done((bf16[4,4,144,256]{3,2,1,0:T(8,128)(2,1)}, bf16[4,4,144,256]{3,2,1,0:T(8,128)(2,1)}, u32[]{:S(2)}, u32[]{:S(2)}) %collective-permute-start.7) | collective-permute-done | bytes 1179680 | tf_op jit(solution)/shard_map/ppermute | solution.py:70
  33.4 1.2 %convolution_bitcast_fusion = f32[128,144]{1,0:T(8,128)S(1)} fusion(bf16[4,4,144,256]{3,2,1,0:T(8,128)(2,1)} %collective-permute-done.7, bf16[4,128,2048]{2,1,0:T(8,128)(2,1)S(1)} %copy-done, s32[]{:T(128)S(6)} %select_n.46), kind=kOutput, calls=%fused_computation.2 | convolution fusion | flops 37748736 | bytes 630788 | tf_op jit(solution)/shard_map/rsk,rtk->st/dot_general | solution.py:33
  34.6 1.2 %convolution_bitcast_fusion.1 = f32[128,144]{1,0:T(8,128)S(1)} fusion(bf16[4,4,144,256]{3,2,1,0:T(8,128)(2,1)} %collective-permute-done.7, bf16[4,128,2048]{2,1,0:T(8,128)(2,1)S(1)} %copy-done, s32[]{:T(128)S(6)} %select_n.45), kind=kOutput, calls=%fused_computation.3 | convolution fusion | flops 37748736 | bytes 630788 | tf_op jit(solution)/shard_map/rsk,rtk->st/dot_general | solution.py:33
  35.8 1.2 %convolution_bitcast_fusion.2 = f32[128,144]{1,0:T(8,128)S(1)} fusion(bf16[4,4,144,256]{3,2,1,0:T(8,128)(2,1)} %collective-permute-done.7, bf16[4,128,2048]{2,1,0:T(8,128)(2,1)S(1)} %copy-done, s32[]{:T(128)S(6)} %select_n.44), kind=kOutput, calls=%fused_computation.4 | convolution fusion | flops 37748736 | bytes 630788 | tf_op jit(solution)/shard_map/rsk,rtk->st/dot_general | solution.py:33
  37.1 1.2 %convolution_bitcast_fusion.3 = f32[128,144]{1,0:T(8,128)S(1)} fusion(bf16[4,4,144,256]{3,2,1,0:T(8,128)(2,1)} %collective-permute-done.7, bf16[4,128,2048]{2,1,0:T(8,128)(2,1)S(1)} %copy-done, s32[]{:T(128)S(6)} %select_n.43), kind=kOutput, calls=%fused_computation.5 | convolution fusion | flops 37748736 | bytes 630788 | tf_op jit(solution)/shard_map/rsk,rtk->st/dot_general | solution.py:33
  38.3 0.3 fusion.7
  38.5 0.4 convolution_convert_fusion
  38.9 0.1 copy.8
  39.0 8.1 %all_to_all.12 = bf16[8,32,192]{2,1,0:T(8,128)(2,1)S(1)} all-to-all(bf16[8,32,192]{2,1,0:T(8,128)(2,1)S(1)} %bitcast.68), channel_id=1, replica_groups=mesh['blk'=4,'rows'=8] {'rows'}, dimensions={0} | all-to-all | bytes 196608 | tf_op jit(solution)/shard_map/all_to_all | solution.py:81
  47.1 0.7 %copy.9 = bf16[256,192]{0,1:T(8,128)(2,1)} copy(bf16[256,192]{1,0:T(8,128)(2,1)S(1)} %bitcast.69) | data formatting | bytes 196608 | tf_op jit(solution)/shard_map/all_to_all | solution.py:81
  (6 shorter events, 0.1 us)
Async XLA Ops:
  0.0 8.0 %copy-start = (bf16[4,128,2048]{2,1,0:T(8,128)(2,1)S(1)}, bf16[4,128,2048]{2,1,0:T(8,128)(2,1)}, u32[]{:S(2)}) copy-start(bf16[4,128,2048]{2,1,0:T(8,128)(2,1)} %param.3) | copy-start | bytes 6291460
  0.0 10.0 %copy-start.1 = (s32[128,1]{0,1:T(1,128)S(1)}, s32[128,1]{0,1:T(1,128)}, u32[]{:S(2)}) copy-start(s32[128,1]{0,1:T(1,128)} %param.4) | copy-start | bytes 1540
  1.1 9.4 %collective-permute-start.2 = (bf16[4,48,256]{2,1,0:T(8,128)(2,1)S(1)}, bf16[4,48,256]{2,1,0:T(8,128)(2,1)S(1)}, u32[]{:S(2)}, u32[]{:S(2)}) collective-permute-start(bf16[4,48,256]{2,1,0:T(8,128)(2,1)S(1)} %constant_dynamic-slice_fusion), channel_id=1, source_target_pairs={{0,8},{8,16},{16,24},{24,0},{1,9},{9,17},{17,25},{25,1},{2,10},{10... | collective-permute-start | bytes 294920 | tf_op jit(solution)/shard_map/ppermute | solution.py:39
  4.1 9.2 %collective-permute-start.1 = (bf16[4,48,256]{2,1,0:T(8,128)(2,1)S(1)}, bf16[4,48,256]{2,1,0:T(8,128)(2,1)S(1)}, u32[]{:S(2)}, u32[]{:S(2)}) collective-permute-start(bf16[4,48,256]{2,1,0:T(8,128)(2,1)S(1)} %constant_dynamic-slice_fusion), channel_id=1, source_target_pairs={{0,16},{8,24},{16,0},{24,8},{1,17},{9,25},{17,1},{25,9},{2,18},{10... | collective-permute-start | bytes 294920 | tf_op jit(solution)/shard_map/ppermute | solution.py:39
  6.7 6.6 %collective-permute-start = (bf16[4,48,256]{2,1,0:T(8,128)(2,1)S(1)}, bf16[4,48,256]{2,1,0:T(8,128)(2,1)S(1)}, u32[]{:S(2)}, u32[]{:S(2)}) collective-permute-start(bf16[4,48,256]{2,1,0:T(8,128)(2,1)S(1)} %constant_dynamic-slice_fusion), channel_id=1, source_target_pairs={{0,24},{8,0},{16,8},{24,16},{1,25},{9,1},{17,9},{25,17},{2,26},{10... | collective-permute-start | bytes 294920 | tf_op jit(solution)/shard_map/ppermute | solution.py:39
  13.3 8.9 %collective-permute-start.4 = (bf16[4,144,256]{2,1,0:T(8,128)(2,1)S(1)}, bf16[4,144,256]{2,1,0:T(8,128)(2,1)S(1)}, u32[]{:S(2)}, u32[]{:S(2)}) collective-permute-start(bf16[4,144,256]{2,1,0:T(8,128)(2,1)S(1)} %pad_maximum_fusion.1), channel_id=1, source_target_pairs={{0,4},{1,5},{2,6},{3,7},{4,0},{5,1},{6,2},{7,3},{8,12},{9,13},{10,... | collective-permute-start | bytes 884744 | tf_op jit(solution)/shard_map/ppermute | solution.py:49
  14.9 8.9 %collective-permute-start.3 = (bf16[4,144,256]{2,1,0:T(8,128)(2,1)S(1)}, bf16[4,144,256]{2,1,0:T(8,128)(2,1)S(1)}, u32[]{:S(2)}, u32[]{:S(2)}) collective-permute-start(bf16[4,144,256]{2,1,0:T(8,128)(2,1)S(1)} %pad_maximum_fusion.1), channel_id=1, source_target_pairs={{0,2},{1,3},{2,0},{3,1},{4,6},{5,7},{6,4},{7,5},{8,10},{9,11},{10,... | collective-permute-start | bytes 884744 | tf_op jit(solution)/shard_map/ppermute | solution.py:48
  22.2 5.2 %collective-permute-start.5 = (bf16[4,144,128]{2,1,0:T(8,128)(2,1)S(1)}, bf16[4,144,128]{2,1,0:T(8,128)(2,1)S(1)}, u32[]{:S(2)}, u32[]{:S(2)}) collective-permute-start(bf16[4,144,128]{2,1,0:T(8,128)(2,1)S(1)} %slice.24), channel_id=1, source_target_pairs={{0,2},{1,3},{2,0},{3,1},{4,6},{5,7},{6,4},{7,5},{8,10},{9,11},{10,... | collective-permute-start | bytes 442376 | tf_op jit(solution)/shard_map/ppermute | solution.py:53
  23.8 5.2 %collective-permute-start.6 = (bf16[4,144,128]{2,1,0:T(8,128)(2,1)S(1)}, bf16[4,144,128]{2,1,0:T(8,128)(2,1)S(1)}, u32[]{:S(2)}, u32[]{:S(2)}) collective-permute-start(bf16[4,144,128]{2,1,0:T(8,128)(2,1)S(1)} %slice.25), channel_id=1, source_target_pairs={{0,4},{1,5},{2,6},{3,7},{4,0},{5,1},{6,2},{7,3},{8,12},{9,13},{10,... | collective-permute-start | bytes 442376 | tf_op jit(solution)/shard_map/ppermute | solution.py:54
  30.2 3.2 %collective-permute-start.7 = (bf16[4,4,144,256]{3,2,1,0:T(8,128)(2,1)}, bf16[4,4,144,256]{3,2,1,0:T(8,128)(2,1)}, u32[]{:S(2)}, u32[]{:S(2)}) collective-permute-start(bf16[4,4,144,256]{3,2,1,0:T(8,128)(2,1)} %pad_maximum_fusion), channel_id=1, source_target_pairs={{0,1},{1,0},{2,3},{3,2},{4,5},{5,4},{6,7},{7,6},{8,9},{9,8},{10,11... | collective-permute-start | bytes 3538952 | tf_op jit(solution)/shard_map/ppermute | solution.py:70

commit v8 on v7

--- a/solution.py
+++ b/solution.py
@@ -54,9 +54,12 @@
         second = lax.ppermute(along_x[:, :, half:], "rows", xor_pairs(owners_n, by))
         corner = (here ^ bx ^ by) * chunk
         remote = remote + term(corner, half, first) + term(corner + half, half, second)
-        diagonal = jnp.concatenate([first, second], axis=2)
-        held = jnp.stack([mine, along_x, along_y, diagonal])
-        masks = [0, bx, by, bx ^ by]
+        sibling = xor_pairs(owners_n, 1)
+        for mask, got in ((0, mine), (bx, along_x), (by, along_y)):
+            remote = remote + term((here ^ 1 ^ mask) * chunk, chunk, lax.ppermute(got, "rows", sibling))
+        far = (here ^ 1 ^ bx ^ by) * chunk
+        remote = remote + term(far, half, lax.ppermute(first, "rows", sibling))
+        remote = remote + term(far + half, half, lax.ppermute(second, "rows", sibling))
     else:
         held = mine[None]
         masks = [0]
@@ -66,10 +69,10 @@
                 remote = remote + term((here ^ mask ^ m) * chunk, chunk, got[j])
             held = jnp.concatenate([held, got], axis=0)
             masks = masks + [m ^ mask for m in masks]
-    if owners_n > 1:
-        got = lax.ppermute(held, "rows", xor_pairs(owners_n, 1))
-        for j, m in enumerate(masks):
-            remote = remote + term((here ^ 1 ^ m) * chunk, chunk, got[j])
+        if owners_n > 1:
+            got = lax.ppermute(held, "rows", xor_pairs(owners_n, 1))
+            for j, m in enumerate(masks):
+                remote = remote + term((here ^ 1 ^ m) * chunk, chunk, got[j])
     relative = jnp.concatenate([own, remote], axis=1)
     doubled = jnp.concatenate([relative, relative], axis=1)
     start = ((blocks_n - block) % blocks_n) * width

time: 48.2 us -> 40.7 us (0.84)
  matrix products: 8.33 us -> 4.54 us
  waiting for transfers between devices: 14.4 us -> 11.4 us
  other arithmetic: 1.68 us -> 0.48 us
  starting transfers between devices: 13.2 us -> 13.7 us
    dot_general x9 -> x10, matrix products: 6 us -> 2.22 us  [term(): jnp.einsum('rsk,rtk->st', part, tests, preferred_element_type=jnp.float32)]
    ppermute x1 -> x5, waiting for transfers between devices: 2.15 us -> 0.72 us  [the longest x1 0.7 us: on_device(): lax.ppermute(second, 'rows', sibling)]
    another operation x2 -> x0, other arithmetic: 1.2 us -> none  [on_device(): held = jnp.stack([mine, along_x, along_y, diagonal])]
    ppermute x1, waiting for transfers between devices: 2.03 us -> 1.03 us  [on_device(): first = lax.ppermute(along_y[:, :, :half], 'rows', xor_pairs(owners_n, bx))]
    ppermute x1 -> x5, starting transfers between devices: 0.01 us -> 0.52 us  [the longest x3 0.51 us: on_device(): lax.ppermute(got, 'rows', sibling)]
  transfers between devices with their start and end apart: 8 -> 12, of which waited for: 5 -> 5; matrix products, arithmetic and copies ran while one was open for 7% -> 11% of each run, Pallas kernels for 0% -> 0%
where the time goes in v8:
time: 40.7 us; the launch traced here: 40.5 us
  starting transfers between devices  13.7 us (34%)
  waiting for transfers between devices  11.4 us (28%)
  blocking collectives  8.13 us (20%)
  matrix products  4.54 us (11%)
  local copies, waits for them, and re-layouts  2.07 us (5%)
  other arithmetic  0.48 us (1%)
    all_to_all x1, blocking collectives, on_device(): lax.all_to_all(placed, 'rows', split_axis=0, concat_axis=0, tiled=True)  8.13 us
    ppermute x3, starting transfers between devices, on_device(): arrived.append(lax.ppermute(piece, 'blk', pairs))  6.96 us
    ppermute x1, waiting for transfers between devices, on_device(): along_y = lax.ppermute(mine, 'rows', xor_pairs(owners_n, by))  5.42 us
    ppermute x3, waiting for transfers between devices, on_device(): arrived.append(lax.ppermute(piece, 'blk', pairs))  2.8 us
    dot_general x10, matrix products, term(): jnp.einsum('rsk,rtk->st', part, tests, preferred_element_type=jnp.float32)  2.22 us
    dot_general x1, matrix products, on_device(): jnp.einsum('rsk,rtk->st', features, test_blocks, preferred_element_type=j...  1.96 us
    ppermute x1, starting transfers between devices, on_device(): along_y = lax.ppermute(mine, 'rows', xor_pairs(owners_n, by))  1.58 us
    ppermute x1, starting transfers between devices, on_device(): second = lax.ppermute(along_x[:, :, half:], 'rows', xor_pairs(owners_n, by))  1.58 us
  transfers between devices with their start and end apart: 12, of which 5 were waited for; matrix products, arithmetic and copies ran while one was open for 11% of the time, Pallas kernels for 0%

profile of v8, /device:TPU:0, one launch (start us, length us, event | category | flops | bytes accessed | tf_op | source)
XLA Modules:
  0.0 40.5 jit_solution(8956478357839819982)
XLA Ops:
  0.0 0.0 copy-start
  0.0 0.0 copy-start.1
  0.0 1.0 %constant_dynamic-slice_fusion = bf16[4,48,256]{2,1,0:T(8,128)(2,1)S(1)} fusion(bf16[4,48,2048]{2,1,0:T(8,128)(2,1)} %param.5, s32[]{:T(128)S(6)} %select_n.41), kind=kLoop, calls=%fused_computation.56 | loop fusion | bytes 196612 | tf_op jit(solution)/shard_map/dynamic_slice | solution.py:35
  1.1 3.0 %collective-permute-start.2 = (bf16[4,48,256]{2,1,0:T(8,128)(2,1)S(1)}, bf16[4,48,256]{2,1,0:T(8,128)(2,1)S(1)}, u32[]{:S(2)}, u32[]{:S(2)}) collective-permute-start(bf16[4,48,256]{2,1,0:T(8,128)(2,1)S(1)} %constant_dynamic-slice_fusion), channel_id=1, source_target_pairs={{0,8},{8,16},{16,24},{24,0},{1,9},{9,17},{17,25},{25,1},{2,10},{10... | collective-permute-start | bytes 294920 | tf_op jit(solution)/shard_map/ppermute | solution.py:39
  4.1 2.6 %collective-permute-start.1 = (bf16[4,48,256]{2,1,0:T(8,128)(2,1)S(1)}, bf16[4,48,256]{2,1,0:T(8,128)(2,1)S(1)}, u32[]{:S(2)}, u32[]{:S(2)}) collective-permute-start(bf16[4,48,256]{2,1,0:T(8,128)(2,1)S(1)} %constant_dynamic-slice_fusion), channel_id=1, source_target_pairs={{0,16},{8,24},{16,0},{24,8},{1,17},{9,25},{17,1},{25,9},{2,18},{10... | collective-permute-start | bytes 294920 | tf_op jit(solution)/shard_map/ppermute | solution.py:39
  6.7 1.3 %collective-permute-start = (bf16[4,48,256]{2,1,0:T(8,128)(2,1)S(1)}, bf16[4,48,256]{2,1,0:T(8,128)(2,1)S(1)}, u32[]{:S(2)}, u32[]{:S(2)}) collective-permute-start(bf16[4,48,256]{2,1,0:T(8,128)(2,1)S(1)} %constant_dynamic-slice_fusion), channel_id=1, source_target_pairs={{0,24},{8,0},{16,8},{24,16},{1,25},{9,1},{17,9},{25,17},{2,26},{10... | collective-permute-start | bytes 294920 | tf_op jit(solution)/shard_map/ppermute | solution.py:39
  8.0 0.0 copy-done
  8.0 2.0 %convolution_bitcast_fusion.10 = bf16[128,48]{0,1:T(8,128)(2,1)S(1)} fusion(bf16[4,128,2048]{2,1,0:T(8,128)(2,1)S(1)} %copy-done, bf16[4,48,2048]{2,1,0:T(8,128)(2,1)} %param.5), kind=kOutput, calls=%fused_computation.20 | convolution fusion | flops 100663296 | bytes 2895872 | tf_op jit(solution)/shard_map/rsk,rtk->st/dot_general | solution.py:41
  10.0 0.0 copy-done.1
  10.0 0.1 fusion.25
  10.1 0.2 reduce_window_sum.11
  10.3 0.2 select_reduce_fusion
  10.5 0.0 collective-permute-done.2
  10.5 2.8 %collective-permute-done.1 = bf16[4,48,256]{2,1,0:T(8,128)(2,1)S(1)} collective-permute-done((bf16[4,48,256]{2,1,0:T(8,128)(2,1)S(1)}, bf16[4,48,256]{2,1,0:T(8,128)(2,1)S(1)}, u32[]{:S(2)}, u32[]{:S(2)}) %collective-permute-start.1) | collective-permute-done | bytes 98336 | tf_op jit(solution)/shard_map/ppermute | solution.py:39
  13.2 0.0 collective-permute-done
  13.3 1.6 %collective-permute-start.4 = (bf16[4,144,256]{2,1,0:T(8,128)(2,1)S(1)}, bf16[4,144,256]{2,1,0:T(8,128)(2,1)S(1)}, u32[]{:S(2)}, u32[]{:S(2)}) collective-permute-start(bf16[4,144,256]{2,1,0:T(8,128)(2,1)S(1)} %pad_maximum_fusion), channel_id=1, source_target_pairs={{0,4},{1,5},{2,6},{3,7},{4,0},{5,1},{6,2},{7,3},{8,12},{9,13},{10,... | collective-permute-start | bytes 884744 | tf_op jit(solution)/shard_map/ppermute | solution.py:49
  14.9 1.5 %collective-permute-start.3 = (bf16[4,144,256]{2,1,0:T(8,128)(2,1)S(1)}, bf16[4,144,256]{2,1,0:T(8,128)(2,1)S(1)}, u32[]{:S(2)}, u32[]{:S(2)}) collective-permute-start(bf16[4,144,256]{2,1,0:T(8,128)(2,1)S(1)} %pad_maximum_fusion), channel_id=1, source_target_pairs={{0,2},{1,3},{2,0},{3,1},{4,6},{5,7},{6,4},{7,5},{8,10},{9,11},{10,... | collective-permute-start | bytes 884744 | tf_op jit(solution)/shard_map/ppermute | solution.py:48
  16.4 0.0 collective-permute-start.7
  16.4 0.1 copy.6
  16.5 0.2 convolution_bitcast_fusion.5
  16.8 5.4 %collective-permute-done.4 = bf16[4,144,256]{2,1,0:T(8,128)(2,1)S(1)} collective-permute-done((bf16[4,144,256]{2,1,0:T(8,128)(2,1)S(1)}, bf16[4,144,256]{2,1,0:T(8,128)(2,1)S(1)}, u32[]{:S(2)}, u32[]{:S(2)}) %collective-permute-start.4) | collective-permute-done | bytes 294944 | tf_op jit(solution)/shard_map/ppermute | solution.py:49
  22.2 1.6 %collective-permute-start.5 = (bf16[4,144,128]{2,1,0:T(8,128)(2,1)S(1)}, bf16[4,144,128]{2,1,0:T(8,128)(2,1)S(1)}, u32[]{:S(2)}, u32[]{:S(2)}) collective-permute-start(bf16[4,144,128]{2,1,0:T(8,128)(2,1)S(1)} %slice.8), channel_id=1, source_target_pairs={{0,2},{1,3},{2,0},{3,1},{4,6},{5,7},{6,4},{7,5},{8,10},{9,11},{10,... | collective-permute-start | bytes 442376 | tf_op jit(solution)/shard_map/ppermute | solution.py:53
  23.8 0.0 collective-permute-done.3
  23.8 1.6 %collective-permute-start.6 = (bf16[4,144,128]{2,1,0:T(8,128)(2,1)S(1)}, bf16[4,144,128]{2,1,0:T(8,128)(2,1)S(1)}, u32[]{:S(2)}, u32[]{:S(2)}) collective-permute-start(bf16[4,144,128]{2,1,0:T(8,128)(2,1)S(1)} %slice.9), channel_id=1, source_target_pairs={{0,4},{1,5},{2,6},{3,7},{4,0},{5,1},{6,2},{7,3},{8,12},{9,13},{10,... | collective-permute-start | bytes 442376 | tf_op jit(solution)/shard_map/ppermute | solution.py:54
  25.4 0.0 collective-permute-start.9
  25.4 0.5 %collective-permute-start.8 = (bf16[4,144,256]{2,1,0:T(8,128)(2,1)S(1)}, bf16[4,144,256]{2,1,0:T(8,128)(2,1)S(1)}, u32[]{:S(2)}, u32[]{:S(2)}) collective-permute-start(bf16[4,144,256]{2,1,0:T(8,128)(2,1)S(1)} %collective-permute-done.3), channel_id=1, source_target_pairs={{0,1},{1,0},{2,3},{3,2},{4,5},{5,4},{6,7},{7,6},{8,9},{9,8},{10,11... | collective-permute-start | bytes 884744 | tf_op jit(solution)/shard_map/ppermute | solution.py:59
  25.9 0.2 convolution_bitcast_fusion.3
  26.1 0.0 collective-permute-done.7
  26.1 0.2 convolution_bitcast_fusion.2
  26.4 1.0 %collective-permute-done.5 = bf16[4,144,128]{2,1,0:T(8,128)(2,1)S(1)} collective-permute-done((bf16[4,144,128]{2,1,0:T(8,128)(2,1)S(1)}, bf16[4,144,128]{2,1,0:T(8,128)(2,1)S(1)}, u32[]{:S(2)}, u32[]{:S(2)}) %collective-permute-start.5) | collective-permute-done | bytes 147488 | tf_op jit(solution)/shard_map/ppermute | solution.py:53
  27.4 0.0 collective-permute-start.10
  27.4 0.2 convolution_bitcast_fusion.9
  27.6 1.4 %collective-permute-done.6 = bf16[4,144,128]{2,1,0:T(8,128)(2,1)S(1)} collective-permute-done((bf16[4,144,128]{2,1,0:T(8,128)(2,1)S(1)}, bf16[4,144,128]{2,1,0:T(8,128)(2,1)S(1)}, u32[]{:S(2)}, u32[]{:S(2)}) %collective-permute-start.6) | collective-permute-done | bytes 147488 | tf_op jit(solution)/shard_map/ppermute | solution.py:54
  29.0 0.0 collective-permute-start.11
  29.0 0.2 convolution_bitcast_fusion.8
  29.2 0.2 fusion.4
  29.5 0.0 collective-permute-done.10
  29.5 0.2 convolution_bitcast_fusion.7
  29.7 0.7 %collective-permute-done.11 = bf16[4,144,128]{2,1,0:T(8,128)(2,1)S(1)} collective-permute-done((bf16[4,144,128]{2,1,0:T(8,128)(2,1)S(1)}, bf16[4,144,128]{2,1,0:T(8,128)(2,1)S(1)}, u32[]{:S(2)}, u32[]{:S(2)}) %collective-permute-start.11) | collective-permute-done | bytes 147488 | tf_op jit(solution)/shard_map/ppermute | solution.py:62
  30.4 0.2 convolution_bitcast_fusion.6
  30.6 0.0 collective-permute-done.9
  30.6 0.2 convolution_bitcast_fusion
  30.8 0.0 collective-permute-done.8
  30.9 0.3 fusion.8
  31.1 0.4 convolution_convert_fusion
  31.5 0.1 copy.8
  31.6 8.1 %all_to_all.12 = bf16[8,32,192]{2,1,0:T(8,128)(2,1)S(1)} all-to-all(bf16[8,32,192]{2,1,0:T(8,128)(2,1)S(1)} %bitcast.57), channel_id=1, replica_groups=mesh['blk'=4,'rows'=8] {'rows'}, dimensions={0} | all-to-all | bytes 196608 | tf_op jit(solution)/shard_map/all_to_all | solution.py:84
  39.7 0.7 %copy.9 = bf16[256,192]{0,1:T(8,128)(2,1)} copy(bf16[256,192]{1,0:T(8,128)(2,1)S(1)} %bitcast.58) | data formatting | bytes 196608 | tf_op jit(solution)/shard_map/all_to_all | solution.py:84
  (5 shorter events, 0.1 us)
Async XLA Ops:
  0.0 8.0 %copy-start = (bf16[4,128,2048]{2,1,0:T(8,128)(2,1)S(1)}, bf16[4,128,2048]{2,1,0:T(8,128)(2,1)}, u32[]{:S(2)}) copy-start(bf16[4,128,2048]{2,1,0:T(8,128)(2,1)} %param.3) | copy-start | bytes 6291460
  0.0 10.0 %copy-start.1 = (s32[128,1]{0,1:T(1,128)S(1)}, s32[128,1]{0,1:T(1,128)}, u32[]{:S(2)}) copy-start(s32[128,1]{0,1:T(1,128)} %param.4) | copy-start | bytes 1540
  1.1 9.4 %collective-permute-start.2 = (bf16[4,48,256]{2,1,0:T(8,128)(2,1)S(1)}, bf16[4,48,256]{2,1,0:T(8,128)(2,1)S(1)}, u32[]{:S(2)}, u32[]{:S(2)}) collective-permute-start(bf16[4,48,256]{2,1,0:T(8,128)(2,1)S(1)} %constant_dynamic-slice_fusion), channel_id=1, source_target_pairs={{0,8},{8,16},{16,24},{24,0},{1,9},{9,17},{17,25},{25,1},{2,10},{10... | collective-permute-start | bytes 294920 | tf_op jit(solution)/shard_map/ppermute | solution.py:39
  4.1 9.2 %collective-permute-start.1 = (bf16[4,48,256]{2,1,0:T(8,128)(2,1)S(1)}, bf16[4,48,256]{2,1,0:T(8,128)(2,1)S(1)}, u32[]{:S(2)}, u32[]{:S(2)}) collective-permute-start(bf16[4,48,256]{2,1,0:T(8,128)(2,1)S(1)} %constant_dynamic-slice_fusion), channel_id=1, source_target_pairs={{0,16},{8,24},{16,0},{24,8},{1,17},{9,25},{17,1},{25,9},{2,18},{10... | collective-permute-start | bytes 294920 | tf_op jit(solution)/shard_map/ppermute | solution.py:39
  6.7 6.6 %collective-permute-start = (bf16[4,48,256]{2,1,0:T(8,128)(2,1)S(1)}, bf16[4,48,256]{2,1,0:T(8,128)(2,1)S(1)}, u32[]{:S(2)}, u32[]{:S(2)}) collective-permute-start(bf16[4,48,256]{2,1,0:T(8,128)(2,1)S(1)} %constant_dynamic-slice_fusion), channel_id=1, source_target_pairs={{0,24},{8,0},{16,8},{24,16},{1,25},{9,1},{17,9},{25,17},{2,26},{10... | collective-permute-start | bytes 294920 | tf_op jit(solution)/shard_map/ppermute | solution.py:39
  13.3 8.9 %collective-permute-start.4 = (bf16[4,144,256]{2,1,0:T(8,128)(2,1)S(1)}, bf16[4,144,256]{2,1,0:T(8,128)(2,1)S(1)}, u32[]{:S(2)}, u32[]{:S(2)}) collective-permute-start(bf16[4,144,256]{2,1,0:T(8,128)(2,1)S(1)} %pad_maximum_fusion), channel_id=1, source_target_pairs={{0,4},{1,5},{2,6},{3,7},{4,0},{5,1},{6,2},{7,3},{8,12},{9,13},{10,... | collective-permute-start | bytes 884744 | tf_op jit(solution)/shard_map/ppermute | solution.py:49
  14.9 8.9 %collective-permute-start.3 = (bf16[4,144,256]{2,1,0:T(8,128)(2,1)S(1)}, bf16[4,144,256]{2,1,0:T(8,128)(2,1)S(1)}, u32[]{:S(2)}, u32[]{:S(2)}) collective-permute-start(bf16[4,144,256]{2,1,0:T(8,128)(2,1)S(1)} %pad_maximum_fusion), channel_id=1, source_target_pairs={{0,2},{1,3},{2,0},{3,1},{4,6},{5,7},{6,4},{7,5},{8,10},{9,11},{10,... | collective-permute-start | bytes 884744 | tf_op jit(solution)/shard_map/ppermute | solution.py:48
  16.4 9.7 %collective-permute-start.7 = (bf16[4,144,256]{2,1,0:T(8,128)(2,1)S(1)}, bf16[4,144,256]{2,1,0:T(8,128)(2,1)S(1)}, u32[]{:S(2)}, u32[]{:S(2)}) collective-permute-start(bf16[4,144,256]{2,1,0:T(8,128)(2,1)S(1)} %pad_maximum_fusion), channel_id=1, source_target_pairs={{0,1},{1,0},{2,3},{3,2},{4,5},{5,4},{6,7},{7,6},{8,9},{9,8},{10,11... | collective-permute-start | bytes 884744 | tf_op jit(solution)/shard_map/ppermute | solution.py:59
  22.2 5.2 %collective-permute-start.5 = (bf16[4,144,128]{2,1,0:T(8,128)(2,1)S(1)}, bf16[4,144,128]{2,1,0:T(8,128)(2,1)S(1)}, u32[]{:S(2)}, u32[]{:S(2)}) collective-permute-start(bf16[4,144,128]{2,1,0:T(8,128)(2,1)S(1)} %slice.8), channel_id=1, source_target_pairs={{0,2},{1,3},{2,0},{3,1},{4,6},{5,7},{6,4},{7,5},{8,10},{9,11},{10,... | collective-permute-start | bytes 442376 | tf_op jit(solution)/shard_map/ppermute | solution.py:53
  23.8 5.2 %collective-permute-start.6 = (bf16[4,144,128]{2,1,0:T(8,128)(2,1)S(1)}, bf16[4,144,128]{2,1,0:T(8,128)(2,1)S(1)}, u32[]{:S(2)}, u32[]{:S(2)}) collective-permute-start(bf16[4,144,128]{2,1,0:T(8,128)(2,1)S(1)} %slice.9), channel_id=1, source_target_pairs={{0,4},{1,5},{2,6},{3,7},{4,0},{5,1},{6,2},{7,3},{8,12},{9,13},{10,... | collective-permute-start | bytes 442376 | tf_op jit(solution)/shard_map/ppermute | solution.py:54
  25.4 5.2 %collective-permute-start.9 = (bf16[4,144,256]{2,1,0:T(8,128)(2,1)S(1)}, bf16[4,144,256]{2,1,0:T(8,128)(2,1)S(1)}, u32[]{:S(2)}, u32[]{:S(2)}) collective-permute-start(bf16[4,144,256]{2,1,0:T(8,128)(2,1)S(1)} %collective-permute-done.4), channel_id=1, source_target_pairs={{0,1},{1,0},{2,3},{3,2},{4,5},{5,4},{6,7},{7,6},{8,9},{9,8},{10,11... | collective-permute-start | bytes 884744 | tf_op jit(solution)/shard_map/ppermute | solution.py:59
  25.4 5.5 %collective-permute-start.8 = (bf16[4,144,256]{2,1,0:T(8,128)(2,1)S(1)}, bf16[4,144,256]{2,1,0:T(8,128)(2,1)S(1)}, u32[]{:S(2)}, u32[]{:S(2)}) collective-permute-start(bf16[4,144,256]{2,1,0:T(8,128)(2,1)S(1)} %collective-permute-done.3), channel_id=1, source_target_pairs={{0,1},{1,0},{2,3},{3,2},{4,5},{5,4},{6,7},{7,6},{8,9},{9,8},{10,11... | collective-permute-start | bytes 884744 | tf_op jit(solution)/shard_map/ppermute | solution.py:59
  27.4 2.0 %collective-permute-start.10 = (bf16[4,144,128]{2,1,0:T(8,128)(2,1)S(1)}, bf16[4,144,128]{2,1,0:T(8,128)(2,1)S(1)}, u32[]{:S(2)}, u32[]{:S(2)}) collective-permute-start(bf16[4,144,128]{2,1,0:T(8,128)(2,1)S(1)} %collective-permute-done.5), channel_id=1, source_target_pairs={{0,1},{1,0},{2,3},{3,2},{4,5},{5,4},{6,7},{7,6},{8,9},{9,8},{10,11... | collective-permute-start | bytes 442376 | tf_op jit(solution)/shard_map/ppermute | solution.py:61
  29.0 1.4 %collective-permute-start.11 = (bf16[4,144,128]{2,1,0:T(8,128)(2,1)S(1)}, bf16[4,144,128]{2,1,0:T(8,128)(2,1)S(1)}, u32[]{:S(2)}, u32[]{:S(2)}) collective-permute-start(bf16[4,144,128]{2,1,0:T(8,128)(2,1)S(1)} %collective-permute-done.6), channel_id=1, source_target_pairs={{0,1},{1,0},{2,3},{3,2},{4,5},{5,4},{6,7},{7,6},{8,9},{9,8},{10,11... | collective-permute-start | bytes 442376 | tf_op jit(solution)/shard_map/ppermute | solution.py:62

commit v9 on v8

--- a/solution.py
+++ b/solution.py
@@ -49,17 +49,11 @@
         along_y = lax.ppermute(mine, "rows", xor_pairs(owners_n, by))
         remote = remote + term((here ^ bx) * chunk, chunk, along_x)
         remote = remote + term((here ^ by) * chunk, chunk, along_y)
-        half = chunk // 2
-        first = lax.ppermute(along_y[:, :, :half], "rows", xor_pairs(owners_n, bx))
-        second = lax.ppermute(along_x[:, :, half:], "rows", xor_pairs(owners_n, by))
-        corner = (here ^ bx ^ by) * chunk
-        remote = remote + term(corner, half, first) + term(corner + half, half, second)
+        across = lax.ppermute(mine, "rows", xor_pairs(owners_n, bx ^ by))
+        remote = remote + term((here ^ bx ^ by) * chunk, chunk, across)
         sibling = xor_pairs(owners_n, 1)
-        for mask, got in ((0, mine), (bx, along_x), (by, along_y)):
+        for mask, got in ((0, mine), (bx, along_x), (by, along_y), (bx ^ by, across)):
             remote = remote + term((here ^ 1 ^ mask) * chunk, chunk, lax.ppermute(got, "rows", sibling))
-        far = (here ^ 1 ^ bx ^ by) * chunk
-        remote = remote + term(far, half, lax.ppermute(first, "rows", sibling))
-        remote = remote + term(far + half, half, lax.ppermute(second, "rows", sibling))
     else:
         held = mine[None]
         masks = [0]

time: 40.7 us -> 42.5 us (1.044)
  waiting for transfers between devices: 11.4 us -> 15.1 us
  starting transfers between devices: 13.7 us -> 11 us
  matrix products: 4.54 us -> 5.24 us
    ppermute x4 -> x1, waiting for transfers between devices: 3.13 us -> 6.98 us  [on_device(): across = lax.ppermute(mine, 'rows', xor_pairs(owners_n, bx ^ by))]
    ppermute x1, starting transfers between devices: 1.58 us -> 0.51 us  [on_device(): along_y = lax.ppermute(mine, 'rows', xor_pairs(owners_n, by))]
    ppermute x1, starting transfers between devices: 1.49 us -> 0.54 us  [on_device(): along_x = lax.ppermute(mine, 'rows', xor_pairs(owners_n, bx))]
    dot_general x10 -> x8, matrix products: 2.22 us -> 2.91 us  [term(): jnp.einsum('rsk,rtk->st', part, tests, preferred_element_type=jnp.float32)]
    ppermute x4 -> x1, starting transfers between devices: 3.15 us -> 2.51 us  [on_device(): across = lax.ppermute(mine, 'rows', xor_pairs(owners_n, bx ^ by))]
  transfers between devices with their start and end apart: 12 -> 10, of which waited for: 5 -> 4; matrix products, arithmetic and copies ran while one was open for 11% -> 12% of each run, Pallas kernels for 0% -> 0%
where the time goes in v9:
time: 42.5 us; the launch traced here: 42.2 us
  waiting for transfers between devices  15.1 us (36%)
  starting transfers between devices  11 us (26%)
  blocking collectives  8.34 us (20%)
  matrix products  5.24 us (12%)
  local copies, waits for them, and re-layouts  2.02 us (5%)
  other arithmetic  0.48 us (1%)
    all_to_all x1, blocking collectives, on_device(): lax.all_to_all(placed, 'rows', split_axis=0, concat_axis=0, tiled=True)  8.34 us
    ppermute x1, waiting for transfers between devices, on_device(): across = lax.ppermute(mine, 'rows', xor_pairs(owners_n, bx ^ by))  6.98 us
    ppermute x3, starting transfers between devices, on_device(): arrived.append(lax.ppermute(piece, 'blk', pairs))  6.96 us
    ppermute x1, waiting for transfers between devices, on_device(): along_y = lax.ppermute(mine, 'rows', xor_pairs(owners_n, by))  5.18 us
    dot_general x8, matrix products, term(): jnp.einsum('rsk,rtk->st', part, tests, preferred_element_type=jnp.float32)  2.91 us
    ppermute x3, waiting for transfers between devices, on_device(): arrived.append(lax.ppermute(piece, 'blk', pairs))  2.8 us
    ppermute x1, starting transfers between devices, on_device(): across = lax.ppermute(mine, 'rows', xor_pairs(owners_n, bx ^ by))  2.51 us
    dot_general x1, matrix products, on_device(): jnp.einsum('rsk,rtk->st', features, test_blocks, preferred_element_type=j...  1.96 us
  transfers between devices with their start and end apart: 10, of which 4 were waited for; matrix products, arithmetic and copies ran while one was open for 12% of the time, Pallas kernels for 0%

profile of v9, /device:TPU:0, one launch (start us, length us, event | category | flops | bytes accessed | tf_op | source)
XLA Modules:
  0.0 42.2 jit_solution(4498711682319896142)
XLA Ops:
  0.0 0.0 copy-start
  0.0 0.0 copy-start.1
  0.0 1.0 %constant_dynamic-slice_fusion = bf16[4,48,256]{2,1,0:T(8,128)(2,1)S(1)} fusion(bf16[4,48,2048]{2,1,0:T(8,128)(2,1)} %param.5, s32[]{:T(128)S(6)} %select_n.35), kind=kLoop, calls=%fused_computation.48 | loop fusion | bytes 196612 | tf_op jit(solution)/shard_map/dynamic_slice | solution.py:35
  1.1 3.0 %collective-permute-start.2 = (bf16[4,48,256]{2,1,0:T(8,128)(2,1)S(1)}, bf16[4,48,256]{2,1,0:T(8,128)(2,1)S(1)}, u32[]{:S(2)}, u32[]{:S(2)}) collective-permute-start(bf16[4,48,256]{2,1,0:T(8,128)(2,1)S(1)} %constant_dynamic-slice_fusion), channel_id=1, source_target_pairs={{0,8},{8,16},{16,24},{24,0},{1,9},{9,17},{17,25},{25,1},{2,10},{10... | collective-permute-start | bytes 294920 | tf_op jit(solution)/shard_map/ppermute | solution.py:39
  4.1 2.6 %collective-permute-start.1 = (bf16[4,48,256]{2,1,0:T(8,128)(2,1)S(1)}, bf16[4,48,256]{2,1,0:T(8,128)(2,1)S(1)}, u32[]{:S(2)}, u32[]{:S(2)}) collective-permute-start(bf16[4,48,256]{2,1,0:T(8,128)(2,1)S(1)} %constant_dynamic-slice_fusion), channel_id=1, source_target_pairs={{0,16},{8,24},{16,0},{24,8},{1,17},{9,25},{17,1},{25,9},{2,18},{10... | collective-permute-start | bytes 294920 | tf_op jit(solution)/shard_map/ppermute | solution.py:39
  6.7 1.3 %collective-permute-start = (bf16[4,48,256]{2,1,0:T(8,128)(2,1)S(1)}, bf16[4,48,256]{2,1,0:T(8,128)(2,1)S(1)}, u32[]{:S(2)}, u32[]{:S(2)}) collective-permute-start(bf16[4,48,256]{2,1,0:T(8,128)(2,1)S(1)} %constant_dynamic-slice_fusion), channel_id=1, source_target_pairs={{0,24},{8,0},{16,8},{24,16},{1,25},{9,1},{17,9},{25,17},{2,26},{10... | collective-permute-start | bytes 294920 | tf_op jit(solution)/shard_map/ppermute | solution.py:39
  8.0 0.0 copy-done
  8.0 2.0 %convolution_bitcast_fusion.8 = bf16[128,48]{0,1:T(8,128)(2,1)S(1)} fusion(bf16[4,128,2048]{2,1,0:T(8,128)(2,1)S(1)} %copy-done, bf16[4,48,2048]{2,1,0:T(8,128)(2,1)} %param.5), kind=kOutput, calls=%fused_computation.16 | convolution fusion | flops 100663296 | bytes 2895872 | tf_op jit(solution)/shard_map/rsk,rtk->st/dot_general | solution.py:41
  10.0 0.0 copy-done.1
  10.0 0.1 fusion.21
  10.1 0.2 reduce_window_sum.11
  10.3 0.2 select_reduce_fusion
  10.5 0.0 collective-permute-done.2
  10.5 2.8 %collective-permute-done.1 = bf16[4,48,256]{2,1,0:T(8,128)(2,1)S(1)} collective-permute-done((bf16[4,48,256]{2,1,0:T(8,128)(2,1)S(1)}, bf16[4,48,256]{2,1,0:T(8,128)(2,1)S(1)}, u32[]{:S(2)}, u32[]{:S(2)}) %collective-permute-start.1) | collective-permute-done | bytes 98336 | tf_op jit(solution)/shard_map/ppermute | solution.py:39
  13.2 0.0 collective-permute-done
  13.3 2.5 %collective-permute-start.5 = (bf16[4,144,256]{2,1,0:T(8,128)(2,1)S(1)}, bf16[4,144,256]{2,1,0:T(8,128)(2,1)S(1)}, u32[]{:S(2)}, u32[]{:S(2)}) collective-permute-start(bf16[4,144,256]{2,1,0:T(8,128)(2,1)S(1)} %pad_maximum_fusion), channel_id=1, source_target_pairs={{0,6},{1,7},{2,4},{3,5},{4,2},{5,3},{6,0},{7,1},{8,14},{9,15},{10,... | collective-permute-start | bytes 884744 | tf_op jit(solution)/shard_map/ppermute | solution.py:52
  15.8 0.5 %collective-permute-start.4 = (bf16[4,144,256]{2,1,0:T(8,128)(2,1)S(1)}, bf16[4,144,256]{2,1,0:T(8,128)(2,1)S(1)}, u32[]{:S(2)}, u32[]{:S(2)}) collective-permute-start(bf16[4,144,256]{2,1,0:T(8,128)(2,1)S(1)} %pad_maximum_fusion), channel_id=1, source_target_pairs={{0,4},{1,5},{2,6},{3,7},{4,0},{5,1},{6,2},{7,3},{8,12},{9,13},{10,... | collective-permute-start | bytes 884744 | tf_op jit(solution)/shard_map/ppermute | solution.py:49
  16.3 0.5 %collective-permute-start.3 = (bf16[4,144,256]{2,1,0:T(8,128)(2,1)S(1)}, bf16[4,144,256]{2,1,0:T(8,128)(2,1)}, u32[]{:S(2)}, u32[]{:S(2)}) collective-permute-start(bf16[4,144,256]{2,1,0:T(8,128)(2,1)S(1)} %pad_maximum_fusion), channel_id=1, source_target_pairs={{0,2},{1,3},{2,0},{3,1},{4,6},{5,7},{6,4},{7,5},{8,10},{9,11},{10,... | collective-permute-start | bytes 884744 | tf_op jit(solution)/shard_map/ppermute | solution.py:48
  16.9 0.0 collective-permute-start.6
  16.9 0.2 convolution_bitcast_fusion.7
  17.1 0.1 copy.6
  17.2 7.0 %collective-permute-done.5 = bf16[4,144,256]{2,1,0:T(8,128)(2,1)S(1)} collective-permute-done((bf16[4,144,256]{2,1,0:T(8,128)(2,1)S(1)}, bf16[4,144,256]{2,1,0:T(8,128)(2,1)S(1)}, u32[]{:S(2)}, u32[]{:S(2)}) %collective-permute-start.5) | collective-permute-done | bytes 294944 | tf_op jit(solution)/shard_map/ppermute | solution.py:52
  24.2 0.0 collective-permute-start.9
  24.2 5.2 %collective-permute-done.4 = bf16[4,144,256]{2,1,0:T(8,128)(2,1)S(1)} collective-permute-done((bf16[4,144,256]{2,1,0:T(8,128)(2,1)S(1)}, bf16[4,144,256]{2,1,0:T(8,128)(2,1)S(1)}, u32[]{:S(2)}, u32[]{:S(2)}) %collective-permute-start.4) | collective-permute-done | bytes 294944 | tf_op jit(solution)/shard_map/ppermute | solution.py:49
  29.4 0.1 collective-permute-start.8
  29.5 0.1 collective-permute-done.3
  29.6 0.3 collective-permute-start.7
  29.9 0.2 convolution_bitcast_fusion.4
  30.2 0.2 convolution_bitcast_fusion.5
  30.4 0.0 collective-permute-done.6
  30.4 0.2 convolution_bitcast_fusion.3
  30.7 1.2 %fusion.3 = f32[128,144]{1,0:T(8,128)S(1)} fusion(f32[128,144]{1,0:T(8,128)S(1)} %convolution_bitcast_fusion.3, f32[128,144]{1,0:T(8,128)S(1)} %convolution_bitcast_fusion.4, f32[128,144]{1,0:T(8,128)S(1)} %convolution_bitcast_fusion.5, f32[128,144]{1,0:T(8,128)S(1)} %convolution_bitcast_fusion.7, bf16[4,144,256]{2,1,0:T(8,128)(2,1)} %collective-permute-done.3, ...), kind=kOutput, calls=%fused_computation.12 | convolution fusion | flops 37822464 | bytes 1155076 | tf_op jit(solution)/shard_map/rsk,rtk->st/dot_general | solution.py:33
  31.9 0.0 collective-permute-done.9
  31.9 0.2 convolution_bitcast_fusion
  32.2 0.0 collective-permute-done.8
  32.2 0.2 convolution_bitcast_fusion.1
  32.4 0.0 collective-permute-done.7
  32.4 0.2 fusion.6
  32.7 0.4 convolution_convert_fusion
  33.0 0.1 copy.8
  33.2 8.3 %all_to_all.12 = bf16[8,32,192]{2,1,0:T(8,128)(2,1)S(1)} all-to-all(bf16[8,32,192]{2,1,0:T(8,128)(2,1)S(1)} %bitcast.47), channel_id=1, replica_groups=mesh['blk'=4,'rows'=8] {'rows'}, dimensions={0} | all-to-all | bytes 196608 | tf_op jit(solution)/shard_map/all_to_all | solution.py:78
  41.5 0.7 %copy.9 = bf16[256,192]{0,1:T(8,128)(2,1)} copy(bf16[256,192]{1,0:T(8,128)(2,1)S(1)} %bitcast.48) | data formatting | bytes 196608 | tf_op jit(solution)/shard_map/all_to_all | solution.py:78
  (3 shorter events, 0.1 us)
Async XLA Ops:
  0.0 8.0 %copy-start = (bf16[4,128,2048]{2,1,0:T(8,128)(2,1)S(1)}, bf16[4,128,2048]{2,1,0:T(8,128)(2,1)}, u32[]{:S(2)}) copy-start(bf16[4,128,2048]{2,1,0:T(8,128)(2,1)} %param.3) | copy-start | bytes 6291460
  0.0 10.0 %copy-start.1 = (s32[128,1]{0,1:T(1,128)S(1)}, s32[128,1]{0,1:T(1,128)}, u32[]{:S(2)}) copy-start(s32[128,1]{0,1:T(1,128)} %param.4) | copy-start | bytes 1540
  1.1 9.4 %collective-permute-start.2 = (bf16[4,48,256]{2,1,0:T(8,128)(2,1)S(1)}, bf16[4,48,256]{2,1,0:T(8,128)(2,1)S(1)}, u32[]{:S(2)}, u32[]{:S(2)}) collective-permute-start(bf16[4,48,256]{2,1,0:T(8,128)(2,1)S(1)} %constant_dynamic-slice_fusion), channel_id=1, source_target_pairs={{0,8},{8,16},{16,24},{24,0},{1,9},{9,17},{17,25},{25,1},{2,10},{10... | collective-permute-start | bytes 294920 | tf_op jit(solution)/shard_map/ppermute | solution.py:39
  4.1 9.2 %collective-permute-start.1 = (bf16[4,48,256]{2,1,0:T(8,128)(2,1)S(1)}, bf16[4,48,256]{2,1,0:T(8,128)(2,1)S(1)}, u32[]{:S(2)}, u32[]{:S(2)}) collective-permute-start(bf16[4,48,256]{2,1,0:T(8,128)(2,1)S(1)} %constant_dynamic-slice_fusion), channel_id=1, source_target_pairs={{0,16},{8,24},{16,0},{24,8},{1,17},{9,25},{17,1},{25,9},{2,18},{10... | collective-permute-start | bytes 294920 | tf_op jit(solution)/shard_map/ppermute | solution.py:39
  6.7 6.6 %collective-permute-start = (bf16[4,48,256]{2,1,0:T(8,128)(2,1)S(1)}, bf16[4,48,256]{2,1,0:T(8,128)(2,1)S(1)}, u32[]{:S(2)}, u32[]{:S(2)}) collective-permute-start(bf16[4,48,256]{2,1,0:T(8,128)(2,1)S(1)} %constant_dynamic-slice_fusion), channel_id=1, source_target_pairs={{0,24},{8,0},{16,8},{24,16},{1,25},{9,1},{17,9},{25,17},{2,26},{10... | collective-permute-start | bytes 294920 | tf_op jit(solution)/shard_map/ppermute | solution.py:39
  13.3 10.9 %collective-permute-start.5 = (bf16[4,144,256]{2,1,0:T(8,128)(2,1)S(1)}, bf16[4,144,256]{2,1,0:T(8,128)(2,1)S(1)}, u32[]{:S(2)}, u32[]{:S(2)}) collective-permute-start(bf16[4,144,256]{2,1,0:T(8,128)(2,1)S(1)} %pad_maximum_fusion), channel_id=1, source_target_pairs={{0,6},{1,7},{2,4},{3,5},{4,2},{5,3},{6,0},{7,1},{8,14},{9,15},{10,... | collective-permute-start | bytes 884744 | tf_op jit(solution)/shard_map/ppermute | solution.py:52
  15.8 13.6 %collective-permute-start.4 = (bf16[4,144,256]{2,1,0:T(8,128)(2,1)S(1)}, bf16[4,144,256]{2,1,0:T(8,128)(2,1)S(1)}, u32[]{:S(2)}, u32[]{:S(2)}) collective-permute-start(bf16[4,144,256]{2,1,0:T(8,128)(2,1)S(1)} %pad_maximum_fusion), channel_id=1, source_target_pairs={{0,4},{1,5},{2,6},{3,7},{4,0},{5,1},{6,2},{7,3},{8,12},{9,13},{10,... | collective-permute-start | bytes 884744 | tf_op jit(solution)/shard_map/ppermute | solution.py:49
  16.3 13.3 %collective-permute-start.3 = (bf16[4,144,256]{2,1,0:T(8,128)(2,1)S(1)}, bf16[4,144,256]{2,1,0:T(8,128)(2,1)}, u32[]{:S(2)}, u32[]{:S(2)}) collective-permute-start(bf16[4,144,256]{2,1,0:T(8,128)(2,1)S(1)} %pad_maximum_fusion), channel_id=1, source_target_pairs={{0,2},{1,3},{2,0},{3,1},{4,6},{5,7},{6,4},{7,5},{8,10},{9,11},{10,... | collective-permute-start | bytes 884744 | tf_op jit(solution)/shard_map/ppermute | solution.py:48
  16.9 13.5 %collective-permute-start.6 = (bf16[4,144,256]{2,1,0:T(8,128)(2,1)S(1)}, bf16[4,144,256]{2,1,0:T(8,128)(2,1)S(1)}, u32[]{:S(2)}, u32[]{:S(2)}) collective-permute-start(bf16[4,144,256]{2,1,0:T(8,128)(2,1)S(1)} %pad_maximum_fusion), channel_id=1, source_target_pairs={{0,1},{1,0},{2,3},{3,2},{4,5},{5,4},{6,7},{7,6},{8,9},{9,8},{10,11... | collective-permute-start | bytes 884744 | tf_op jit(solution)/shard_map/ppermute | solution.py:56
  24.2 7.7 %collective-permute-start.9 = (bf16[4,144,256]{2,1,0:T(8,128)(2,1)S(1)}, bf16[4,144,256]{2,1,0:T(8,128)(2,1)S(1)}, u32[]{:S(2)}, u32[]{:S(2)}) collective-permute-start(bf16[4,144,256]{2,1,0:T(8,128)(2,1)S(1)} %collective-permute-done.5), channel_id=1, source_target_pairs={{0,1},{1,0},{2,3},{3,2},{4,5},{5,4},{6,7},{7,6},{8,9},{9,8},{10,11... | collective-permute-start | bytes 884744 | tf_op jit(solution)/shard_map/ppermute | solution.py:56
  29.4 2.8 %collective-permute-start.8 = (bf16[4,144,256]{2,1,0:T(8,128)(2,1)S(1)}, bf16[4,144,256]{2,1,0:T(8,128)(2,1)S(1)}, u32[]{:S(2)}, u32[]{:S(2)}) collective-permute-start(bf16[4,144,256]{2,1,0:T(8,128)(2,1)S(1)} %collective-permute-done.4), channel_id=1, source_target_pairs={{0,1},{1,0},{2,3},{3,2},{4,5},{5,4},{6,7},{7,6},{8,9},{9,8},{10,11... | collective-permute-start | bytes 884744 | tf_op jit(solution)/shard_map/ppermute | solution.py:56
  29.6 2.8 %collective-permute-start.7 = (bf16[4,144,256]{2,1,0:T(8,128)(2,1)}, bf16[4,144,256]{2,1,0:T(8,128)(2,1)S(1)}, u32[]{:S(2)}, u32[]{:S(2)}) collective-permute-start(bf16[4,144,256]{2,1,0:T(8,128)(2,1)} %collective-permute-done.3), channel_id=1, source_target_pairs={{0,1},{1,0},{2,3},{3,2},{4,5},{5,4},{6,7},{7,6},{8,9},{9,8},{10,11... | collective-permute-start | bytes 884744 | tf_op jit(solution)/shard_map/ppermute | solution.py:56

commit v10 on v8

--- a/solution.py
+++ b/solution.py
@@ -32,7 +32,9 @@
         part = lax.dynamic_slice_in_dim(features, offset, size, axis=2)
         return jnp.einsum("rsk,rtk->st", part, tests, preferred_element_type=jnp.float32)
 
-    piece = lax.dynamic_slice_in_dim(test_blocks, here * chunk, chunk, axis=2)
+    piece = test_blocks[:, :, :chunk]
+    for c in range(1, owners_n):
+        piece = jnp.where(here == c, test_blocks[:, :, c * chunk:(c + 1) * chunk], piece)
     arrived = []
     for step in range(1, blocks_n):
         pairs = [(b, (b - step) % blocks_n) for b in range(blocks_n)]

time: 40.7 us -> 41.1 us (level)
  other arithmetic: 0.48 us -> 1.88 us
  local copies, waits for them, and re-layouts: 2.07 us -> 1.02 us
    select_n x0 -> x1, other arithmetic: none -> 1.41 us  [on_device(): jnp.where(here == c, test_blocks[:, :, c * chunk:(c + 1) * chunk], piece)]
    dynamic_slice x1 -> x0, local copies, waits for them, and re-layouts: 1.05 us -> none  [on_device(): piece = lax.dynamic_slice_in_dim(test_blocks, here * chunk, chunk, axis=2)]
where the time goes in v10:
time: 41.1 us; the launch traced here: 40.9 us
  starting transfers between devices  13.7 us (33%)
  waiting for transfers between devices  11.3 us (27%)
  blocking collectives  8.12 us (20%)
  matrix products  4.56 us (11%)
  other arithmetic  1.88 us (5%)
  local copies, waits for them, and re-layouts  1.02 us (2%)
    all_to_all x1, blocking collectives, on_device(): lax.all_to_all(placed, 'rows', split_axis=0, concat_axis=0, tiled=True)  8.12 us
    ppermute x3, starting transfers between devices, on_device(): arrived.append(lax.ppermute(piece, 'blk', pairs))  7.01 us
    ppermute x1, waiting for transfers between devices, on_device(): along_y = lax.ppermute(mine, 'rows', xor_pairs(owners_n, by))  5.41 us
    ppermute x3, waiting for transfers between devices, on_device(): arrived.append(lax.ppermute(piece, 'blk', pairs))  2.8 us
    dot_general x10, matrix products, term(): jnp.einsum('rsk,rtk->st', part, tests, preferred_element_type=jnp.float32)  2.24 us
    dot_general x1, matrix products, on_device(): jnp.einsum('rsk,rtk->st', features, test_blocks, preferred_element_type=j...  1.96 us
    ppermute x1, starting transfers between devices, on_device(): along_y = lax.ppermute(mine, 'rows', xor_pairs(owners_n, by))  1.58 us
    ppermute x1, starting transfers between devices, on_device(): second = lax.ppermute(along_x[:, :, half:], 'rows', xor_pairs(owners_n, by))  1.58 us
  transfers between devices with their start and end apart: 12, of which 5 were waited for; matrix products, arithmetic and copies ran while one was open for 11% of the time, Pallas kernels for 0%

profile of v10, /device:TPU:0, one launch (start us, length us, event | category | flops | bytes accessed | tf_op | source)
XLA Modules:
  0.0 40.9 jit_solution(12867095894787320318)
XLA Ops:
  0.0 0.0 copy-start
  0.0 0.0 copy-start.1
  0.0 1.4 %select_select_fusion = bf16[4,48,256]{2,1,0:T(8,128)(2,1)S(1)} fusion(bf16[4,48,2048]{2,1,0:T(8,128)(2,1)} %param.5, pred[]{:T(512)S(6)} %eq.55, pred[]{:T(512)S(6)} %eq.54, pred[]{:T(512)S(6)} %eq.53, pred[]{:T(512)S(6)} %eq.52, pred[]{:T(512)S(6)} %eq.51, pred[]{:T(512)S(6)} %eq.50, pred[]{:T(512)S(6)} %eq.49), kind=kLoop, calls=%fused_computation.42 | loop fusion | flops 344064 | bytes 884743 | tf_op jit(solution)/shard_map/jit(_where)/select_n | solution.py:37
  1.4 3.1 %collective-permute-start.2 = (bf16[4,48,256]{2,1,0:T(8,128)(2,1)S(1)}, bf16[4,48,256]{2,1,0:T(8,128)(2,1)S(1)}, u32[]{:S(2)}, u32[]{:S(2)}) collective-permute-start(bf16[4,48,256]{2,1,0:T(8,128)(2,1)S(1)} %select_select_fusion), channel_id=1, source_target_pairs={{0,8},{8,16},{16,24},{24,0},{1,9},{9,17},{17,25},{25,1},{2,10},{10... | collective-permute-start | bytes 294920 | tf_op jit(solution)/shard_map/ppermute | solution.py:41
  4.5 2.6 %collective-permute-start.1 = (bf16[4,48,256]{2,1,0:T(8,128)(2,1)S(1)}, bf16[4,48,256]{2,1,0:T(8,128)(2,1)S(1)}, u32[]{:S(2)}, u32[]{:S(2)}) collective-permute-start(bf16[4,48,256]{2,1,0:T(8,128)(2,1)S(1)} %select_select_fusion), channel_id=1, source_target_pairs={{0,16},{8,24},{16,0},{24,8},{1,17},{9,25},{17,1},{25,9},{2,18},{10... | collective-permute-start | bytes 294920 | tf_op jit(solution)/shard_map/ppermute | solution.py:41
  7.1 1.3 %collective-permute-start = (bf16[4,48,256]{2,1,0:T(8,128)(2,1)S(1)}, bf16[4,48,256]{2,1,0:T(8,128)(2,1)S(1)}, u32[]{:S(2)}, u32[]{:S(2)}) collective-permute-start(bf16[4,48,256]{2,1,0:T(8,128)(2,1)S(1)} %select_select_fusion), channel_id=1, source_target_pairs={{0,24},{8,0},{16,8},{24,16},{1,25},{9,1},{17,9},{25,17},{2,26},{10... | collective-permute-start | bytes 294920 | tf_op jit(solution)/shard_map/ppermute | solution.py:41
  8.4 0.0 copy-done
  8.4 2.0 %convolution_bitcast_fusion.10 = bf16[128,48]{0,1:T(8,128)(2,1)S(1)} fusion(bf16[4,128,2048]{2,1,0:T(8,128)(2,1)S(1)} %copy-done, bf16[4,48,2048]{2,1,0:T(8,128)(2,1)} %param.5), kind=kOutput, calls=%fused_computation.20 | convolution fusion | flops 100663296 | bytes 2895872 | tf_op jit(solution)/shard_map/rsk,rtk->st/dot_general | solution.py:43
  10.4 0.0 copy-done.1
  10.4 0.1 fusion.25
  10.5 0.2 reduce_window_sum.11
  10.7 0.2 select_reduce_fusion
  10.9 0.0 collective-permute-done.2
  10.9 2.8 %collective-permute-done.1 = bf16[4,48,256]{2,1,0:T(8,128)(2,1)S(1)} collective-permute-done((bf16[4,48,256]{2,1,0:T(8,128)(2,1)S(1)}, bf16[4,48,256]{2,1,0:T(8,128)(2,1)S(1)}, u32[]{:S(2)}, u32[]{:S(2)}) %collective-permute-start.1) | collective-permute-done | bytes 98336 | tf_op jit(solution)/shard_map/ppermute | solution.py:41
  13.7 0.0 collective-permute-done
  13.7 1.6 %collective-permute-start.4 = (bf16[4,144,256]{2,1,0:T(8,128)(2,1)S(1)}, bf16[4,144,256]{2,1,0:T(8,128)(2,1)S(1)}, u32[]{:S(2)}, u32[]{:S(2)}) collective-permute-start(bf16[4,144,256]{2,1,0:T(8,128)(2,1)S(1)} %pad_maximum_fusion), channel_id=1, source_target_pairs={{0,4},{1,5},{2,6},{3,7},{4,0},{5,1},{6,2},{7,3},{8,12},{9,13},{10,... | collective-permute-start | bytes 884744 | tf_op jit(solution)/shard_map/ppermute | solution.py:51
  15.3 1.5 %collective-permute-start.3 = (bf16[4,144,256]{2,1,0:T(8,128)(2,1)S(1)}, bf16[4,144,256]{2,1,0:T(8,128)(2,1)S(1)}, u32[]{:S(2)}, u32[]{:S(2)}) collective-permute-start(bf16[4,144,256]{2,1,0:T(8,128)(2,1)S(1)} %pad_maximum_fusion), channel_id=1, source_target_pairs={{0,2},{1,3},{2,0},{3,1},{4,6},{5,7},{6,4},{7,5},{8,10},{9,11},{10,... | collective-permute-start | bytes 884744 | tf_op jit(solution)/shard_map/ppermute | solution.py:50
  16.8 0.0 collective-permute-start.7
  16.8 0.1 copy.6
  16.9 0.3 convolution_bitcast_fusion.5
  17.2 5.4 %collective-permute-done.4 = bf16[4,144,256]{2,1,0:T(8,128)(2,1)S(1)} collective-permute-done((bf16[4,144,256]{2,1,0:T(8,128)(2,1)S(1)}, bf16[4,144,256]{2,1,0:T(8,128)(2,1)S(1)}, u32[]{:S(2)}, u32[]{:S(2)}) %collective-permute-start.4) | collective-permute-done | bytes 294944 | tf_op jit(solution)/shard_map/ppermute | solution.py:51
  22.6 1.6 %collective-permute-start.5 = (bf16[4,144,128]{2,1,0:T(8,128)(2,1)S(1)}, bf16[4,144,128]{2,1,0:T(8,128)(2,1)S(1)}, u32[]{:S(2)}, u32[]{:S(2)}) collective-permute-start(bf16[4,144,128]{2,1,0:T(8,128)(2,1)S(1)} %slice.40), channel_id=1, source_target_pairs={{0,2},{1,3},{2,0},{3,1},{4,6},{5,7},{6,4},{7,5},{8,10},{9,11},{10,... | collective-permute-start | bytes 442376 | tf_op jit(solution)/shard_map/ppermute | solution.py:55
  24.2 0.0 collective-permute-done.3
  24.2 1.6 %collective-permute-start.6 = (bf16[4,144,128]{2,1,0:T(8,128)(2,1)S(1)}, bf16[4,144,128]{2,1,0:T(8,128)(2,1)S(1)}, u32[]{:S(2)}, u32[]{:S(2)}) collective-permute-start(bf16[4,144,128]{2,1,0:T(8,128)(2,1)S(1)} %slice.41), channel_id=1, source_target_pairs={{0,4},{1,5},{2,6},{3,7},{4,0},{5,1},{6,2},{7,3},{8,12},{9,13},{10,... | collective-permute-start | bytes 442376 | tf_op jit(solution)/shard_map/ppermute | solution.py:56
  25.8 0.0 collective-permute-start.9
  25.8 0.5 %collective-permute-start.8 = (bf16[4,144,256]{2,1,0:T(8,128)(2,1)S(1)}, bf16[4,144,256]{2,1,0:T(8,128)(2,1)S(1)}, u32[]{:S(2)}, u32[]{:S(2)}) collective-permute-start(bf16[4,144,256]{2,1,0:T(8,128)(2,1)S(1)} %collective-permute-done.3), channel_id=1, source_target_pairs={{0,1},{1,0},{2,3},{3,2},{4,5},{5,4},{6,7},{7,6},{8,9},{9,8},{10,11... | collective-permute-start | bytes 884744 | tf_op jit(solution)/shard_map/ppermute | solution.py:61
  26.3 0.2 convolution_bitcast_fusion.3
  26.6 0.0 collective-permute-done.7
  26.6 0.2 convolution_bitcast_fusion.2
  26.8 1.0 %collective-permute-done.5 = bf16[4,144,128]{2,1,0:T(8,128)(2,1)S(1)} collective-permute-done((bf16[4,144,128]{2,1,0:T(8,128)(2,1)S(1)}, bf16[4,144,128]{2,1,0:T(8,128)(2,1)S(1)}, u32[]{:S(2)}, u32[]{:S(2)}) %collective-permute-start.5) | collective-permute-done | bytes 147488 | tf_op jit(solution)/shard_map/ppermute | solution.py:55
  27.8 0.0 collective-permute-start.10
  27.8 0.2 convolution_bitcast_fusion.9
  28.0 1.4 %collective-permute-done.6 = bf16[4,144,128]{2,1,0:T(8,128)(2,1)S(1)} collective-permute-done((bf16[4,144,128]{2,1,0:T(8,128)(2,1)S(1)}, bf16[4,144,128]{2,1,0:T(8,128)(2,1)S(1)}, u32[]{:S(2)}, u32[]{:S(2)}) %collective-permute-start.6) | collective-permute-done | bytes 147488 | tf_op jit(solution)/shard_map/ppermute | solution.py:56
  29.4 0.0 collective-permute-start.11
  29.4 0.2 convolution_bitcast_fusion.8
  29.6 0.2 fusion.4
  29.9 0.0 collective-permute-done.10
  29.9 0.2 convolution_bitcast_fusion.7
  30.1 0.7 %collective-permute-done.11 = bf16[4,144,128]{2,1,0:T(8,128)(2,1)S(1)} collective-permute-done((bf16[4,144,128]{2,1,0:T(8,128)(2,1)S(1)}, bf16[4,144,128]{2,1,0:T(8,128)(2,1)S(1)}, u32[]{:S(2)}, u32[]{:S(2)}) %collective-permute-start.11) | collective-permute-done | bytes 147488 | tf_op jit(solution)/shard_map/ppermute | solution.py:64
  30.8 0.2 convolution_bitcast_fusion.6
  31.0 0.0 collective-permute-done.9
  31.0 0.2 convolution_bitcast_fusion
  31.2 0.0 collective-permute-done.8
  31.3 0.3 fusion.8
  31.5 0.4 convolution_convert_fusion
  31.9 0.1 copy.8
  32.0 8.1 %all_to_all.12 = bf16[8,32,192]{2,1,0:T(8,128)(2,1)S(1)} all-to-all(bf16[8,32,192]{2,1,0:T(8,128)(2,1)S(1)} %bitcast.57), channel_id=1, replica_groups=mesh['blk'=4,'rows'=8] {'rows'}, dimensions={0} | all-to-all | bytes 196608 | tf_op jit(solution)/shard_map/all_to_all | solution.py:86
  40.1 0.7 %copy.9 = bf16[256,192]{0,1:T(8,128)(2,1)} copy(bf16[256,192]{1,0:T(8,128)(2,1)S(1)} %bitcast.58) | data formatting | bytes 196608 | tf_op jit(solution)/shard_map/all_to_all | solution.py:86
  (5 shorter events, 0.1 us)
Async XLA Ops:
  0.0 8.4 %copy-start = (bf16[4,128,2048]{2,1,0:T(8,128)(2,1)S(1)}, bf16[4,128,2048]{2,1,0:T(8,128)(2,1)}, u32[]{:S(2)}) copy-start(bf16[4,128,2048]{2,1,0:T(8,128)(2,1)} %param.3) | copy-start | bytes 6291460
  0.0 10.4 %copy-start.1 = (s32[128,1]{0,1:T(1,128)S(1)}, s32[128,1]{0,1:T(1,128)}, u32[]{:S(2)}) copy-start(s32[128,1]{0,1:T(1,128)} %param.4) | copy-start | bytes 1540
  1.4 9.5 %collective-permute-start.2 = (bf16[4,48,256]{2,1,0:T(8,128)(2,1)S(1)}, bf16[4,48,256]{2,1,0:T(8,128)(2,1)S(1)}, u32[]{:S(2)}, u32[]{:S(2)}) collective-permute-start(bf16[4,48,256]{2,1,0:T(8,128)(2,1)S(1)} %select_select_fusion), channel_id=1, source_target_pairs={{0,8},{8,16},{16,24},{24,0},{1,9},{9,17},{17,25},{25,1},{2,10},{10... | collective-permute-start | bytes 294920 | tf_op jit(solution)/shard_map/ppermute | solution.py:41
  4.5 9.2 %collective-permute-start.1 = (bf16[4,48,256]{2,1,0:T(8,128)(2,1)S(1)}, bf16[4,48,256]{2,1,0:T(8,128)(2,1)S(1)}, u32[]{:S(2)}, u32[]{:S(2)}) collective-permute-start(bf16[4,48,256]{2,1,0:T(8,128)(2,1)S(1)} %select_select_fusion), channel_id=1, source_target_pairs={{0,16},{8,24},{16,0},{24,8},{1,17},{9,25},{17,1},{25,9},{2,18},{10... | collective-permute-start | bytes 294920 | tf_op jit(solution)/shard_map/ppermute | solution.py:41
  7.1 6.6 %collective-permute-start = (bf16[4,48,256]{2,1,0:T(8,128)(2,1)S(1)}, bf16[4,48,256]{2,1,0:T(8,128)(2,1)S(1)}, u32[]{:S(2)}, u32[]{:S(2)}) collective-permute-start(bf16[4,48,256]{2,1,0:T(8,128)(2,1)S(1)} %select_select_fusion), channel_id=1, source_target_pairs={{0,24},{8,0},{16,8},{24,16},{1,25},{9,1},{17,9},{25,17},{2,26},{10... | collective-permute-start | bytes 294920 | tf_op jit(solution)/shard_map/ppermute | solution.py:41
  13.7 8.9 %collective-permute-start.4 = (bf16[4,144,256]{2,1,0:T(8,128)(2,1)S(1)}, bf16[4,144,256]{2,1,0:T(8,128)(2,1)S(1)}, u32[]{:S(2)}, u32[]{:S(2)}) collective-permute-start(bf16[4,144,256]{2,1,0:T(8,128)(2,1)S(1)} %pad_maximum_fusion), channel_id=1, source_target_pairs={{0,4},{1,5},{2,6},{3,7},{4,0},{5,1},{6,2},{7,3},{8,12},{9,13},{10,... | collective-permute-start | bytes 884744 | tf_op jit(solution)/shard_map/ppermute | solution.py:51
  15.3 8.9 %collective-permute-start.3 = (bf16[4,144,256]{2,1,0:T(8,128)(2,1)S(1)}, bf16[4,144,256]{2,1,0:T(8,128)(2,1)S(1)}, u32[]{:S(2)}, u32[]{:S(2)}) collective-permute-start(bf16[4,144,256]{2,1,0:T(8,128)(2,1)S(1)} %pad_maximum_fusion), channel_id=1, source_target_pairs={{0,2},{1,3},{2,0},{3,1},{4,6},{5,7},{6,4},{7,5},{8,10},{9,11},{10,... | collective-permute-start | bytes 884744 | tf_op jit(solution)/shard_map/ppermute | solution.py:50
  16.8 9.7 %collective-permute-start.7 = (bf16[4,144,256]{2,1,0:T(8,128)(2,1)S(1)}, bf16[4,144,256]{2,1,0:T(8,128)(2,1)S(1)}, u32[]{:S(2)}, u32[]{:S(2)}) collective-permute-start(bf16[4,144,256]{2,1,0:T(8,128)(2,1)S(1)} %pad_maximum_fusion), channel_id=1, source_target_pairs={{0,1},{1,0},{2,3},{3,2},{4,5},{5,4},{6,7},{7,6},{8,9},{9,8},{10,11... | collective-permute-start | bytes 884744 | tf_op jit(solution)/shard_map/ppermute | solution.py:61
  22.6 5.2 %collective-permute-start.5 = (bf16[4,144,128]{2,1,0:T(8,128)(2,1)S(1)}, bf16[4,144,128]{2,1,0:T(8,128)(2,1)S(1)}, u32[]{:S(2)}, u32[]{:S(2)}) collective-permute-start(bf16[4,144,128]{2,1,0:T(8,128)(2,1)S(1)} %slice.40), channel_id=1, source_target_pairs={{0,2},{1,3},{2,0},{3,1},{4,6},{5,7},{6,4},{7,5},{8,10},{9,11},{10,... | collective-permute-start | bytes 442376 | tf_op jit(solution)/shard_map/ppermute | solution.py:55
  24.2 5.2 %collective-permute-start.6 = (bf16[4,144,128]{2,1,0:T(8,128)(2,1)S(1)}, bf16[4,144,128]{2,1,0:T(8,128)(2,1)S(1)}, u32[]{:S(2)}, u32[]{:S(2)}) collective-permute-start(bf16[4,144,128]{2,1,0:T(8,128)(2,1)S(1)} %slice.41), channel_id=1, source_target_pairs={{0,4},{1,5},{2,6},{3,7},{4,0},{5,1},{6,2},{7,3},{8,12},{9,13},{10,... | collective-permute-start | bytes 442376 | tf_op jit(solution)/shard_map/ppermute | solution.py:56
  25.8 5.2 %collective-permute-start.9 = (bf16[4,144,256]{2,1,0:T(8,128)(2,1)S(1)}, bf16[4,144,256]{2,1,0:T(8,128)(2,1)S(1)}, u32[]{:S(2)}, u32[]{:S(2)}) collective-permute-start(bf16[4,144,256]{2,1,0:T(8,128)(2,1)S(1)} %collective-permute-done.4), channel_id=1, source_target_pairs={{0,1},{1,0},{2,3},{3,2},{4,5},{5,4},{6,7},{7,6},{8,9},{9,8},{10,11... | collective-permute-start | bytes 884744 | tf_op jit(solution)/shard_map/ppermute | solution.py:61
  25.8 5.4 %collective-permute-start.8 = (bf16[4,144,256]{2,1,0:T(8,128)(2,1)S(1)}, bf16[4,144,256]{2,1,0:T(8,128)(2,1)S(1)}, u32[]{:S(2)}, u32[]{:S(2)}) collective-permute-start(bf16[4,144,256]{2,1,0:T(8,128)(2,1)S(1)} %collective-permute-done.3), channel_id=1, source_target_pairs={{0,1},{1,0},{2,3},{3,2},{4,5},{5,4},{6,7},{7,6},{8,9},{9,8},{10,11... | collective-permute-start | bytes 884744 | tf_op jit(solution)/shard_map/ppermute | solution.py:61
  27.8 2.0 %collective-permute-start.10 = (bf16[4,144,128]{2,1,0:T(8,128)(2,1)S(1)}, bf16[4,144,128]{2,1,0:T(8,128)(2,1)S(1)}, u32[]{:S(2)}, u32[]{:S(2)}) collective-permute-start(bf16[4,144,128]{2,1,0:T(8,128)(2,1)S(1)} %collective-permute-done.5), channel_id=1, source_target_pairs={{0,1},{1,0},{2,3},{3,2},{4,5},{5,4},{6,7},{7,6},{8,9},{9,8},{10,11... | collective-permute-start | bytes 442376 | tf_op jit(solution)/shard_map/ppermute | solution.py:63
  29.4 1.4 %collective-permute-start.11 = (bf16[4,144,128]{2,1,0:T(8,128)(2,1)S(1)}, bf16[4,144,128]{2,1,0:T(8,128)(2,1)S(1)}, u32[]{:S(2)}, u32[]{:S(2)}) collective-permute-start(bf16[4,144,128]{2,1,0:T(8,128)(2,1)S(1)} %collective-permute-done.6), channel_id=1, source_target_pairs={{0,1},{1,0},{2,3},{3,2},{4,5},{5,4},{6,7},{7,6},{8,9},{9,8},{10,11... | collective-permute-start | bytes 442376 | tf_op jit(solution)/shard_map/ppermute | solution.py:64

commit v11 on v7

--- a/solution.py
+++ b/solution.py
@@ -21,6 +21,7 @@
 def on_device(features, owner_ids, test_blocks):
     owners_n = lax.axis_size("rows")
     blocks_n = lax.axis_size("blk")
+    runs = features.shape[0]
     local_rows = features.shape[1]
     width = test_blocks.shape[1]
     capacity = 2 * local_rows // owners_n
@@ -32,7 +33,17 @@
         part = lax.dynamic_slice_in_dim(features, offset, size, axis=2)
         return jnp.einsum("rsk,rtk->st", part, tests, preferred_element_type=jnp.float32)
 
-    piece = lax.dynamic_slice_in_dim(test_blocks, here * chunk, chunk, axis=2)
+    chip_bits = [1 << i for i in range(1, owners_n.bit_length() - 1)]
+    split_runs = len(chip_bits) == 2 and runs % 2 == 0
+    if split_runs:
+        span = runs // 2
+        quarter = features.shape[2] // (owners_n // 2)
+        core = here % 2
+        chip = here // 2
+        piece = lax.dynamic_slice(test_blocks, (core * span, 0, chip * quarter), (span, width, quarter))
+        lent = lax.dynamic_slice_in_dim(features, (1 - core) * span, span, axis=0)
+    else:
+        piece = lax.dynamic_slice_in_dim(test_blocks, here * chunk, chunk, axis=2)
     arrived = []
     for step in range(1, blocks_n):
         pairs = [(b, (b - step) % blocks_n) for b in range(blocks_n)]
@@ -40,36 +51,37 @@
     mine = jnp.concatenate(arrived, axis=1)
     own = jnp.einsum("rsk,rtk->st", features, test_blocks, preferred_element_type=jnp.float32)
     slotting = slot_matrix(owner_ids, owners_n, capacity)
-    mine, own, slotting = lax.optimization_barrier((mine, own, slotting))
-    remote = term(here * chunk, chunk, mine)
-    chip_bits = [1 << i for i in range(1, owners_n.bit_length() - 1)]
-    if len(chip_bits) == 2:
+    if split_runs:
         bx, by = chip_bits
+        lent = lax.ppermute(lent, "rows", xor_pairs(owners_n, 1))
+        mine, own, slotting = lax.optimization_barrier((mine, own, slotting))
+        rows_all = jnp.concatenate([lax.dynamic_slice_in_dim(features, core * span, span, axis=0), lent], axis=1)
+
+        def pair_term(chip_of, tests, lo=0, size=quarter):
+            part = lax.dynamic_slice_in_dim(rows_all, chip_of * quarter + lo, size, axis=2)
+            return jnp.einsum("rsk,rtk->st", part, tests, preferred_element_type=jnp.float32)
+
         along_x = lax.ppermute(mine, "rows", xor_pairs(owners_n, bx))
         along_y = lax.ppermute(mine, "rows", xor_pairs(owners_n, by))
-        remote = remote + term((here ^ bx) * chunk, chunk, along_x)
-        remote = remote + term((here ^ by) * chunk, chunk, along_y)
-        half = chunk // 2
+        half = quarter // 2
         first = lax.ppermute(along_y[:, :, :half], "rows", xor_pairs(owners_n, bx))
         second = lax.ppermute(along_x[:, :, half:], "rows", xor_pairs(owners_n, by))
-        corner = (here ^ bx ^ by) * chunk
-        remote = remote + term(corner, half, first) + term(corner + half, half, second)
-        diagonal = jnp.concatenate([first, second], axis=2)
-        held = jnp.stack([mine, along_x, along_y, diagonal])
-        masks = [0, bx, by, bx ^ by]
+        paired = pair_term(chip, mine) + pair_term(chip ^ (bx // 2), along_x) + pair_term(chip ^ (by // 2), along_y)
+        corner = chip ^ ((bx ^ by) // 2)
+        paired = paired + pair_term(corner, first, 0, half) + pair_term(corner, second, half, half)
+        returned = lax.ppermute(paired[local_rows:], "rows", xor_pairs(owners_n, 1))
+        remote = paired[:local_rows] + returned
     else:
+        mine, own, slotting = lax.optimization_barrier((mine, own, slotting))
+        remote = term(here * chunk, chunk, mine)
         held = mine[None]
         masks = [0]
-        for mask in chip_bits:
+        for mask in chip_bits + [1]:
             got = lax.ppermute(held, "rows", xor_pairs(owners_n, mask))
             for j, m in enumerate(masks):
                 remote = remote + term((here ^ mask ^ m) * chunk, chunk, got[j])
             held = jnp.concatenate([held, got], axis=0)
             masks = masks + [m ^ mask for m in masks]
-    if owners_n > 1:
-        got = lax.ppermute(held, "rows", xor_pairs(owners_n, 1))
-        for j, m in enumerate(masks):
-            remote = remote + term((here ^ 1 ^ m) * chunk, chunk, got[j])
     relative = jnp.concatenate([own, remote], axis=1)
     doubled = jnp.concatenate([relative, relative], axis=1)
     start = ((blocks_n - block) % blocks_n) * width

time: 48.2 us -> 42.9 us (0.89)
  waiting for transfers between devices: 14.4 us -> 10.5 us
  local copies, waits for them, and re-layouts: 2.07 us -> 5.65 us
  matrix products: 8.33 us -> 5.28 us
  other arithmetic: 1.68 us -> 0.48 us
  starting transfers between devices: 13.2 us -> 12.4 us
    dot_general x9 -> x5, matrix products: 6 us -> 2.41 us  [pair_term(): jnp.einsum('rsk,rtk->st', part, tests, preferred_element_type=jnp.float32)]
    ppermute x1, waiting for transfers between devices: 2.03 us -> 0.01 us  [on_device(): first = lax.ppermute(along_y[:, :, :half], 'rows', xor_pairs(owners_n, bx))]
    dynamic_slice x1 -> x2, local copies, waits for them, and re-layouts: 1.05 us -> 2.72 us  [the longest x1 2.72 us: on_device(): lent = lax.dynamic_slice_in_dim(features, (1 - core) * span, span, axis=0)]
    another operation x2 -> x0, other arithmetic: 1.2 us -> none  [on_device(): held = jnp.stack([mine, along_x, along_y, diagonal])]
    unnamed x4, local copies, waits for them, and re-layouts: 0.01 us -> 1.14 us
    ppermute x1 -> x2, waiting for transfers between devices: 2.15 us -> 1.24 us  [the longest x1 1.23 us: on_device(): returned = lax.ppermute(paired[local_rows:], 'rows', xor_pairs(owners_n, 1))]
    slice x1, local copies, waits for them, and re-layouts: 0.03 us -> 0.92 us  [on_device(): second = lax.ppermute(along_x[:, :, half:], 'rows', xor_pairs(owners_n, by))]
    ppermute x3, starting transfers between devices: 6.96 us -> 6.11 us  [on_device(): arrived.append(lax.ppermute(piece, 'blk', pairs))]
  transfers between devices with their start and end apart: 8 -> 9, of which waited for: 5 -> 4; matrix products, arithmetic and copies ran while one was open for 7% -> 20% of each run, Pallas kernels for 0% -> 0%
where the time goes in v11:
time: 42.9 us; the launch traced here: 42.6 us
  starting transfers between devices  12.4 us (29%)
  waiting for transfers between devices  10.5 us (24%)
  blocking collectives  8.13 us (19%)
  local copies, waits for them, and re-layouts  5.65 us (13%)
  matrix products  5.28 us (12%)
  other arithmetic  0.48 us (1%)
    all_to_all x1, blocking collectives, on_device(): lax.all_to_all(placed, 'rows', split_axis=0, concat_axis=0, tiled=True)  8.13 us
    ppermute x3, starting transfers between devices, on_device(): arrived.append(lax.ppermute(piece, 'blk', pairs))  6.11 us
    ppermute x1, waiting for transfers between devices, on_device(): along_y = lax.ppermute(mine, 'rows', xor_pairs(owners_n, by))  5.43 us
    dynamic_slice x1, local copies, waits for them, and re-layouts, on_device(): lent = lax.dynamic_slice_in_dim(features, (1 - core) * span, span, axis=0)  2.72 us
    dot_general x1, matrix products, on_device(): jnp.einsum('rsk,rtk->st', features, test_blocks, preferred_element_type=j...  2.42 us
    dot_general x5, matrix products, pair_term(): jnp.einsum('rsk,rtk->st', part, tests, preferred_element_type=jnp.float32)  2.41 us
    ppermute x3, waiting for transfers between devices, on_device(): arrived.append(lax.ppermute(piece, 'blk', pairs))  2.09 us
    ppermute x1, waiting for transfers between devices, on_device(): second = lax.ppermute(along_x[:, :, half:], 'rows', xor_pairs(owners_n, by))  1.75 us
  transfers between devices with their start and end apart: 9, of which 4 were waited for; matrix products, arithmetic and copies ran while one was open for 20% of the time, Pallas kernels for 0%

profile of v11, /device:TPU:0, one launch (start us, length us, event | category | flops | bytes accessed | tf_op | source)
XLA Modules:
  0.0 42.6 jit_solution(6693749163892897778)
XLA Ops:
  0.0 0.0 copy-start
  0.0 1.1 %copy-done = bf16[4,48,2048]{2,1,0:T(8,128)(2,1)S(1)} copy-done((bf16[4,48,2048]{2,1,0:T(8,128)(2,1)S(1)}, bf16[4,48,2048]{2,1,0:T(8,128)(2,1)}, u32[]{:S(2)}) %copy-start) | copy-done | bytes 786456
  1.1 5.1 %collective-permute-start = (bf16[2,48,512]{2,1,0:T(8,128)(2,1)S(1)}, bf16[2,48,512]{2,1,0:T(8,128)(2,1)S(1)}, u32[]{:S(2)}, u32[]{:S(2)}) collective-permute-start(bf16[2,48,512]{2,1,0:T(8,128)(2,1)S(1)} %constant_dynamic-slice_fusion.2), channel_id=1, source_target_pairs={{0,24},{8,0},{16,8},{24,16},{1,25},{9,1},{17,9},{25,17},{2,26},{10... | collective-permute-start | bytes 294920 | tf_op jit(solution)/shard_map/ppermute | solution.py:50
  6.2 0.0 collective-permute-start.1
  6.2 1.0 %collective-permute-start.2 = (bf16[2,48,512]{2,1,0:T(8,128)(2,1)S(1)}, bf16[2,48,512]{2,1,0:T(8,128)(2,1)S(1)}, u32[]{:S(2)}, u32[]{:S(2)}) collective-permute-start(bf16[2,48,512]{2,1,0:T(8,128)(2,1)S(1)} %constant_dynamic-slice_fusion.2), channel_id=1, source_target_pairs={{0,8},{8,16},{16,24},{24,0},{1,9},{9,17},{17,25},{25,1},{2,10},{10... | collective-permute-start | bytes 294920 | tf_op jit(solution)/shard_map/ppermute | solution.py:50
  7.3 0.0 copy-start.1
  7.3 2.7 %constant_dynamic-slice_fusion = (bf16[2,128,2048]{2,1,0:T(8,128)(2,1)}, bf16[2,128,2048]{2,1,0:T(8,128)(2,1)S(1)}) fusion(bf16[4,128,2048]{2,1,0:T(8,128)(2,1)} %param.3, s32[]{:T(128)S(6)} %select_n.45, s32[]{:T(128)S(6)} %select_n.42), kind=kLoop, calls=%fused_computation.46 | loop fusion | bytes 4194312 | tf_op jit(solution)/shard_map/dynamic_slice | solution.py:44
  10.0 0.0 collective-permute-start.3
  10.0 0.0 copy-done.1
  10.0 0.1 fusion.19
  10.1 0.2 reduce_window_sum.11
  10.2 0.2 select_reduce_fusion
  10.4 2.4 %convolution_bitcast_fusion.5 = bf16[128,48]{0,1:T(8,128)(2,1)S(1)} fusion(bf16[4,128,2048]{2,1,0:T(8,128)(2,1)} %param.3, bf16[4,48,2048]{2,1,0:T(8,128)(2,1)S(1)} %copy-done), kind=kOutput, calls=%fused_computation.20 | convolution fusion | flops 100663296 | bytes 2895872 | tf_op jit(solution)/shard_map/rsk,rtk->st/dot_general | solution.py:52
  12.9 0.0 collective-permute-done
  12.9 2.1 %collective-permute-done.1 = bf16[2,48,512]{2,1,0:T(8,128)(2,1)S(1)} collective-permute-done((bf16[2,48,512]{2,1,0:T(8,128)(2,1)S(1)}, bf16[2,48,512]{2,1,0:T(8,128)(2,1)S(1)}, u32[]{:S(2)}, u32[]{:S(2)}) %collective-permute-start.1) | collective-permute-done | bytes 98336 | tf_op jit(solution)/shard_map/ppermute | solution.py:50
  15.0 0.0 collective-permute-done.2
  15.0 1.6 %collective-permute-start.5 = (bf16[2,144,512]{2,1,0:T(8,128)(2,1)S(1)}, bf16[2,144,512]{2,1,0:T(8,128)(2,1)S(1)}, u32[]{:S(2)}, u32[]{:S(2)}) collective-permute-start(bf16[2,144,512]{2,1,0:T(8,128)(2,1)S(1)} %pad_maximum_fusion), channel_id=1, source_target_pairs={{0,4},{1,5},{2,6},{3,7},{4,0},{5,1},{6,2},{7,3},{8,12},{9,13},{10,... | collective-permute-start | bytes 884744 | tf_op jit(solution)/shard_map/ppermute | solution.py:65
  16.6 1.5 %collective-permute-start.4 = (bf16[2,144,512]{2,1,0:T(8,128)(2,1)S(1)}, bf16[2,144,512]{2,1,0:T(8,128)(2,1)}, u32[]{:S(2)}, u32[]{:S(2)}) collective-permute-start(bf16[2,144,512]{2,1,0:T(8,128)(2,1)S(1)} %pad_maximum_fusion), channel_id=1, source_target_pairs={{0,2},{1,3},{2,0},{3,1},{4,6},{5,7},{6,4},{7,5},{8,10},{9,11},{10,... | collective-permute-start | bytes 884744 | tf_op jit(solution)/shard_map/ppermute | solution.py:64
  18.1 5.4 %collective-permute-done.5 = bf16[2,144,512]{2,1,0:T(8,128)(2,1)S(1)} collective-permute-done((bf16[2,144,512]{2,1,0:T(8,128)(2,1)S(1)}, bf16[2,144,512]{2,1,0:T(8,128)(2,1)S(1)}, u32[]{:S(2)}, u32[]{:S(2)}) %collective-permute-start.5) | collective-permute-done | bytes 294944 | tf_op jit(solution)/shard_map/ppermute | solution.py:65
  23.5 1.6 %collective-permute-start.6 = (bf16[2,144,256]{2,1,0:T(8,128)(2,1)S(1)}, bf16[2,144,256]{2,1,0:T(8,128)(2,1)S(1)}, u32[]{:S(2)}, u32[]{:S(2)}) collective-permute-start(bf16[2,144,256]{2,1,0:T(8,128)(2,1)S(1)} %slice.16), channel_id=1, source_target_pairs={{0,2},{1,3},{2,0},{3,1},{4,6},{5,7},{6,4},{7,5},{8,10},{9,11},{10,... | collective-permute-start | bytes 442376 | tf_op jit(solution)/shard_map/ppermute | solution.py:67
  25.1 0.0 collective-permute-done.4
  25.1 0.9 %slice.17 = bf16[2,144,256]{2,1,0:T(8,128)(2,1)S(1)} slice(bf16[2,144,512]{2,1,0:T(8,128)(2,1)} %collective-permute-done.4), slice={[0:2], [0:144], [256:512]} | slice | bytes 294912 | tf_op jit(solution)/shard_map/slice | solution.py:68
  26.0 1.6 %collective-permute-start.7 = (bf16[2,144,256]{2,1,0:T(8,128)(2,1)S(1)}, bf16[2,144,256]{2,1,0:T(8,128)(2,1)S(1)}, u32[]{:S(2)}, u32[]{:S(2)}) collective-permute-start(bf16[2,144,256]{2,1,0:T(8,128)(2,1)S(1)} %slice.17), channel_id=1, source_target_pairs={{0,4},{1,5},{2,6},{3,7},{4,0},{5,1},{6,2},{7,3},{8,12},{9,13},{10,... | collective-permute-start | bytes 442376 | tf_op jit(solution)/shard_map/ppermute | solution.py:68
  27.6 0.0 collective-permute-done.3
  27.6 1.3 %convolution_bitcast_fusion.3 = f32[256,144]{0,1:T(8,128)S(1)} fusion(bf16[2,144,512]{2,1,0:T(8,128)(2,1)} %collective-permute-done.4, s32[]{:T(128)S(6)} %select_n.46, bf16[2,128,2048]{2,1,0:T(8,128)(2,1)S(1)} %get-tuple-element.12, bf16[2,128,2048]{2,1,0:T(8,128)(2,1)S(1)} %collective-permute-done.3), kind=kOutput, calls=%fused_computation.13 | convolution fusion | flops 76546048 | bytes 2539524 | tf_op jit(solution)/shard_map/rsk,rtk->st/dot_general | solution.py:62
  28.9 0.3 convolution_bitcast_fusion.2
  29.2 0.0 collective-permute-done.6
  29.2 0.2 convolution_bitcast_fusion.1
  29.5 1.8 %collective-permute-done.7 = bf16[2,144,256]{2,1,0:T(8,128)(2,1)S(1)} collective-permute-done((bf16[2,144,256]{2,1,0:T(8,128)(2,1)S(1)}, bf16[2,144,256]{2,1,0:T(8,128)(2,1)S(1)}, u32[]{:S(2)}, u32[]{:S(2)}) %collective-permute-start.7) | collective-permute-done | bytes 147488 | tf_op jit(solution)/shard_map/ppermute | solution.py:68
  31.2 0.2 convolution_bitcast_fusion
  31.5 0.3 fusion.3
  31.8 0.1 collective-permute-start.8
  31.9 1.2 %collective-permute-done.8 = f32[128,144]{0,1:T(8,128)S(1)} collective-permute-done((f32[128,144]{0,1:T(8,128)S(1)}, f32[128,144]{0,1:T(8,128)S(1)}, u32[]{:S(2)}, u32[]{:S(2)}) %collective-permute-start.8) | collective-permute-done | bytes 73760 | tf_op jit(solution)/shard_map/ppermute | solution.py:72
  33.2 0.4 %convolution_convert_fusion = bf16[256,192]{0,1:T(8,128)(2,1)S(1)} fusion(bf16[256,128]{1,0:T(8,128)(2,1)S(1)} %fusion.14, s32[]{:T(128)S(6)} %select_n.51, bf16[128,48]{0,1:T(8,128)(2,1)S(1)} %convolution_bitcast_fusion.5, bf16[128,144]{0,1:T(8,128)(2,1)S(1)} %slice_add_fusion), kind=kOutput, calls=%fused_computation.15 | convolution fusion | flops 12828672 | bytes 212996 | tf_op jit(solution)/shard_map/dot_general | solution.py:90
  33.6 0.1 copy.4
  33.7 8.1 %all_to_all.12 = bf16[8,32,192]{2,1,0:T(8,128)(2,1)S(1)} all-to-all(bf16[8,32,192]{2,1,0:T(8,128)(2,1)S(1)} %bitcast.32), channel_id=1, replica_groups=mesh['blk'=4,'rows'=8] {'rows'}, dimensions={0} | all-to-all | bytes 196608 | tf_op jit(solution)/shard_map/all_to_all | solution.py:93
  41.9 0.7 %copy.5 = bf16[256,192]{0,1:T(8,128)(2,1)} copy(bf16[256,192]{1,0:T(8,128)(2,1)S(1)} %bitcast.33) | data formatting | bytes 196608 | tf_op jit(solution)/shard_map/all_to_all | solution.py:93
  (7 shorter events, 0.1 us)
Async XLA Ops:
  0.0 1.1 %copy-start = (bf16[4,48,2048]{2,1,0:T(8,128)(2,1)S(1)}, bf16[4,48,2048]{2,1,0:T(8,128)(2,1)}, u32[]{:S(2)}) copy-start(bf16[4,48,2048]{2,1,0:T(8,128)(2,1)} %param.5) | copy-start | bytes 2359300
  1.1 11.8 %collective-permute-start = (bf16[2,48,512]{2,1,0:T(8,128)(2,1)S(1)}, bf16[2,48,512]{2,1,0:T(8,128)(2,1)S(1)}, u32[]{:S(2)}, u32[]{:S(2)}) collective-permute-start(bf16[2,48,512]{2,1,0:T(8,128)(2,1)S(1)} %constant_dynamic-slice_fusion.2), channel_id=1, source_target_pairs={{0,24},{8,0},{16,8},{24,16},{1,25},{9,1},{17,9},{25,17},{2,26},{10... | collective-permute-start | bytes 294920 | tf_op jit(solution)/shard_map/ppermute | solution.py:50
  6.2 8.7 %collective-permute-start.1 = (bf16[2,48,512]{2,1,0:T(8,128)(2,1)S(1)}, bf16[2,48,512]{2,1,0:T(8,128)(2,1)S(1)}, u32[]{:S(2)}, u32[]{:S(2)}) collective-permute-start(bf16[2,48,512]{2,1,0:T(8,128)(2,1)S(1)} %constant_dynamic-slice_fusion.2), channel_id=1, source_target_pairs={{0,16},{8,24},{16,0},{24,8},{1,17},{9,25},{17,1},{25,9},{2,18},{10... | collective-permute-start | bytes 294920 | tf_op jit(solution)/shard_map/ppermute | solution.py:50
  6.2 8.7 %collective-permute-start.2 = (bf16[2,48,512]{2,1,0:T(8,128)(2,1)S(1)}, bf16[2,48,512]{2,1,0:T(8,128)(2,1)S(1)}, u32[]{:S(2)}, u32[]{:S(2)}) collective-permute-start(bf16[2,48,512]{2,1,0:T(8,128)(2,1)S(1)} %constant_dynamic-slice_fusion.2), channel_id=1, source_target_pairs={{0,8},{8,16},{16,24},{24,0},{1,9},{9,17},{17,25},{25,1},{2,10},{10... | collective-permute-start | bytes 294920 | tf_op jit(solution)/shard_map/ppermute | solution.py:50
  7.3 2.7 %copy-start.1 = (s32[128,1]{0,1:T(1,128)S(1)}, s32[128,1]{0,1:T(1,128)}, u32[]{:S(2)}) copy-start(s32[128,1]{0,1:T(1,128)} %param.4) | copy-start | bytes 1540
  10.0 17.6 %collective-permute-start.3 = (bf16[2,128,2048]{2,1,0:T(8,128)(2,1)}, bf16[2,128,2048]{2,1,0:T(8,128)(2,1)S(1)}, u32[]{:S(2)}, u32[]{:S(2)}) collective-permute-start(bf16[2,128,2048]{2,1,0:T(8,128)(2,1)} %get-tuple-element.11), channel_id=1, source_target_pairs={{0,1},{1,0},{2,3},{3,2},{4,5},{5,4},{6,7},{7,6},{8,9},{9,8},{10,11... | collective-permute-start | bytes 3145736 | tf_op jit(solution)/shard_map/ppermute | solution.py:56
  15.0 8.5 %collective-permute-start.5 = (bf16[2,144,512]{2,1,0:T(8,128)(2,1)S(1)}, bf16[2,144,512]{2,1,0:T(8,128)(2,1)S(1)}, u32[]{:S(2)}, u32[]{:S(2)}) collective-permute-start(bf16[2,144,512]{2,1,0:T(8,128)(2,1)S(1)} %pad_maximum_fusion), channel_id=1, source_target_pairs={{0,4},{1,5},{2,6},{3,7},{4,0},{5,1},{6,2},{7,3},{8,12},{9,13},{10,... | collective-permute-start | bytes 884744 | tf_op jit(solution)/shard_map/ppermute | solution.py:65
  16.6 8.5 %collective-permute-start.4 = (bf16[2,144,512]{2,1,0:T(8,128)(2,1)S(1)}, bf16[2,144,512]{2,1,0:T(8,128)(2,1)}, u32[]{:S(2)}, u32[]{:S(2)}) collective-permute-start(bf16[2,144,512]{2,1,0:T(8,128)(2,1)S(1)} %pad_maximum_fusion), channel_id=1, source_target_pairs={{0,2},{1,3},{2,0},{3,1},{4,6},{5,7},{6,4},{7,5},{8,10},{9,11},{10,... | collective-permute-start | bytes 884744 | tf_op jit(solution)/shard_map/ppermute | solution.py:64
  23.5 5.7 %collective-permute-start.6 = (bf16[2,144,256]{2,1,0:T(8,128)(2,1)S(1)}, bf16[2,144,256]{2,1,0:T(8,128)(2,1)S(1)}, u32[]{:S(2)}, u32[]{:S(2)}) collective-permute-start(bf16[2,144,256]{2,1,0:T(8,128)(2,1)S(1)} %slice.16), channel_id=1, source_target_pairs={{0,2},{1,3},{2,0},{3,1},{4,6},{5,7},{6,4},{7,5},{8,10},{9,11},{10,... | collective-permute-start | bytes 442376 | tf_op jit(solution)/shard_map/ppermute | solution.py:67
  26.0 5.2 %collective-permute-start.7 = (bf16[2,144,256]{2,1,0:T(8,128)(2,1)S(1)}, bf16[2,144,256]{2,1,0:T(8,128)(2,1)S(1)}, u32[]{:S(2)}, u32[]{:S(2)}) collective-permute-start(bf16[2,144,256]{2,1,0:T(8,128)(2,1)S(1)} %slice.17), channel_id=1, source_target_pairs={{0,4},{1,5},{2,6},{3,7},{4,0},{5,1},{6,2},{7,3},{8,12},{9,13},{10,... | collective-permute-start | bytes 442376 | tf_op jit(solution)/shard_map/ppermute | solution.py:68
  31.8 1.3 %collective-permute-start.8 = (f32[128,144]{0,1:T(8,128)S(1)}, f32[128,144]{0,1:T(8,128)S(1)}, u32[]{:S(2)}, u32[]{:S(2)}) collective-permute-start(f32[128,144]{0,1:T(8,128)S(1)} %slice.19), channel_id=1, source_target_pairs={{0,1},{1,0},{2,3},{3,2},{4,5},{5,4},{6,7},{7,6},{8,9},{9,8},{10,11... | collective-permute-start | bytes 221192 | tf_op jit(solution)/shard_map/ppermute | solution.py:72

commit v12 on v8

--- a/solution.py
+++ b/solution.py
@@ -47,6 +47,7 @@
         bx, by = chip_bits
         along_x = lax.ppermute(mine, "rows", xor_pairs(owners_n, bx))
         along_y = lax.ppermute(mine, "rows", xor_pairs(owners_n, by))
+        mine, along_x, along_y = lax.optimization_barrier((mine, along_x, along_y))
         remote = remote + term((here ^ bx) * chunk, chunk, along_x)
         remote = remote + term((here ^ by) * chunk, chunk, along_y)
         half = chunk // 2

time: 40.7 us -> 43.3 us (1.064)
  waiting for transfers between devices: 11.4 us -> 15 us
  starting transfers between devices: 13.7 us -> 12.9 us
    ppermute x1, waiting for transfers between devices: 0.01 us -> 5.78 us  [on_device(): along_x = lax.ppermute(mine, 'rows', xor_pairs(owners_n, bx))]
    ppermute x1, waiting for transfers between devices: 5.42 us -> 1.21 us  [on_device(): along_y = lax.ppermute(mine, 'rows', xor_pairs(owners_n, by))]
    ppermute x1, waiting for transfers between devices: 1.03 us -> 3.48 us  [on_device(): first = lax.ppermute(along_y[:, :, :half], 'rows', xor_pairs(owners_n, bx))]
    ppermute x1, starting transfers between devices: 1.56 us -> 0.54 us  [on_device(): first = lax.ppermute(along_y[:, :, :half], 'rows', xor_pairs(owners_n, bx))]
    ppermute x1, waiting for transfers between devices: 0.7 us -> 0.01 us  [on_device(): lax.ppermute(second, 'rows', sibling)]
where the time goes in v12:
time: 43.3 us; the launch traced here: 43.1 us
  waiting for transfers between devices  15 us (35%)
  starting transfers between devices  12.9 us (30%)
  blocking collectives  7.92 us (18%)
  matrix products  4.56 us (11%)
  local copies, waits for them, and re-layouts  2.07 us (5%)
  other arithmetic  0.48 us (1%)
    all_to_all x1, blocking collectives, on_device(): lax.all_to_all(placed, 'rows', split_axis=0, concat_axis=0, tiled=True)  7.92 us
    ppermute x3, starting transfers between devices, on_device(): arrived.append(lax.ppermute(piece, 'blk', pairs))  6.96 us
    ppermute x1, waiting for transfers between devices, on_device(): along_x = lax.ppermute(mine, 'rows', xor_pairs(owners_n, bx))  5.78 us
    ppermute x1, waiting for transfers between devices, on_device(): first = lax.ppermute(along_y[:, :, :half], 'rows', xor_pairs(owners_n, bx))  3.48 us
    ppermute x3, waiting for transfers between devices, on_device(): arrived.append(lax.ppermute(piece, 'blk', pairs))  2.8 us
    dot_general x10, matrix products, term(): jnp.einsum('rsk,rtk->st', part, tests, preferred_element_type=jnp.float32)  2.23 us
    dot_general x1, matrix products, on_device(): jnp.einsum('rsk,rtk->st', features, test_blocks, preferred_element_type=j...  1.96 us
    ppermute x1, waiting for transfers between devices, on_device(): second = lax.ppermute(along_x[:, :, half:], 'rows', xor_pairs(owners_n, by))  1.74 us
  transfers between devices with their start and end apart: 12, of which 5 were waited for; matrix products, arithmetic and copies ran while one was open for 11% of the time, Pallas kernels for 0%

profile of v12, /device:TPU:0, one launch (start us, length us, event | category | flops | bytes accessed | tf_op | source)
XLA Modules:
  0.0 43.1 jit_solution(4411665986449576133)
XLA Ops:
  0.0 0.0 copy-start
  0.0 0.0 copy-start.1
  0.0 1.0 %constant_dynamic-slice_fusion = bf16[4,48,256]{2,1,0:T(8,128)(2,1)S(1)} fusion(bf16[4,48,2048]{2,1,0:T(8,128)(2,1)} %param.5, s32[]{:T(128)S(6)} %select_n.41), kind=kLoop, calls=%fused_computation.56 | loop fusion | bytes 196612 | tf_op jit(solution)/shard_map/dynamic_slice | solution.py:35
  1.1 3.0 %collective-permute-start.2 = (bf16[4,48,256]{2,1,0:T(8,128)(2,1)S(1)}, bf16[4,48,256]{2,1,0:T(8,128)(2,1)S(1)}, u32[]{:S(2)}, u32[]{:S(2)}) collective-permute-start(bf16[4,48,256]{2,1,0:T(8,128)(2,1)S(1)} %constant_dynamic-slice_fusion), channel_id=1, source_target_pairs={{0,8},{8,16},{16,24},{24,0},{1,9},{9,17},{17,25},{25,1},{2,10},{10... | collective-permute-start | bytes 294920 | tf_op jit(solution)/shard_map/ppermute | solution.py:39
  4.1 2.6 %collective-permute-start.1 = (bf16[4,48,256]{2,1,0:T(8,128)(2,1)S(1)}, bf16[4,48,256]{2,1,0:T(8,128)(2,1)S(1)}, u32[]{:S(2)}, u32[]{:S(2)}) collective-permute-start(bf16[4,48,256]{2,1,0:T(8,128)(2,1)S(1)} %constant_dynamic-slice_fusion), channel_id=1, source_target_pairs={{0,16},{8,24},{16,0},{24,8},{1,17},{9,25},{17,1},{25,9},{2,18},{10... | collective-permute-start | bytes 294920 | tf_op jit(solution)/shard_map/ppermute | solution.py:39
  6.7 1.3 %collective-permute-start = (bf16[4,48,256]{2,1,0:T(8,128)(2,1)S(1)}, bf16[4,48,256]{2,1,0:T(8,128)(2,1)S(1)}, u32[]{:S(2)}, u32[]{:S(2)}) collective-permute-start(bf16[4,48,256]{2,1,0:T(8,128)(2,1)S(1)} %constant_dynamic-slice_fusion), channel_id=1, source_target_pairs={{0,24},{8,0},{16,8},{24,16},{1,25},{9,1},{17,9},{25,17},{2,26},{10... | collective-permute-start | bytes 294920 | tf_op jit(solution)/shard_map/ppermute | solution.py:39
  8.0 0.0 copy-done
  8.0 2.0 %convolution_bitcast_fusion.10 = bf16[128,48]{0,1:T(8,128)(2,1)S(1)} fusion(bf16[4,128,2048]{2,1,0:T(8,128)(2,1)S(1)} %copy-done, bf16[4,48,2048]{2,1,0:T(8,128)(2,1)} %param.5), kind=kOutput, calls=%fused_computation.20 | convolution fusion | flops 100663296 | bytes 2895872 | tf_op jit(solution)/shard_map/rsk,rtk->st/dot_general | solution.py:41
  10.0 0.0 copy-done.1
  10.0 0.1 fusion.25
  10.1 0.2 reduce_window_sum.11
  10.3 0.2 select_reduce_fusion
  10.5 0.0 collective-permute-done.2
  10.5 2.8 %collective-permute-done.1 = bf16[4,48,256]{2,1,0:T(8,128)(2,1)S(1)} collective-permute-done((bf16[4,48,256]{2,1,0:T(8,128)(2,1)S(1)}, bf16[4,48,256]{2,1,0:T(8,128)(2,1)S(1)}, u32[]{:S(2)}, u32[]{:S(2)}) %collective-permute-start.1) | collective-permute-done | bytes 98336 | tf_op jit(solution)/shard_map/ppermute | solution.py:39
  13.2 0.0 collective-permute-done
  13.3 1.6 %collective-permute-start.3 = (bf16[4,144,256]{2,1,0:T(8,128)(2,1)S(1)}, bf16[4,144,256]{2,1,0:T(8,128)(2,1)S(1)}, u32[]{:S(2)}, u32[]{:S(2)}) collective-permute-start(bf16[4,144,256]{2,1,0:T(8,128)(2,1)S(1)} %pad_maximum_fusion), channel_id=1, source_target_pairs={{0,2},{1,3},{2,0},{3,1},{4,6},{5,7},{6,4},{7,5},{8,10},{9,11},{10,... | collective-permute-start | bytes 884744 | tf_op jit(solution)/shard_map/ppermute | solution.py:48
  14.9 1.5 %collective-permute-start.4 = (bf16[4,144,256]{2,1,0:T(8,128)(2,1)S(1)}, bf16[4,144,256]{2,1,0:T(8,128)(2,1)S(1)}, u32[]{:S(2)}, u32[]{:S(2)}) collective-permute-start(bf16[4,144,256]{2,1,0:T(8,128)(2,1)S(1)} %pad_maximum_fusion), channel_id=1, source_target_pairs={{0,4},{1,5},{2,6},{3,7},{4,0},{5,1},{6,2},{7,3},{8,12},{9,13},{10,... | collective-permute-start | bytes 884744 | tf_op jit(solution)/shard_map/ppermute | solution.py:49
  16.4 5.8 %collective-permute-done.3 = bf16[4,144,256]{2,1,0:T(8,128)(2,1)S(1)} collective-permute-done((bf16[4,144,256]{2,1,0:T(8,128)(2,1)S(1)}, bf16[4,144,256]{2,1,0:T(8,128)(2,1)S(1)}, u32[]{:S(2)}, u32[]{:S(2)}) %collective-permute-start.3) | collective-permute-done | bytes 294944 | tf_op jit(solution)/shard_map/ppermute | solution.py:48
  22.2 1.2 %collective-permute-done.4 = bf16[4,144,256]{2,1,0:T(8,128)(2,1)S(1)} collective-permute-done((bf16[4,144,256]{2,1,0:T(8,128)(2,1)S(1)}, bf16[4,144,256]{2,1,0:T(8,128)(2,1)S(1)}, u32[]{:S(2)}, u32[]{:S(2)}) %collective-permute-start.4) | collective-permute-done | bytes 294944 | tf_op jit(solution)/shard_map/ppermute | solution.py:49
  23.4 1.6 %collective-permute-start.6 = (bf16[4,144,128]{2,1,0:T(8,128)(2,1)S(1)}, bf16[4,144,128]{2,1,0:T(8,128)(2,1)S(1)}, u32[]{:S(2)}, u32[]{:S(2)}) collective-permute-start(bf16[4,144,128]{2,1,0:T(8,128)(2,1)S(1)} %slice.7), channel_id=1, source_target_pairs={{0,4},{1,5},{2,6},{3,7},{4,0},{5,1},{6,2},{7,3},{8,12},{9,13},{10,... | collective-permute-start | bytes 442376 | tf_op jit(solution)/shard_map/ppermute | solution.py:55
  25.0 0.2 convolution_bitcast_fusion.5
  25.2 0.1 copy.6
  25.4 0.1 collective-permute-start.8
  25.4 0.5 %collective-permute-start.9 = (bf16[4,144,256]{2,1,0:T(8,128)(2,1)S(1)}, bf16[4,144,256]{2,1,0:T(8,128)(2,1)S(1)}, u32[]{:S(2)}, u32[]{:S(2)}) collective-permute-start(bf16[4,144,256]{2,1,0:T(8,128)(2,1)S(1)} %collective-permute-done.4), channel_id=1, source_target_pairs={{0,1},{1,0},{2,3},{3,2},{4,5},{5,4},{6,7},{7,6},{8,9},{9,8},{10,11... | collective-permute-start | bytes 884744 | tf_op jit(solution)/shard_map/ppermute | solution.py:60
  26.0 0.1 collective-permute-start.7
  26.1 0.5 %collective-permute-start.5 = (bf16[4,144,128]{2,1,0:T(8,128)(2,1)S(1)}, bf16[4,144,128]{2,1,0:T(8,128)(2,1)S(1)}, u32[]{:S(2)}, u32[]{:S(2)}) collective-permute-start(bf16[4,144,128]{2,1,0:T(8,128)(2,1)S(1)} %slice.6), channel_id=1, source_target_pairs={{0,2},{1,3},{2,0},{3,1},{4,6},{5,7},{6,4},{7,5},{8,10},{9,11},{10,... | collective-permute-start | bytes 442376 | tf_op jit(solution)/shard_map/ppermute | solution.py:54
  26.7 0.2 convolution_bitcast_fusion.3
  26.9 1.7 %collective-permute-done.6 = bf16[4,144,128]{2,1,0:T(8,128)(2,1)S(1)} collective-permute-done((bf16[4,144,128]{2,1,0:T(8,128)(2,1)S(1)}, bf16[4,144,128]{2,1,0:T(8,128)(2,1)S(1)}, u32[]{:S(2)}, u32[]{:S(2)}) %collective-permute-start.6) | collective-permute-done | bytes 147488 | tf_op jit(solution)/shard_map/ppermute | solution.py:55
  28.6 0.0 collective-permute-start.11
  28.6 0.2 convolution_bitcast_fusion.8
  28.8 3.5 %collective-permute-done.5 = bf16[4,144,128]{2,1,0:T(8,128)(2,1)S(1)} collective-permute-done((bf16[4,144,128]{2,1,0:T(8,128)(2,1)S(1)}, bf16[4,144,128]{2,1,0:T(8,128)(2,1)S(1)}, u32[]{:S(2)}, u32[]{:S(2)}) %collective-permute-start.5) | collective-permute-done | bytes 147488 | tf_op jit(solution)/shard_map/ppermute | solution.py:54
  32.3 0.0 collective-permute-start.10
  32.3 0.2 convolution_bitcast_fusion.9
  32.5 0.0 collective-permute-done.9
  32.5 0.2 convolution_bitcast_fusion
  32.8 0.0 collective-permute-done.8
  32.8 0.2 convolution_bitcast_fusion.1
  33.0 0.0 collective-permute-done.7
  33.0 0.2 convolution_bitcast_fusion.2
  33.3 0.3 fusion.8
  33.6 0.0 collective-permute-done.11
  33.6 0.2 convolution_bitcast_fusion.6
  33.8 0.0 collective-permute-done.10
  33.8 0.2 fusion.1
  34.0 0.4 convolution_convert_fusion
  34.4 0.1 copy.8
  34.5 7.9 %all_to_all.12 = bf16[8,32,192]{2,1,0:T(8,128)(2,1)S(1)} all-to-all(bf16[8,32,192]{2,1,0:T(8,128)(2,1)S(1)} %bitcast.57), channel_id=1, replica_groups=mesh['blk'=4,'rows'=8] {'rows'}, dimensions={0} | all-to-all | bytes 196608 | tf_op jit(solution)/shard_map/all_to_all | solution.py:85
  42.4 0.7 %copy.9 = bf16[256,192]{0,1:T(8,128)(2,1)} copy(bf16[256,192]{1,0:T(8,128)(2,1)S(1)} %bitcast.58) | data formatting | bytes 196608 | tf_op jit(solution)/shard_map/all_to_all | solution.py:85
  (5 shorter events, 0.1 us)
Async XLA Ops:
  0.0 8.0 %copy-start = (bf16[4,128,2048]{2,1,0:T(8,128)(2,1)S(1)}, bf16[4,128,2048]{2,1,0:T(8,128)(2,1)}, u32[]{:S(2)}) copy-start(bf16[4,128,2048]{2,1,0:T(8,128)(2,1)} %param.3) | copy-start | bytes 6291460
  0.0 10.0 %copy-start.1 = (s32[128,1]{0,1:T(1,128)S(1)}, s32[128,1]{0,1:T(1,128)}, u32[]{:S(2)}) copy-start(s32[128,1]{0,1:T(1,128)} %param.4) | copy-start | bytes 1540
  1.1 9.4 %collective-permute-start.2 = (bf16[4,48,256]{2,1,0:T(8,128)(2,1)S(1)}, bf16[4,48,256]{2,1,0:T(8,128)(2,1)S(1)}, u32[]{:S(2)}, u32[]{:S(2)}) collective-permute-start(bf16[4,48,256]{2,1,0:T(8,128)(2,1)S(1)} %constant_dynamic-slice_fusion), channel_id=1, source_target_pairs={{0,8},{8,16},{16,24},{24,0},{1,9},{9,17},{17,25},{25,1},{2,10},{10... | collective-permute-start | bytes 294920 | tf_op jit(solution)/shard_map/ppermute | solution.py:39
  4.1 9.2 %collective-permute-start.1 = (bf16[4,48,256]{2,1,0:T(8,128)(2,1)S(1)}, bf16[4,48,256]{2,1,0:T(8,128)(2,1)S(1)}, u32[]{:S(2)}, u32[]{:S(2)}) collective-permute-start(bf16[4,48,256]{2,1,0:T(8,128)(2,1)S(1)} %constant_dynamic-slice_fusion), channel_id=1, source_target_pairs={{0,16},{8,24},{16,0},{24,8},{1,17},{9,25},{17,1},{25,9},{2,18},{10... | collective-permute-start | bytes 294920 | tf_op jit(solution)/shard_map/ppermute | solution.py:39
  6.7 6.6 %collective-permute-start = (bf16[4,48,256]{2,1,0:T(8,128)(2,1)S(1)}, bf16[4,48,256]{2,1,0:T(8,128)(2,1)S(1)}, u32[]{:S(2)}, u32[]{:S(2)}) collective-permute-start(bf16[4,48,256]{2,1,0:T(8,128)(2,1)S(1)} %constant_dynamic-slice_fusion), channel_id=1, source_target_pairs={{0,24},{8,0},{16,8},{24,16},{1,25},{9,1},{17,9},{25,17},{2,26},{10... | collective-permute-start | bytes 294920 | tf_op jit(solution)/shard_map/ppermute | solution.py:39
  13.3 8.9 %collective-permute-start.3 = (bf16[4,144,256]{2,1,0:T(8,128)(2,1)S(1)}, bf16[4,144,256]{2,1,0:T(8,128)(2,1)S(1)}, u32[]{:S(2)}, u32[]{:S(2)}) collective-permute-start(bf16[4,144,256]{2,1,0:T(8,128)(2,1)S(1)} %pad_maximum_fusion), channel_id=1, source_target_pairs={{0,2},{1,3},{2,0},{3,1},{4,6},{5,7},{6,4},{7,5},{8,10},{9,11},{10,... | collective-permute-start | bytes 884744 | tf_op jit(solution)/shard_map/ppermute | solution.py:48
  14.9 8.5 %collective-permute-start.4 = (bf16[4,144,256]{2,1,0:T(8,128)(2,1)S(1)}, bf16[4,144,256]{2,1,0:T(8,128)(2,1)S(1)}, u32[]{:S(2)}, u32[]{:S(2)}) collective-permute-start(bf16[4,144,256]{2,1,0:T(8,128)(2,1)S(1)} %pad_maximum_fusion), channel_id=1, source_target_pairs={{0,4},{1,5},{2,6},{3,7},{4,0},{5,1},{6,2},{7,3},{8,12},{9,13},{10,... | collective-permute-start | bytes 884744 | tf_op jit(solution)/shard_map/ppermute | solution.py:49
  23.4 5.2 %collective-permute-start.6 = (bf16[4,144,128]{2,1,0:T(8,128)(2,1)S(1)}, bf16[4,144,128]{2,1,0:T(8,128)(2,1)S(1)}, u32[]{:S(2)}, u32[]{:S(2)}) collective-permute-start(bf16[4,144,128]{2,1,0:T(8,128)(2,1)S(1)} %slice.7), channel_id=1, source_target_pairs={{0,4},{1,5},{2,6},{3,7},{4,0},{5,1},{6,2},{7,3},{8,12},{9,13},{10,... | collective-permute-start | bytes 442376 | tf_op jit(solution)/shard_map/ppermute | solution.py:55
  25.4 7.4 %collective-permute-start.8 = (bf16[4,144,256]{2,1,0:T(8,128)(2,1)S(1)}, bf16[4,144,256]{2,1,0:T(8,128)(2,1)S(1)}, u32[]{:S(2)}, u32[]{:S(2)}) collective-permute-start(bf16[4,144,256]{2,1,0:T(8,128)(2,1)S(1)} %collective-permute-done.3), channel_id=1, source_target_pairs={{0,1},{1,0},{2,3},{3,2},{4,5},{5,4},{6,7},{7,6},{8,9},{9,8},{10,11... | collective-permute-start | bytes 884744 | tf_op jit(solution)/shard_map/ppermute | solution.py:60
  25.4 7.1 %collective-permute-start.9 = (bf16[4,144,256]{2,1,0:T(8,128)(2,1)S(1)}, bf16[4,144,256]{2,1,0:T(8,128)(2,1)S(1)}, u32[]{:S(2)}, u32[]{:S(2)}) collective-permute-start(bf16[4,144,256]{2,1,0:T(8,128)(2,1)S(1)} %collective-permute-done.4), channel_id=1, source_target_pairs={{0,1},{1,0},{2,3},{3,2},{4,5},{5,4},{6,7},{7,6},{8,9},{9,8},{10,11... | collective-permute-start | bytes 884744 | tf_op jit(solution)/shard_map/ppermute | solution.py:60
  26.0 7.1 %collective-permute-start.7 = (bf16[4,144,256]{2,1,0:T(8,128)(2,1)S(1)}, bf16[4,144,256]{2,1,0:T(8,128)(2,1)S(1)}, u32[]{:S(2)}, u32[]{:S(2)}) collective-permute-start(bf16[4,144,256]{2,1,0:T(8,128)(2,1)S(1)} %pad_maximum_fusion), channel_id=1, source_target_pairs={{0,1},{1,0},{2,3},{3,2},{4,5},{5,4},{6,7},{7,6},{8,9},{9,8},{10,11... | collective-permute-start | bytes 884744 | tf_op jit(solution)/shard_map/ppermute | solution.py:60
  26.1 6.2 %collective-permute-start.5 = (bf16[4,144,128]{2,1,0:T(8,128)(2,1)S(1)}, bf16[4,144,128]{2,1,0:T(8,128)(2,1)S(1)}, u32[]{:S(2)}, u32[]{:S(2)}) collective-permute-start(bf16[4,144,128]{2,1,0:T(8,128)(2,1)S(1)} %slice.6), channel_id=1, source_target_pairs={{0,2},{1,3},{2,0},{3,1},{4,6},{5,7},{6,4},{7,5},{8,10},{9,11},{10,... | collective-permute-start | bytes 442376 | tf_op jit(solution)/shard_map/ppermute | solution.py:54
  28.6 4.9 %collective-permute-start.11 = (bf16[4,144,128]{2,1,0:T(8,128)(2,1)S(1)}, bf16[4,144,128]{2,1,0:T(8,128)(2,1)S(1)}, u32[]{:S(2)}, u32[]{:S(2)}) collective-permute-start(bf16[4,144,128]{2,1,0:T(8,128)(2,1)S(1)} %collective-permute-done.6), channel_id=1, source_target_pairs={{0,1},{1,0},{2,3},{3,2},{4,5},{5,4},{6,7},{7,6},{8,9},{9,8},{10,11... | collective-permute-start | bytes 442376 | tf_op jit(solution)/shard_map/ppermute | solution.py:63
  32.3 1.5 %collective-permute-start.10 = (bf16[4,144,128]{2,1,0:T(8,128)(2,1)S(1)}, bf16[4,144,128]{2,1,0:T(8,128)(2,1)S(1)}, u32[]{:S(2)}, u32[]{:S(2)}) collective-permute-start(bf16[4,144,128]{2,1,0:T(8,128)(2,1)S(1)} %collective-permute-done.5), channel_id=1, source_target_pairs={{0,1},{1,0},{2,3},{3,2},{4,5},{5,4},{6,7},{7,6},{8,9},{9,8},{10,11... | collective-permute-start | bytes 442376 | tf_op jit(solution)/shard_map/ppermute | solution.py:62

commit v13 on v8

--- a/solution.py
+++ b/solution.py
@@ -49,14 +49,14 @@
         along_y = lax.ppermute(mine, "rows", xor_pairs(owners_n, by))
         remote = remote + term((here ^ bx) * chunk, chunk, along_x)
         remote = remote + term((here ^ by) * chunk, chunk, along_y)
+        sibling = xor_pairs(owners_n, 1)
+        for mask, got in ((0, mine), (bx, along_x), (by, along_y)):
+            remote = remote + term((here ^ 1 ^ mask) * chunk, chunk, lax.ppermute(got, "rows", sibling))
         half = chunk // 2
         first = lax.ppermute(along_y[:, :, :half], "rows", xor_pairs(owners_n, bx))
         second = lax.ppermute(along_x[:, :, half:], "rows", xor_pairs(owners_n, by))
         corner = (here ^ bx ^ by) * chunk
         remote = remote + term(corner, half, first) + term(corner + half, half, second)
-        sibling = xor_pairs(owners_n, 1)
-        for mask, got in ((0, mine), (bx, along_x), (by, along_y)):
-            remote = remote + term((here ^ 1 ^ mask) * chunk, chunk, lax.ppermute(got, "rows", sibling))
         far = (here ^ 1 ^ bx ^ by) * chunk
         remote = remote + term(far, half, lax.ppermute(first, "rows", sibling))
         remote = remote + term(far + half, half, lax.ppermute(second, "rows", sibling))

time: 40.7 us -> 41.4 us (1.017)
  other arithmetic: 0.48 us -> 2.44 us
  starting transfers between devices: 13.7 us -> 12.8 us
    ppermute x1, waiting for transfers between devices: 5.42 us -> 0.01 us  [on_device(): along_y = lax.ppermute(mine, 'rows', xor_pairs(owners_n, by))]
    ppermute x1, waiting for transfers between devices: 0.01 us -> 5.05 us  [on_device(): along_x = lax.ppermute(mine, 'rows', xor_pairs(owners_n, bx))]
    ppermute x3, starting transfers between devices: 6.96 us -> 6.06 us  [on_device(): arrived.append(lax.ppermute(piece, 'blk', pairs))]
    ppermute x1, waiting for transfers between devices: 0.7 us -> 0.01 us  [on_device(): lax.ppermute(second, 'rows', sibling)]
    add x1, other arithmetic: 0.01 us -> 0.67 us  [slot_matrix(): slot = owner * capacity + rank]
    reduce_sum x1, other arithmetic: 0.17 us -> 0.83 us  [slot_matrix(): rank = jnp.sum(before * onehot, axis=1)]
    convert_element_type x1, other arithmetic: 0.08 us -> 0.73 us  [slot_matrix(): (owner[:, None] == jnp.arange(owners_n, dtype=jnp.int32)[None, :]).astype...]
    ppermute x1, waiting for transfers between devices: 1.39 us -> 0.76 us  [on_device(): second = lax.ppermute(along_x[:, :, half:], 'rows', xor_pairs(owners_n, by))]
  transfers between devices with their start and end apart: 12 -> 12, of which waited for: 5 -> 5; matrix products, arithmetic and copies ran while one was open for 11% -> 16% of each run, Pallas kernels for 0% -> 0%
where the time goes in v13:
time: 41.4 us; the launch traced here: 41.1 us
  starting transfers between devices  12.8 us (31%)
  waiting for transfers between devices  11 us (27%)
  blocking collectives  8.09 us (20%)
  matrix products  4.57 us (11%)
  other arithmetic  2.44 us (6%)
  local copies, waits for them, and re-layouts  2.06 us (5%)
    all_to_all x1, blocking collectives, on_device(): lax.all_to_all(placed, 'rows', split_axis=0, concat_axis=0, tiled=True)  8.09 us
    ppermute x3, starting transfers between devices, on_device(): arrived.append(lax.ppermute(piece, 'blk', pairs))  6.06 us
    ppermute x1, waiting for transfers between devices, on_device(): along_x = lax.ppermute(mine, 'rows', xor_pairs(owners_n, bx))  5.05 us
    ppermute x3, waiting for transfers between devices, on_device(): arrived.append(lax.ppermute(piece, 'blk', pairs))  3.31 us
    dot_general x10, matrix products, term(): jnp.einsum('rsk,rtk->st', part, tests, preferred_element_type=jnp.float32)  2.25 us
    dot_general x1, matrix products, on_device(): jnp.einsum('rsk,rtk->st', features, test_blocks, preferred_element_type=j...  1.96 us
    ppermute x1, starting transfers between devices, on_device(): second = lax.ppermute(along_x[:, :, half:], 'rows', xor_pairs(owners_n, by))  1.58 us
    ppermute x1, starting transfers between devices, on_device(): along_x = lax.ppermute(mine, 'rows', xor_pairs(owners_n, bx))  1.56 us
  transfers between devices with their start and end apart: 12, of which 5 were waited for; matrix products, arithmetic and copies ran while one was open for 16% of the time, Pallas kernels for 0%

profile of v13, /device:TPU:0, one launch (start us, length us, event | category | flops | bytes accessed | tf_op | source)
XLA Modules:
  0.0 41.1 jit_solution(178302009617102202)
XLA Ops:
  0.0 0.0 copy-start
  0.0 1.0 %constant_dynamic-slice_fusion = bf16[4,48,256]{2,1,0:T(8,128)(2,1)S(1)} fusion(bf16[4,48,2048]{2,1,0:T(8,128)(2,1)} %param.5, s32[]{:T(128)S(6)} %select_n.41), kind=kLoop, calls=%fused_computation.56 | loop fusion | bytes 196612 | tf_op jit(solution)/shard_map/dynamic_slice | solution.py:35
  1.1 5.0 %collective-permute-start = (bf16[4,48,256]{2,1,0:T(8,128)(2,1)S(1)}, bf16[4,48,256]{2,1,0:T(8,128)(2,1)S(1)}, u32[]{:S(2)}, u32[]{:S(2)}) collective-permute-start(bf16[4,48,256]{2,1,0:T(8,128)(2,1)S(1)} %constant_dynamic-slice_fusion), channel_id=1, source_target_pairs={{0,24},{8,0},{16,8},{24,16},{1,25},{9,1},{17,9},{25,17},{2,26},{10... | collective-permute-start | bytes 294920 | tf_op jit(solution)/shard_map/ppermute | solution.py:39
  6.1 0.0 collective-permute-start.1
  6.1 1.0 %collective-permute-start.2 = (bf16[4,48,256]{2,1,0:T(8,128)(2,1)S(1)}, bf16[4,48,256]{2,1,0:T(8,128)(2,1)S(1)}, u32[]{:S(2)}, u32[]{:S(2)}) collective-permute-start(bf16[4,48,256]{2,1,0:T(8,128)(2,1)S(1)} %constant_dynamic-slice_fusion), channel_id=1, source_target_pairs={{0,8},{8,16},{16,24},{24,0},{1,9},{9,17},{17,25},{25,1},{2,10},{10... | collective-permute-start | bytes 294920 | tf_op jit(solution)/shard_map/ppermute | solution.py:39
  7.1 0.7 %fusion.25 = s32[128,8]{1,0:T(8,128)S(1)} fusion(s32[128]{0:T(128)} %bitcast.59), kind=kLoop, calls=%fused_computation.44 | loop fusion | flops 2048 | bytes 4608 | tf_op jit(solution)/shard_map/convert_element_type | solution.py:9
  7.9 0.2 reduce_window_sum.11
  8.0 0.8 %select_reduce_fusion = s32[128]{0:T(128)S(1)} fusion(s32[128,8]{1,0:T(8,128)S(1)} %reduce_window_sum.11, s32[128]{0:T(128)} %bitcast.60), kind=kLoop, calls=%fused_computation.42 | loop fusion | flops 4992 | bytes 5120 | tf_op jit(solution)/shard_map/reduce_sum | solution.py:11
  8.9 0.7 %multiply_add_fusion = s32[128]{0:T(128)S(1)} fusion(s32[128]{0:T(128)S(1)} %select_reduce_fusion, s32[128,1]{0,1:T(1,128)} %param.4), kind=kLoop, calls=%fused_computation.57 | loop fusion | flops 256 | bytes 1536 | tf_op jit(solution)/shard_map/add | solution.py:12
  9.5 0.0 copy-done
  9.5 2.0 %convolution_bitcast_fusion.10 = bf16[128,48]{0,1:T(8,128)(2,1)S(1)} fusion(bf16[4,128,2048]{2,1,0:T(8,128)(2,1)S(1)} %copy-done, bf16[4,48,2048]{2,1,0:T(8,128)(2,1)} %param.5), kind=kOutput, calls=%fused_computation.20 | convolution fusion | flops 100663296 | bytes 2895872 | tf_op jit(solution)/shard_map/rsk,rtk->st/dot_general | solution.py:41
  11.5 0.0 collective-permute-done
  11.5 3.3 %collective-permute-done.1 = bf16[4,48,256]{2,1,0:T(8,128)(2,1)S(1)} collective-permute-done((bf16[4,48,256]{2,1,0:T(8,128)(2,1)S(1)}, bf16[4,48,256]{2,1,0:T(8,128)(2,1)S(1)}, u32[]{:S(2)}, u32[]{:S(2)}) %collective-permute-start.1) | collective-permute-done | bytes 98336 | tf_op jit(solution)/shard_map/ppermute | solution.py:39
  14.8 0.0 collective-permute-done.2
  14.9 1.6 %collective-permute-start.3 = (bf16[4,144,256]{2,1,0:T(8,128)(2,1)S(1)}, bf16[4,144,256]{2,1,0:T(8,128)(2,1)S(1)}, u32[]{:S(2)}, u32[]{:S(2)}) collective-permute-start(bf16[4,144,256]{2,1,0:T(8,128)(2,1)S(1)} %pad_maximum_fusion), channel_id=1, source_target_pairs={{0,2},{1,3},{2,0},{3,1},{4,6},{5,7},{6,4},{7,5},{8,10},{9,11},{10,... | collective-permute-start | bytes 884744 | tf_op jit(solution)/shard_map/ppermute | solution.py:48
  16.4 1.5 %collective-permute-start.4 = (bf16[4,144,256]{2,1,0:T(8,128)(2,1)S(1)}, bf16[4,144,256]{2,1,0:T(8,128)(2,1)S(1)}, u32[]{:S(2)}, u32[]{:S(2)}) collective-permute-start(bf16[4,144,256]{2,1,0:T(8,128)(2,1)S(1)} %pad_maximum_fusion), channel_id=1, source_target_pairs={{0,4},{1,5},{2,6},{3,7},{4,0},{5,1},{6,2},{7,3},{8,12},{9,13},{10,... | collective-permute-start | bytes 884744 | tf_op jit(solution)/shard_map/ppermute | solution.py:49
  18.0 0.0 collective-permute-start.5
  18.0 0.1 copy.6
  18.1 0.3 convolution_bitcast_fusion.5
  18.3 5.0 %collective-permute-done.3 = bf16[4,144,256]{2,1,0:T(8,128)(2,1)S(1)} collective-permute-done((bf16[4,144,256]{2,1,0:T(8,128)(2,1)S(1)}, bf16[4,144,256]{2,1,0:T(8,128)(2,1)S(1)}, u32[]{:S(2)}, u32[]{:S(2)}) %collective-permute-start.3) | collective-permute-done | bytes 294944 | tf_op jit(solution)/shard_map/ppermute | solution.py:48
  23.4 1.6 %collective-permute-start.9 = (bf16[4,144,128]{2,1,0:T(8,128)(2,1)S(1)}, bf16[4,144,128]{2,1,0:T(8,128)(2,1)S(1)}, u32[]{:S(2)}, u32[]{:S(2)}) collective-permute-start(bf16[4,144,128]{2,1,0:T(8,128)(2,1)S(1)} %slice.9), channel_id=1, source_target_pairs={{0,4},{1,5},{2,6},{3,7},{4,0},{5,1},{6,2},{7,3},{8,12},{9,13},{10,... | collective-permute-start | bytes 442376 | tf_op jit(solution)/shard_map/ppermute | solution.py:57
  25.0 0.0 collective-permute-done.4
  25.0 1.6 %collective-permute-start.8 = (bf16[4,144,128]{2,1,0:T(8,128)(2,1)S(1)}, bf16[4,144,128]{2,1,0:T(8,128)(2,1)S(1)}, u32[]{:S(2)}, u32[]{:S(2)}) collective-permute-start(bf16[4,144,128]{2,1,0:T(8,128)(2,1)S(1)} %slice.8), channel_id=1, source_target_pairs={{0,2},{1,3},{2,0},{3,1},{4,6},{5,7},{6,4},{7,5},{8,10},{9,11},{10,... | collective-permute-start | bytes 442376 | tf_op jit(solution)/shard_map/ppermute | solution.py:56
  26.6 0.0 collective-permute-start.7
  26.6 0.5 %collective-permute-start.6 = (bf16[4,144,256]{2,1,0:T(8,128)(2,1)S(1)}, bf16[4,144,256]{2,1,0:T(8,128)(2,1)S(1)}, u32[]{:S(2)}, u32[]{:S(2)}) collective-permute-start(bf16[4,144,256]{2,1,0:T(8,128)(2,1)S(1)} %collective-permute-done.3), channel_id=1, source_target_pairs={{0,1},{1,0},{2,3},{3,2},{4,5},{5,4},{6,7},{7,6},{8,9},{9,8},{10,11... | collective-permute-start | bytes 884744 | tf_op jit(solution)/shard_map/ppermute | solution.py:54
  27.1 0.2 convolution_bitcast_fusion.3
  27.3 0.0 collective-permute-done.5
  27.4 0.2 convolution_bitcast_fusion.2
  27.6 0.2 fusion.4
  27.9 0.8 %collective-permute-done.9 = bf16[4,144,128]{2,1,0:T(8,128)(2,1)S(1)} collective-permute-done((bf16[4,144,128]{2,1,0:T(8,128)(2,1)S(1)}, bf16[4,144,128]{2,1,0:T(8,128)(2,1)S(1)}, u32[]{:S(2)}, u32[]{:S(2)}) %collective-permute-start.9) | collective-permute-done | bytes 147488 | tf_op jit(solution)/shard_map/ppermute | solution.py:57
  28.6 0.0 collective-permute-start.11
  28.6 0.2 convolution_bitcast_fusion.8
  28.8 1.4 %collective-permute-done.8 = bf16[4,144,128]{2,1,0:T(8,128)(2,1)S(1)} collective-permute-done((bf16[4,144,128]{2,1,0:T(8,128)(2,1)S(1)}, bf16[4,144,128]{2,1,0:T(8,128)(2,1)S(1)}, u32[]{:S(2)}, u32[]{:S(2)}) %collective-permute-start.8) | collective-permute-done | bytes 147488 | tf_op jit(solution)/shard_map/ppermute | solution.py:56
  30.2 0.0 collective-permute-start.10
  30.2 0.2 convolution_bitcast_fusion.9
  30.4 0.0 collective-permute-done.7
  30.5 0.2 convolution_bitcast_fusion
  30.7 0.0 collective-permute-done.6
  30.7 0.3 fusion.8
  31.0 0.0 collective-permute-done.11
  31.0 0.2 convolution_bitcast_fusion.6
  31.2 0.4 %collective-permute-done.10 = bf16[4,144,128]{2,1,0:T(8,128)(2,1)S(1)} collective-permute-done((bf16[4,144,128]{2,1,0:T(8,128)(2,1)S(1)}, bf16[4,144,128]{2,1,0:T(8,128)(2,1)S(1)}, u32[]{:S(2)}, u32[]{:S(2)}) %collective-permute-start.10) | collective-permute-done | bytes 147488 | tf_op jit(solution)/shard_map/ppermute | solution.py:61
  31.6 0.2 fusion.1
  31.8 0.4 convolution_convert_fusion
  32.2 0.1 copy.8
  32.3 8.1 %all_to_all.12 = bf16[8,32,192]{2,1,0:T(8,128)(2,1)S(1)} all-to-all(bf16[8,32,192]{2,1,0:T(8,128)(2,1)S(1)} %bitcast.57), channel_id=1, replica_groups=mesh['blk'=4,'rows'=8] {'rows'}, dimensions={0} | all-to-all | bytes 196608 | tf_op jit(solution)/shard_map/all_to_all | solution.py:84
  40.4 0.7 %copy.9 = bf16[256,192]{0,1:T(8,128)(2,1)} copy(bf16[256,192]{1,0:T(8,128)(2,1)S(1)} %bitcast.58) | data formatting | bytes 196608 | tf_op jit(solution)/shard_map/all_to_all | solution.py:84
  (4 shorter events, 0.1 us)
Async XLA Ops:
  0.0 9.5 %copy-start = (bf16[4,128,2048]{2,1,0:T(8,128)(2,1)S(1)}, bf16[4,128,2048]{2,1,0:T(8,128)(2,1)}, u32[]{:S(2)}) copy-start(bf16[4,128,2048]{2,1,0:T(8,128)(2,1)} %param.3) | copy-start | bytes 6291460
  1.1 10.5 %collective-permute-start = (bf16[4,48,256]{2,1,0:T(8,128)(2,1)S(1)}, bf16[4,48,256]{2,1,0:T(8,128)(2,1)S(1)}, u32[]{:S(2)}, u32[]{:S(2)}) collective-permute-start(bf16[4,48,256]{2,1,0:T(8,128)(2,1)S(1)} %constant_dynamic-slice_fusion), channel_id=1, source_target_pairs={{0,24},{8,0},{16,8},{24,16},{1,25},{9,1},{17,9},{25,17},{2,26},{10... | collective-permute-start | bytes 294920 | tf_op jit(solution)/shard_map/ppermute | solution.py:39
  6.1 8.7 %collective-permute-start.1 = (bf16[4,48,256]{2,1,0:T(8,128)(2,1)S(1)}, bf16[4,48,256]{2,1,0:T(8,128)(2,1)S(1)}, u32[]{:S(2)}, u32[]{:S(2)}) collective-permute-start(bf16[4,48,256]{2,1,0:T(8,128)(2,1)S(1)} %constant_dynamic-slice_fusion), channel_id=1, source_target_pairs={{0,16},{8,24},{16,0},{24,8},{1,17},{9,25},{17,1},{25,9},{2,18},{10... | collective-permute-start | bytes 294920 | tf_op jit(solution)/shard_map/ppermute | solution.py:39
  6.1 8.7 %collective-permute-start.2 = (bf16[4,48,256]{2,1,0:T(8,128)(2,1)S(1)}, bf16[4,48,256]{2,1,0:T(8,128)(2,1)S(1)}, u32[]{:S(2)}, u32[]{:S(2)}) collective-permute-start(bf16[4,48,256]{2,1,0:T(8,128)(2,1)S(1)} %constant_dynamic-slice_fusion), channel_id=1, source_target_pairs={{0,8},{8,16},{16,24},{24,0},{1,9},{9,17},{17,25},{25,1},{2,10},{10... | collective-permute-start | bytes 294920 | tf_op jit(solution)/shard_map/ppermute | solution.py:39
  14.9 8.5 %collective-permute-start.3 = (bf16[4,144,256]{2,1,0:T(8,128)(2,1)S(1)}, bf16[4,144,256]{2,1,0:T(8,128)(2,1)S(1)}, u32[]{:S(2)}, u32[]{:S(2)}) collective-permute-start(bf16[4,144,256]{2,1,0:T(8,128)(2,1)S(1)} %pad_maximum_fusion), channel_id=1, source_target_pairs={{0,2},{1,3},{2,0},{3,1},{4,6},{5,7},{6,4},{7,5},{8,10},{9,11},{10,... | collective-permute-start | bytes 884744 | tf_op jit(solution)/shard_map/ppermute | solution.py:48
  16.4 8.6 %collective-permute-start.4 = (bf16[4,144,256]{2,1,0:T(8,128)(2,1)S(1)}, bf16[4,144,256]{2,1,0:T(8,128)(2,1)S(1)}, u32[]{:S(2)}, u32[]{:S(2)}) collective-permute-start(bf16[4,144,256]{2,1,0:T(8,128)(2,1)S(1)} %pad_maximum_fusion), channel_id=1, source_target_pairs={{0,4},{1,5},{2,6},{3,7},{4,0},{5,1},{6,2},{7,3},{8,12},{9,13},{10,... | collective-permute-start | bytes 884744 | tf_op jit(solution)/shard_map/ppermute | solution.py:49
  18.0 9.4 %collective-permute-start.5 = (bf16[4,144,256]{2,1,0:T(8,128)(2,1)S(1)}, bf16[4,144,256]{2,1,0:T(8,128)(2,1)S(1)}, u32[]{:S(2)}, u32[]{:S(2)}) collective-permute-start(bf16[4,144,256]{2,1,0:T(8,128)(2,1)S(1)} %pad_maximum_fusion), channel_id=1, source_target_pairs={{0,1},{1,0},{2,3},{3,2},{4,5},{5,4},{6,7},{7,6},{8,9},{9,8},{10,11... | collective-permute-start | bytes 884744 | tf_op jit(solution)/shard_map/ppermute | solution.py:54
  23.4 5.2 %collective-permute-start.9 = (bf16[4,144,128]{2,1,0:T(8,128)(2,1)S(1)}, bf16[4,144,128]{2,1,0:T(8,128)(2,1)S(1)}, u32[]{:S(2)}, u32[]{:S(2)}) collective-permute-start(bf16[4,144,128]{2,1,0:T(8,128)(2,1)S(1)} %slice.9), channel_id=1, source_target_pairs={{0,4},{1,5},{2,6},{3,7},{4,0},{5,1},{6,2},{7,3},{8,12},{9,13},{10,... | collective-permute-start | bytes 442376 | tf_op jit(solution)/shard_map/ppermute | solution.py:57
  25.0 5.2 %collective-permute-start.8 = (bf16[4,144,128]{2,1,0:T(8,128)(2,1)S(1)}, bf16[4,144,128]{2,1,0:T(8,128)(2,1)S(1)}, u32[]{:S(2)}, u32[]{:S(2)}) collective-permute-start(bf16[4,144,128]{2,1,0:T(8,128)(2,1)S(1)} %slice.8), channel_id=1, source_target_pairs={{0,2},{1,3},{2,0},{3,1},{4,6},{5,7},{6,4},{7,5},{8,10},{9,11},{10,... | collective-permute-start | bytes 442376 | tf_op jit(solution)/shard_map/ppermute | solution.py:56
  26.6 3.9 %collective-permute-start.7 = (bf16[4,144,256]{2,1,0:T(8,128)(2,1)S(1)}, bf16[4,144,256]{2,1,0:T(8,128)(2,1)S(1)}, u32[]{:S(2)}, u32[]{:S(2)}) collective-permute-start(bf16[4,144,256]{2,1,0:T(8,128)(2,1)S(1)} %collective-permute-done.4), channel_id=1, source_target_pairs={{0,1},{1,0},{2,3},{3,2},{4,5},{5,4},{6,7},{7,6},{8,9},{9,8},{10,11... | collective-permute-start | bytes 884744 | tf_op jit(solution)/shard_map/ppermute | solution.py:54
  26.6 4.1 %collective-permute-start.6 = (bf16[4,144,256]{2,1,0:T(8,128)(2,1)S(1)}, bf16[4,144,256]{2,1,0:T(8,128)(2,1)S(1)}, u32[]{:S(2)}, u32[]{:S(2)}) collective-permute-start(bf16[4,144,256]{2,1,0:T(8,128)(2,1)S(1)} %collective-permute-done.3), channel_id=1, source_target_pairs={{0,1},{1,0},{2,3},{3,2},{4,5},{5,4},{6,7},{7,6},{8,9},{9,8},{10,11... | collective-permute-start | bytes 884744 | tf_op jit(solution)/shard_map/ppermute | solution.py:54
  28.6 2.4 %collective-permute-start.11 = (bf16[4,144,128]{2,1,0:T(8,128)(2,1)S(1)}, bf16[4,144,128]{2,1,0:T(8,128)(2,1)S(1)}, u32[]{:S(2)}, u32[]{:S(2)}) collective-permute-start(bf16[4,144,128]{2,1,0:T(8,128)(2,1)S(1)} %collective-permute-done.9), channel_id=1, source_target_pairs={{0,1},{1,0},{2,3},{3,2},{4,5},{5,4},{6,7},{7,6},{8,9},{9,8},{10,11... | collective-permute-start | bytes 442376 | tf_op jit(solution)/shard_map/ppermute | solution.py:62
  30.2 1.4 %collective-permute-start.10 = (bf16[4,144,128]{2,1,0:T(8,128)(2,1)S(1)}, bf16[4,144,128]{2,1,0:T(8,128)(2,1)S(1)}, u32[]{:S(2)}, u32[]{:S(2)}) collective-permute-start(bf16[4,144,128]{2,1,0:T(8,128)(2,1)S(1)} %collective-permute-done.8), channel_id=1, source_target_pairs={{0,1},{1,0},{2,3},{3,2},{4,5},{5,4},{6,7},{7,6},{8,9},{9,8},{10,11... | collective-permute-start | bytes 442376 | tf_op jit(solution)/shard_map/ppermute | solution.py:61

commit v14 on v9

--- a/solution.py
+++ b/solution.py
@@ -49,7 +49,9 @@
         along_y = lax.ppermute(mine, "rows", xor_pairs(owners_n, by))
         remote = remote + term((here ^ bx) * chunk, chunk, along_x)
         remote = remote + term((here ^ by) * chunk, chunk, along_y)
-        across = lax.ppermute(mine, "rows", xor_pairs(owners_n, bx ^ by))
+        relay = jnp.where(here % 2 == 0, along_y, along_x)
+        pairs = [(s ^ (bx if s % 2 == 0 else by), s) for s in range(owners_n)]
+        across = lax.ppermute(relay, "rows", pairs)
         remote = remote + term((here ^ bx ^ by) * chunk, chunk, across)
         sibling = xor_pairs(owners_n, 1)
         for mask, got in ((0, mine), (bx, along_x), (by, along_y), (bx ^ by, across)):

time: 42.5 us -> 42.3 us (level)
  waiting for transfers between devices: 15.1 us -> 12.8 us
  starting transfers between devices: 11 us -> 12.2 us
  matrix products: 5.24 us -> 6.2 us
    ppermute x1, waiting for transfers between devices: 6.98 us -> 2.93 us  [on_device(): across = lax.ppermute(relay, 'rows', pairs)]
    ppermute x1, waiting for transfers between devices: 0.08 us -> 1.24 us  [on_device(): along_x = lax.ppermute(mine, 'rows', xor_pairs(owners_n, bx))]
    ppermute x1, starting transfers between devices: 0.51 us -> 1.58 us  [on_device(): along_y = lax.ppermute(mine, 'rows', xor_pairs(owners_n, by))]
    dot_general x8, matrix products: 2.91 us -> 3.88 us  [term(): jnp.einsum('rsk,rtk->st', part, tests, preferred_element_type=jnp.float32)]
    ppermute x1, starting transfers between devices: 2.51 us -> 1.56 us  [on_device(): across = lax.ppermute(relay, 'rows', pairs)]
    ppermute x1, starting transfers between devices: 0.54 us -> 1.49 us  [on_device(): along_x = lax.ppermute(mine, 'rows', xor_pairs(owners_n, bx))]
    ppermute x1, waiting for transfers between devices: 5.18 us -> 5.78 us  [on_device(): along_y = lax.ppermute(mine, 'rows', xor_pairs(owners_n, by))]
  transfers between devices with their start and end apart: 10 -> 10, of which waited for: 4 -> 5; matrix products, arithmetic and copies ran while one was open for 12% -> 15% of each run, Pallas kernels for 0% -> 0%
where the time goes in v14:
time: 42.3 us; the launch traced here: 42 us
  waiting for transfers between devices  12.8 us (30%)
  starting transfers between devices  12.2 us (29%)
  blocking collectives  8.13 us (19%)
  matrix products  6.2 us (15%)
  local copies, waits for them, and re-layouts  2.02 us (5%)
  other arithmetic  0.51 us (1%)
    all_to_all x1, blocking collectives, on_device(): lax.all_to_all(placed, 'rows', split_axis=0, concat_axis=0, tiled=True)  8.13 us
    ppermute x3, starting transfers between devices, on_device(): arrived.append(lax.ppermute(piece, 'blk', pairs))  6.96 us
    ppermute x1, waiting for transfers between devices, on_device(): along_y = lax.ppermute(mine, 'rows', xor_pairs(owners_n, by))  5.78 us
    dot_general x8, matrix products, term(): jnp.einsum('rsk,rtk->st', part, tests, preferred_element_type=jnp.float32)  3.88 us
    ppermute x1, waiting for transfers between devices, on_device(): across = lax.ppermute(relay, 'rows', pairs)  2.93 us
    ppermute x3, waiting for transfers between devices, on_device(): arrived.append(lax.ppermute(piece, 'blk', pairs))  2.8 us
    dot_general x1, matrix products, on_device(): jnp.einsum('rsk,rtk->st', features, test_blocks, preferred_element_type=j...  1.96 us
    ppermute x1, starting transfers between devices, on_device(): along_y = lax.ppermute(mine, 'rows', xor_pairs(owners_n, by))  1.58 us
  transfers between devices with their start and end apart: 10, of which 5 were waited for; matrix products, arithmetic and copies ran while one was open for 15% of the time, Pallas kernels for 0%

profile of v14, /device:TPU:0, one launch (start us, length us, event | category | flops | bytes accessed | tf_op | source)
XLA Modules:
  0.0 42.0 jit_solution(5362280720589580234)
XLA Ops:
  0.0 0.0 copy-start
  0.0 0.0 copy-start.1
  0.0 1.0 %constant_dynamic-slice_fusion = bf16[4,48,256]{2,1,0:T(8,128)(2,1)S(1)} fusion(bf16[4,48,2048]{2,1,0:T(8,128)(2,1)} %param.5, s32[]{:T(128)S(6)} %select_n.47), kind=kLoop, calls=%fused_computation.49 | loop fusion | bytes 196612 | tf_op jit(solution)/shard_map/dynamic_slice | solution.py:35
  1.1 3.0 %collective-permute-start.2 = (bf16[4,48,256]{2,1,0:T(8,128)(2,1)S(1)}, bf16[4,48,256]{2,1,0:T(8,128)(2,1)S(1)}, u32[]{:S(2)}, u32[]{:S(2)}) collective-permute-start(bf16[4,48,256]{2,1,0:T(8,128)(2,1)S(1)} %constant_dynamic-slice_fusion), channel_id=1, source_target_pairs={{0,8},{8,16},{16,24},{24,0},{1,9},{9,17},{17,25},{25,1},{2,10},{10... | collective-permute-start | bytes 294920 | tf_op jit(solution)/shard_map/ppermute | solution.py:39
  4.1 2.6 %collective-permute-start.1 = (bf16[4,48,256]{2,1,0:T(8,128)(2,1)S(1)}, bf16[4,48,256]{2,1,0:T(8,128)(2,1)S(1)}, u32[]{:S(2)}, u32[]{:S(2)}) collective-permute-start(bf16[4,48,256]{2,1,0:T(8,128)(2,1)S(1)} %constant_dynamic-slice_fusion), channel_id=1, source_target_pairs={{0,16},{8,24},{16,0},{24,8},{1,17},{9,25},{17,1},{25,9},{2,18},{10... | collective-permute-start | bytes 294920 | tf_op jit(solution)/shard_map/ppermute | solution.py:39
  6.7 1.3 %collective-permute-start = (bf16[4,48,256]{2,1,0:T(8,128)(2,1)S(1)}, bf16[4,48,256]{2,1,0:T(8,128)(2,1)S(1)}, u32[]{:S(2)}, u32[]{:S(2)}) collective-permute-start(bf16[4,48,256]{2,1,0:T(8,128)(2,1)S(1)} %constant_dynamic-slice_fusion), channel_id=1, source_target_pairs={{0,24},{8,0},{16,8},{24,16},{1,25},{9,1},{17,9},{25,17},{2,26},{10... | collective-permute-start | bytes 294920 | tf_op jit(solution)/shard_map/ppermute | solution.py:39
  8.0 0.0 copy-done
  8.0 2.0 %convolution_bitcast_fusion.8 = bf16[128,48]{0,1:T(8,128)(2,1)S(1)} fusion(bf16[4,128,2048]{2,1,0:T(8,128)(2,1)S(1)} %copy-done, bf16[4,48,2048]{2,1,0:T(8,128)(2,1)} %param.5), kind=kOutput, calls=%fused_computation.16 | convolution fusion | flops 100663296 | bytes 2895872 | tf_op jit(solution)/shard_map/rsk,rtk->st/dot_general | solution.py:41
  10.0 0.0 copy-done.1
  10.0 0.1 fusion.21
  10.1 0.2 reduce_window_sum.11
  10.3 0.2 select_reduce_fusion
  10.5 0.0 collective-permute-done.2
  10.5 2.8 %collective-permute-done.1 = bf16[4,48,256]{2,1,0:T(8,128)(2,1)S(1)} collective-permute-done((bf16[4,48,256]{2,1,0:T(8,128)(2,1)S(1)}, bf16[4,48,256]{2,1,0:T(8,128)(2,1)S(1)}, u32[]{:S(2)}, u32[]{:S(2)}) %collective-permute-start.1) | collective-permute-done | bytes 98336 | tf_op jit(solution)/shard_map/ppermute | solution.py:39
  13.2 0.0 collective-permute-done
  13.3 1.6 %collective-permute-start.4 = (bf16[4,144,256]{2,1,0:T(8,128)(2,1)S(1)}, bf16[4,144,256]{2,1,0:T(8,128)(2,1)S(1)}, u32[]{:S(2)}, u32[]{:S(2)}) collective-permute-start(bf16[4,144,256]{2,1,0:T(8,128)(2,1)S(1)} %pad_maximum_fusion), channel_id=1, source_target_pairs={{0,4},{1,5},{2,6},{3,7},{4,0},{5,1},{6,2},{7,3},{8,12},{9,13},{10,... | collective-permute-start | bytes 884744 | tf_op jit(solution)/shard_map/ppermute | solution.py:49
  14.9 1.5 %collective-permute-start.3 = (bf16[4,144,256]{2,1,0:T(8,128)(2,1)S(1)}, bf16[4,144,256]{2,1,0:T(8,128)(2,1)S(1)}, u32[]{:S(2)}, u32[]{:S(2)}) collective-permute-start(bf16[4,144,256]{2,1,0:T(8,128)(2,1)S(1)} %pad_maximum_fusion), channel_id=1, source_target_pairs={{0,2},{1,3},{2,0},{3,1},{4,6},{5,7},{6,4},{7,5},{8,10},{9,11},{10,... | collective-permute-start | bytes 884744 | tf_op jit(solution)/shard_map/ppermute | solution.py:48
  16.4 0.0 collective-permute-start.6
  16.4 5.8 %collective-permute-done.4 = bf16[4,144,256]{2,1,0:T(8,128)(2,1)S(1)} collective-permute-done((bf16[4,144,256]{2,1,0:T(8,128)(2,1)S(1)}, bf16[4,144,256]{2,1,0:T(8,128)(2,1)S(1)}, u32[]{:S(2)}, u32[]{:S(2)}) %collective-permute-start.4) | collective-permute-done | bytes 294944 | tf_op jit(solution)/shard_map/ppermute | solution.py:49
  22.2 1.2 %collective-permute-done.3 = bf16[4,144,256]{2,1,0:T(8,128)(2,1)S(1)} collective-permute-done((bf16[4,144,256]{2,1,0:T(8,128)(2,1)S(1)}, bf16[4,144,256]{2,1,0:T(8,128)(2,1)S(1)}, u32[]{:S(2)}, u32[]{:S(2)}) %collective-permute-start.3) | collective-permute-done | bytes 294944 | tf_op jit(solution)/shard_map/ppermute | solution.py:48
  23.5 1.6 %collective-permute-start.5 = (bf16[4,144,256]{2,1,0:T(8,128)(2,1)S(1)}, bf16[4,144,256]{2,1,0:T(8,128)(2,1)}, u32[]{:S(2)}, u32[]{:S(2)}) collective-permute-start(bf16[4,144,256]{2,1,0:T(8,128)(2,1)S(1)} %broadcast_select_fusion), channel_id=1, source_target_pairs={{2,0},{5,1},{0,2},{7,3},{6,4},{1,5},{4,6},{3,7},{10,8},{13,9},{8,1... | collective-permute-start | bytes 884744 | tf_op jit(solution)/shard_map/ppermute | solution.py:54
  25.0 0.2 convolution_bitcast_fusion.7
  25.2 0.1 copy.6
  25.4 0.1 collective-permute-start.8
  25.4 0.5 %collective-permute-start.7 = (bf16[4,144,256]{2,1,0:T(8,128)(2,1)S(1)}, bf16[4,144,256]{2,1,0:T(8,128)(2,1)S(1)}, u32[]{:S(2)}, u32[]{:S(2)}) collective-permute-start(bf16[4,144,256]{2,1,0:T(8,128)(2,1)S(1)} %collective-permute-done.3), channel_id=1, source_target_pairs={{0,1},{1,0},{2,3},{3,2},{4,5},{5,4},{6,7},{7,6},{8,9},{9,8},{10,11... | collective-permute-start | bytes 884744 | tf_op jit(solution)/shard_map/ppermute | solution.py:58
  25.9 0.2 convolution_bitcast_fusion.5
  26.2 0.0 collective-permute-done.6
  26.2 1.2 %convolution_bitcast_fusion.3 = f32[128,144]{1,0:T(8,128)S(1)} fusion(bf16[4,144,256]{2,1,0:T(8,128)(2,1)} %collective-permute-done.6, bf16[4,128,2048]{2,1,0:T(8,128)(2,1)S(1)} %copy-done, s32[]{:T(128)S(6)} %select_n.54), kind=kOutput, calls=%fused_computation.4 | convolution fusion | flops 37748736 | bytes 630788 | tf_op jit(solution)/shard_map/rsk,rtk->st/dot_general | solution.py:33
  27.4 2.9 %collective-permute-done.5 = bf16[4,144,256]{2,1,0:T(8,128)(2,1)} collective-permute-done((bf16[4,144,256]{2,1,0:T(8,128)(2,1)S(1)}, bf16[4,144,256]{2,1,0:T(8,128)(2,1)}, u32[]{:S(2)}, u32[]{:S(2)}) %collective-permute-start.5) | collective-permute-done | bytes 294944 | tf_op jit(solution)/shard_map/ppermute | solution.py:54
  30.3 0.0 collective-permute-start.9
  30.4 1.2 %convolution_bitcast_fusion.4 = f32[128,144]{1,0:T(8,128)S(1)} fusion(bf16[4,144,256]{2,1,0:T(8,128)(2,1)} %collective-permute-done.5, bf16[4,128,2048]{2,1,0:T(8,128)(2,1)S(1)} %copy-done, s32[]{:T(128)S(6)} %select_n.50), kind=kOutput, calls=%fused_computation.5 | convolution fusion | flops 37748736 | bytes 630788 | tf_op jit(solution)/shard_map/rsk,rtk->st/dot_general | solution.py:33
  31.6 0.3 fusion.3
  31.8 0.0 collective-permute-done.8
  31.8 0.2 convolution_bitcast_fusion.1
  32.1 0.1 collective-permute-done.9
  32.1 0.2 convolution_bitcast_fusion
  32.4 0.0 collective-permute-done.7
  32.4 0.3 fusion.6
  32.7 0.4 convolution_convert_fusion
  33.0 0.1 copy.8
  33.1 8.1 %all_to_all.12 = bf16[8,32,192]{2,1,0:T(8,128)(2,1)S(1)} all-to-all(bf16[8,32,192]{2,1,0:T(8,128)(2,1)S(1)} %bitcast.47), channel_id=1, replica_groups=mesh['blk'=4,'rows'=8] {'rows'}, dimensions={0} | all-to-all | bytes 196608 | tf_op jit(solution)/shard_map/all_to_all | solution.py:80
  41.3 0.7 %copy.9 = bf16[256,192]{0,1:T(8,128)(2,1)} copy(bf16[256,192]{1,0:T(8,128)(2,1)S(1)} %bitcast.48) | data formatting | bytes 196608 | tf_op jit(solution)/shard_map/all_to_all | solution.py:80
  (4 shorter events, 0.1 us)
Async XLA Ops:
  0.0 8.0 %copy-start = (bf16[4,128,2048]{2,1,0:T(8,128)(2,1)S(1)}, bf16[4,128,2048]{2,1,0:T(8,128)(2,1)}, u32[]{:S(2)}) copy-start(bf16[4,128,2048]{2,1,0:T(8,128)(2,1)} %param.3) | copy-start | bytes 6291460
  0.0 10.0 %copy-start.1 = (s32[128,1]{0,1:T(1,128)S(1)}, s32[128,1]{0,1:T(1,128)}, u32[]{:S(2)}) copy-start(s32[128,1]{0,1:T(1,128)} %param.4) | copy-start | bytes 1540
  1.1 9.4 %collective-permute-start.2 = (bf16[4,48,256]{2,1,0:T(8,128)(2,1)S(1)}, bf16[4,48,256]{2,1,0:T(8,128)(2,1)S(1)}, u32[]{:S(2)}, u32[]{:S(2)}) collective-permute-start(bf16[4,48,256]{2,1,0:T(8,128)(2,1)S(1)} %constant_dynamic-slice_fusion), channel_id=1, source_target_pairs={{0,8},{8,16},{16,24},{24,0},{1,9},{9,17},{17,25},{25,1},{2,10},{10... | collective-permute-start | bytes 294920 | tf_op jit(solution)/shard_map/ppermute | solution.py:39
  4.1 9.2 %collective-permute-start.1 = (bf16[4,48,256]{2,1,0:T(8,128)(2,1)S(1)}, bf16[4,48,256]{2,1,0:T(8,128)(2,1)S(1)}, u32[]{:S(2)}, u32[]{:S(2)}) collective-permute-start(bf16[4,48,256]{2,1,0:T(8,128)(2,1)S(1)} %constant_dynamic-slice_fusion), channel_id=1, source_target_pairs={{0,16},{8,24},{16,0},{24,8},{1,17},{9,25},{17,1},{25,9},{2,18},{10... | collective-permute-start | bytes 294920 | tf_op jit(solution)/shard_map/ppermute | solution.py:39
  6.7 6.6 %collective-permute-start = (bf16[4,48,256]{2,1,0:T(8,128)(2,1)S(1)}, bf16[4,48,256]{2,1,0:T(8,128)(2,1)S(1)}, u32[]{:S(2)}, u32[]{:S(2)}) collective-permute-start(bf16[4,48,256]{2,1,0:T(8,128)(2,1)S(1)} %constant_dynamic-slice_fusion), channel_id=1, source_target_pairs={{0,24},{8,0},{16,8},{24,16},{1,25},{9,1},{17,9},{25,17},{2,26},{10... | collective-permute-start | bytes 294920 | tf_op jit(solution)/shard_map/ppermute | solution.py:39
  13.3 8.9 %collective-permute-start.4 = (bf16[4,144,256]{2,1,0:T(8,128)(2,1)S(1)}, bf16[4,144,256]{2,1,0:T(8,128)(2,1)S(1)}, u32[]{:S(2)}, u32[]{:S(2)}) collective-permute-start(bf16[4,144,256]{2,1,0:T(8,128)(2,1)S(1)} %pad_maximum_fusion), channel_id=1, source_target_pairs={{0,4},{1,5},{2,6},{3,7},{4,0},{5,1},{6,2},{7,3},{8,12},{9,13},{10,... | collective-permute-start | bytes 884744 | tf_op jit(solution)/shard_map/ppermute | solution.py:49
  14.9 8.5 %collective-permute-start.3 = (bf16[4,144,256]{2,1,0:T(8,128)(2,1)S(1)}, bf16[4,144,256]{2,1,0:T(8,128)(2,1)S(1)}, u32[]{:S(2)}, u32[]{:S(2)}) collective-permute-start(bf16[4,144,256]{2,1,0:T(8,128)(2,1)S(1)} %pad_maximum_fusion), channel_id=1, source_target_pairs={{0,2},{1,3},{2,0},{3,1},{4,6},{5,7},{6,4},{7,5},{8,10},{9,11},{10,... | collective-permute-start | bytes 884744 | tf_op jit(solution)/shard_map/ppermute | solution.py:48
  16.4 9.8 %collective-permute-start.6 = (bf16[4,144,256]{2,1,0:T(8,128)(2,1)S(1)}, bf16[4,144,256]{2,1,0:T(8,128)(2,1)}, u32[]{:S(2)}, u32[]{:S(2)}) collective-permute-start(bf16[4,144,256]{2,1,0:T(8,128)(2,1)S(1)} %pad_maximum_fusion), channel_id=1, source_target_pairs={{0,1},{1,0},{2,3},{3,2},{4,5},{5,4},{6,7},{7,6},{8,9},{9,8},{10,11... | collective-permute-start | bytes 884744 | tf_op jit(solution)/shard_map/ppermute | solution.py:58
  23.5 6.9 %collective-permute-start.5 = (bf16[4,144,256]{2,1,0:T(8,128)(2,1)S(1)}, bf16[4,144,256]{2,1,0:T(8,128)(2,1)}, u32[]{:S(2)}, u32[]{:S(2)}) collective-permute-start(bf16[4,144,256]{2,1,0:T(8,128)(2,1)S(1)} %broadcast_select_fusion), channel_id=1, source_target_pairs={{2,0},{5,1},{0,2},{7,3},{6,4},{1,5},{4,6},{3,7},{10,8},{13,9},{8,1... | collective-permute-start | bytes 884744 | tf_op jit(solution)/shard_map/ppermute | solution.py:54
  25.4 6.5 %collective-permute-start.8 = (bf16[4,144,256]{2,1,0:T(8,128)(2,1)S(1)}, bf16[4,144,256]{2,1,0:T(8,128)(2,1)S(1)}, u32[]{:S(2)}, u32[]{:S(2)}) collective-permute-start(bf16[4,144,256]{2,1,0:T(8,128)(2,1)S(1)} %collective-permute-done.4), channel_id=1, source_target_pairs={{0,1},{1,0},{2,3},{3,2},{4,5},{5,4},{6,7},{7,6},{8,9},{9,8},{10,11... | collective-permute-start | bytes 884744 | tf_op jit(solution)/shard_map/ppermute | solution.py:58
  25.4 6.9 %collective-permute-start.7 = (bf16[4,144,256]{2,1,0:T(8,128)(2,1)S(1)}, bf16[4,144,256]{2,1,0:T(8,128)(2,1)S(1)}, u32[]{:S(2)}, u32[]{:S(2)}) collective-permute-start(bf16[4,144,256]{2,1,0:T(8,128)(2,1)S(1)} %collective-permute-done.3), channel_id=1, source_target_pairs={{0,1},{1,0},{2,3},{3,2},{4,5},{5,4},{6,7},{7,6},{8,9},{9,8},{10,11... | collective-permute-start | bytes 884744 | tf_op jit(solution)/shard_map/ppermute | solution.py:58
  30.3 1.8 %collective-permute-start.9 = (bf16[4,144,256]{2,1,0:T(8,128)(2,1)}, bf16[4,144,256]{2,1,0:T(8,128)(2,1)S(1)}, u32[]{:S(2)}, u32[]{:S(2)}) collective-permute-start(bf16[4,144,256]{2,1,0:T(8,128)(2,1)} %collective-permute-done.5), channel_id=1, source_target_pairs={{0,1},{1,0},{2,3},{3,2},{4,5},{5,4},{6,7},{7,6},{8,9},{9,8},{10,11... | collective-permute-start | bytes 884744 | tf_op jit(solution)/shard_map/ppermute | solution.py:58

commit v15 on v8

--- a/solution.py
+++ b/solution.py
@@ -45,8 +45,8 @@
     chip_bits = [1 << i for i in range(1, owners_n.bit_length() - 1)]
     if len(chip_bits) == 2:
         bx, by = chip_bits
-        along_x = lax.ppermute(mine, "rows", xor_pairs(owners_n, bx))
-        along_y = lax.ppermute(mine, "rows", xor_pairs(owners_n, by))
+        along_x = jnp.concatenate([lax.ppermute(a, "rows", xor_pairs(owners_n, bx)) for a in arrived], axis=1)
+        along_y = jnp.concatenate([lax.ppermute(a, "rows", xor_pairs(owners_n, by)) for a in arrived], axis=1)
         remote = remote + term((here ^ bx) * chunk, chunk, along_x)
         remote = remote + term((here ^ by) * chunk, chunk, along_y)
         half = chunk // 2

time: 40.7 us -> 44.6 us (1.096)
  starting transfers between devices: 13.7 us -> 18.4 us
  waiting for transfers between devices: 11.4 us -> 9.34 us
  blocking collectives: 8.13 us -> 9.16 us
    ppermute x2 -> x6, starting transfers between devices: 3.08 us -> 8.14 us  [the longest x3 4.56 us: on_device(): lax.ppermute(a, 'rows', xor_pairs(owners_n, by))]
    ppermute x2 -> x6, waiting for transfers between devices: 5.42 us -> 2.26 us  [the longest x3 1.24 us: on_device(): lax.ppermute(a, 'rows', xor_pairs(owners_n, by))]
    ppermute x1, waiting for transfers between devices: 1.03 us -> 2.83 us  [on_device(): first = lax.ppermute(along_y[:, :, :half], 'rows', xor_pairs(owners_n, bx))]
    all_to_all x1, blocking collectives: 8.13 us -> 9.16 us  [on_device(): lax.all_to_all(placed, 'rows', split_axis=0, concat_axis=0, tiled=True)]
    ppermute x1, waiting for transfers between devices: 0.7 us -> 0.01 us  [on_device(): lax.ppermute(second, 'rows', sibling)]
  transfers between devices with their start and end apart: 12 -> 16, of which waited for: 5 -> 7; matrix products, arithmetic and copies ran while one was open for 11% -> 10% of each run, Pallas kernels for 0% -> 0%
where the time goes in v15:
time: 44.6 us; the launch traced here: 44.4 us
  starting transfers between devices  18.4 us (41%)
  waiting for transfers between devices  9.34 us (21%)
  blocking collectives  9.16 us (21%)
  matrix products  4.53 us (10%)
  local copies, waits for them, and re-layouts  2.12 us (5%)
  other arithmetic  0.48 us (1%)
    all_to_all x1, blocking collectives, on_device(): lax.all_to_all(placed, 'rows', split_axis=0, concat_axis=0, tiled=True)  9.16 us
    ppermute x3, starting transfers between devices, on_device(): arrived.append(lax.ppermute(piece, 'blk', pairs))  6.96 us
    ppermute x3, starting transfers between devices, on_device(): lax.ppermute(a, 'rows', xor_pairs(owners_n, by))  4.56 us
    ppermute x3, starting transfers between devices, on_device(): lax.ppermute(a, 'rows', xor_pairs(owners_n, bx))  3.58 us
    ppermute x1, waiting for transfers between devices, on_device(): first = lax.ppermute(along_y[:, :, :half], 'rows', xor_pairs(owners_n, bx))  2.83 us
    ppermute x3, waiting for transfers between devices, on_device(): arrived.append(lax.ppermute(piece, 'blk', pairs))  2.73 us
    dot_general x10, matrix products, term(): jnp.einsum('rsk,rtk->st', part, tests, preferred_element_type=jnp.float32)  2.21 us
    dot_general x1, matrix products, on_device(): jnp.einsum('rsk,rtk->st', features, test_blocks, preferred_element_type=j...  1.96 us
  transfers between devices with their start and end apart: 16, of which 7 were waited for; matrix products, arithmetic and copies ran while one was open for 10% of the time, Pallas kernels for 0%

profile of v15, /device:TPU:0, one launch (start us, length us, event | category | flops | bytes accessed | tf_op | source)
XLA Modules:
  0.0 44.4 jit_solution(4388297166197101986)
XLA Ops:
  0.0 0.0 copy-start
  0.0 0.0 copy-start.1
  0.0 1.0 %constant_dynamic-slice_fusion = bf16[4,48,256]{2,1,0:T(8,128)(2,1)S(1)} fusion(bf16[4,48,2048]{2,1,0:T(8,128)(2,1)} %param.5, s32[]{:T(128)S(6)} %select_n.41), kind=kLoop, calls=%fused_computation.62 | loop fusion | bytes 196612 | tf_op jit(solution)/shard_map/dynamic_slice | solution.py:35
  1.1 3.0 %collective-permute-start.2 = (bf16[4,48,256]{2,1,0:T(8,128)(2,1)S(1)}, bf16[4,48,256]{2,1,0:T(8,128)(2,1)S(1)}, u32[]{:S(2)}, u32[]{:S(2)}) collective-permute-start(bf16[4,48,256]{2,1,0:T(8,128)(2,1)S(1)} %constant_dynamic-slice_fusion), channel_id=1, source_target_pairs={{0,8},{8,16},{16,24},{24,0},{1,9},{9,17},{17,25},{25,1},{2,10},{10... | collective-permute-start | bytes 294920 | tf_op jit(solution)/shard_map/ppermute | solution.py:39
  4.1 2.6 %collective-permute-start.1 = (bf16[4,48,256]{2,1,0:T(8,128)(2,1)S(1)}, bf16[4,48,256]{2,1,0:T(8,128)(2,1)S(1)}, u32[]{:S(2)}, u32[]{:S(2)}) collective-permute-start(bf16[4,48,256]{2,1,0:T(8,128)(2,1)S(1)} %constant_dynamic-slice_fusion), channel_id=1, source_target_pairs={{0,16},{8,24},{16,0},{24,8},{1,17},{9,25},{17,1},{25,9},{2,18},{10... | collective-permute-start | bytes 294920 | tf_op jit(solution)/shard_map/ppermute | solution.py:39
  6.7 1.3 %collective-permute-start = (bf16[4,48,256]{2,1,0:T(8,128)(2,1)S(1)}, bf16[4,48,256]{2,1,0:T(8,128)(2,1)S(1)}, u32[]{:S(2)}, u32[]{:S(2)}) collective-permute-start(bf16[4,48,256]{2,1,0:T(8,128)(2,1)S(1)} %constant_dynamic-slice_fusion), channel_id=1, source_target_pairs={{0,24},{8,0},{16,8},{24,16},{1,25},{9,1},{17,9},{25,17},{2,26},{10... | collective-permute-start | bytes 294920 | tf_op jit(solution)/shard_map/ppermute | solution.py:39
  8.0 0.0 copy-done
  8.0 2.0 %convolution_bitcast_fusion.10 = bf16[128,48]{0,1:T(8,128)(2,1)S(1)} fusion(bf16[4,128,2048]{2,1,0:T(8,128)(2,1)S(1)} %copy-done, bf16[4,48,2048]{2,1,0:T(8,128)(2,1)} %param.5), kind=kOutput, calls=%fused_computation.20 | convolution fusion | flops 100663296 | bytes 2895872 | tf_op jit(solution)/shard_map/rsk,rtk->st/dot_general | solution.py:41
  10.0 0.0 copy-done.1
  10.0 0.1 fusion.25
  10.1 0.2 reduce_window_sum.11
  10.3 0.2 select_reduce_fusion
  10.6 0.0 collective-permute-done.2
  10.6 2.7 %collective-permute-done.1 = bf16[4,48,256]{2,1,0:T(8,128)(2,1)S(1)} collective-permute-done((bf16[4,48,256]{2,1,0:T(8,128)(2,1)S(1)}, bf16[4,48,256]{2,1,0:T(8,128)(2,1)S(1)}, u32[]{:S(2)}, u32[]{:S(2)}) %collective-permute-start.1) | collective-permute-done | bytes 98336 | tf_op jit(solution)/shard_map/ppermute | solution.py:39
  13.2 0.0 collective-permute-done
  13.3 0.1 copy.6
  13.4 0.1 collective-permute-start.11
  13.5 1.6 %collective-permute-start.3 = (bf16[4,48,256]{2,1,0:T(8,128)(2,1)S(1)}, bf16[4,48,256]{2,1,0:T(8,128)(2,1)S(1)}, u32[]{:S(2)}, u32[]{:S(2)}) collective-permute-start(bf16[4,48,256]{2,1,0:T(8,128)(2,1)S(1)} %collective-permute-done), channel_id=1, source_target_pairs={{0,2},{1,3},{2,0},{3,1},{4,6},{5,7},{6,4},{7,5},{8,10},{9,11},{10,... | collective-permute-start | bytes 294920 | tf_op jit(solution)/shard_map/ppermute | solution.py:48
  15.1 0.5 %collective-permute-start.4 = (bf16[4,48,256]{2,1,0:T(8,128)(2,1)S(1)}, bf16[4,48,256]{2,1,0:T(8,128)(2,1)S(1)}, u32[]{:S(2)}, u32[]{:S(2)}) collective-permute-start(bf16[4,48,256]{2,1,0:T(8,128)(2,1)S(1)} %collective-permute-done.1), channel_id=1, source_target_pairs={{0,2},{1,3},{2,0},{3,1},{4,6},{5,7},{6,4},{7,5},{8,10},{9,11},{10,... | collective-permute-start | bytes 294920 | tf_op jit(solution)/shard_map/ppermute | solution.py:48
  15.6 1.5 %collective-permute-start.5 = (bf16[4,48,256]{2,1,0:T(8,128)(2,1)S(1)}, bf16[4,48,256]{2,1,0:T(8,128)(2,1)S(1)}, u32[]{:S(2)}, u32[]{:S(2)}) collective-permute-start(bf16[4,48,256]{2,1,0:T(8,128)(2,1)S(1)} %collective-permute-done.2), channel_id=1, source_target_pairs={{0,2},{1,3},{2,0},{3,1},{4,6},{5,7},{6,4},{7,5},{8,10},{9,11},{10,... | collective-permute-start | bytes 294920 | tf_op jit(solution)/shard_map/ppermute | solution.py:48
  17.1 1.5 %collective-permute-start.6 = (bf16[4,48,256]{2,1,0:T(8,128)(2,1)S(1)}, bf16[4,48,256]{2,1,0:T(8,128)(2,1)S(1)}, u32[]{:S(2)}, u32[]{:S(2)}) collective-permute-start(bf16[4,48,256]{2,1,0:T(8,128)(2,1)S(1)} %collective-permute-done), channel_id=1, source_target_pairs={{0,4},{1,5},{2,6},{3,7},{4,0},{5,1},{6,2},{7,3},{8,12},{9,13},{10,... | collective-permute-start | bytes 294920 | tf_op jit(solution)/shard_map/ppermute | solution.py:49
  18.6 0.2 convolution_bitcast_fusion.5
  18.9 0.3 collective-permute-done.3
  19.2 1.5 %collective-permute-start.7 = (bf16[4,48,256]{2,1,0:T(8,128)(2,1)S(1)}, bf16[4,48,256]{2,1,0:T(8,128)(2,1)S(1)}, u32[]{:S(2)}, u32[]{:S(2)}) collective-permute-start(bf16[4,48,256]{2,1,0:T(8,128)(2,1)S(1)} %collective-permute-done.1), channel_id=1, source_target_pairs={{0,4},{1,5},{2,6},{3,7},{4,0},{5,1},{6,2},{7,3},{8,12},{9,13},{10,... | collective-permute-start | bytes 294920 | tf_op jit(solution)/shard_map/ppermute | solution.py:49
  20.7 0.6 %collective-permute-done.4 = bf16[4,48,256]{2,1,0:T(8,128)(2,1)S(1)} collective-permute-done((bf16[4,48,256]{2,1,0:T(8,128)(2,1)S(1)}, bf16[4,48,256]{2,1,0:T(8,128)(2,1)S(1)}, u32[]{:S(2)}, u32[]{:S(2)}) %collective-permute-start.4) | collective-permute-done | bytes 98336 | tf_op jit(solution)/shard_map/ppermute | solution.py:48
  21.3 1.5 %collective-permute-start.8 = (bf16[4,48,256]{2,1,0:T(8,128)(2,1)S(1)}, bf16[4,48,256]{2,1,0:T(8,128)(2,1)S(1)}, u32[]{:S(2)}, u32[]{:S(2)}) collective-permute-start(bf16[4,48,256]{2,1,0:T(8,128)(2,1)S(1)} %collective-permute-done.2), channel_id=1, source_target_pairs={{0,4},{1,5},{2,6},{3,7},{4,0},{5,1},{6,2},{7,3},{8,12},{9,13},{10,... | collective-permute-start | bytes 294920 | tf_op jit(solution)/shard_map/ppermute | solution.py:49
  22.8 0.1 collective-permute-done.5
  23.0 0.1 collective-permute-start.12
  23.1 0.0 collective-permute-done.6
  23.1 1.6 %collective-permute-start.10 = (bf16[4,144,128]{2,1,0:T(8,128)(2,1)S(1)}, bf16[4,144,128]{2,1,0:T(8,128)(2,1)S(1)}, u32[]{:S(2)}, u32[]{:S(2)}) collective-permute-start(bf16[4,144,128]{2,1,0:T(8,128)(2,1)S(1)} %slice.9), channel_id=1, source_target_pairs={{0,4},{1,5},{2,6},{3,7},{4,0},{5,1},{6,2},{7,3},{8,12},{9,13},{10,... | collective-permute-start | bytes 442376 | tf_op jit(solution)/shard_map/ppermute | solution.py:54
  24.7 0.0 collective-permute-done.7
  24.7 1.2 %collective-permute-done.8 = bf16[4,48,256]{2,1,0:T(8,128)(2,1)S(1)} collective-permute-done((bf16[4,48,256]{2,1,0:T(8,128)(2,1)S(1)}, bf16[4,48,256]{2,1,0:T(8,128)(2,1)S(1)}, u32[]{:S(2)}, u32[]{:S(2)}) %collective-permute-start.8) | collective-permute-done | bytes 98336 | tf_op jit(solution)/shard_map/ppermute | solution.py:49
  25.9 0.1 collective-permute-start.13
  26.1 1.5 %collective-permute-start.9 = (bf16[4,144,128]{2,1,0:T(8,128)(2,1)S(1)}, bf16[4,144,128]{2,1,0:T(8,128)(2,1)S(1)}, u32[]{:S(2)}, u32[]{:S(2)}) collective-permute-start(bf16[4,144,128]{2,1,0:T(8,128)(2,1)S(1)} %slice.8), channel_id=1, source_target_pairs={{0,2},{1,3},{2,0},{3,1},{4,6},{5,7},{6,4},{7,5},{8,10},{9,11},{10,... | collective-permute-start | bytes 442376 | tf_op jit(solution)/shard_map/ppermute | solution.py:53
  27.6 0.2 convolution_bitcast_fusion.3
  27.8 1.5 %collective-permute-done.10 = bf16[4,144,128]{2,1,0:T(8,128)(2,1)S(1)} collective-permute-done((bf16[4,144,128]{2,1,0:T(8,128)(2,1)S(1)}, bf16[4,144,128]{2,1,0:T(8,128)(2,1)S(1)}, u32[]{:S(2)}, u32[]{:S(2)}) %collective-permute-start.10) | collective-permute-done | bytes 147488 | tf_op jit(solution)/shard_map/ppermute | solution.py:54
  29.3 0.0 collective-permute-start.15
  29.3 0.2 convolution_bitcast_fusion.8
  29.5 2.8 %collective-permute-done.9 = bf16[4,144,128]{2,1,0:T(8,128)(2,1)S(1)} collective-permute-done((bf16[4,144,128]{2,1,0:T(8,128)(2,1)S(1)}, bf16[4,144,128]{2,1,0:T(8,128)(2,1)S(1)}, u32[]{:S(2)}, u32[]{:S(2)}) %collective-permute-start.9) | collective-permute-done | bytes 147488 | tf_op jit(solution)/shard_map/ppermute | solution.py:53
  32.4 0.0 collective-permute-start.14
  32.4 0.2 convolution_bitcast_fusion.9
  32.6 0.0 collective-permute-done.11
  32.6 0.2 convolution_bitcast_fusion.2
  32.8 0.0 collective-permute-done.13
  32.8 0.2 convolution_bitcast_fusion
  33.1 0.0 collective-permute-done.12
  33.1 0.2 convolution_bitcast_fusion.1
  33.3 0.2 fusion.8
  33.6 0.0 collective-permute-done.15
  33.6 0.2 convolution_bitcast_fusion.6
  33.8 0.0 collective-permute-done.14
  33.8 0.2 fusion.1
  34.0 0.4 convolution_convert_fusion
  34.4 0.1 copy.8
  34.5 9.2 %all_to_all.12 = bf16[8,32,192]{2,1,0:T(8,128)(2,1)S(1)} all-to-all(bf16[8,32,192]{2,1,0:T(8,128)(2,1)S(1)} %bitcast.57), channel_id=1, replica_groups=mesh['blk'=4,'rows'=8] {'rows'}, dimensions={0} | all-to-all | bytes 196608 | tf_op jit(solution)/shard_map/all_to_all | solution.py:84
  43.6 0.7 %copy.9 = bf16[256,192]{0,1:T(8,128)(2,1)} copy(bf16[256,192]{1,0:T(8,128)(2,1)S(1)} %bitcast.58) | data formatting | bytes 196608 | tf_op jit(solution)/shard_map/all_to_all | solution.py:84
  (11 shorter events, 0.2 us)
Async XLA Ops:
  0.0 8.0 %copy-start = (bf16[4,128,2048]{2,1,0:T(8,128)(2,1)S(1)}, bf16[4,128,2048]{2,1,0:T(8,128)(2,1)}, u32[]{:S(2)}) copy-start(bf16[4,128,2048]{2,1,0:T(8,128)(2,1)} %param.3) | copy-start | bytes 6291460
  0.0 10.0 %copy-start.1 = (s32[128,1]{0,1:T(1,128)S(1)}, s32[128,1]{0,1:T(1,128)}, u32[]{:S(2)}) copy-start(s32[128,1]{0,1:T(1,128)} %param.4) | copy-start | bytes 1540
  1.1 9.5 %collective-permute-start.2 = (bf16[4,48,256]{2,1,0:T(8,128)(2,1)S(1)}, bf16[4,48,256]{2,1,0:T(8,128)(2,1)S(1)}, u32[]{:S(2)}, u32[]{:S(2)}) collective-permute-start(bf16[4,48,256]{2,1,0:T(8,128)(2,1)S(1)} %constant_dynamic-slice_fusion), channel_id=1, source_target_pairs={{0,8},{8,16},{16,24},{24,0},{1,9},{9,17},{17,25},{25,1},{2,10},{10... | collective-permute-start | bytes 294920 | tf_op jit(solution)/shard_map/ppermute | solution.py:39
  4.1 9.2 %collective-permute-start.1 = (bf16[4,48,256]{2,1,0:T(8,128)(2,1)S(1)}, bf16[4,48,256]{2,1,0:T(8,128)(2,1)S(1)}, u32[]{:S(2)}, u32[]{:S(2)}) collective-permute-start(bf16[4,48,256]{2,1,0:T(8,128)(2,1)S(1)} %constant_dynamic-slice_fusion), channel_id=1, source_target_pairs={{0,16},{8,24},{16,0},{24,8},{1,17},{9,25},{17,1},{25,9},{2,18},{10... | collective-permute-start | bytes 294920 | tf_op jit(solution)/shard_map/ppermute | solution.py:39
  6.7 6.6 %collective-permute-start = (bf16[4,48,256]{2,1,0:T(8,128)(2,1)S(1)}, bf16[4,48,256]{2,1,0:T(8,128)(2,1)S(1)}, u32[]{:S(2)}, u32[]{:S(2)}) collective-permute-start(bf16[4,48,256]{2,1,0:T(8,128)(2,1)S(1)} %constant_dynamic-slice_fusion), channel_id=1, source_target_pairs={{0,24},{8,0},{16,8},{24,16},{1,25},{9,1},{17,9},{25,17},{2,26},{10... | collective-permute-start | bytes 294920 | tf_op jit(solution)/shard_map/ppermute | solution.py:39
  13.4 19.1 %collective-permute-start.11 = (bf16[4,144,256]{2,1,0:T(8,128)(2,1)S(1)}, bf16[4,144,256]{2,1,0:T(8,128)(2,1)S(1)}, u32[]{:S(2)}, u32[]{:S(2)}) collective-permute-start(bf16[4,144,256]{2,1,0:T(8,128)(2,1)S(1)} %pad_maximum_fusion), channel_id=1, source_target_pairs={{0,1},{1,0},{2,3},{3,2},{4,5},{5,4},{6,7},{7,6},{8,9},{9,8},{10,11... | collective-permute-start | bytes 884744 | tf_op jit(solution)/shard_map/ppermute | solution.py:59
  13.5 5.7 %collective-permute-start.3 = (bf16[4,48,256]{2,1,0:T(8,128)(2,1)S(1)}, bf16[4,48,256]{2,1,0:T(8,128)(2,1)S(1)}, u32[]{:S(2)}, u32[]{:S(2)}) collective-permute-start(bf16[4,48,256]{2,1,0:T(8,128)(2,1)S(1)} %collective-permute-done), channel_id=1, source_target_pairs={{0,2},{1,3},{2,0},{3,1},{4,6},{5,7},{6,4},{7,5},{8,10},{9,11},{10,... | collective-permute-start | bytes 294920 | tf_op jit(solution)/shard_map/ppermute | solution.py:48
  15.1 6.2 %collective-permute-start.4 = (bf16[4,48,256]{2,1,0:T(8,128)(2,1)S(1)}, bf16[4,48,256]{2,1,0:T(8,128)(2,1)S(1)}, u32[]{:S(2)}, u32[]{:S(2)}) collective-permute-start(bf16[4,48,256]{2,1,0:T(8,128)(2,1)S(1)} %collective-permute-done.1), channel_id=1, source_target_pairs={{0,2},{1,3},{2,0},{3,1},{4,6},{5,7},{6,4},{7,5},{8,10},{9,11},{10,... | collective-permute-start | bytes 294920 | tf_op jit(solution)/shard_map/ppermute | solution.py:48
  15.6 7.3 %collective-permute-start.5 = (bf16[4,48,256]{2,1,0:T(8,128)(2,1)S(1)}, bf16[4,48,256]{2,1,0:T(8,128)(2,1)S(1)}, u32[]{:S(2)}, u32[]{:S(2)}) collective-permute-start(bf16[4,48,256]{2,1,0:T(8,128)(2,1)S(1)} %collective-permute-done.2), channel_id=1, source_target_pairs={{0,2},{1,3},{2,0},{3,1},{4,6},{5,7},{6,4},{7,5},{8,10},{9,11},{10,... | collective-permute-start | bytes 294920 | tf_op jit(solution)/shard_map/ppermute | solution.py:48
  17.1 6.0 %collective-permute-start.6 = (bf16[4,48,256]{2,1,0:T(8,128)(2,1)S(1)}, bf16[4,48,256]{2,1,0:T(8,128)(2,1)S(1)}, u32[]{:S(2)}, u32[]{:S(2)}) collective-permute-start(bf16[4,48,256]{2,1,0:T(8,128)(2,1)S(1)} %collective-permute-done), channel_id=1, source_target_pairs={{0,4},{1,5},{2,6},{3,7},{4,0},{5,1},{6,2},{7,3},{8,12},{9,13},{10,... | collective-permute-start | bytes 294920 | tf_op jit(solution)/shard_map/ppermute | solution.py:49
  19.2 5.5 %collective-permute-start.7 = (bf16[4,48,256]{2,1,0:T(8,128)(2,1)S(1)}, bf16[4,48,256]{2,1,0:T(8,128)(2,1)S(1)}, u32[]{:S(2)}, u32[]{:S(2)}) collective-permute-start(bf16[4,48,256]{2,1,0:T(8,128)(2,1)S(1)} %collective-permute-done.1), channel_id=1, source_target_pairs={{0,4},{1,5},{2,6},{3,7},{4,0},{5,1},{6,2},{7,3},{8,12},{9,13},{10,... | collective-permute-start | bytes 294920 | tf_op jit(solution)/shard_map/ppermute | solution.py:49
  21.3 4.6 %collective-permute-start.8 = (bf16[4,48,256]{2,1,0:T(8,128)(2,1)S(1)}, bf16[4,48,256]{2,1,0:T(8,128)(2,1)S(1)}, u32[]{:S(2)}, u32[]{:S(2)}) collective-permute-start(bf16[4,48,256]{2,1,0:T(8,128)(2,1)S(1)} %collective-permute-done.2), channel_id=1, source_target_pairs={{0,4},{1,5},{2,6},{3,7},{4,0},{5,1},{6,2},{7,3},{8,12},{9,13},{10,... | collective-permute-start | bytes 294920 | tf_op jit(solution)/shard_map/ppermute | solution.py:49
  23.0 10.1 %collective-permute-start.12 = (bf16[4,144,256]{2,1,0:T(8,128)(2,1)S(1)}, bf16[4,144,256]{2,1,0:T(8,128)(2,1)S(1)}, u32[]{:S(2)}, u32[]{:S(2)}) collective-permute-start(bf16[4,144,256]{2,1,0:T(8,128)(2,1)S(1)} %constant_dynamic-update-slice_fusion), channel_id=1, source_target_pairs={{0,1},{1,0},{2,3},{3,2},{4,5},{5,4},{6,7},{7,6},{8,9},{9,8},{10,11... | collective-permute-start | bytes 884744 | tf_op jit(solution)/shard_map/ppermute | solution.py:59
  23.1 6.3 %collective-permute-start.10 = (bf16[4,144,128]{2,1,0:T(8,128)(2,1)S(1)}, bf16[4,144,128]{2,1,0:T(8,128)(2,1)S(1)}, u32[]{:S(2)}, u32[]{:S(2)}) collective-permute-start(bf16[4,144,128]{2,1,0:T(8,128)(2,1)S(1)} %slice.9), channel_id=1, source_target_pairs={{0,4},{1,5},{2,6},{3,7},{4,0},{5,1},{6,2},{7,3},{8,12},{9,13},{10,... | collective-permute-start | bytes 442376 | tf_op jit(solution)/shard_map/ppermute | solution.py:54
  25.9 6.9 %collective-permute-start.13 = (bf16[4,144,256]{2,1,0:T(8,128)(2,1)S(1)}, bf16[4,144,256]{2,1,0:T(8,128)(2,1)S(1)}, u32[]{:S(2)}, u32[]{:S(2)}) collective-permute-start(bf16[4,144,256]{2,1,0:T(8,128)(2,1)S(1)} %constant_dynamic-update-slice_fusion.3), channel_id=1, source_target_pairs={{0,1},{1,0},{2,3},{3,2},{4,5},{5,4},{6,7},{7,6},{8,9},{9,8},{10,11... | collective-permute-start | bytes 884744 | tf_op jit(solution)/shard_map/ppermute | solution.py:59
  26.1 6.3 %collective-permute-start.9 = (bf16[4,144,128]{2,1,0:T(8,128)(2,1)S(1)}, bf16[4,144,128]{2,1,0:T(8,128)(2,1)S(1)}, u32[]{:S(2)}, u32[]{:S(2)}) collective-permute-start(bf16[4,144,128]{2,1,0:T(8,128)(2,1)S(1)} %slice.8), channel_id=1, source_target_pairs={{0,2},{1,3},{2,0},{3,1},{4,6},{5,7},{6,4},{7,5},{8,10},{9,11},{10,... | collective-permute-start | bytes 442376 | tf_op jit(solution)/shard_map/ppermute | solution.py:53
  29.3 4.3 %collective-permute-start.15 = (bf16[4,144,128]{2,1,0:T(8,128)(2,1)S(1)}, bf16[4,144,128]{2,1,0:T(8,128)(2,1)S(1)}, u32[]{:S(2)}, u32[]{:S(2)}) collective-permute-start(bf16[4,144,128]{2,1,0:T(8,128)(2,1)S(1)} %collective-permute-done.10), channel_id=1, source_target_pairs={{0,1},{1,0},{2,3},{3,2},{4,5},{5,4},{6,7},{7,6},{8,9},{9,8},{10,11... | collective-permute-start | bytes 442376 | tf_op jit(solution)/shard_map/ppermute | solution.py:62
  32.4 1.4 %collective-permute-start.14 = (bf16[4,144,128]{2,1,0:T(8,128)(2,1)S(1)}, bf16[4,144,128]{2,1,0:T(8,128)(2,1)S(1)}, u32[]{:S(2)}, u32[]{:S(2)}) collective-permute-start(bf16[4,144,128]{2,1,0:T(8,128)(2,1)S(1)} %collective-permute-done.9), channel_id=1, source_target_pairs={{0,1},{1,0},{2,3},{3,2},{4,5},{5,4},{6,7},{7,6},{8,9},{9,8},{10,11... | collective-permute-start | bytes 442376 | tf_op jit(solution)/shard_map/ppermute | solution.py:61

commit v16 on v9

--- a/solution.py
+++ b/solution.py
@@ -32,7 +32,15 @@
         part = lax.dynamic_slice_in_dim(features, offset, size, axis=2)
         return jnp.einsum("rsk,rtk->st", part, tests, preferred_element_type=jnp.float32)
 
-    piece = lax.dynamic_slice_in_dim(test_blocks, here * chunk, chunk, axis=2)
+    chip_bits = [1 << i for i in range(1, owners_n.bit_length() - 1)]
+    paired = len(chip_bits) == 2
+    if paired:
+        core = here % 2
+        twin = ((here // 2) ^ (here // 4)) % 2
+        pair = 2 * core + twin
+        piece = lax.dynamic_slice_in_dim(test_blocks, pair * 2 * chunk, 2 * chunk, axis=2)
+    else:
+        piece = lax.dynamic_slice_in_dim(test_blocks, here * chunk, chunk, axis=2)
     arrived = []
     for step in range(1, blocks_n):
         pairs = [(b, (b - step) % blocks_n) for b in range(blocks_n)]
@@ -41,20 +49,22 @@
     own = jnp.einsum("rsk,rtk->st", features, test_blocks, preferred_element_type=jnp.float32)
     slotting = slot_matrix(owner_ids, owners_n, capacity)
     mine, own, slotting = lax.optimization_barrier((mine, own, slotting))
-    remote = term(here * chunk, chunk, mine)
-    chip_bits = [1 << i for i in range(1, owners_n.bit_length() - 1)]
-    if len(chip_bits) == 2:
+    if paired:
         bx, by = chip_bits
-        along_x = lax.ppermute(mine, "rows", xor_pairs(owners_n, bx))
-        along_y = lax.ppermute(mine, "rows", xor_pairs(owners_n, by))
-        remote = remote + term((here ^ bx) * chunk, chunk, along_x)
-        remote = remote + term((here ^ by) * chunk, chunk, along_y)
-        across = lax.ppermute(mine, "rows", xor_pairs(owners_n, bx ^ by))
-        remote = remote + term((here ^ bx ^ by) * chunk, chunk, across)
+        other = 2 * core + 1 - twin
+        remote = term(pair * 2 * chunk, 2 * chunk, mine)
+        along_x = lax.ppermute(mine[:, :, :chunk], "rows", xor_pairs(owners_n, bx))
+        along_y = lax.ppermute(mine[:, :, chunk:], "rows", xor_pairs(owners_n, by))
+        remote = remote + term(other * 2 * chunk, chunk, along_x)
+        remote = remote + term(other * 2 * chunk + chunk, chunk, along_y)
         sibling = xor_pairs(owners_n, 1)
-        for mask, got in ((0, mine), (bx, along_x), (by, along_y), (bx ^ by, across)):
-            remote = remote + term((here ^ 1 ^ mask) * chunk, chunk, lax.ppermute(got, "rows", sibling))
+        far = 2 * (1 - core) + twin
+        near = 2 * (1 - core) + 1 - twin
+        remote = remote + term(far * 2 * chunk, 2 * chunk, lax.ppermute(mine, "rows", sibling))
+        remote = remote + term(near * 2 * chunk, chunk, lax.ppermute(along_x, "rows", sibling))
+        remote = remote + term(near * 2 * chunk + chunk, chunk, lax.ppermute(along_y, "rows", sibling))
     else:
+        remote = term(here * chunk, chunk, mine)
         held = mine[None]
         masks = [0]
         for mask in chip_bits:

time: 42.5 us -> 48 us (1.13)
  waiting for transfers between devices: 15.1 us -> 18.8 us
  other arithmetic: 0.48 us -> 2.46 us
  starting transfers between devices: 11 us -> 9.2 us
  local copies, waits for them, and re-layouts: 2.02 us -> 2.92 us
  matrix products: 5.24 us -> 5.88 us
    ppermute x3, waiting for transfers between devices: 2.8 us -> 11.3 us  [on_device(): arrived.append(lax.ppermute(piece, 'blk', pairs))]
    ppermute x7 -> x5, waiting for transfers between devices: 12.3 us -> 7.51 us  [the longest x1 6.26 us: on_device(): along_y = lax.ppermute(mine[:, :, chunk:], 'rows', xor_pairs(owners_n, by))]
    ppermute x7 -> x5, starting transfers between devices: 3.99 us -> 3.09 us  [the longest x1 1.52 us: on_device(): along_y = lax.ppermute(mine[:, :, chunk:], 'rows', xor_pairs(owners_n, by))]
    slice x0 -> x1, local copies, waits for them, and re-layouts: none -> 0.87 us  [on_device(): along_x = lax.ppermute(mine[:, :, :chunk], 'rows', xor_pairs(owners_n, bx))]
    ppermute x3, starting transfers between devices: 6.96 us -> 6.11 us  [on_device(): arrived.append(lax.ppermute(piece, 'blk', pairs))]
    add x1, other arithmetic: 0.01 us -> 0.67 us  [slot_matrix(): slot = owner * capacity + rank]
    reduce_sum x1, other arithmetic: 0.17 us -> 0.83 us  [slot_matrix(): rank = jnp.sum(before * onehot, axis=1)]
    convert_element_type x1, other arithmetic: 0.08 us -> 0.73 us  [slot_matrix(): (owner[:, None] == jnp.arange(owners_n, dtype=jnp.int32)[None, :]).astype...]
  transfers between devices with their start and end apart: 10 -> 8, of which waited for: 4 -> 3; matrix products, arithmetic and copies ran while one was open for 12% -> 18% of each run, Pallas kernels for 0% -> 0%
where the time goes in v16:
time: 48 us; the launch traced here: 47.7 us
  waiting for transfers between devices  18.8 us (39%)
  starting transfers between devices  9.2 us (19%)
  blocking collectives  8.33 us (17%)
  matrix products  5.88 us (12%)
  local copies, waits for them, and re-layouts  2.92 us (6%)
  other arithmetic  2.46 us (5%)
    ppermute x3, waiting for transfers between devices, on_device(): arrived.append(lax.ppermute(piece, 'blk', pairs))  11.3 us
    all_to_all x1, blocking collectives, on_device(): lax.all_to_all(placed, 'rows', split_axis=0, concat_axis=0, tiled=True)  8.33 us
    ppermute x1, waiting for transfers between devices, on_device(): along_y = lax.ppermute(mine[:, :, chunk:], 'rows', xor_pairs(owners_n, by))  6.26 us
    ppermute x3, starting transfers between devices, on_device(): arrived.append(lax.ppermute(piece, 'blk', pairs))  6.11 us
    dot_general x6, matrix products, term(): jnp.einsum('rsk,rtk->st', part, tests, preferred_element_type=jnp.float32)  3.56 us
    dot_general x1, matrix products, on_device(): jnp.einsum('rsk,rtk->st', features, test_blocks, preferred_element_type=j...  1.96 us
    ppermute x1, starting transfers between devices, on_device(): along_y = lax.ppermute(mine[:, :, chunk:], 'rows', xor_pairs(owners_n, by))  1.52 us
    ppermute x1, starting transfers between devices, on_device(): along_x = lax.ppermute(mine[:, :, :chunk], 'rows', xor_pairs(owners_n, bx))  1.49 us
  transfers between devices with their start and end apart: 8, of which 3 were waited for; matrix products, arithmetic and copies ran while one was open for 18% of the time, Pallas kernels for 0%

profile of v16, /device:TPU:0, one launch (start us, length us, event | category | flops | bytes accessed | tf_op | source)
XLA Modules:
  0.0 47.7 jit_solution(16467092458062381140)
XLA Ops:
  0.0 0.0 copy-start
  0.0 1.1 %constant_dynamic-slice_fusion = bf16[4,48,512]{2,1,0:T(8,128)(2,1)S(1)} fusion(bf16[4,48,2048]{2,1,0:T(8,128)(2,1)} %param.5, s32[]{:T(128)S(6)} %select_n.48), kind=kLoop, calls=%fused_computation.40 | loop fusion | bytes 393220 | tf_op jit(solution)/shard_map/dynamic_slice | solution.py:41
  1.1 5.1 %collective-permute-start = (bf16[4,48,512]{2,1,0:T(8,128)(2,1)S(1)}, bf16[4,48,512]{2,1,0:T(8,128)(2,1)S(1)}, u32[]{:S(2)}, u32[]{:S(2)}) collective-permute-start(bf16[4,48,512]{2,1,0:T(8,128)(2,1)S(1)} %constant_dynamic-slice_fusion), channel_id=1, source_target_pairs={{0,24},{8,0},{16,8},{24,16},{1,25},{9,1},{17,9},{25,17},{2,26},{10... | collective-permute-start | bytes 589832 | tf_op jit(solution)/shard_map/ppermute | solution.py:47
  6.2 0.0 collective-permute-start.1
  6.2 1.0 %collective-permute-start.2 = (bf16[4,48,512]{2,1,0:T(8,128)(2,1)S(1)}, bf16[4,48,512]{2,1,0:T(8,128)(2,1)S(1)}, u32[]{:S(2)}, u32[]{:S(2)}) collective-permute-start(bf16[4,48,512]{2,1,0:T(8,128)(2,1)S(1)} %constant_dynamic-slice_fusion), channel_id=1, source_target_pairs={{0,8},{8,16},{16,24},{24,0},{1,9},{9,17},{17,25},{25,1},{2,10},{10... | collective-permute-start | bytes 589832 | tf_op jit(solution)/shard_map/ppermute | solution.py:47
  7.2 0.7 %fusion.17 = s32[128,8]{1,0:T(8,128)S(1)} fusion(s32[128]{0:T(128)} %bitcast.39), kind=kLoop, calls=%fused_computation.32 | loop fusion | flops 2048 | bytes 4608 | tf_op jit(solution)/shard_map/convert_element_type | solution.py:9
  8.0 0.2 reduce_window_sum.11
  8.1 0.8 %select_reduce_fusion = s32[128]{0:T(128)S(1)} fusion(s32[128,8]{1,0:T(8,128)S(1)} %reduce_window_sum.11, s32[128]{0:T(128)} %bitcast.40), kind=kLoop, calls=%fused_computation.30 | loop fusion | flops 4992 | bytes 5120 | tf_op jit(solution)/shard_map/reduce_sum | solution.py:11
  9.0 0.7 %multiply_add_fusion = s32[128]{0:T(128)S(1)} fusion(s32[128]{0:T(128)S(1)} %select_reduce_fusion, s32[128,1]{0,1:T(1,128)} %param.4), kind=kLoop, calls=%fused_computation.41 | loop fusion | flops 256 | bytes 1536 | tf_op jit(solution)/shard_map/add | solution.py:12
  9.6 0.0 copy-done
  9.6 2.0 %convolution_bitcast_fusion.6 = bf16[128,48]{0,1:T(8,128)(2,1)S(1)} fusion(bf16[4,128,2048]{2,1,0:T(8,128)(2,1)S(1)} %copy-done, bf16[4,48,2048]{2,1,0:T(8,128)(2,1)} %param.5), kind=kOutput, calls=%fused_computation.12 | convolution fusion | flops 100663296 | bytes 2895872 | tf_op jit(solution)/shard_map/rsk,rtk->st/dot_general | solution.py:49
  11.6 0.0 collective-permute-done
  11.6 11.3 %collective-permute-done.1 = bf16[4,48,512]{2,1,0:T(8,128)(2,1)S(1)} collective-permute-done((bf16[4,48,512]{2,1,0:T(8,128)(2,1)S(1)}, bf16[4,48,512]{2,1,0:T(8,128)(2,1)S(1)}, u32[]{:S(2)}, u32[]{:S(2)}) %collective-permute-start.1) | collective-permute-done | bytes 196640 | tf_op jit(solution)/shard_map/ppermute | solution.py:47
  22.9 0.0 collective-permute-done.2
  22.9 0.1 collective-permute-start.5
  23.0 0.9 %fusion.26 = (bf16[4,144,256]{2,1,0:T(8,128)(2,1)}, bf16[4,144,256]{2,1,0:T(8,128)(2,1)}) fusion(bf16[4,144,512]{2,1,0:T(8,128)(2,1)S(1)} %pad_maximum_fusion), kind=kLoop, calls=%fused_computation.43 | loop fusion | bytes 1179648 | tf_op jit(solution)/shard_map/slice | solution.py:56
  23.9 1.5 %collective-permute-start.4 = (bf16[4,144,256]{2,1,0:T(8,128)(2,1)}, bf16[4,144,256]{2,1,0:T(8,128)(2,1)}, u32[]{:S(2)}, u32[]{:S(2)}) collective-permute-start(bf16[4,144,256]{2,1,0:T(8,128)(2,1)} %get-tuple-element.12), channel_id=1, source_target_pairs={{0,4},{1,5},{2,6},{3,7},{4,0},{5,1},{6,2},{7,3},{8,12},{9,13},{10,... | collective-permute-start | bytes 884744 | tf_op jit(solution)/shard_map/ppermute | solution.py:57
  25.4 1.5 %collective-permute-start.3 = (bf16[4,144,256]{2,1,0:T(8,128)(2,1)}, bf16[4,144,256]{2,1,0:T(8,128)(2,1)}, u32[]{:S(2)}, u32[]{:S(2)}) collective-permute-start(bf16[4,144,256]{2,1,0:T(8,128)(2,1)} %get-tuple-element.11), channel_id=1, source_target_pairs={{0,2},{1,3},{2,0},{3,1},{4,6},{5,7},{6,4},{7,5},{8,10},{9,11},{10,... | collective-permute-start | bytes 884744 | tf_op jit(solution)/shard_map/ppermute | solution.py:56
  26.9 0.1 copy.6
  27.0 0.3 convolution_bitcast_fusion.5
  27.3 6.3 %collective-permute-done.4 = bf16[4,144,256]{2,1,0:T(8,128)(2,1)} collective-permute-done((bf16[4,144,256]{2,1,0:T(8,128)(2,1)}, bf16[4,144,256]{2,1,0:T(8,128)(2,1)}, u32[]{:S(2)}, u32[]{:S(2)}) %collective-permute-start.4) | collective-permute-done | bytes 294944 | tf_op jit(solution)/shard_map/ppermute | solution.py:57
  33.6 0.0 collective-permute-start.7
  33.6 1.2 %collective-permute-done.3 = bf16[4,144,256]{2,1,0:T(8,128)(2,1)} collective-permute-done((bf16[4,144,256]{2,1,0:T(8,128)(2,1)}, bf16[4,144,256]{2,1,0:T(8,128)(2,1)}, u32[]{:S(2)}, u32[]{:S(2)}) %collective-permute-start.3) | collective-permute-done | bytes 294944 | tf_op jit(solution)/shard_map/ppermute | solution.py:56
  34.9 0.0 collective-permute-start.6
  34.9 1.2 %convolution_bitcast_fusion.3 = f32[128,144]{1,0:T(8,128)S(1)} fusion(bf16[4,144,256]{2,1,0:T(8,128)(2,1)} %collective-permute-done.4, bf16[4,128,2048]{2,1,0:T(8,128)(2,1)S(1)} %copy-done, s32[]{:T(128)S(6)} %select_n.50), kind=kOutput, calls=%fused_computation.4 | convolution fusion | flops 37748736 | bytes 630788 | tf_op jit(solution)/shard_map/rsk,rtk->st/dot_general | solution.py:33
  36.1 0.0 collective-permute-done.5
  36.1 0.3 convolution_bitcast_fusion.2
  36.4 1.2 %fusion.2 = f32[128,144]{1,0:T(8,128)S(1)} fusion(f32[128,144]{1,0:T(8,128)S(1)} %convolution_bitcast_fusion.2, f32[128,144]{1,0:T(8,128)S(1)} %convolution_bitcast_fusion.3, f32[128,144]{1,0:T(8,128)S(1)} %convolution_bitcast_fusion.5, bf16[4,144,256]{2,1,0:T(8,128)(2,1)} %collective-permute-done.3, bf16[4,128,2048]{2,1,0:T(8,128)(2,1)S(1)} %copy-done, ...), kind=kOutput, calls=%fused_computation.9 | convolution fusion | flops 37804032 | bytes 1024004 | tf_op jit(solution)/shard_map/rsk,rtk->st/dot_general | solution.py:33
  37.6 0.0 collective-permute-done.7
  37.7 0.2 convolution_bitcast_fusion
  37.9 0.0 collective-permute-done.6
  37.9 0.2 fusion.4
  38.2 0.4 convolution_convert_fusion
  38.5 0.1 copy.8
  38.6 8.3 %all_to_all.12 = bf16[8,32,192]{2,1,0:T(8,128)(2,1)S(1)} all-to-all(bf16[8,32,192]{2,1,0:T(8,128)(2,1)S(1)} %bitcast.37), channel_id=1, replica_groups=mesh['blk'=4,'rows'=8] {'rows'}, dimensions={0} | all-to-all | bytes 196608 | tf_op jit(solution)/shard_map/all_to_all | solution.py:88
  47.0 0.7 %copy.9 = bf16[256,192]{0,1:T(8,128)(2,1)} copy(bf16[256,192]{1,0:T(8,128)(2,1)S(1)} %bitcast.38) | data formatting | bytes 196608 | tf_op jit(solution)/shard_map/all_to_all | solution.py:88
  (2 shorter events, 0.1 us)
Async XLA Ops:
  0.0 9.6 %copy-start = (bf16[4,128,2048]{2,1,0:T(8,128)(2,1)S(1)}, bf16[4,128,2048]{2,1,0:T(8,128)(2,1)}, u32[]{:S(2)}) copy-start(bf16[4,128,2048]{2,1,0:T(8,128)(2,1)} %param.3) | copy-start | bytes 6291460
  1.1 10.5 %collective-permute-start = (bf16[4,48,512]{2,1,0:T(8,128)(2,1)S(1)}, bf16[4,48,512]{2,1,0:T(8,128)(2,1)S(1)}, u32[]{:S(2)}, u32[]{:S(2)}) collective-permute-start(bf16[4,48,512]{2,1,0:T(8,128)(2,1)S(1)} %constant_dynamic-slice_fusion), channel_id=1, source_target_pairs={{0,24},{8,0},{16,8},{24,16},{1,25},{9,1},{17,9},{25,17},{2,26},{10... | collective-permute-start | bytes 589832 | tf_op jit(solution)/shard_map/ppermute | solution.py:47
  6.2 16.7 %collective-permute-start.1 = (bf16[4,48,512]{2,1,0:T(8,128)(2,1)S(1)}, bf16[4,48,512]{2,1,0:T(8,128)(2,1)S(1)}, u32[]{:S(2)}, u32[]{:S(2)}) collective-permute-start(bf16[4,48,512]{2,1,0:T(8,128)(2,1)S(1)} %constant_dynamic-slice_fusion), channel_id=1, source_target_pairs={{0,16},{8,24},{16,0},{24,8},{1,17},{9,25},{17,1},{25,9},{2,18},{10... | collective-permute-start | bytes 589832 | tf_op jit(solution)/shard_map/ppermute | solution.py:47
  6.2 16.7 %collective-permute-start.2 = (bf16[4,48,512]{2,1,0:T(8,128)(2,1)S(1)}, bf16[4,48,512]{2,1,0:T(8,128)(2,1)S(1)}, u32[]{:S(2)}, u32[]{:S(2)}) collective-permute-start(bf16[4,48,512]{2,1,0:T(8,128)(2,1)S(1)} %constant_dynamic-slice_fusion), channel_id=1, source_target_pairs={{0,8},{8,16},{16,24},{24,0},{1,9},{9,17},{17,25},{25,1},{2,10},{10... | collective-permute-start | bytes 589832 | tf_op jit(solution)/shard_map/ppermute | solution.py:47
  22.9 13.1 %collective-permute-start.5 = (bf16[4,144,512]{2,1,0:T(8,128)(2,1)S(1)}, bf16[4,144,512]{2,1,0:T(8,128)(2,1)S(1)}, u32[]{:S(2)}, u32[]{:S(2)}) collective-permute-start(bf16[4,144,512]{2,1,0:T(8,128)(2,1)S(1)} %pad_maximum_fusion), channel_id=1, source_target_pairs={{0,1},{1,0},{2,3},{3,2},{4,5},{5,4},{6,7},{7,6},{8,9},{9,8},{10,11... | collective-permute-start | bytes 1769480 | tf_op jit(solution)/shard_map/ppermute | solution.py:63
  23.9 9.7 %collective-permute-start.4 = (bf16[4,144,256]{2,1,0:T(8,128)(2,1)}, bf16[4,144,256]{2,1,0:T(8,128)(2,1)}, u32[]{:S(2)}, u32[]{:S(2)}) collective-permute-start(bf16[4,144,256]{2,1,0:T(8,128)(2,1)} %get-tuple-element.12), channel_id=1, source_target_pairs={{0,4},{1,5},{2,6},{3,7},{4,0},{5,1},{6,2},{7,3},{8,12},{9,13},{10,... | collective-permute-start | bytes 884744 | tf_op jit(solution)/shard_map/ppermute | solution.py:57
  25.4 9.4 %collective-permute-start.3 = (bf16[4,144,256]{2,1,0:T(8,128)(2,1)}, bf16[4,144,256]{2,1,0:T(8,128)(2,1)}, u32[]{:S(2)}, u32[]{:S(2)}) collective-permute-start(bf16[4,144,256]{2,1,0:T(8,128)(2,1)} %get-tuple-element.11), channel_id=1, source_target_pairs={{0,2},{1,3},{2,0},{3,1},{4,6},{5,7},{6,4},{7,5},{8,10},{9,11},{10,... | collective-permute-start | bytes 884744 | tf_op jit(solution)/shard_map/ppermute | solution.py:56
  33.6 4.0 %collective-permute-start.7 = (bf16[4,144,256]{2,1,0:T(8,128)(2,1)}, bf16[4,144,256]{2,1,0:T(8,128)(2,1)S(1)}, u32[]{:S(2)}, u32[]{:S(2)}) collective-permute-start(bf16[4,144,256]{2,1,0:T(8,128)(2,1)} %collective-permute-done.4), channel_id=1, source_target_pairs={{0,1},{1,0},{2,3},{3,2},{4,5},{5,4},{6,7},{7,6},{8,9},{9,8},{10,11... | collective-permute-start | bytes 884744 | tf_op jit(solution)/shard_map/ppermute | solution.py:65
  34.9 3.1 %collective-permute-start.6 = (bf16[4,144,256]{2,1,0:T(8,128)(2,1)}, bf16[4,144,256]{2,1,0:T(8,128)(2,1)S(1)}, u32[]{:S(2)}, u32[]{:S(2)}) collective-permute-start(bf16[4,144,256]{2,1,0:T(8,128)(2,1)} %collective-permute-done.3), channel_id=1, source_target_pairs={{0,1},{1,0},{2,3},{3,2},{4,5},{5,4},{6,7},{7,6},{8,9},{9,8},{10,11... | collective-permute-start | bytes 884744 | tf_op jit(solution)/shard_map/ppermute | solution.py:64

commit v17 on v8

--- a/solution.py
+++ b/solution.py
@@ -33,12 +33,13 @@
         return jnp.einsum("rsk,rtk->st", part, tests, preferred_element_type=jnp.float32)
 
     piece = lax.dynamic_slice_in_dim(test_blocks, here * chunk, chunk, axis=2)
+    own = jnp.einsum("rsk,rtk->st", features, test_blocks, preferred_element_type=jnp.float32)
+    piece, own = lax.optimization_barrier((piece, own))
     arrived = []
     for step in range(1, blocks_n):
         pairs = [(b, (b - step) % blocks_n) for b in range(blocks_n)]
         arrived.append(lax.ppermute(piece, "blk", pairs))
     mine = jnp.concatenate(arrived, axis=1)
-    own = jnp.einsum("rsk,rtk->st", features, test_blocks, preferred_element_type=jnp.float32)
     slotting = slot_matrix(owner_ids, owners_n, capacity)
     mine, own, slotting = lax.optimization_barrier((mine, own, slotting))
     remote = term(here * chunk, chunk, mine)

time: 40.7 us -> 44.1 us (1.084)
  waiting for transfers between devices: 11.4 us -> 13.3 us
  local copies, waits for them, and re-layouts: 2.07 us -> 3.51 us
    ppermute x3, waiting for transfers between devices: 2.8 us -> 4.79 us  [on_device(): arrived.append(lax.ppermute(piece, 'blk', pairs))]
    unnamed x4, local copies, waits for them, and re-layouts: 0.01 us -> 1.59 us
  transfers between devices with their start and end apart: 12 -> 12, of which waited for: 5 -> 6; matrix products, arithmetic and copies ran while one was open for 11% -> 6% of each run, Pallas kernels for 0% -> 0%
where the time goes in v17:
time: 44.1 us; the launch traced here: 43.9 us
  starting transfers between devices  13.7 us (31%)
  waiting for transfers between devices  13.3 us (30%)
  blocking collectives  8.12 us (18%)
  matrix products  4.56 us (10%)
  local copies, waits for them, and re-layouts  3.51 us (8%)
  other arithmetic  0.47 us (1%)
    all_to_all x1, blocking collectives, on_device(): lax.all_to_all(placed, 'rows', split_axis=0, concat_axis=0, tiled=True)  8.12 us
    ppermute x3, starting transfers between devices, on_device(): arrived.append(lax.ppermute(piece, 'blk', pairs))  6.96 us
    ppermute x1, waiting for transfers between devices, on_device(): along_y = lax.ppermute(mine, 'rows', xor_pairs(owners_n, by))  5.4 us
    ppermute x3, waiting for transfers between devices, on_device(): arrived.append(lax.ppermute(piece, 'blk', pairs))  4.79 us
    dot_general x10, matrix products, term(): jnp.einsum('rsk,rtk->st', part, tests, preferred_element_type=jnp.float32)  2.24 us
    dot_general x1, matrix products, on_device(): jnp.einsum('rsk,rtk->st', features, test_blocks, preferred_element_type=j...  1.96 us
    unnamed x4, local copies, waits for them, and re-layouts  1.59 us
    ppermute x1, starting transfers between devices, on_device(): second = lax.ppermute(along_x[:, :, half:], 'rows', xor_pairs(owners_n, by))  1.59 us
  transfers between devices with their start and end apart: 12, of which 6 were waited for; matrix products, arithmetic and copies ran while one was open for 6% of the time, Pallas kernels for 0%

profile of v17, /device:TPU:0, one launch (start us, length us, event | category | flops | bytes accessed | tf_op | source)
XLA Modules:
  0.0 43.9 jit_solution(4024280361013051029)
XLA Ops:
  0.0 0.0 copy-start
  0.0 0.0 copy-start.1
  0.0 1.6 %copy-done = bf16[4,128,2048]{2,1,0:T(8,128)(2,1)S(1)} copy-done((bf16[4,128,2048]{2,1,0:T(8,128)(2,1)S(1)}, bf16[4,128,2048]{2,1,0:T(8,128)(2,1)}, u32[]{:S(2)}) %copy-start) | copy-done | bytes 2097176
  1.6 2.0 %convolution_bitcast_fusion.10 = bf16[128,48]{0,1:T(8,128)(2,1)S(1)} fusion(bf16[4,128,2048]{2,1,0:T(8,128)(2,1)S(1)} %copy-done, bf16[4,48,2048]{2,1,0:T(8,128)(2,1)} %param.5), kind=kOutput, calls=%fused_computation.20 | convolution fusion | flops 100663296 | bytes 2895872 | tf_op jit(solution)/shard_map/rsk,rtk->st/dot_general | solution.py:36
  3.6 0.9 %constant_dynamic-slice_fusion = bf16[4,48,256]{2,1,0:T(8,128)(2,1)S(1)} fusion(bf16[4,48,2048]{2,1,0:T(8,128)(2,1)} %param.5, s32[]{:T(128)S(6)} %select_n.41), kind=kLoop, calls=%fused_computation.56 | loop fusion | bytes 196612 | tf_op jit(solution)/shard_map/dynamic_slice | solution.py:35
  4.5 3.0 %collective-permute-start.2 = (bf16[4,48,256]{2,1,0:T(8,128)(2,1)S(1)}, bf16[4,48,256]{2,1,0:T(8,128)(2,1)S(1)}, u32[]{:S(2)}, u32[]{:S(2)}) collective-permute-start(bf16[4,48,256]{2,1,0:T(8,128)(2,1)S(1)} %constant_dynamic-slice_fusion), channel_id=1, source_target_pairs={{0,8},{8,16},{16,24},{24,0},{1,9},{9,17},{17,25},{25,1},{2,10},{10... | collective-permute-start | bytes 294920 | tf_op jit(solution)/shard_map/ppermute | solution.py:41
  7.5 2.6 %collective-permute-start.1 = (bf16[4,48,256]{2,1,0:T(8,128)(2,1)S(1)}, bf16[4,48,256]{2,1,0:T(8,128)(2,1)S(1)}, u32[]{:S(2)}, u32[]{:S(2)}) collective-permute-start(bf16[4,48,256]{2,1,0:T(8,128)(2,1)S(1)} %constant_dynamic-slice_fusion), channel_id=1, source_target_pairs={{0,16},{8,24},{16,0},{24,8},{1,17},{9,25},{17,1},{25,9},{2,18},{10... | collective-permute-start | bytes 294920 | tf_op jit(solution)/shard_map/ppermute | solution.py:41
  10.1 1.3 %collective-permute-start = (bf16[4,48,256]{2,1,0:T(8,128)(2,1)S(1)}, bf16[4,48,256]{2,1,0:T(8,128)(2,1)S(1)}, u32[]{:S(2)}, u32[]{:S(2)}) collective-permute-start(bf16[4,48,256]{2,1,0:T(8,128)(2,1)S(1)} %constant_dynamic-slice_fusion), channel_id=1, source_target_pairs={{0,24},{8,0},{16,8},{24,16},{1,25},{9,1},{17,9},{25,17},{2,26},{10... | collective-permute-start | bytes 294920 | tf_op jit(solution)/shard_map/ppermute | solution.py:41
  11.4 0.0 copy-done.1
  11.4 0.1 fusion.25
  11.5 0.2 reduce_window_sum.11
  11.7 0.2 select_reduce_fusion
  11.9 1.2 %collective-permute-done.2 = bf16[4,48,256]{2,1,0:T(8,128)(2,1)S(1)} collective-permute-done((bf16[4,48,256]{2,1,0:T(8,128)(2,1)S(1)}, bf16[4,48,256]{2,1,0:T(8,128)(2,1)S(1)}, u32[]{:S(2)}, u32[]{:S(2)}) %collective-permute-start.2) | collective-permute-done | bytes 98336 | tf_op jit(solution)/shard_map/ppermute | solution.py:41
  13.2 3.5 %collective-permute-done.1 = bf16[4,48,256]{2,1,0:T(8,128)(2,1)S(1)} collective-permute-done((bf16[4,48,256]{2,1,0:T(8,128)(2,1)S(1)}, bf16[4,48,256]{2,1,0:T(8,128)(2,1)S(1)}, u32[]{:S(2)}, u32[]{:S(2)}) %collective-permute-start.1) | collective-permute-done | bytes 98336 | tf_op jit(solution)/shard_map/ppermute | solution.py:41
  16.7 0.0 collective-permute-done
  16.7 1.6 %collective-permute-start.4 = (bf16[4,144,256]{2,1,0:T(8,128)(2,1)S(1)}, bf16[4,144,256]{2,1,0:T(8,128)(2,1)S(1)}, u32[]{:S(2)}, u32[]{:S(2)}) collective-permute-start(bf16[4,144,256]{2,1,0:T(8,128)(2,1)S(1)} %pad_maximum_fusion), channel_id=1, source_target_pairs={{0,4},{1,5},{2,6},{3,7},{4,0},{5,1},{6,2},{7,3},{8,12},{9,13},{10,... | collective-permute-start | bytes 884744 | tf_op jit(solution)/shard_map/ppermute | solution.py:50
  18.3 1.5 %collective-permute-start.3 = (bf16[4,144,256]{2,1,0:T(8,128)(2,1)S(1)}, bf16[4,144,256]{2,1,0:T(8,128)(2,1)S(1)}, u32[]{:S(2)}, u32[]{:S(2)}) collective-permute-start(bf16[4,144,256]{2,1,0:T(8,128)(2,1)S(1)} %pad_maximum_fusion), channel_id=1, source_target_pairs={{0,2},{1,3},{2,0},{3,1},{4,6},{5,7},{6,4},{7,5},{8,10},{9,11},{10,... | collective-permute-start | bytes 884744 | tf_op jit(solution)/shard_map/ppermute | solution.py:49
  19.8 0.0 collective-permute-start.7
  19.8 0.1 copy.6
  19.9 0.3 convolution_bitcast_fusion.5
  20.2 5.4 %collective-permute-done.4 = bf16[4,144,256]{2,1,0:T(8,128)(2,1)S(1)} collective-permute-done((bf16[4,144,256]{2,1,0:T(8,128)(2,1)S(1)}, bf16[4,144,256]{2,1,0:T(8,128)(2,1)S(1)}, u32[]{:S(2)}, u32[]{:S(2)}) %collective-permute-start.4) | collective-permute-done | bytes 294944 | tf_op jit(solution)/shard_map/ppermute | solution.py:50
  25.6 1.6 %collective-permute-start.5 = (bf16[4,144,128]{2,1,0:T(8,128)(2,1)S(1)}, bf16[4,144,128]{2,1,0:T(8,128)(2,1)S(1)}, u32[]{:S(2)}, u32[]{:S(2)}) collective-permute-start(bf16[4,144,128]{2,1,0:T(8,128)(2,1)S(1)} %slice.8), channel_id=1, source_target_pairs={{0,2},{1,3},{2,0},{3,1},{4,6},{5,7},{6,4},{7,5},{8,10},{9,11},{10,... | collective-permute-start | bytes 442376 | tf_op jit(solution)/shard_map/ppermute | solution.py:54
  27.2 0.0 collective-permute-done.3
  27.2 1.6 %collective-permute-start.6 = (bf16[4,144,128]{2,1,0:T(8,128)(2,1)S(1)}, bf16[4,144,128]{2,1,0:T(8,128)(2,1)S(1)}, u32[]{:S(2)}, u32[]{:S(2)}) collective-permute-start(bf16[4,144,128]{2,1,0:T(8,128)(2,1)S(1)} %slice.9), channel_id=1, source_target_pairs={{0,4},{1,5},{2,6},{3,7},{4,0},{5,1},{6,2},{7,3},{8,12},{9,13},{10,... | collective-permute-start | bytes 442376 | tf_op jit(solution)/shard_map/ppermute | solution.py:55
  28.8 0.0 collective-permute-start.9
  28.8 0.5 %collective-permute-start.8 = (bf16[4,144,256]{2,1,0:T(8,128)(2,1)S(1)}, bf16[4,144,256]{2,1,0:T(8,128)(2,1)S(1)}, u32[]{:S(2)}, u32[]{:S(2)}) collective-permute-start(bf16[4,144,256]{2,1,0:T(8,128)(2,1)S(1)} %collective-permute-done.3), channel_id=1, source_target_pairs={{0,1},{1,0},{2,3},{3,2},{4,5},{5,4},{6,7},{7,6},{8,9},{9,8},{10,11... | collective-permute-start | bytes 884744 | tf_op jit(solution)/shard_map/ppermute | solution.py:60
  29.3 0.2 convolution_bitcast_fusion.3
  29.6 0.0 collective-permute-done.7
  29.6 0.2 convolution_bitcast_fusion.2
  29.8 1.0 %collective-permute-done.5 = bf16[4,144,128]{2,1,0:T(8,128)(2,1)S(1)} collective-permute-done((bf16[4,144,128]{2,1,0:T(8,128)(2,1)S(1)}, bf16[4,144,128]{2,1,0:T(8,128)(2,1)S(1)}, u32[]{:S(2)}, u32[]{:S(2)}) %collective-permute-start.5) | collective-permute-done | bytes 147488 | tf_op jit(solution)/shard_map/ppermute | solution.py:54
  30.8 0.0 collective-permute-start.10
  30.8 0.2 convolution_bitcast_fusion.9
  31.0 1.4 %collective-permute-done.6 = bf16[4,144,128]{2,1,0:T(8,128)(2,1)S(1)} collective-permute-done((bf16[4,144,128]{2,1,0:T(8,128)(2,1)S(1)}, bf16[4,144,128]{2,1,0:T(8,128)(2,1)S(1)}, u32[]{:S(2)}, u32[]{:S(2)}) %collective-permute-start.6) | collective-permute-done | bytes 147488 | tf_op jit(solution)/shard_map/ppermute | solution.py:55
  32.4 0.0 collective-permute-start.11
  32.4 0.2 convolution_bitcast_fusion.8
  32.6 0.2 fusion.4
  32.9 0.0 collective-permute-done.10
  32.9 0.2 convolution_bitcast_fusion.7
  33.1 0.7 %collective-permute-done.11 = bf16[4,144,128]{2,1,0:T(8,128)(2,1)S(1)} collective-permute-done((bf16[4,144,128]{2,1,0:T(8,128)(2,1)S(1)}, bf16[4,144,128]{2,1,0:T(8,128)(2,1)S(1)}, u32[]{:S(2)}, u32[]{:S(2)}) %collective-permute-start.11) | collective-permute-done | bytes 147488 | tf_op jit(solution)/shard_map/ppermute | solution.py:63
  33.8 0.2 convolution_bitcast_fusion.6
  34.0 0.0 collective-permute-done.9
  34.0 0.2 convolution_bitcast_fusion
  34.2 0.0 collective-permute-done.8
  34.3 0.3 fusion.8
  34.5 0.4 convolution_convert_fusion
  34.9 0.1 copy.8
  35.0 8.1 %all_to_all.12 = bf16[8,32,192]{2,1,0:T(8,128)(2,1)S(1)} all-to-all(bf16[8,32,192]{2,1,0:T(8,128)(2,1)S(1)} %bitcast.57), channel_id=1, replica_groups=mesh['blk'=4,'rows'=8] {'rows'}, dimensions={0} | all-to-all | bytes 196608 | tf_op jit(solution)/shard_map/all_to_all | solution.py:85
  43.1 0.7 %copy.9 = bf16[256,192]{0,1:T(8,128)(2,1)} copy(bf16[256,192]{1,0:T(8,128)(2,1)S(1)} %bitcast.58) | data formatting | bytes 196608 | tf_op jit(solution)/shard_map/all_to_all | solution.py:85
  (5 shorter events, 0.1 us)
Async XLA Ops:
  0.0 1.6 %copy-start = (bf16[4,128,2048]{2,1,0:T(8,128)(2,1)S(1)}, bf16[4,128,2048]{2,1,0:T(8,128)(2,1)}, u32[]{:S(2)}) copy-start(bf16[4,128,2048]{2,1,0:T(8,128)(2,1)} %param.3) | copy-start | bytes 6291460
  0.0 11.4 %copy-start.1 = (s32[128,1]{0,1:T(1,128)S(1)}, s32[128,1]{0,1:T(1,128)}, u32[]{:S(2)}) copy-start(s32[128,1]{0,1:T(1,128)} %param.4) | copy-start | bytes 1540
  4.5 8.7 %collective-permute-start.2 = (bf16[4,48,256]{2,1,0:T(8,128)(2,1)S(1)}, bf16[4,48,256]{2,1,0:T(8,128)(2,1)S(1)}, u32[]{:S(2)}, u32[]{:S(2)}) collective-permute-start(bf16[4,48,256]{2,1,0:T(8,128)(2,1)S(1)} %constant_dynamic-slice_fusion), channel_id=1, source_target_pairs={{0,8},{8,16},{16,24},{24,0},{1,9},{9,17},{17,25},{25,1},{2,10},{10... | collective-permute-start | bytes 294920 | tf_op jit(solution)/shard_map/ppermute | solution.py:41
  7.5 9.2 %collective-permute-start.1 = (bf16[4,48,256]{2,1,0:T(8,128)(2,1)S(1)}, bf16[4,48,256]{2,1,0:T(8,128)(2,1)S(1)}, u32[]{:S(2)}, u32[]{:S(2)}) collective-permute-start(bf16[4,48,256]{2,1,0:T(8,128)(2,1)S(1)} %constant_dynamic-slice_fusion), channel_id=1, source_target_pairs={{0,16},{8,24},{16,0},{24,8},{1,17},{9,25},{17,1},{25,9},{2,18},{10... | collective-permute-start | bytes 294920 | tf_op jit(solution)/shard_map/ppermute | solution.py:41
  10.1 6.6 %collective-permute-start = (bf16[4,48,256]{2,1,0:T(8,128)(2,1)S(1)}, bf16[4,48,256]{2,1,0:T(8,128)(2,1)S(1)}, u32[]{:S(2)}, u32[]{:S(2)}) collective-permute-start(bf16[4,48,256]{2,1,0:T(8,128)(2,1)S(1)} %constant_dynamic-slice_fusion), channel_id=1, source_target_pairs={{0,24},{8,0},{16,8},{24,16},{1,25},{9,1},{17,9},{25,17},{2,26},{10... | collective-permute-start | bytes 294920 | tf_op jit(solution)/shard_map/ppermute | solution.py:41
  16.7 8.9 %collective-permute-start.4 = (bf16[4,144,256]{2,1,0:T(8,128)(2,1)S(1)}, bf16[4,144,256]{2,1,0:T(8,128)(2,1)S(1)}, u32[]{:S(2)}, u32[]{:S(2)}) collective-permute-start(bf16[4,144,256]{2,1,0:T(8,128)(2,1)S(1)} %pad_maximum_fusion), channel_id=1, source_target_pairs={{0,4},{1,5},{2,6},{3,7},{4,0},{5,1},{6,2},{7,3},{8,12},{9,13},{10,... | collective-permute-start | bytes 884744 | tf_op jit(solution)/shard_map/ppermute | solution.py:50
  18.3 8.9 %collective-permute-start.3 = (bf16[4,144,256]{2,1,0:T(8,128)(2,1)S(1)}, bf16[4,144,256]{2,1,0:T(8,128)(2,1)S(1)}, u32[]{:S(2)}, u32[]{:S(2)}) collective-permute-start(bf16[4,144,256]{2,1,0:T(8,128)(2,1)S(1)} %pad_maximum_fusion), channel_id=1, source_target_pairs={{0,2},{1,3},{2,0},{3,1},{4,6},{5,7},{6,4},{7,5},{8,10},{9,11},{10,... | collective-permute-start | bytes 884744 | tf_op jit(solution)/shard_map/ppermute | solution.py:49
  19.8 9.8 %collective-permute-start.7 = (bf16[4,144,256]{2,1,0:T(8,128)(2,1)S(1)}, bf16[4,144,256]{2,1,0:T(8,128)(2,1)S(1)}, u32[]{:S(2)}, u32[]{:S(2)}) collective-permute-start(bf16[4,144,256]{2,1,0:T(8,128)(2,1)S(1)} %pad_maximum_fusion), channel_id=1, source_target_pairs={{0,1},{1,0},{2,3},{3,2},{4,5},{5,4},{6,7},{7,6},{8,9},{9,8},{10,11... | collective-permute-start | bytes 884744 | tf_op jit(solution)/shard_map/ppermute | solution.py:60
  25.6 5.2 %collective-permute-start.5 = (bf16[4,144,128]{2,1,0:T(8,128)(2,1)S(1)}, bf16[4,144,128]{2,1,0:T(8,128)(2,1)S(1)}, u32[]{:S(2)}, u32[]{:S(2)}) collective-permute-start(bf16[4,144,128]{2,1,0:T(8,128)(2,1)S(1)} %slice.8), channel_id=1, source_target_pairs={{0,2},{1,3},{2,0},{3,1},{4,6},{5,7},{6,4},{7,5},{8,10},{9,11},{10,... | collective-permute-start | bytes 442376 | tf_op jit(solution)/shard_map/ppermute | solution.py:54
  27.2 5.2 %collective-permute-start.6 = (bf16[4,144,128]{2,1,0:T(8,128)(2,1)S(1)}, bf16[4,144,128]{2,1,0:T(8,128)(2,1)S(1)}, u32[]{:S(2)}, u32[]{:S(2)}) collective-permute-start(bf16[4,144,128]{2,1,0:T(8,128)(2,1)S(1)} %slice.9), channel_id=1, source_target_pairs={{0,4},{1,5},{2,6},{3,7},{4,0},{5,1},{6,2},{7,3},{8,12},{9,13},{10,... | collective-permute-start | bytes 442376 | tf_op jit(solution)/shard_map/ppermute | solution.py:55
  28.8 5.2 %collective-permute-start.9 = (bf16[4,144,256]{2,1,0:T(8,128)(2,1)S(1)}, bf16[4,144,256]{2,1,0:T(8,128)(2,1)S(1)}, u32[]{:S(2)}, u32[]{:S(2)}) collective-permute-start(bf16[4,144,256]{2,1,0:T(8,128)(2,1)S(1)} %collective-permute-done.4), channel_id=1, source_target_pairs={{0,1},{1,0},{2,3},{3,2},{4,5},{5,4},{6,7},{7,6},{8,9},{9,8},{10,11... | collective-permute-start | bytes 884744 | tf_op jit(solution)/shard_map/ppermute | solution.py:60
  28.8 5.4 %collective-permute-start.8 = (bf16[4,144,256]{2,1,0:T(8,128)(2,1)S(1)}, bf16[4,144,256]{2,1,0:T(8,128)(2,1)S(1)}, u32[]{:S(2)}, u32[]{:S(2)}) collective-permute-start(bf16[4,144,256]{2,1,0:T(8,128)(2,1)S(1)} %collective-permute-done.3), channel_id=1, source_target_pairs={{0,1},{1,0},{2,3},{3,2},{4,5},{5,4},{6,7},{7,6},{8,9},{9,8},{10,11... | collective-permute-start | bytes 884744 | tf_op jit(solution)/shard_map/ppermute | solution.py:60
  30.8 2.1 %collective-permute-start.10 = (bf16[4,144,128]{2,1,0:T(8,128)(2,1)S(1)}, bf16[4,144,128]{2,1,0:T(8,128)(2,1)S(1)}, u32[]{:S(2)}, u32[]{:S(2)}) collective-permute-start(bf16[4,144,128]{2,1,0:T(8,128)(2,1)S(1)} %collective-permute-done.5), channel_id=1, source_target_pairs={{0,1},{1,0},{2,3},{3,2},{4,5},{5,4},{6,7},{7,6},{8,9},{9,8},{10,11... | collective-permute-start | bytes 442376 | tf_op jit(solution)/shard_map/ppermute | solution.py:62
  32.4 1.4 %collective-permute-start.11 = (bf16[4,144,128]{2,1,0:T(8,128)(2,1)S(1)}, bf16[4,144,128]{2,1,0:T(8,128)(2,1)S(1)}, u32[]{:S(2)}, u32[]{:S(2)}) collective-permute-start(bf16[4,144,128]{2,1,0:T(8,128)(2,1)S(1)} %collective-permute-done.6), channel_id=1, source_target_pairs={{0,1},{1,0},{2,3},{3,2},{4,5},{5,4},{6,7},{7,6},{8,9},{9,8},{10,11... | collective-permute-start | bytes 442376 | tf_op jit(solution)/shard_map/ppermute | solution.py:63
